TPU v7x, 128 devices: a whole 4x4x4 slice. The times are simulated.
128 devices in a mesh: phase: 16 (over z_hi, y, core), axial: 2 (over z_lo), radial: 4 (over x).
Axes of the slice: x: 4, y: 4, z: 4 (z_hi: 2, z_lo: 2; z = z_hi * 2 + z_lo), core: 2. Of those that a mesh axis runs over, the one named last changes fastest.
Arguments:
- psi_start: float32 [16, 10, 8, 64, 128], P('phase', None, 'axial', 'radial'), may hold values from -6 to 6
- source: float32 [16, 10, 8, 64, 128], P('phase', None, 'axial', 'radial'), may hold values from -6 to 6
- face_coef: bfloat16 [6, 8, 64, 128], P(None, 'axial', 'radial'), may hold values from 0.099609375 to 1
- diag_coef: float32 [8, 64, 128], P('axial', 'radial'), may hold values from 6 to 10
- flux_jac: float32 [6, 2, 5, 5], replicated, may hold values from -2 to 2
- omega: float32 [1], replicated, may hold values from 0.5 to 2
- metric: float32 [3, 10], replicated, may hold values from -2 to 2
- mode_shape: bfloat16 [12, 3, 8, 64, 128], P(None, None, 'axial', 'radial'), may hold values from -6 to 6
- phase_weight: float32 [16], P('phase'), may hold values from 0.05 to 0.5
- pairing: int32 [2, 4, 64], P('axial', 'radial'), may hold values from 0 to 63, each once within a row
- owner_order: int32 [2, 4, 8192], P('axial', 'radial'), may hold values from 0 to 8191, each once within a row
Outputs:
- psi_out: float32 [16, 10, 8, 64, 128], P('phase', None, 'axial', 'radial')
- sens: float32 [12, 2, 4, 8192], P(None, 'axial', 'radial', 'phase')
Inputs may be any that keep to these rules, and one draw needn't show every extreme that they name: `pairing`: each tile's row is a permutation of its pitch-end nodes. `owner_order`: each tile's row is a permutation of its cells.
All inputs are finite; a program needn't handle non-finite values.
Results may differ from a plain program's by a relative error of at most 0.0003.
Values sent between devices are 32-bit elements; how exact they have to be, the bound alone decides.
No kernel may reach another device: no remote copies, remote signals or barrier semaphores. Data moves between devices by JAX's collectives and lax.ppermute only.
A program may use at most 64 MiB of HBM per device.

v0:
```python
import math

import jax
import jax.numpy as jnp
from jax import lax
from jax.sharding import PartitionSpec as P

BLADES = 16
ITERS = 4


RELAX = 0.8


def padded(value, sides, width):
    for axis, dim in sides:
        count, length = (lax.axis_size(axis), value.shape[dim])
        up = [(i, (i + 1) % count) for i in range(count - 1)]
        down = [(j, i) for i, j in up]
        last = lax.slice_in_dim(value, length - width, length, axis=dim)
        leading = lax.slice_in_dim(value, 0, width, axis=dim)
        before = lax.ppermute(last, axis, up)
        after = lax.ppermute(leading, axis, down)
        value = jnp.concatenate([before, value, after], axis=dim)
    return value


def split_up(value, dim, count):
    dims = value.shape
    blocks = value.reshape(*dims[:dim], count, dims[dim] // count, *dims[dim + 1 :])
    return jnp.moveaxis(blocks, dim, 0)


def sum_at_owner(value, axis, dim):
    count = lax.axis_size(axis)
    blocks = lax.all_to_all(split_up(value, dim, count), axis, 0, 0, tiled=True)
    return jnp.sum(blocks, axis=0)


def build_matrices(flux_jac):
    real_part = jnp.swapaxes(flux_jac[:, 0], 1, 2)
    imag_part = jnp.swapaxes(flux_jac[:, 1], 1, 2)
    top_rows = jnp.concatenate([real_part, imag_part], axis=2)
    low_rows = jnp.concatenate([-imag_part, real_part], axis=2)
    return jnp.concatenate([top_rows, low_rows], axis=1)


def rotate(values, angle):
    shape = (-1,) + (1,) * (values.ndim - 1)
    cosine = jnp.cos(angle).reshape(shape)
    sine = jnp.sin(angle).reshape(shape)
    half = values.shape[1] // 2
    real_part = values[:, :half]
    imag_part = values[:, half:]
    return jnp.concatenate(
        [cosine * real_part - sine * imag_part, sine * real_part + cosine * imag_part], axis=1
    )


def pair_face(face, partner):
    phases, comps, tile_a, tile_r = face.shape
    flat = face.reshape(phases, comps, tile_a * tile_r)
    return jnp.take(flat, partner, axis=2).reshape(phases, comps, tile_a, tile_r)


def body(
    psi_start,
    source,
    face_coef,
    diag_coef,
    flux_jac,
    omega,
    metric,
    mode_shape,
    phase_weight,
    pairing,
    owner_order,
):
    matrices = build_matrices(flux_jac)
    comps = matrices.shape[1]
    stacked = matrices.reshape(6 * comps, comps)
    coef = face_coef.astype(jnp.float32)
    local_phases, _, tile_a, tile_r, pitch = psi_start.shape
    first = lax.axis_index("phase") * local_phases
    angle = (first + jnp.arange(local_phases, dtype=jnp.int32)).astype(jnp.float32) * (
        2.0 * math.pi / BLADES
    )
    half = comps // 2
    partner = pairing[0, 0]
    psi = psi_start
    for section in range(ITERS):
        flat = psi.reshape(local_phases, comps, tile_a * tile_r * pitch)
        applied = jnp.einsum("yc,pcn->pyn", stacked, flat, precision=lax.Precision.HIGHEST)
        applied = applied.reshape(local_phases, 6, comps, tile_a, tile_r, pitch)
        parts = [applied[:, d] * coef[d][None, None] for d in range(6)]
        axial_edge = jnp.concatenate([parts[1][:, :, :1], parts[0][:, :, -1:]], axis=2)
        radial_edge = jnp.concatenate([parts[3][:, :, :, :1], parts[2][:, :, :, -1:]], axis=3)
        axial_got = padded(axial_edge, (("axial", 2),), 1)
        radial_got = padded(radial_edge, (("radial", 3),), 1)
        plus_wrap = rotate(pair_face(parts[4][..., -1], partner), angle)
        minus_wrap = rotate(pair_face(parts[5][..., 0], partner), -angle)
        from_lower_a = jnp.concatenate([axial_got[:, :, 0:1], parts[0][:, :, :-1]], axis=2)
        from_upper_a = jnp.concatenate([parts[1][:, :, 1:], axial_got[:, :, 3:4]], axis=2)
        from_lower_r = jnp.concatenate([radial_got[:, :, :, 0:1], parts[2][:, :, :, :-1]], axis=3)
        from_upper_r = jnp.concatenate([parts[3][:, :, :, 1:], radial_got[:, :, :, 3:4]], axis=3)
        from_lower_t = jnp.concatenate([plus_wrap[..., None], parts[4][..., :-1]], axis=4)
        from_upper_t = jnp.concatenate([parts[5][..., 1:], minus_wrap[..., None]], axis=4)
        swapped = jnp.concatenate([psi[:, half:], -psi[:, :half]], axis=1)
        residual = (
            source
            - (diag_coef * psi + omega[0] * swapped)
            + (
                from_lower_a
                + from_upper_a
                + from_lower_r
                + from_upper_r
                + from_lower_t
                + from_upper_t
            )
        )
        psi = psi + RELAX * residual / diag_coef
    cells = tile_a * tile_r * pitch
    heights = jnp.einsum(
        "dc,pcn->pdn",
        metric,
        psi.reshape(local_phases, comps, cells),
        precision=lax.Precision.HIGHEST,
    )
    weighted = jnp.sum(phase_weight[:, None, None] * heights, axis=0)
    order = owner_order[0, 0]
    owned = cells // lax.axis_size("phase")
    count_k = mode_shape.shape[0]
    modes = mode_shape.reshape(count_k, 3, cells).astype(jnp.float32)
    total = modes[:, 0] * weighted[0] + modes[:, 1] * weighted[1] + modes[:, 2] * weighted[2]
    ordered = jnp.take(total, order, axis=1)
    sens = sum_at_owner(ordered, "phase", 1)
    return (psi, sens.reshape(count_k, 1, 1, owned))


def solution(mesh):
    return jax.shard_map(
        body,
        mesh=mesh,
        in_specs=(
            P("phase", None, "axial", "radial", None),
            P("phase", None, "axial", "radial", None),
            P(None, "axial", "radial", None),
            P("axial", "radial", None),
            P(),
            P(),
            P(),
            P(None, None, "axial", "radial", None),
            P("phase"),
            P("axial", "radial", None),
            P("axial", "radial", None),
        ),
        out_specs=(P("phase", None, "axial", "radial", None), P(None, "axial", "radial", "phase")),
        check_vma=False,
    )
```

profile of v0, /device:TPU:0, one launch (start us, length us, event | category | flops | bytes accessed | tf_op | source)
XLA Modules:
  0.0 190.1 jit_solution(5474043242598856862)
XLA Ops:
  2.9 1.8 fusion.84
  7.0 4.5 %collective-permute-start = (f32[1,10,1,16,128]{4,3,2,1,0:T(8,128)}, f32[1,10,1,16,128]{4,3,2,1,0:T(8,128)}, u32[]{:S(2)}, u32[]{:S(2)}) collective-permute-start(f32[1,10,1,16,128]{4,3,2,1,0:T(8,128)} %slice.481), channel_id=1, source_target_pairs={{0,4},{1,5},{2,6},{3,7},{8,12},{9,13},{10,14},{11,15},{16,20},{17,... | collective-permute-start | bytes 245768 | tf_op jit(solution)/shard_map/ppermute | solution.py:22
  14.1 4.0 %collective-permute-start.2 = (f32[1,10,4,1,128]{4,3,2,1,0:T(1,128)}, f32[1,10,4,1,128]{4,3,2,1,0:T(1,128)}, u32[]{:S(2)}, u32[]{:S(2)}) collective-permute-start(f32[1,10,4,1,128]{4,3,2,1,0:T(1,128)} %slice.489), channel_id=1, source_target_pairs={{0,1},{1,2},{2,3},{4,5},{5,6},{6,7},{8,9},{9,10},{10,11},{12,13},{... | collective-permute-start | bytes 61448 | tf_op jit(solution)/shard_map/ppermute | solution.py:22
  18.7 1.3 collective-permute-start.3
  32.3 7.4 %copy.328 = f32[12,3,4,16,128]{0,4,3,2,1:T(8,128)} copy(bf16[12,3,4,16,128]{4,3,2,1,0:T(8,128)(2,1)} %param.20) | data formatting | bytes 1769472 | tf_op jit(solution)/shard_map/convert_element_type | solution.py:133
  39.6 1.5 fusion.35
  42.0 1.8 fusion.85
  48.8 5.8 %collective-permute-start.4 = (f32[1,10,1,16,128]{4,3,2,1,0:T(8,128)}, f32[1,10,1,16,128]{4,3,2,1,0:T(8,128)}, u32[]{:S(2)}, u32[]{:S(2)}) collective-permute-start(f32[1,10,1,16,128]{4,3,2,1,0:T(8,128)} %slice.510), channel_id=1, source_target_pairs={{0,4},{1,5},{2,6},{3,7},{8,12},{9,13},{10,14},{11,15},{16,20},{17,... | collective-permute-start | bytes 245768 | tf_op jit(solution)/shard_map/ppermute | solution.py:22
  57.1 5.1 %collective-permute-start.6 = (f32[1,10,4,1,128]{4,3,2,1,0:T(1,128)}, f32[1,10,4,1,128]{4,3,2,1,0:T(1,128)}, u32[]{:S(2)}, u32[]{:S(2)}) collective-permute-start(f32[1,10,4,1,128]{4,3,2,1,0:T(1,128)} %slice.516), channel_id=1, source_target_pairs={{0,1},{1,2},{2,3},{4,5},{5,6},{6,7},{8,9},{9,10},{10,11},{12,13},{... | collective-permute-start | bytes 61448 | tf_op jit(solution)/shard_map/ppermute | solution.py:22
  62.9 1.5 collective-permute-start.7
  68.9 1.5 fusion.45
  71.2 1.8 fusion.86
  78.0 5.8 %collective-permute-start.8 = (f32[1,10,1,16,128]{4,3,2,1,0:T(8,128)}, f32[1,10,1,16,128]{4,3,2,1,0:T(8,128)}, u32[]{:S(2)}, u32[]{:S(2)}) collective-permute-start(f32[1,10,1,16,128]{4,3,2,1,0:T(8,128)} %slice.534), channel_id=1, source_target_pairs={{0,4},{1,5},{2,6},{3,7},{8,12},{9,13},{10,14},{11,15},{16,20},{17,... | collective-permute-start | bytes 245768 | tf_op jit(solution)/shard_map/ppermute | solution.py:22
  86.3 4.2 %collective-permute-start.10 = (f32[1,10,4,1,128]{4,3,2,1,0:T(1,128)}, f32[1,10,4,1,128]{4,3,2,1,0:T(1,128)}, u32[]{:S(2)}, u32[]{:S(2)}) collective-permute-start(f32[1,10,4,1,128]{4,3,2,1,0:T(1,128)} %slice.540), channel_id=1, source_target_pairs={{0,1},{1,2},{2,3},{4,5},{5,6},{6,7},{8,9},{9,10},{10,11},{12,13},{... | collective-permute-start | bytes 61448 | tf_op jit(solution)/shard_map/ppermute | solution.py:22
  97.1 1.5 fusion.55
  99.5 1.8 fusion.87
  106.3 5.8 %collective-permute-start.12 = (f32[1,10,1,16,128]{4,3,2,1,0:T(8,128)}, f32[1,10,1,16,128]{4,3,2,1,0:T(8,128)}, u32[]{:S(2)}, u32[]{:S(2)}) collective-permute-start(f32[1,10,1,16,128]{4,3,2,1,0:T(8,128)} %slice.558), channel_id=1, source_target_pairs={{0,4},{1,5},{2,6},{3,7},{8,12},{9,13},{10,14},{11,15},{16,20},{17,... | collective-permute-start | bytes 245768 | tf_op jit(solution)/shard_map/ppermute | solution.py:22
  114.0 4.0 %collective-permute-start.14 = (f32[1,10,4,1,128]{4,3,2,1,0:T(1,128)S(1)}, f32[1,10,4,1,128]{4,3,2,1,0:T(1,128)}, u32[]{:S(2)}, u32[]{:S(2)}) collective-permute-start(f32[1,10,4,1,128]{4,3,2,1,0:T(1,128)S(1)} %slice.564), channel_id=1, source_target_pairs={{0,1},{1,2},{2,3},{4,5},{5,6},{6,7},{8,9},{9,10},{10,11},{12,13},{... | collective-permute-start | bytes 61448 | tf_op jit(solution)/shard_map/ppermute | solution.py:22
  120.9 3.8 %collective-permute-done.15 = f32[1,10,4,1,128]{4,3,2,1,0:T(1,128)} collective-permute-done((f32[1,10,4,1,128]{4,3,2,1,0:T(1,128)}, f32[1,10,4,1,128]{4,3,2,1,0:T(1,128)}, u32[]{:S(2)}, u32[]{:S(2)}) %collective-permute-start.15) | collective-permute-done | bytes 20512 | tf_op jit(solution)/shard_map/ppermute | solution.py:23
  124.6 1.5 fusion.65
  126.8 9.9 %fusion.2 = f32[12,8192]{0,1:T(8,128)} fusion(f32[12,3,8192]{0,2,1:T(8,128)} %bitcast.342, f32[8192]{0:T(1024)S(1)} %bitcast.388, f32[8192]{0:T(1024)S(1)} %bitcast.389, f32[8192]{0:T(1024)S(1)} %bitcast.387), kind=kLoop, calls=%fused_computation.13 | loop fusion | flops 491520 | bytes 1671168 | tf_op jit(solution)/shard_map/add | solution.py:134
  136.7 29.9 %gather_fusion = f32[8192,12]{1,0:T(8,128)} fusion(f32[12,8192]{0,1:T(8,128)} %fusion.2, s32[8192]{0:T(1024)S(1)} %copy-done.22), kind=kCustom, calls=%fused_computation.8 | custom fusion | bytes 819200 | tf_op jit(solution)/shard_map/jit(_take)/gather | solution.py:135
  166.5 2.9 %copy.329 = f32[12,16,512]{2,0,1:T(8,128)S(1)} copy(f32[12,16,512]{0,2,1:T(8,128)} %bitcast.356) | data formatting | bytes 786432 | tf_op jit(solution)/shard_map/jit(_take)/gather | solution.py:135
  169.5 19.7 %all_to_all.5 = f32[16,12,512]{2,1,0:T(8,128)S(1)} all-to-all(f32[16,12,512]{2,1,0:T(8,128)S(1)} %select_bitcast_fusion), channel_id=1, replica_groups=mesh['phase'=16,'axial'=2,'radial'=4] {'phase'}, dimensions={0} | all-to-all | bytes 786432 | tf_op jit(solution)/shard_map/all_to_all | solution.py:36
  (230 shorter events, 58.2 us)
Async XLA Ops:
  0.6 125.6 %copy-start = (f32[3,10]{1,0:T(4,128)S(1)}, f32[3,10]{1,0:T(4,128)}, u32[]{:S(2)}) copy-start(f32[3,10]{1,0:T(4,128)} %param.19) | copy-start | bytes 364
  6.1 13.9 %copy-start.29 = (s32[1,1,64]{2,1,0:T(1,128)S(1)}, s32[1,1,64]{2,1,0:T(1,128)}, u32[]{:S(2)}) copy-start(s32[1,1,64]{2,1,0:T(1,128)} %param.22) | copy-start | bytes 772
  6.1 14.8 %copy-start.2 = (f32[1,10,4,16,128]{4,3,2,1,0:T(8,128)S(1)}, f32[1,10,4,16,128]{4,3,2,1,0:T(8,128)}, u32[]{:S(2)}) copy-start(f32[1,10,4,16,128]{4,3,2,1,0:T(8,128)} %param.13) | copy-start | bytes 983044
  6.1 15.5 %copy-start.9 = (f32[4,16,128]{2,1,0:T(8,128)}, f32[4,16,128]{2,1,0:T(8,128)S(1)}, u32[]{:S(2)}) copy-start(f32[4,16,128]{2,1,0:T(8,128)S(1)} %get-tuple-element.40) | copy-start | bytes 98308
  6.1 15.5 %copy-start.13 = (f32[4,16,128]{2,1,0:T(8,128)}, f32[4,16,128]{2,1,0:T(8,128)S(1)}, u32[]{:S(2)}) copy-start(f32[4,16,128]{2,1,0:T(8,128)S(1)} %get-tuple-element.41) | copy-start | bytes 98308
  6.1 16.1 %copy-start.17 = (f32[4,16,128]{2,1,0:T(8,128)}, f32[4,16,128]{2,1,0:T(8,128)S(1)}, u32[]{:S(2)}) copy-start(f32[4,16,128]{2,1,0:T(8,128)S(1)} %get-tuple-element.36) | copy-start | bytes 98308
  6.4 18.8 %copy-start.23 = (s32[1,1,8192]{2,1,0:T(1,128)S(1)}, s32[1,1,8192]{2,1,0:T(1,128)}, u32[]{:S(2)}) copy-start(s32[1,1,8192]{2,1,0:T(1,128)} %param.23) | copy-start | bytes 98308
  7.0 32.6 %collective-permute-start = (f32[1,10,1,16,128]{4,3,2,1,0:T(8,128)}, f32[1,10,1,16,128]{4,3,2,1,0:T(8,128)}, u32[]{:S(2)}, u32[]{:S(2)}) collective-permute-start(f32[1,10,1,16,128]{4,3,2,1,0:T(8,128)} %slice.481), channel_id=1, source_target_pairs={{0,4},{1,5},{2,6},{3,7},{8,12},{9,13},{10,14},{11,15},{16,20},{17,... | collective-permute-start | bytes 245768 | tf_op jit(solution)/shard_map/ppermute | solution.py:22
  12.2 27.5 %collective-permute-start.1 = (f32[1,10,1,16,128]{4,3,2,1,0:T(8,128)}, f32[1,10,1,16,128]{4,3,2,1,0:T(8,128)}, u32[]{:S(2)}, u32[]{:S(2)}) collective-permute-start(f32[1,10,1,16,128]{4,3,2,1,0:T(8,128)} %slice.486), channel_id=1, source_target_pairs={{4,0},{5,1},{6,2},{7,3},{12,8},{13,9},{14,10},{15,11},{20,16},{21,... | collective-permute-start | bytes 245768 | tf_op jit(solution)/shard_map/ppermute | solution.py:23
  14.1 25.5 %collective-permute-start.2 = (f32[1,10,4,1,128]{4,3,2,1,0:T(1,128)}, f32[1,10,4,1,128]{4,3,2,1,0:T(1,128)}, u32[]{:S(2)}, u32[]{:S(2)}) collective-permute-start(f32[1,10,4,1,128]{4,3,2,1,0:T(1,128)} %slice.489), channel_id=1, source_target_pairs={{0,1},{1,2},{2,3},{4,5},{5,6},{6,7},{8,9},{9,10},{10,11},{12,13},{... | collective-permute-start | bytes 61448 | tf_op jit(solution)/shard_map/ppermute | solution.py:22
  18.7 20.9 %collective-permute-start.3 = (f32[1,10,4,1,128]{4,3,2,1,0:T(1,128)}, f32[1,10,4,1,128]{4,3,2,1,0:T(1,128)}, u32[]{:S(2)}, u32[]{:S(2)}) collective-permute-start(f32[1,10,4,1,128]{4,3,2,1,0:T(1,128)} %slice.494), channel_id=1, source_target_pairs={{1,0},{2,1},{3,2},{5,4},{6,5},{7,6},{9,8},{10,9},{11,10},{13,12},{... | collective-permute-start | bytes 61448 | tf_op jit(solution)/shard_map/ppermute | solution.py:23
  48.8 20.1 %collective-permute-start.4 = (f32[1,10,1,16,128]{4,3,2,1,0:T(8,128)}, f32[1,10,1,16,128]{4,3,2,1,0:T(8,128)}, u32[]{:S(2)}, u32[]{:S(2)}) collective-permute-start(f32[1,10,1,16,128]{4,3,2,1,0:T(8,128)} %slice.510), channel_id=1, source_target_pairs={{0,4},{1,5},{2,6},{3,7},{8,12},{9,13},{10,14},{11,15},{16,20},{17,... | collective-permute-start | bytes 245768 | tf_op jit(solution)/shard_map/ppermute | solution.py:22
  55.2 13.7 %collective-permute-start.5 = (f32[1,10,1,16,128]{4,3,2,1,0:T(8,128)}, f32[1,10,1,16,128]{4,3,2,1,0:T(8,128)}, u32[]{:S(2)}, u32[]{:S(2)}) collective-permute-start(f32[1,10,1,16,128]{4,3,2,1,0:T(8,128)} %slice.514), channel_id=1, source_target_pairs={{4,0},{5,1},{6,2},{7,3},{12,8},{13,9},{14,10},{15,11},{20,16},{21,... | collective-permute-start | bytes 245768 | tf_op jit(solution)/shard_map/ppermute | solution.py:23
  57.1 10.8 %collective-permute-start.6 = (f32[1,10,4,1,128]{4,3,2,1,0:T(1,128)}, f32[1,10,4,1,128]{4,3,2,1,0:T(1,128)}, u32[]{:S(2)}, u32[]{:S(2)}) collective-permute-start(f32[1,10,4,1,128]{4,3,2,1,0:T(1,128)} %slice.516), channel_id=1, source_target_pairs={{0,1},{1,2},{2,3},{4,5},{5,6},{6,7},{8,9},{9,10},{10,11},{12,13},{... | collective-permute-start | bytes 61448 | tf_op jit(solution)/shard_map/ppermute | solution.py:22
  62.9 6.0 %collective-permute-start.7 = (f32[1,10,4,1,128]{4,3,2,1,0:T(1,128)}, f32[1,10,4,1,128]{4,3,2,1,0:T(1,128)}, u32[]{:S(2)}, u32[]{:S(2)}) collective-permute-start(f32[1,10,4,1,128]{4,3,2,1,0:T(1,128)} %slice.520), channel_id=1, source_target_pairs={{1,0},{2,1},{3,2},{5,4},{6,5},{7,6},{9,8},{10,9},{11,10},{13,12},{... | collective-permute-start | bytes 61448 | tf_op jit(solution)/shard_map/ppermute | solution.py:23
  78.0 19.1 %collective-permute-start.8 = (f32[1,10,1,16,128]{4,3,2,1,0:T(8,128)}, f32[1,10,1,16,128]{4,3,2,1,0:T(8,128)}, u32[]{:S(2)}, u32[]{:S(2)}) collective-permute-start(f32[1,10,1,16,128]{4,3,2,1,0:T(8,128)} %slice.534), channel_id=1, source_target_pairs={{0,4},{1,5},{2,6},{3,7},{8,12},{9,13},{10,14},{11,15},{16,20},{17,... | collective-permute-start | bytes 245768 | tf_op jit(solution)/shard_map/ppermute | solution.py:22
  84.4 12.7 %collective-permute-start.9 = (f32[1,10,1,16,128]{4,3,2,1,0:T(8,128)}, f32[1,10,1,16,128]{4,3,2,1,0:T(8,128)}, u32[]{:S(2)}, u32[]{:S(2)}) collective-permute-start(f32[1,10,1,16,128]{4,3,2,1,0:T(8,128)} %slice.538), channel_id=1, source_target_pairs={{4,0},{5,1},{6,2},{7,3},{12,8},{13,9},{14,10},{15,11},{20,16},{21,... | collective-permute-start | bytes 245768 | tf_op jit(solution)/shard_map/ppermute | solution.py:23
  86.3 9.6 %collective-permute-start.10 = (f32[1,10,4,1,128]{4,3,2,1,0:T(1,128)}, f32[1,10,4,1,128]{4,3,2,1,0:T(1,128)}, u32[]{:S(2)}, u32[]{:S(2)}) collective-permute-start(f32[1,10,4,1,128]{4,3,2,1,0:T(1,128)} %slice.540), channel_id=1, source_target_pairs={{0,1},{1,2},{2,3},{4,5},{5,6},{6,7},{8,9},{9,10},{10,11},{12,13},{... | collective-permute-start | bytes 61448 | tf_op jit(solution)/shard_map/ppermute | solution.py:22
  91.1 6.0 %collective-permute-start.11 = (f32[1,10,4,1,128]{4,3,2,1,0:T(1,128)}, f32[1,10,4,1,128]{4,3,2,1,0:T(1,128)}, u32[]{:S(2)}, u32[]{:S(2)}) collective-permute-start(f32[1,10,4,1,128]{4,3,2,1,0:T(1,128)} %slice.544), channel_id=1, source_target_pairs={{1,0},{2,1},{3,2},{5,4},{6,5},{7,6},{9,8},{10,9},{11,10},{13,12},{... | collective-permute-start | bytes 61448 | tf_op jit(solution)/shard_map/ppermute | solution.py:23
  105.0 19.6 %copy-start.21 = (f32[4,16,128]{2,1,0:T(8,128)S(1)}, f32[4,16,128]{2,1,0:T(8,128)}, u32[]{:S(2)}) copy-start(f32[4,16,128]{2,1,0:T(8,128)} %param.16) | copy-start | bytes 98308
  106.3 18.3 %collective-permute-start.12 = (f32[1,10,1,16,128]{4,3,2,1,0:T(8,128)}, f32[1,10,1,16,128]{4,3,2,1,0:T(8,128)}, u32[]{:S(2)}, u32[]{:S(2)}) collective-permute-start(f32[1,10,1,16,128]{4,3,2,1,0:T(8,128)} %slice.558), channel_id=1, source_target_pairs={{0,4},{1,5},{2,6},{3,7},{8,12},{9,13},{10,14},{11,15},{16,20},{17,... | collective-permute-start | bytes 245768 | tf_op jit(solution)/shard_map/ppermute | solution.py:22
  112.7 11.9 %collective-permute-start.13 = (f32[1,10,1,16,128]{4,3,2,1,0:T(8,128)}, f32[1,10,1,16,128]{4,3,2,1,0:T(8,128)}, u32[]{:S(2)}, u32[]{:S(2)}) collective-permute-start(f32[1,10,1,16,128]{4,3,2,1,0:T(8,128)} %slice.562), channel_id=1, source_target_pairs={{4,0},{5,1},{6,2},{7,3},{12,8},{13,9},{14,10},{15,11},{20,16},{21,... | collective-permute-start | bytes 245768 | tf_op jit(solution)/shard_map/ppermute | solution.py:23
  114.0 6.8 %collective-permute-start.14 = (f32[1,10,4,1,128]{4,3,2,1,0:T(1,128)S(1)}, f32[1,10,4,1,128]{4,3,2,1,0:T(1,128)}, u32[]{:S(2)}, u32[]{:S(2)}) collective-permute-start(f32[1,10,4,1,128]{4,3,2,1,0:T(1,128)S(1)} %slice.564), channel_id=1, source_target_pairs={{0,1},{1,2},{2,3},{4,5},{5,6},{6,7},{8,9},{9,10},{10,11},{12,13},{... | collective-permute-start | bytes 61448 | tf_op jit(solution)/shard_map/ppermute | solution.py:22
  118.7 6.0 %collective-permute-start.15 = (f32[1,10,4,1,128]{4,3,2,1,0:T(1,128)}, f32[1,10,4,1,128]{4,3,2,1,0:T(1,128)}, u32[]{:S(2)}, u32[]{:S(2)}) collective-permute-start(f32[1,10,4,1,128]{4,3,2,1,0:T(1,128)} %slice.568), channel_id=1, source_target_pairs={{1,0},{2,1},{3,2},{5,4},{6,5},{7,6},{9,8},{10,9},{11,10},{13,12},{... | collective-permute-start | bytes 61448 | tf_op jit(solution)/shard_map/ppermute | solution.py:23
  (22 other events, 97.9 us)
where the time goes:
time: 192 us; the launch traced here: 190 us
  local copies, waits for them, and re-layouts  77.5 us (40%)
  starting transfers between devices  49.6 us (26%)
  other arithmetic  26.4 us (14%)
  blocking collectives  19.7 us (10%)
  matrix products  7.76 us (4%)
  waiting for transfers between devices  5.94 us (3%)
  between operations  3.12 us (2%)
    ppermute x8, starting transfers between devices, padded(): before = lax.ppermute(last, axis, up)  39.2 us
    gather x2, local copies, waits for them, and re-layouts, body(): ordered = jnp.take(total, order, axis=1)  32.7 us
    all_to_all x1, blocking collectives, sum_at_owner(): blocks = lax.all_to_all(split_up(value, dim, count), axis, 0, 0, tiled=True)  19.7 us
    ppermute x8, starting transfers between devices, padded(): after = lax.ppermute(leading, axis, down)  10.4 us
    add x1, other arithmetic, body(): modes[:, 0] * weighted[0] + modes[:, 1] * weighted[1]  9.86 us
    unnamed x89, local copies, waits for them, and re-layouts  7.92 us
    convert_element_type x1, local copies, waits for them, and re-layouts, body(): modes = mode_shape.reshape(count_k, 3, cells).astype(jnp.float32)  7.36 us
    dot_general x4, matrix products, body(): jnp.einsum('yc,pcn->pyn', stacked, flat, precision=lax.Precision.HIGHEST)  7.32 us
  transfers between devices with their start and end apart: 16, of which 3 were waited for; matrix products, arithmetic and copies ran while one was open for 17% of the time, Pallas kernels for 0%

commit v1 on v0

--- a/solution.py
+++ b/solution.py
@@ -23,6 +23,17 @@
         after = lax.ppermute(leading, axis, down)
         value = jnp.concatenate([before, value, after], axis=dim)
     return value
+
+
+def exchange_pair(value, axis, dim):
+    me = lax.axis_index(axis)
+    leading = lax.slice_in_dim(value, 0, 1, axis=dim)
+    last = lax.slice_in_dim(value, value.shape[dim] - 1, value.shape[dim], axis=dim)
+    got = lax.ppermute(jnp.where(me == 0, last, leading), axis, [(0, 1), (1, 0)])
+    zero = jnp.zeros_like(got)
+    before = jnp.where(me == 1, got, zero)
+    after = jnp.where(me == 0, got, zero)
+    return jnp.concatenate([before, value, after], axis=dim)
 
 
 def split_up(value, dim, count):
@@ -95,7 +106,7 @@
         parts = [applied[:, d] * coef[d][None, None] for d in range(6)]
         axial_edge = jnp.concatenate([parts[1][:, :, :1], parts[0][:, :, -1:]], axis=2)
         radial_edge = jnp.concatenate([parts[3][:, :, :, :1], parts[2][:, :, :, -1:]], axis=3)
-        axial_got = padded(axial_edge, (("axial", 2),), 1)
+        axial_got = exchange_pair(axial_edge, "axial", 2) if lax.axis_size("axial") == 2 else padded(axial_edge, (("axial", 2),), 1)
         radial_got = padded(radial_edge, (("radial", 3),), 1)
         plus_wrap = rotate(pair_face(parts[4][..., -1], partner), angle)
         minus_wrap = rotate(pair_face(parts[5][..., 0], partner), -angle)
@@ -128,12 +139,27 @@
     )
     weighted = jnp.sum(phase_weight[:, None, None] * heights, axis=0)
     order = owner_order[0, 0]
-    owned = cells // lax.axis_size("phase")
+    owners = lax.axis_size("phase")
+    owned = cells // owners
+    dims = weighted.shape[0]
+    lanes = 128
+    rows = cells // lanes
+    lane_of = order % lanes
+    row_of = order // lanes
+    pick_lane = (lane_of[None, :] == jnp.arange(lanes, dtype=order.dtype)[:, None]).astype(jnp.float32)
+    by_lane = jnp.einsum(
+        "xl,lj->xj",
+        weighted.reshape(dims * rows, lanes),
+        pick_lane,
+        precision=lax.Precision.HIGHEST,
+    ).reshape(dims, rows, cells)
+    pick_row = row_of[None, None, :] == jnp.arange(rows, dtype=order.dtype)[None, :, None]
+    in_order = jnp.sum(jnp.where(pick_row, by_lane, 0.0), axis=1)
+    gathered = sum_at_owner(in_order, "phase", 1)
+    mine = lax.dynamic_slice_in_dim(order, lax.axis_index("phase") * owned, owned)
     count_k = mode_shape.shape[0]
-    modes = mode_shape.reshape(count_k, 3, cells).astype(jnp.float32)
-    total = modes[:, 0] * weighted[0] + modes[:, 1] * weighted[1] + modes[:, 2] * weighted[2]
-    ordered = jnp.take(total, order, axis=1)
-    sens = sum_at_owner(ordered, "phase", 1)
+    modes = jnp.take(mode_shape.reshape(count_k, 3, cells), mine, axis=2).astype(jnp.float32)
+    sens = modes[:, 0] * gathered[0] + modes[:, 1] * gathered[1] + modes[:, 2] * gathered[2]
     return (psi, sens.reshape(count_k, 1, 1, owned))
 
 

time: 192 us -> 152 us (0.79)
  blocking collectives: 19.7 us -> 0 us
  local copies, waits for them, and re-layouts: 77.5 us -> 62.9 us
  starting transfers between devices: 49.6 us -> 37.2 us
  matrix products: 7.76 us -> 12.7 us
    gather x2 -> x1, local copies, waits for them, and re-layouts: 32.7 us -> 5.61 us  [body(): jnp.take(mode_shape.reshape(count_k, 3, cells), mine, axis=2)]
    ppermute x8 -> x4, starting transfers between devices: 39.2 us -> 19.4 us  [padded(): before = lax.ppermute(last, axis, up)]
    all_to_all x1 -> x0, blocking collectives: 19.7 us -> none  [sum_at_owner(): blocks = lax.all_to_all(split_up(value, dim, count), axis, 0, 0, tiled=True)]
    add x1, other arithmetic: 9.86 us -> 0.27 us  [body(): modes[:, 0] * gathered[0] + modes[:, 1] * gathered[1]]
    all_to_all x0 -> x1, starting transfers between devices: none -> 7.88 us  [sum_at_owner(): blocks = lax.all_to_all(split_up(value, dim, count), axis, 0, 0, tiled=True)]
    all_to_all x0 -> x1, waiting for transfers between devices: none -> 7.44 us  [sum_at_owner(): blocks = lax.all_to_all(split_up(value, dim, count), axis, 0, 0, tiled=True)]
    convert_element_type x1 -> x0, local copies, waits for them, and re-layouts: 7.36 us -> none  [body(): modes = mode_shape.reshape(count_k, 3, cells).astype(jnp.float32)]
    select_n x1 -> x11, other arithmetic: 0.06 us -> 6.95 us  [the longest x4 3.6 us: exchange_pair(): after = jnp.where(me == 0, got, zero)]
  transfers between devices with their start and end apart: 16 -> 13, of which waited for: 3 -> 1; matrix products, arithmetic and copies ran while one was open for 17% -> 42% of each run, Pallas kernels for 0% -> 0%
where the time goes in v1:
time: 152 us; the launch traced here: 149 us
  local copies, waits for them, and re-layouts  62.9 us (41%)
  starting transfers between devices  37.2 us (24%)
  other arithmetic  25.7 us (17%)
  matrix products  12.7 us (8%)
  waiting for transfers between devices  7.47 us (5%)
  between operations  3.08 us (2%)
    ppermute x4, starting transfers between devices, padded(): before = lax.ppermute(last, axis, up)  19.4 us
    unnamed x60, local copies, waits for them, and re-layouts  13.5 us
    gather x8, local copies, waits for them, and re-layouts, pair_face(): jnp.take(flat, partner, axis=2).reshape(phases, comps, tile_a, tile_r)  11.1 us
    all_to_all x1, starting transfers between devices, sum_at_owner(): blocks = lax.all_to_all(split_up(value, dim, count), axis, 0, 0, tiled=True)  7.88 us
    add x4, other arithmetic, body(): psi = psi + RELAX * residual / diag_coef  7.6 us
    all_to_all x1, waiting for transfers between devices, sum_at_owner(): blocks = lax.all_to_all(split_up(value, dim, count), axis, 0, 0, tiled=True)  7.44 us
    dot_general x4, matrix products, body(): jnp.einsum('yc,pcn->pyn', stacked, flat, precision=lax.Precision.HIGHEST)  7.33 us
    gather x1, local copies, waits for them, and re-layouts, body(): jnp.take(mode_shape.reshape(count_k, 3, cells), mine, axis=2)  5.61 us
  transfers between devices with their start and end apart: 13, of which 1 were waited for; matrix products, arithmetic and copies ran while one was open for 42% of the time, Pallas kernels for 0%

profile of v1, /device:TPU:0, one launch (start us, length us, event | category | flops | bytes accessed | tf_op | source)
XLA Modules:
  0.0 149.1 jit_solution(1163138416343323284)
XLA Ops:
  2.9 1.8 %fusion.89 = f32[60,8192]{1,0:T(8,128)S(1)} fusion(f32[60,10]{0,1:T(8,128)S(1)} %reshape.1465, f32[10,8192]{1,0:T(8,128)S(1)} %reshape.1466), kind=kOutput, calls=%fused_computation.204 | convolution fusion | flops 58982400 | bytes 2296160 | tf_op jit(solution)/shard_map/yc,pcn->pyn/dot_general | solution.py:104
  7.0 2.0 %collective-permute-start = (f32[1,10,1,16,128]{4,3,2,1,0:T(8,128)}, f32[1,10,1,16,128]{4,3,2,1,0:T(8,128)}, u32[]{:S(2)}, u32[]{:S(2)}) collective-permute-start(f32[1,10,1,16,128]{4,3,2,1,0:T(8,128)} %slice_select_fusion.3), channel_id=1, source_target_pairs={{0,4},{4,0},{1,5},{5,1},{2,6},{6,2},{3,7},{7,3},{8,12},{12,8},{9,1... | collective-permute-start | bytes 245768 | tf_op jit(solution)/shard_map/ppermute | solution.py:32
  9.6 4.0 %collective-permute-start.1 = (f32[1,10,4,1,128]{4,3,2,1,0:T(1,128)}, f32[1,10,4,1,128]{4,3,2,1,0:T(1,128)}, u32[]{:S(2)}, u32[]{:S(2)}) collective-permute-start(f32[1,10,4,1,128]{4,3,2,1,0:T(1,128)} %slice.495), channel_id=1, source_target_pairs={{0,1},{1,2},{2,3},{4,5},{5,6},{6,7},{8,9},{9,10},{10,11},{12,13},{... | collective-permute-start | bytes 61448 | tf_op jit(solution)/shard_map/ppermute | solution.py:22
  25.0 6.7 %copy.340 = bf16[12,3,4,16,128]{0,1,4,3,2:T(4,128)(2,1)} copy(bf16[12,3,4,16,128]{4,3,2,1,0:T(8,128)(2,1)S(1)} %copy-done.7) | data formatting | bytes 1179648 | tf_op args[7]
  33.6 5.6 %gather_fusion = bf16[512,12,3]{1,2,0:T(4,128)(2,1)} fusion(bf16[12,3,8192]{0,1,2:T(4,128)(2,1)} %bitcast.341, s32[1024]{0:T(1024)S(1)} %pad_clamp_fusion), kind=kCustom, calls=%fused_computation.8 | custom fusion | bytes 75776 | tf_op jit(solution)/shard_map/jit(_take)/gather | solution.py:161
  39.2 3.0 %convert_bitcast_fusion = f32[12,3,512]{0,1,2:T(4,128)S(1)} fusion(bf16[512,12,3]{1,2,0:T(4,128)(2,1)} %gather_fusion, pred[512]{0:T(512)(128)(4,1)S(1)} %compare_and_fusion.1), kind=kLoop, calls=%fused_computation.17 | loop fusion | flops 36864 | bytes 111104 | tf_op jit(solution)/shard_map/convert_element_type | solution.py:161
  45.6 1.9 %fusion.36 = f32[1,10,4,16,128]{4,3,2,1,0:T(8,128)S(1)} fusion(f32[1,10,4,16,128]{4,3,2,1,0:T(8,128)S(1)} %copy-done.2, f32[1,10,4,16,128]{4,3,2,1,0:T(8,128)S(1)} %copy-done.1, f32[1,5,4,16,128]{4,3,2,1,0:T(8,128)} %get-tuple-element.48, f32[1,5,4,16,128]{4,3,2,1,0:T(8,128)} %get-tuple-element.47, f32[1,10,3,16,128]{4,3,2,1,0:T(8,128)} %slice.491, ...), kind=kLoop, calls=%fused_computation.72 | loop fusion | flops 1638400 | bytes 3309572 | tf_op jit(solution)/shard_map/add | solution.py:132
  48.3 1.8 %fusion.90 = f32[8192,60]{0,1:T(8,128)S(1)} fusion(f32[10,8192]{1,0:T(8,128)S(1)} %reshape.1470, f32[60,10]{0,1:T(8,128)S(1)} %reshape.1465), kind=kOutput, calls=%fused_computation.205 | convolution fusion | flops 58982400 | bytes 2296160 | tf_op jit(solution)/shard_map/yc,pcn->pyn/dot_general | solution.py:104
  54.5 5.1 %collective-permute-start.4 = (f32[1,10,4,1,128]{4,3,2,1,0:T(1,128)}, f32[1,10,4,1,128]{4,3,2,1,0:T(1,128)}, u32[]{:S(2)}, u32[]{:S(2)}) collective-permute-start(f32[1,10,4,1,128]{4,3,2,1,0:T(1,128)} %slice.522), channel_id=1, source_target_pairs={{0,1},{1,2},{2,3},{4,5},{5,6},{6,7},{8,9},{9,10},{10,11},{12,13},{... | collective-permute-start | bytes 61448 | tf_op jit(solution)/shard_map/ppermute | solution.py:22
  62.4 1.9 %gather_fusion.4 = f32[64,10]{1,0:T(8,128)} fusion(f32[10,64]{0,1:T(8,128)} %bitcast.381, s32[1024]{0:T(1024)S(1)} %pad_clamp_fusion.1), kind=kCustom, calls=%fused_computation.3.clone | custom fusion | bytes 5376 | tf_op jit(solution)/shard_map/jit(_take)/gather | solution.py:74
  71.4 1.9 %fusion.46 = f32[1,10,4,16,128]{4,3,2,1,0:T(8,128)S(1)} fusion(f32[1,10,4,16,128]{4,3,2,1,0:T(8,128)S(1)} %fusion.36, f32[1,10,4,16,128]{4,3,2,1,0:T(8,128)S(1)} %copy-done.1, f32[1,5,4,16,128]{4,3,2,1,0:T(8,128)} %get-tuple-element.46, f32[1,5,4,16,128]{4,3,2,1,0:T(8,128)} %get-tuple-element.45, f32[1,10,3,16,128]{4,3,2,1,0:T(8,128)} %slice.519, ...), kind=kLoop, calls=%fused_computation.84 | loop fusion | flops 1638400 | bytes 3309572 | tf_op jit(solution)/shard_map/add | solution.py:132
  74.1 1.8 %fusion.91 = f32[8192,60]{0,1:T(8,128)S(1)} fusion(f32[10,8192]{1,0:T(8,128)S(1)} %reshape.1474, f32[60,10]{0,1:T(8,128)S(1)} %reshape.1465), kind=kOutput, calls=%fused_computation.206 | convolution fusion | flops 58982400 | bytes 2296160 | tf_op jit(solution)/shard_map/yc,pcn->pyn/dot_general | solution.py:104
  79.5 2.0 %collective-permute-start.6 = (f32[1,10,1,16,128]{4,3,2,1,0:T(8,128)}, f32[1,10,1,16,128]{4,3,2,1,0:T(8,128)}, u32[]{:S(2)}, u32[]{:S(2)}) collective-permute-start(f32[1,10,1,16,128]{4,3,2,1,0:T(8,128)} %slice_select_fusion.1), channel_id=1, source_target_pairs={{0,4},{4,0},{1,5},{5,1},{2,6},{6,2},{3,7},{7,3},{8,12},{12,8},{9,1... | collective-permute-start | bytes 245768 | tf_op jit(solution)/shard_map/ppermute | solution.py:32
  82.2 5.1 %collective-permute-start.7 = (f32[1,10,4,1,128]{4,3,2,1,0:T(1,128)}, f32[1,10,4,1,128]{4,3,2,1,0:T(1,128)}, u32[]{:S(2)}, u32[]{:S(2)}) collective-permute-start(f32[1,10,4,1,128]{4,3,2,1,0:T(1,128)} %slice.546), channel_id=1, source_target_pairs={{0,1},{1,2},{2,3},{4,5},{5,6},{6,7},{8,9},{9,10},{10,11},{12,13},{... | collective-permute-start | bytes 61448 | tf_op jit(solution)/shard_map/ppermute | solution.py:22
  89.8 1.9 %gather_fusion.6 = f32[64,10]{1,0:T(8,128)} fusion(f32[10,64]{0,1:T(8,128)} %bitcast.383, s32[1024]{0:T(1024)S(1)} %pad_clamp_fusion.1), kind=kCustom, calls=%fused_computation.5.clone | custom fusion | bytes 5376 | tf_op jit(solution)/shard_map/jit(_take)/gather | solution.py:74
  98.9 1.9 %fusion.56 = f32[1,10,4,16,128]{4,3,2,1,0:T(8,128)S(1)} fusion(f32[1,10,4,16,128]{4,3,2,1,0:T(8,128)S(1)} %fusion.46, f32[1,10,4,16,128]{4,3,2,1,0:T(8,128)S(1)} %copy-done.1, f32[1,5,4,16,128]{4,3,2,1,0:T(8,128)} %get-tuple-element.44, f32[1,5,4,16,128]{4,3,2,1,0:T(8,128)} %get-tuple-element.43, f32[1,10,3,16,128]{4,3,2,1,0:T(8,128)} %slice.543, ...), kind=kLoop, calls=%fused_computation.96 | loop fusion | flops 1638400 | bytes 3309572 | tf_op jit(solution)/shard_map/add | solution.py:132
  101.6 1.8 %fusion.92 = f32[8192,60]{0,1:T(8,128)S(1)} fusion(f32[10,8192]{1,0:T(8,128)S(1)} %reshape.1478, f32[60,10]{0,1:T(8,128)S(1)} %reshape.1465), kind=kOutput, calls=%fused_computation.207 | convolution fusion | flops 58982400 | bytes 2296160 | tf_op jit(solution)/shard_map/yc,pcn->pyn/dot_general | solution.py:104
  107.8 5.1 %collective-permute-start.10 = (f32[1,10,4,1,128]{4,3,2,1,0:T(1,128)}, f32[1,10,4,1,128]{4,3,2,1,0:T(1,128)}, u32[]{:S(2)}, u32[]{:S(2)}) collective-permute-start(f32[1,10,4,1,128]{4,3,2,1,0:T(1,128)} %slice.570), channel_id=1, source_target_pairs={{0,1},{1,2},{2,3},{4,5},{5,6},{6,7},{8,9},{9,10},{10,11},{12,13},{... | collective-permute-start | bytes 61448 | tf_op jit(solution)/shard_map/ppermute | solution.py:22
  113.0 1.5 %collective-permute-start.11 = (f32[1,10,4,1,128]{4,3,2,1,0:T(1,128)}, f32[1,10,4,1,128]{4,3,2,1,0:T(1,128)}, u32[]{:S(2)}, u32[]{:S(2)}) collective-permute-start(f32[1,10,4,1,128]{4,3,2,1,0:T(1,128)} %slice.574), channel_id=1, source_target_pairs={{1,0},{2,1},{3,2},{5,4},{6,5},{7,6},{9,8},{10,9},{11,10},{13,12},{... | collective-permute-start | bytes 61448 | tf_op jit(solution)/shard_map/ppermute | solution.py:23
  115.7 1.9 %gather_fusion.8 = f32[64,10]{1,0:T(8,128)} fusion(f32[10,64]{0,1:T(8,128)} %bitcast.385, s32[1024]{0:T(1024)S(1)} %pad_clamp_fusion.1), kind=kCustom, calls=%fused_computation.7.clone | custom fusion | bytes 5376 | tf_op jit(solution)/shard_map/jit(_take)/gather | solution.py:74
  124.8 1.9 %fusion.66 = f32[1,10,4,16,128]{4,3,2,1,0:T(8,128)S(1)} fusion(f32[1,10,4,16,128]{4,3,2,1,0:T(8,128)S(1)} %fusion.56, f32[1,10,4,16,128]{4,3,2,1,0:T(8,128)S(1)} %copy-done.1, f32[1,5,4,16,128]{4,3,2,1,0:T(8,128)} %get-tuple-element.42, f32[1,5,4,16,128]{4,3,2,1,0:T(8,128)S(1)} %copy-done.6, f32[1,10,3,16,128]{4,3,2,1,0:T(8,128)} %slice.567, ...), kind=kLoop, calls=%fused_computation.108 | loop fusion | flops 1638400 | bytes 3309572 | tf_op jit(solution)/shard_map/add | solution.py:132
  127.2 5.0 %fusion.3 = f32[3,8192]{1,0:T(4,128)} fusion(s32[8192]{0:T(1024)} %add_select_fusion, pred[64,8192]{1,0:T(8,128)(4,1)} %iota_compare_fusion.1, f32[1,3,64,128]{3,1,2,0:T(4,128)S(1)} %fusion.6), kind=kOutput, calls=%fused_computation.15 | convolution fusion | flops 2420088832 | bytes 753664 | tf_op jit(solution)/shard_map/xl,lj->xj/dot_general | solution.py:150
  132.2 7.9 %all-to-all-start = ((f32[16,3,512]{2,1,0:T(4,128)}), f32[16,3,512]{2,1,0:T(4,128)S(1)}, u32[]{:S(2)}, u32[]{:S(2)}) async-start(f32[16,3,512]{2,1,0:T(4,128)} %bitcast.131), calls=%async_computation | async-start | bytes 262144 | tf_op jit(solution)/shard_map/all_to_all | solution.py:47
  140.6 7.4 %all-to-all-done = f32[16,3,512]{2,1,0:T(4,128)S(1)} async-done(((f32[16,3,512]{2,1,0:T(4,128)}), f32[16,3,512]{2,1,0:T(4,128)S(1)}, u32[]{:S(2)}, u32[]{:S(2)}) %all-to-all-start) | async-done | bytes 98336 | tf_op jit(solution)/shard_map/all_to_all | solution.py:47
  (195 shorter events, 64.7 us)
Async XLA Ops:
  0.6 126.1 %copy-start = (f32[3,10]{1,0:T(4,128)S(1)}, f32[3,10]{1,0:T(4,128)}, u32[]{:S(2)}) copy-start(f32[3,10]{1,0:T(4,128)} %param.19) | copy-start | bytes 364
  6.3 12.1 %copy-start.15 = (s32[1,1,64]{2,1,0:T(1,128)S(1)}, s32[1,1,64]{2,1,0:T(1,128)}, u32[]{:S(2)}) copy-start(s32[1,1,64]{2,1,0:T(1,128)} %param.22) | copy-start | bytes 772
  7.0 37.7 %collective-permute-start = (f32[1,10,1,16,128]{4,3,2,1,0:T(8,128)}, f32[1,10,1,16,128]{4,3,2,1,0:T(8,128)}, u32[]{:S(2)}, u32[]{:S(2)}) collective-permute-start(f32[1,10,1,16,128]{4,3,2,1,0:T(8,128)} %slice_select_fusion.3), channel_id=1, source_target_pairs={{0,4},{4,0},{1,5},{5,1},{2,6},{6,2},{3,7},{7,3},{8,12},{12,8},{9,1... | collective-permute-start | bytes 245768 | tf_op jit(solution)/shard_map/ppermute | solution.py:32
  9.6 35.9 %collective-permute-start.1 = (f32[1,10,4,1,128]{4,3,2,1,0:T(1,128)}, f32[1,10,4,1,128]{4,3,2,1,0:T(1,128)}, u32[]{:S(2)}, u32[]{:S(2)}) collective-permute-start(f32[1,10,4,1,128]{4,3,2,1,0:T(1,128)} %slice.495), channel_id=1, source_target_pairs={{0,1},{1,2},{2,3},{4,5},{5,6},{6,7},{8,9},{9,10},{10,11},{12,13},{... | collective-permute-start | bytes 61448 | tf_op jit(solution)/shard_map/ppermute | solution.py:22
  14.2 31.3 %collective-permute-start.2 = (f32[1,10,4,1,128]{4,3,2,1,0:T(1,128)}, f32[1,10,4,1,128]{4,3,2,1,0:T(1,128)}, u32[]{:S(2)}, u32[]{:S(2)}) collective-permute-start(f32[1,10,4,1,128]{4,3,2,1,0:T(1,128)} %slice.500), channel_id=1, source_target_pairs={{1,0},{2,1},{3,2},{5,4},{6,5},{7,6},{9,8},{10,9},{11,10},{13,12},{... | collective-permute-start | bytes 61448 | tf_op jit(solution)/shard_map/ppermute | solution.py:23
  18.5 13.2 %copy-start.13 = (pred[64]{0:T(512)(128)(4,1)}, pred[64]{0:T(512)(128)(4,1)S(1)}, u32[]{:S(2)}) copy-start(pred[64]{0:T(512)(128)(4,1)S(1)} %compare_and_fusion) | copy-start | bytes 196
  31.7 10.6 %copy-start.11 = (f32[1,5,4,16]{3,2,1,0:T(4,128)S(1)}, f32[1,5,4,16]{3,2,1,0:T(4,128)}, u32[]{:S(2)}) copy-start(f32[1,5,4,16]{3,2,1,0:T(4,128)} %copy.349) | copy-start | bytes 3844
  31.7 10.6 %copy-start.12 = (f32[1,5,4,16]{3,2,1,0:T(4,128)S(1)}, f32[1,5,4,16]{3,2,1,0:T(4,128)}, u32[]{:S(2)}) copy-start(f32[1,5,4,16]{3,2,1,0:T(4,128)} %copy.348) | copy-start | bytes 3844
  31.7 13.9 %copy-start.1 = (f32[1,10,4,16,128]{4,3,2,1,0:T(8,128)S(1)}, f32[1,10,4,16,128]{4,3,2,1,0:T(8,128)}, u32[]{:S(2)}) copy-start(f32[1,10,4,16,128]{4,3,2,1,0:T(8,128)} %param.14) | copy-start | bytes 983044
  31.7 13.9 %copy-start.3 = (f32[1,10,4,15,128]{4,3,2,1,0:T(8,128)S(1)}, f32[1,10,4,15,128]{4,3,2,1,0:T(8,128)}, u32[]{:S(2)}) copy-start(f32[1,10,4,15,128]{4,3,2,1,0:T(8,128)} %slice.499) | copy-start | bytes 921604
  31.7 13.9 %copy-start.4 = (f32[1,10,4,16,127]{4,3,2,1,0:T(8,128)S(1)}, f32[1,10,4,16,127]{4,3,2,1,0:T(8,128)}, u32[]{:S(2)}) copy-start(f32[1,10,4,16,127]{4,3,2,1,0:T(8,128)} %slice.509) | copy-start | bytes 975364
  53.7 16.8 %collective-permute-start.3 = (f32[1,10,1,16,128]{4,3,2,1,0:T(8,128)}, f32[1,10,1,16,128]{4,3,2,1,0:T(8,128)}, u32[]{:S(2)}, u32[]{:S(2)}) collective-permute-start(f32[1,10,1,16,128]{4,3,2,1,0:T(8,128)} %slice_select_fusion.2), channel_id=1, source_target_pairs={{0,4},{4,0},{1,5},{5,1},{2,6},{6,2},{3,7},{7,3},{8,12},{12,8},{9,1... | collective-permute-start | bytes 245768 | tf_op jit(solution)/shard_map/ppermute | solution.py:32
  54.5 16.9 %collective-permute-start.4 = (f32[1,10,4,1,128]{4,3,2,1,0:T(1,128)}, f32[1,10,4,1,128]{4,3,2,1,0:T(1,128)}, u32[]{:S(2)}, u32[]{:S(2)}) collective-permute-start(f32[1,10,4,1,128]{4,3,2,1,0:T(1,128)} %slice.522), channel_id=1, source_target_pairs={{0,1},{1,2},{2,3},{4,5},{5,6},{6,7},{8,9},{9,10},{10,11},{12,13},{... | collective-permute-start | bytes 61448 | tf_op jit(solution)/shard_map/ppermute | solution.py:22
  59.7 11.7 %collective-permute-start.5 = (f32[1,10,4,1,128]{4,3,2,1,0:T(1,128)}, f32[1,10,4,1,128]{4,3,2,1,0:T(1,128)}, u32[]{:S(2)}, u32[]{:S(2)}) collective-permute-start(f32[1,10,4,1,128]{4,3,2,1,0:T(1,128)} %slice.526), channel_id=1, source_target_pairs={{1,0},{2,1},{3,2},{5,4},{6,5},{7,6},{9,8},{10,9},{11,10},{13,12},{... | collective-permute-start | bytes 61448 | tf_op jit(solution)/shard_map/ppermute | solution.py:23
  79.5 18.4 %collective-permute-start.6 = (f32[1,10,1,16,128]{4,3,2,1,0:T(8,128)}, f32[1,10,1,16,128]{4,3,2,1,0:T(8,128)}, u32[]{:S(2)}, u32[]{:S(2)}) collective-permute-start(f32[1,10,1,16,128]{4,3,2,1,0:T(8,128)} %slice_select_fusion.1), channel_id=1, source_target_pairs={{0,4},{4,0},{1,5},{5,1},{2,6},{6,2},{3,7},{7,3},{8,12},{12,8},{9,1... | collective-permute-start | bytes 245768 | tf_op jit(solution)/shard_map/ppermute | solution.py:32
  82.2 16.7 %collective-permute-start.7 = (f32[1,10,4,1,128]{4,3,2,1,0:T(1,128)}, f32[1,10,4,1,128]{4,3,2,1,0:T(1,128)}, u32[]{:S(2)}, u32[]{:S(2)}) collective-permute-start(f32[1,10,4,1,128]{4,3,2,1,0:T(1,128)} %slice.546), channel_id=1, source_target_pairs={{0,1},{1,2},{2,3},{4,5},{5,6},{6,7},{8,9},{9,10},{10,11},{12,13},{... | collective-permute-start | bytes 61448 | tf_op jit(solution)/shard_map/ppermute | solution.py:22
  87.3 11.6 %collective-permute-start.8 = (f32[1,10,4,1,128]{4,3,2,1,0:T(1,128)}, f32[1,10,4,1,128]{4,3,2,1,0:T(1,128)}, u32[]{:S(2)}, u32[]{:S(2)}) collective-permute-start(f32[1,10,4,1,128]{4,3,2,1,0:T(1,128)} %slice.550), channel_id=1, source_target_pairs={{1,0},{2,1},{3,2},{5,4},{6,5},{7,6},{9,8},{10,9},{11,10},{13,12},{... | collective-permute-start | bytes 61448 | tf_op jit(solution)/shard_map/ppermute | solution.py:23
  104.2 16.0 %copy-start.14 = (pred[64]{0:T(512)(128)(4,1)S(1)}, pred[64]{0:T(512)(128)(4,1)}, u32[]{:S(2)}) copy-start(pred[64]{0:T(512)(128)(4,1)} %copy-done.13) | copy-start | bytes 196
  107.0 17.8 %copy-start.6 = (f32[1,5,4,16,128]{4,3,2,1,0:T(8,128)S(1)}, f32[1,5,4,16,128]{4,3,2,1,0:T(8,128)}, u32[]{:S(2)}) copy-start(f32[1,5,4,16,128]{4,3,2,1,0:T(8,128)} %get-tuple-element.41) | copy-start | bytes 491524
  107.0 17.8 %copy-start.8 = (f32[4,16,128]{2,1,0:T(8,128)S(1)}, f32[4,16,128]{2,1,0:T(8,128)}, u32[]{:S(2)}) copy-start(f32[4,16,128]{2,1,0:T(8,128)} %param.16) | copy-start | bytes 98308
  107.0 16.8 %collective-permute-start.9 = (f32[1,10,1,16,128]{4,3,2,1,0:T(8,128)}, f32[1,10,1,16,128]{4,3,2,1,0:T(8,128)}, u32[]{:S(2)}, u32[]{:S(2)}) collective-permute-start(f32[1,10,1,16,128]{4,3,2,1,0:T(8,128)} %slice_select_fusion), channel_id=1, source_target_pairs={{0,4},{4,0},{1,5},{5,1},{2,6},{6,2},{3,7},{7,3},{8,12},{12,8},{9,1... | collective-permute-start | bytes 245768 | tf_op jit(solution)/shard_map/ppermute | solution.py:32
  107.8 16.9 %collective-permute-start.10 = (f32[1,10,4,1,128]{4,3,2,1,0:T(1,128)}, f32[1,10,4,1,128]{4,3,2,1,0:T(1,128)}, u32[]{:S(2)}, u32[]{:S(2)}) collective-permute-start(f32[1,10,4,1,128]{4,3,2,1,0:T(1,128)} %slice.570), channel_id=1, source_target_pairs={{0,1},{1,2},{2,3},{4,5},{5,6},{6,7},{8,9},{9,10},{10,11},{12,13},{... | collective-permute-start | bytes 61448 | tf_op jit(solution)/shard_map/ppermute | solution.py:22
  113.0 11.8 %collective-permute-start.11 = (f32[1,10,4,1,128]{4,3,2,1,0:T(1,128)}, f32[1,10,4,1,128]{4,3,2,1,0:T(1,128)}, u32[]{:S(2)}, u32[]{:S(2)}) collective-permute-start(f32[1,10,4,1,128]{4,3,2,1,0:T(1,128)} %slice.574), channel_id=1, source_target_pairs={{1,0},{2,1},{3,2},{5,4},{6,5},{7,6},{9,8},{10,9},{11,10},{13,12},{... | collective-permute-start | bytes 61448 | tf_op jit(solution)/shard_map/ppermute | solution.py:23
  132.2 15.9 %all-to-all-start = ((f32[16,3,512]{2,1,0:T(4,128)}), f32[16,3,512]{2,1,0:T(4,128)S(1)}, u32[]{:S(2)}, u32[]{:S(2)}) async-start(f32[16,3,512]{2,1,0:T(4,128)} %bitcast.131), calls=%async_computation | async-start | bytes 262144 | tf_op jit(solution)/shard_map/all_to_all | solution.py:47
  (5 other events, 28.7 us)

commit v2 on v1

v2 whole, which is shorter than its diff:
```python
import functools
import math

import jax
import jax.numpy as jnp
from jax import lax
from jax.experimental import pallas as pl
from jax.experimental.pallas import tpu as pltpu
from jax.sharding import PartitionSpec as P

BLADES = 16
ITERS = 4


RELAX = 0.8
LANES = 128
SMEM = pltpu.MemorySpace.SMEM


def split_up(value, dim, count):
    dims = value.shape
    blocks = value.reshape(*dims[:dim], count, dims[dim] // count, *dims[dim + 1 :])
    return jnp.moveaxis(blocks, dim, 0)


def sum_at_owner(value, axis, dim):
    count = lax.axis_size(axis)
    blocks = lax.all_to_all(split_up(value, dim, count), axis, 0, 0, tiled=True)
    return jnp.sum(blocks, axis=0)


def build_matrices(flux_jac):
    real_part = jnp.swapaxes(flux_jac[:, 0], 1, 2)
    imag_part = jnp.swapaxes(flux_jac[:, 1], 1, 2)
    top_rows = jnp.concatenate([real_part, imag_part], axis=2)
    low_rows = jnp.concatenate([-imag_part, real_part], axis=2)
    return jnp.concatenate([top_rows, low_rows], axis=1)


def exact_pick(pick, values):
    first = values.astype(jnp.bfloat16)
    rest = values - first.astype(jnp.float32)
    second = rest.astype(jnp.bfloat16)
    third = (rest - second.astype(jnp.float32)).astype(jnp.bfloat16)
    out = jnp.dot(pick, first, preferred_element_type=jnp.float32)
    out = out + jnp.dot(pick, second, preferred_element_type=jnp.float32)
    return out + jnp.dot(pick, third, preferred_element_type=jnp.float32)


def applied(mat_ref, d, x, comps, load):
    total = mat_ref[(d * comps + x) * comps] * load(0)
    for c in range(1, comps):
        total = total + mat_ref[(d * comps + x) * comps + c] * load(c)
    return total


def write_edges(mat_ref, wt_ref, psi_ref, face_ref, axs_ref, q2_ref, q3_ref, comps, tile_r):
    rows = psi_ref.shape[1]
    layers = rows // tile_r
    top = pl.ds(rows - tile_r, tile_r)
    bottom = pl.ds(0, tile_r)
    r_top = pl.ds(tile_r - 1, layers, stride=tile_r)
    r_bottom = pl.ds(0, layers, stride=tile_r)
    keep_top = wt_ref[1]
    keep_bottom = wt_ref[0]
    for x in range(comps):
        up = face_ref[0, top, :] * applied(mat_ref, 0, x, comps, lambda c: psi_ref[c, top, :])
        down = face_ref[1, bottom, :] * applied(mat_ref, 1, x, comps, lambda c: psi_ref[c, bottom, :])
        axs_ref[x] = up * keep_top + down * keep_bottom
        q2_ref[x] = face_ref[2, r_top, :] * applied(mat_ref, 2, x, comps, lambda c: psi_ref[c, r_top, :])
        q3_ref[x] = face_ref[3, r_bottom, :] * applied(mat_ref, 3, x, comps, lambda c: psi_ref[c, r_bottom, :])


def edges_kernel(mat_ref, wt_ref, psi_ref, face_ref, axs_ref, q2_ref, q3_ref, *, tile_r):
    write_edges(mat_ref, wt_ref, psi_ref, face_ref, axs_ref, q2_ref, q3_ref, psi_ref.shape[0], tile_r)


def section_kernel(
    mat_ref, wt_ref, psi_ref, src_ref, face_ref, diag_ref, pick_ref, axr_ref, ralo_ref, rahi_ref,
    out_ref, axs_ref, q2_ref, q3_ref, inc_ref, *, tile_r, edges,
):
    comps, rows, lanes = psi_ref.shape
    half = comps // 2
    layers = rows // tile_r
    lane = lax.broadcasted_iota(jnp.int32, (rows, lanes), 1)
    row = lax.broadcasted_iota(jnp.int32, (rows, lanes), 0) % tile_r
    omega = wt_ref[2]
    cosine = wt_ref[3]
    sine = wt_ref[4]
    from_below = wt_ref[5]
    from_above = wt_ref[6]
    pack4 = jnp.zeros((rows, lanes), jnp.float32)
    pack5 = jnp.zeros((rows, lanes), jnp.float32)
    load = lambda c: psi_ref[c]
    for x in range(comps):
        q0 = face_ref[0] * applied(mat_ref, 0, x, comps, load)
        q1 = face_ref[1] * applied(mat_ref, 1, x, comps, load)
        q2 = face_ref[2] * applied(mat_ref, 2, x, comps, load)
        q3 = face_ref[3] * applied(mat_ref, 3, x, comps, load)
        q4 = face_ref[4] * applied(mat_ref, 4, x, comps, load)
        q5 = face_ref[5] * applied(mat_ref, 5, x, comps, load)
        got = axr_ref[x]
        lower_a = jnp.concatenate([got * from_below, q0[: rows - tile_r]], axis=0)
        upper_a = jnp.concatenate([q1[tile_r:], got * from_above], axis=0)
        low_r = ralo_ref[x]
        high_r = rahi_ref[x]
        low_rows = jnp.concatenate(
            [jnp.broadcast_to(low_r[j : j + 1, :], (tile_r, lanes)) for j in range(layers)], axis=0
        )
        high_rows = jnp.concatenate(
            [jnp.broadcast_to(high_r[j : j + 1, :], (tile_r, lanes)) for j in range(layers)], axis=0
        )
        lower_r = jnp.where(row == 0, low_rows, pltpu.roll(q2, 1, 0))
        upper_r = jnp.where(row == tile_r - 1, high_rows, pltpu.roll(q3, rows - 1, 0))
        lower_t = jnp.where(lane == 0, 0.0, pltpu.roll(q4, 1, 1))
        upper_t = jnp.where(lane == lanes - 1, 0.0, pltpu.roll(q5, lanes - 1, 1))
        inc_ref[x] = lower_a + upper_a + lower_r + upper_r + lower_t + upper_t
        pack4 = pack4 + jnp.where(lane == x, pltpu.roll(q4, (x + 1) % lanes, 1), 0.0)
        pack5 = pack5 + jnp.where(lane == x, pltpu.roll(q5, x, 1), 0.0) if x else jnp.where(lane == 0, q5, 0.0)
    pick = pick_ref[...]
    got4 = exact_pick(pick, pack4)
    got5 = exact_pick(pick, pack5)
    up4 = pltpu.roll(got4, lanes - half, 1)
    down4 = pltpu.roll(got4, half, 1)
    up5 = pltpu.roll(got5, lanes - half, 1)
    down5 = pltpu.roll(got5, half, 1)
    real_half = lane < half
    wrap4 = jnp.where(real_half, cosine * got4 - sine * up4, sine * down4 + cosine * got4)
    wrap5 = jnp.where(real_half, cosine * got5 - (-sine) * up5, (-sine) * down5 + cosine * got5)
    diag = diag_ref[...]
    for x in range(comps):
        at_start = pltpu.roll(wrap4, (lanes - x) % lanes, 1)
        at_end = pltpu.roll(wrap5, lanes - 1 - x, 1)
        incoming = inc_ref[x] + jnp.where(lane == 0, at_start, 0.0) + jnp.where(lane == lanes - 1, at_end, 0.0)
        psi = psi_ref[x]
        swapped = psi_ref[x + half] if x < half else -psi_ref[x - half]
        residual = src_ref[x] - (diag * psi + omega * swapped) + incoming
        out_ref[x] = psi + RELAX * residual / diag
    if edges:
        write_edges(mat_ref, wt_ref, out_ref, face_ref, axs_ref, q2_ref, q3_ref, comps, tile_r)


def vmem_spec():
    return pl.BlockSpec(memory_space=pltpu.MemorySpace.VMEM)


def smem_spec():
    return pl.BlockSpec(memory_space=SMEM)


def edge_shapes(comps, rows, tile_r):
    layers = rows // tile_r
    return (
        jax.ShapeDtypeStruct((comps, tile_r, LANES), jnp.float32),
        jax.ShapeDtypeStruct((comps, layers, LANES), jnp.float32),
        jax.ShapeDtypeStruct((comps, layers, LANES), jnp.float32),
    )


def run_edges(mat, weights, psi, face, tile_r):
    comps, rows, _ = psi.shape
    return pl.pallas_call(
        functools.partial(edges_kernel, tile_r=tile_r),
        out_shape=edge_shapes(comps, rows, tile_r),
        in_specs=[smem_spec(), smem_spec(), vmem_spec(), vmem_spec()],
        out_specs=tuple(vmem_spec() for _ in range(3)),
    )(mat, weights, psi, face)


def run_section(mat, weights, psi, src, face, diag, pick, axr, ralo, rahi, tile_r, edges):
    comps, rows, lanes = psi.shape
    return pl.pallas_call(
        functools.partial(section_kernel, tile_r=tile_r, edges=edges),
        out_shape=(jax.ShapeDtypeStruct(psi.shape, jnp.float32),) + edge_shapes(comps, rows, tile_r),
        in_specs=[smem_spec(), smem_spec()] + [vmem_spec() for _ in range(8)],
        out_specs=tuple(vmem_spec() for _ in range(4)),
        scratch_shapes=[pltpu.VMEM((comps, rows, lanes), jnp.float32)],
    )(mat, weights, psi, src, face, diag, pick, axr, ralo, rahi)


def neighbours(axis):
    count = lax.axis_size(axis)
    up = [(i, (i + 1) % count) for i in range(count - 1)]
    return up, [(j, i) for i, j in up]


def body(
    psi_start,
    source,
    face_coef,
    diag_coef,
    flux_jac,
    omega,
    metric,
    mode_shape,
    phase_weight,
    pairing,
    owner_order,
):
    matrices = build_matrices(flux_jac)
    comps = matrices.shape[1]
    mat = matrices.reshape(-1)
    local_phases, _, tile_a, tile_r, pitch = psi_start.shape
    rows = tile_a * tile_r
    cells = rows * pitch
    angle = lax.axis_index("phase").astype(jnp.float32) * (2.0 * math.pi / BLADES)
    me_axial = lax.axis_index("axial")
    lower_side = (me_axial == 0).astype(jnp.float32)
    upper_side = 1.0 - lower_side
    weights = jnp.stack(
        [
            upper_side,
            lower_side,
            omega[0],
            jnp.cos(angle),
            jnp.sin(angle),
            upper_side,
            lower_side,
        ]
    ).astype(jnp.float32)
    partner = pairing[0, 0]
    faces = face_coef.astype(jnp.float32).reshape(6, rows, pitch)
    diag = diag_coef.reshape(rows, pitch)
    pick = (partner[:, None] == jnp.arange(rows, dtype=partner.dtype)[None, :]).astype(jnp.bfloat16)
    up_r, down_r = neighbours("radial")
    psi = psi_start.reshape(comps, rows, pitch)
    src = source.reshape(comps, rows, pitch)
    axs, q2, q3 = run_edges(mat, weights, psi, faces, tile_r)
    for section in range(ITERS):
        axr = lax.ppermute(axs, "axial", [(0, 1), (1, 0)])
        ralo = lax.ppermute(q2, "radial", up_r)
        rahi = lax.ppermute(q3, "radial", down_r)
        psi, axs, q2, q3 = run_section(
            mat, weights, psi, src, faces, diag, pick, axr, ralo, rahi, tile_r, section < ITERS - 1
        )
    psi_out = psi.reshape(psi_start.shape)
    heights = jnp.einsum(
        "dc,cn->dn",
        metric,
        psi.reshape(comps, cells),
        precision=lax.Precision.HIGHEST,
    )
    weighted = phase_weight[0] * heights
    order = owner_order[0, 0]
    owners = lax.axis_size("phase")
    owned = cells // owners
    dims = weighted.shape[0]
    lanes = LANES
    blocks = cells // lanes
    lane_of = order % lanes
    row_of = order // lanes
    pick_lane = (lane_of[None, :] == jnp.arange(lanes, dtype=order.dtype)[:, None]).astype(jnp.float32)
    by_lane = jnp.einsum(
        "xl,lj->xj",
        weighted.reshape(dims * blocks, lanes),
        pick_lane,
        precision=lax.Precision.HIGHEST,
    ).reshape(dims, blocks, cells)
    pick_row = row_of[None, None, :] == jnp.arange(blocks, dtype=order.dtype)[None, :, None]
    in_order = jnp.sum(jnp.where(pick_row, by_lane, 0.0), axis=1)
    gathered = sum_at_owner(in_order, "phase", 1)
    mine = lax.dynamic_slice_in_dim(order, lax.axis_index("phase") * owned, owned)
    count_k = mode_shape.shape[0]
    mine_lane = (mine[None, :] % lanes == jnp.arange(lanes, dtype=mine.dtype)[:, None]).astype(jnp.bfloat16)
    mode_lane = jnp.einsum(
        "xl,lj->xj",
        mode_shape.reshape(count_k * 3 * blocks, lanes),
        mine_lane,
        preferred_element_type=jnp.float32,
    ).reshape(count_k, 3, blocks, owned)
    mine_row = (mine // lanes)[None, None, None, :] == jnp.arange(blocks, dtype=mine.dtype)[None, None, :, None]
    modes = jnp.sum(jnp.where(mine_row, mode_lane, 0.0), axis=2)
    sens = modes[:, 0] * gathered[0] + modes[:, 1] * gathered[1] + modes[:, 2] * gathered[2]
    return (psi_out, sens.reshape(count_k, 1, 1, owned))


def solution(mesh):
    return jax.shard_map(
        body,
        mesh=mesh,
        in_specs=(
            P("phase", None, "axial", "radial", None),
            P("phase", None, "axial", "radial", None),
            P(None, "axial", "radial", None),
            P("axial", "radial", None),
            P(),
            P(),
            P(),
            P(None, None, "axial", "radial", None),
            P("phase"),
            P("axial", "radial", None),
            P("axial", "radial", None),
        ),
        out_specs=(P("phase", None, "axial", "radial", None), P(None, "axial", "radial", "phase")),
        check_vma=False,
    )
```

time: 152 us -> 93.3 us (0.61)
  the two profiles are of different devices: /device:TPU:0 before, /device:TPU:3 now
where the time goes in v2:
time: 93.3 us; the launch traced here: 92.5 us
  starting transfers between devices  37 us (40%)
  Pallas kernels  17.3 us (19%)
  local copies, waits for them, and re-layouts  13.3 us (14%)
  other arithmetic  8.01 us (9%)
  matrix products  7.37 us (8%)
  waiting for transfers between devices  7.04 us (8%)
  between operations  2.43 us (3%)
    pallas_call x4, Pallas kernels, run_section(): pl.pallas_call(functools.partial(section_kernel, tile_r=tile_r, edges=edg...  15.4 us
    all_to_all x1, starting transfers between devices, sum_at_owner(): blocks = lax.all_to_all(split_up(value, dim, count), axis, 0, 0, tiled=True)  12.7 us
    ppermute x4, starting transfers between devices, body(): ralo = lax.ppermute(q2, 'radial', up_r)  12.2 us
    ppermute x4, starting transfers between devices, body(): rahi = lax.ppermute(q3, 'radial', down_r)  9.11 us
    dot_general x1, local copies, waits for them, and re-layouts, body(): jnp.einsum('xl,lj->xj', mode_shape.reshape(count_k * 3 * blocks, lanes),...  6.16 us
    all_to_all x1, waiting for transfers between devices, sum_at_owner(): blocks = lax.all_to_all(split_up(value, dim, count), axis, 0, 0, tiled=True)  4.49 us
    unnamed x34, local copies, waits for them, and re-layouts  4.09 us
    dot_general x1, matrix products, body(): jnp.einsum('xl,lj->xj', weighted.reshape(dims * blocks, lanes), pick_lane...  3.96 us
  transfers between devices with their start and end apart: 13, of which 2 were waited for; matrix products, arithmetic and copies ran while one was open for 17% of the time, Pallas kernels for 0%

profile of v2, /device:TPU:3, one launch (start us, length us, event | category | flops | bytes accessed | tf_op | source)
XLA Modules:
  0.0 92.5 jit_solution(3049772292938237433)
XLA Ops:
  3.5 1.6 %bitcast_convert_fusion.face_ref = f32[6,64,128]{2,1,0:T(8,128)} fusion(bf16[6,4,16,128]{3,2,1,0:T(8,128)(2,1)} %param.13), kind=kLoop, calls=%fused_computation.17 | loop fusion | flops 49152 | bytes 294912 | tf_op jit(solution)/shard_map/reshape | solution.py:222
  5.8 1.9 %shard_map.122 = (f32[10,16,128]{2,1,0:T(8,128)}, f32[10,4,128]{2,1,0:T(4,128)}, f32[10,4,128]{2,1,0:T(4,128)}) custom-call(f32[600]{0:T(1024)} %reshape.280.mat_ref, f32[7]{0:T(128)} %stack.21.wt_ref, f32[10,64,128]{2,1,0:T(8,128)} %bitcast.83, f32[6,64,128]{2,1,0:T(8,128)} %bitcast_convert_fusion.face_ref), custom_call_target="tpu_custom_call" | custom-call | tf_op jit(solution)/shard_map/pallas_call | solution.py:162
  7.7 1.6 %collective-permute-start = (f32[10,16,128]{2,1,0:T(8,128)}, f32[10,16,128]{2,1,0:T(8,128)S(1)}, u32[]{:S(2)}, u32[]{:S(2)}) collective-permute-start(f32[10,16,128]{2,1,0:T(8,128)} %get-tuple-element.18), channel_id=1, source_target_pairs={{0,4},{4,0},{1,5},{5,1},{2,6},{6,2},{3,7},{7,3},{8,12},{12,8},{9,1... | collective-permute-start | bytes 245768 | tf_op jit(solution)/shard_map/ppermute | solution.py:230
  9.3 3.1 %collective-permute-start.1 = (f32[10,4,128]{2,1,0:T(4,128)}, f32[10,4,128]{2,1,0:T(4,128)S(1)}, u32[]{:S(2)}, u32[]{:S(2)}) collective-permute-start(f32[10,4,128]{2,1,0:T(4,128)} %get-tuple-element.19), channel_id=1, source_target_pairs={{0,1},{1,2},{2,3},{4,5},{5,6},{6,7},{8,9},{9,10},{10,11},{12,13},{... | collective-permute-start | bytes 61448 | tf_op jit(solution)/shard_map/ppermute | solution.py:231
  12.4 2.2 %collective-permute-start.2 = (f32[10,4,128]{2,1,0:T(4,128)}, f32[10,4,128]{2,1,0:T(4,128)S(1)}, u32[]{:S(2)}, u32[]{:S(2)}) collective-permute-start(f32[10,4,128]{2,1,0:T(4,128)} %get-tuple-element.20), channel_id=1, source_target_pairs={{1,0},{2,1},{3,2},{5,4},{6,5},{7,6},{9,8},{10,9},{11,10},{13,12},{... | collective-permute-start | bytes 61448 | tf_op jit(solution)/shard_map/ppermute | solution.py:232
  14.6 1.3 %fusion.13.pick_ref = bf16[64,64]{1,0:T(8,128)(2,1)} fusion(s32[64]{0:T(128)} %bitcast.98), kind=kLoop, calls=%fused_computation.27 | loop fusion | flops 8192 | bytes 8448 | tf_op jit(solution)/shard_map/convert_element_type | solution.py:224
  18.5 3.9 %shard_map.123 = (f32[10,64,128]{2,1,0:T(8,128)}, f32[10,16,128]{2,1,0:T(8,128)}, f32[10,4,128]{2,1,0:T(4,128)}, f32[10,4,128]{2,1,0:T(4,128)}) custom-call(f32[600]{0:T(1024)} %reshape.280.mat_ref, f32[7]{0:T(128)} %stack.21.wt_ref, f32[10,64,128]{2,1,0:T(8,128)} %bitcast.84, f32[10,64,128]{2,1,0:T(8,128)} %bitcast.77, ...), custom_call_target="tpu_custom_call" | custom-call | tf_op jit(solution)/shard_map/pallas_call | solution.py:172
  22.4 3.1 %collective-permute-start.4 = (f32[10,4,128]{2,1,0:T(4,128)}, f32[10,4,128]{2,1,0:T(4,128)S(1)}, u32[]{:S(2)}, u32[]{:S(2)}) collective-permute-start(f32[10,4,128]{2,1,0:T(4,128)} %get-tuple-element.23), channel_id=1, source_target_pairs={{0,1},{1,2},{2,3},{4,5},{5,6},{6,7},{8,9},{9,10},{10,11},{12,13},{... | collective-permute-start | bytes 61448 | tf_op jit(solution)/shard_map/ppermute | solution.py:231
  25.6 2.2 %collective-permute-start.5 = (f32[10,4,128]{2,1,0:T(4,128)}, f32[10,4,128]{2,1,0:T(4,128)S(1)}, u32[]{:S(2)}, u32[]{:S(2)}) collective-permute-start(f32[10,4,128]{2,1,0:T(4,128)} %get-tuple-element.24), channel_id=1, source_target_pairs={{1,0},{2,1},{3,2},{5,4},{6,5},{7,6},{9,8},{10,9},{11,10},{13,12},{... | collective-permute-start | bytes 61448 | tf_op jit(solution)/shard_map/ppermute | solution.py:232
  27.7 3.0 %convolution_bitcast_fusion = f32[2304,512]{0,1:T(8,128)} fusion(bf16[2304,128]{1,0:T(8,128)(2,1)S(1)} %bitcast.75, s32[512]{0:T(512)S(1)} %get-tuple-element.40), kind=kOutput, calls=%fused_computation.2 | convolution fusion | flops 302120960 | bytes 5310464 | tf_op jit(solution)/shard_map/xl,lj->xj/dot_general | solution.py:265
  31.4 3.9 %shard_map.124 = (f32[10,64,128]{2,1,0:T(8,128)}, f32[10,16,128]{2,1,0:T(8,128)}, f32[10,4,128]{2,1,0:T(4,128)}, f32[10,4,128]{2,1,0:T(4,128)}) custom-call(f32[600]{0:T(1024)} %reshape.280.mat_ref, f32[7]{0:T(128)} %stack.21.wt_ref, f32[10,64,128]{2,1,0:T(8,128)} %get-tuple-element.21.psi_ref, f32[10,64,128]{2,1,0:T(8,128)} %bitcast.78, ...), custom_call_target="tpu_custom_call" | custom-call | tf_op jit(solution)/shard_map/pallas_call | solution.py:172
  35.3 1.4 %collective-permute-start.6 = (f32[10,16,128]{2,1,0:T(8,128)}, f32[10,16,128]{2,1,0:T(8,128)S(1)}, u32[]{:S(2)}, u32[]{:S(2)}) collective-permute-start(f32[10,16,128]{2,1,0:T(8,128)} %get-tuple-element.26), channel_id=1, source_target_pairs={{0,4},{4,0},{1,5},{5,1},{2,6},{6,2},{3,7},{7,3},{8,12},{12,8},{9,1... | collective-permute-start | bytes 245768 | tf_op jit(solution)/shard_map/ppermute | solution.py:230
  36.7 3.1 %collective-permute-start.7 = (f32[10,4,128]{2,1,0:T(4,128)}, f32[10,4,128]{2,1,0:T(4,128)S(1)}, u32[]{:S(2)}, u32[]{:S(2)}) collective-permute-start(f32[10,4,128]{2,1,0:T(4,128)} %get-tuple-element.27), channel_id=1, source_target_pairs={{0,1},{1,2},{2,3},{4,5},{5,6},{6,7},{8,9},{9,10},{10,11},{12,13},{... | collective-permute-start | bytes 61448 | tf_op jit(solution)/shard_map/ppermute | solution.py:231
  39.8 2.2 %collective-permute-start.8 = (f32[10,4,128]{2,1,0:T(4,128)}, f32[10,4,128]{2,1,0:T(4,128)S(1)}, u32[]{:S(2)}, u32[]{:S(2)}) collective-permute-start(f32[10,4,128]{2,1,0:T(4,128)} %get-tuple-element.28), channel_id=1, source_target_pairs={{1,0},{2,1},{3,2},{5,4},{6,5},{7,6},{9,8},{10,9},{11,10},{13,12},{... | collective-permute-start | bytes 61448 | tf_op jit(solution)/shard_map/ppermute | solution.py:232
  42.1 2.5 %collective-permute-done.8.rahi_ref = f32[10,4,128]{2,1,0:T(4,128)S(1)} collective-permute-done((f32[10,4,128]{2,1,0:T(4,128)}, f32[10,4,128]{2,1,0:T(4,128)S(1)}, u32[]{:S(2)}, u32[]{:S(2)}) %collective-permute-start.8) | collective-permute-done | bytes 20512 | tf_op jit(solution)/shard_map/ppermute | solution.py:232
  45.2 3.9 %shard_map.125 = (f32[10,64,128]{2,1,0:T(8,128)}, f32[10,16,128]{2,1,0:T(8,128)}, f32[10,4,128]{2,1,0:T(4,128)}, f32[10,4,128]{2,1,0:T(4,128)}) custom-call(f32[600]{0:T(1024)} %reshape.280.mat_ref, f32[7]{0:T(128)} %stack.21.wt_ref, f32[10,64,128]{2,1,0:T(8,128)} %get-tuple-element.25.psi_ref, f32[10,64,128]{2,1,0:T(8,128)} %bitcast.79, ...), custom_call_target="tpu_custom_call" | custom-call | tf_op jit(solution)/shard_map/pallas_call | solution.py:172
  49.2 2.8 %collective-permute-start.10 = (f32[10,4,128]{2,1,0:T(4,128)}, f32[10,4,128]{2,1,0:T(4,128)S(1)}, u32[]{:S(2)}, u32[]{:S(2)}) collective-permute-start(f32[10,4,128]{2,1,0:T(4,128)} %get-tuple-element.31), channel_id=1, source_target_pairs={{0,1},{1,2},{2,3},{4,5},{5,6},{6,7},{8,9},{9,10},{10,11},{12,13},{... | collective-permute-start | bytes 61448 | tf_op jit(solution)/shard_map/ppermute | solution.py:231
  52.0 2.6 %collective-permute-start.11 = (f32[10,4,128]{2,1,0:T(4,128)}, f32[10,4,128]{2,1,0:T(4,128)S(1)}, u32[]{:S(2)}, u32[]{:S(2)}) collective-permute-start(f32[10,4,128]{2,1,0:T(4,128)} %get-tuple-element.32), channel_id=1, source_target_pairs={{1,0},{2,1},{3,2},{5,4},{6,5},{7,6},{9,8},{10,9},{11,10},{13,12},{... | collective-permute-start | bytes 61448 | tf_op jit(solution)/shard_map/ppermute | solution.py:232
  54.7 6.2 %copy.23 = f32[2304,512]{1,0:T(8,128)} copy(f32[2304,512]{0,1:T(8,128)} %convolution_bitcast_fusion) | data formatting | bytes 9437184 | tf_op jit(solution)/shard_map/xl,lj->xj/dot_general | solution.py:265
  62.2 3.6 %shard_map.126 = (f32[10,64,128]{2,1,0:T(8,128)}, f32[10,16,128]{2,1,0:T(8,128)}, f32[10,4,128]{2,1,0:T(4,128)}, f32[10,4,128]{2,1,0:T(4,128)}) custom-call(f32[600]{0:T(1024)} %reshape.280.mat_ref, f32[7]{0:T(128)} %stack.21.wt_ref, f32[10,64,128]{2,1,0:T(8,128)} %get-tuple-element.29.psi_ref, f32[10,64,128]{2,1,0:T(8,128)} %bitcast.80, ...), custom_call_target="tpu_custom_call" | custom-call | tf_op jit(solution)/shard_map/pallas_call | solution.py:172
  67.6 4.0 %fusion.3 = f32[3,8192]{1,0:T(4,128)} fusion(s32[8192]{0:T(1024)S(1)} %add_select_fusion, pred[64,8192]{1,0:T(8,128)(4,1)S(1)} %iota_compare_fusion.1, f32[1,3,64,128]{3,1,2,0:T(4,128)S(1)} %fusion.6), kind=kOutput, calls=%fused_computation.8 | convolution fusion | flops 2420088832 | bytes 753664 | tf_op jit(solution)/shard_map/xl,lj->xj/dot_general | solution.py:253
  71.6 12.7 %all-to-all-start = ((f32[16,3,512]{2,1,0:T(4,128)}), f32[16,3,512]{2,1,0:T(4,128)S(1)}, u32[]{:S(2)}, u32[]{:S(2)}) async-start(f32[16,3,512]{2,1,0:T(4,128)} %bitcast.28), calls=%async_computation | async-start | bytes 262144 | tf_op jit(solution)/shard_map/all_to_all | solution.py:28
  84.2 3.1 %select_reduce_fusion = f32[12,3,512]{2,1,0:T(4,128)S(1)} fusion(f32[12,3,64,512]{3,2,1,0:T(8,128)} %bitcast.76, pred[64,512]{1,0:T(8,128)(4,1)S(1)} %iota_compare_fusion.3), kind=kLoop, calls=%fused_computation.3 | loop fusion | flops 2340864 | bytes 4825088 | tf_op jit(solution)/shard_map/reduce_sum | solution.py:272
  87.3 4.5 %all-to-all-done = f32[16,3,512]{2,1,0:T(4,128)S(1)} async-done(((f32[16,3,512]{2,1,0:T(4,128)}), f32[16,3,512]{2,1,0:T(4,128)S(1)}, u32[]{:S(2)}, u32[]{:S(2)}) %all-to-all-start) | async-done | bytes 98336 | tf_op jit(solution)/shard_map/all_to_all | solution.py:28
  (63 shorter events, 9.7 us)
Async XLA Ops:
  0.6 27.1 %copy-start = (bf16[12,3,4,16,128]{4,3,2,1,0:T(8,128)(2,1)S(1)}, bf16[12,3,4,16,128]{4,3,2,1,0:T(8,128)(2,1)}, u32[]{:S(2)}) copy-start(bf16[12,3,4,16,128]{4,3,2,1,0:T(8,128)(2,1)} %param.18) | copy-start | bytes 1769476
  0.6 41.4 %copy-start.1 = (s32[1,1,8192]{2,1,0:T(1,128)S(1)}, s32[1,1,8192]{2,1,0:T(1,128)}, u32[]{:S(2)}) copy-start(s32[1,1,8192]{2,1,0:T(1,128)} %param.21) | copy-start | bytes 98308
  7.7 10.2 %collective-permute-start = (f32[10,16,128]{2,1,0:T(8,128)}, f32[10,16,128]{2,1,0:T(8,128)S(1)}, u32[]{:S(2)}, u32[]{:S(2)}) collective-permute-start(f32[10,16,128]{2,1,0:T(8,128)} %get-tuple-element.18), channel_id=1, source_target_pairs={{0,4},{4,0},{1,5},{5,1},{2,6},{6,2},{3,7},{7,3},{8,12},{12,8},{9,1... | collective-permute-start | bytes 245768 | tf_op jit(solution)/shard_map/ppermute | solution.py:230
  9.3 8.5 %collective-permute-start.1 = (f32[10,4,128]{2,1,0:T(4,128)}, f32[10,4,128]{2,1,0:T(4,128)S(1)}, u32[]{:S(2)}, u32[]{:S(2)}) collective-permute-start(f32[10,4,128]{2,1,0:T(4,128)} %get-tuple-element.19), channel_id=1, source_target_pairs={{0,1},{1,2},{2,3},{4,5},{5,6},{6,7},{8,9},{9,10},{10,11},{12,13},{... | collective-permute-start | bytes 61448 | tf_op jit(solution)/shard_map/ppermute | solution.py:231
  12.4 5.4 %collective-permute-start.2 = (f32[10,4,128]{2,1,0:T(4,128)}, f32[10,4,128]{2,1,0:T(4,128)S(1)}, u32[]{:S(2)}, u32[]{:S(2)}) collective-permute-start(f32[10,4,128]{2,1,0:T(4,128)} %get-tuple-element.20), channel_id=1, source_target_pairs={{1,0},{2,1},{3,2},{5,4},{6,5},{7,6},{9,8},{10,9},{11,10},{13,12},{... | collective-permute-start | bytes 61448 | tf_op jit(solution)/shard_map/ppermute | solution.py:232
  17.8 0.6 copy-start.6
  17.9 0.6 copy-start.2
  22.4 8.3 %collective-permute-start.3 = (f32[10,16,128]{2,1,0:T(8,128)}, f32[10,16,128]{2,1,0:T(8,128)S(1)}, u32[]{:S(2)}, u32[]{:S(2)}) collective-permute-start(f32[10,16,128]{2,1,0:T(8,128)} %get-tuple-element.22), channel_id=1, source_target_pairs={{0,4},{4,0},{1,5},{5,1},{2,6},{6,2},{3,7},{7,3},{8,12},{12,8},{9,1... | collective-permute-start | bytes 245768 | tf_op jit(solution)/shard_map/ppermute | solution.py:230
  22.4 8.3 %collective-permute-start.4 = (f32[10,4,128]{2,1,0:T(4,128)}, f32[10,4,128]{2,1,0:T(4,128)S(1)}, u32[]{:S(2)}, u32[]{:S(2)}) collective-permute-start(f32[10,4,128]{2,1,0:T(4,128)} %get-tuple-element.23), channel_id=1, source_target_pairs={{0,1},{1,2},{2,3},{4,5},{5,6},{6,7},{8,9},{9,10},{10,11},{12,13},{... | collective-permute-start | bytes 61448 | tf_op jit(solution)/shard_map/ppermute | solution.py:231
  25.6 5.1 %collective-permute-start.5 = (f32[10,4,128]{2,1,0:T(4,128)}, f32[10,4,128]{2,1,0:T(4,128)S(1)}, u32[]{:S(2)}, u32[]{:S(2)}) collective-permute-start(f32[10,4,128]{2,1,0:T(4,128)} %get-tuple-element.24), channel_id=1, source_target_pairs={{1,0},{2,1},{3,2},{5,4},{6,5},{7,6},{9,8},{10,9},{11,10},{13,12},{... | collective-permute-start | bytes 61448 | tf_op jit(solution)/shard_map/ppermute | solution.py:232
  30.7 0.6 copy-start.12
  30.7 0.6 copy-start.4
  35.3 9.3 %collective-permute-start.6 = (f32[10,16,128]{2,1,0:T(8,128)}, f32[10,16,128]{2,1,0:T(8,128)S(1)}, u32[]{:S(2)}, u32[]{:S(2)}) collective-permute-start(f32[10,16,128]{2,1,0:T(8,128)} %get-tuple-element.26), channel_id=1, source_target_pairs={{0,4},{4,0},{1,5},{5,1},{2,6},{6,2},{3,7},{7,3},{8,12},{12,8},{9,1... | collective-permute-start | bytes 245768 | tf_op jit(solution)/shard_map/ppermute | solution.py:230
  36.7 5.3 %collective-permute-start.7 = (f32[10,4,128]{2,1,0:T(4,128)}, f32[10,4,128]{2,1,0:T(4,128)S(1)}, u32[]{:S(2)}, u32[]{:S(2)}) collective-permute-start(f32[10,4,128]{2,1,0:T(4,128)} %get-tuple-element.27), channel_id=1, source_target_pairs={{0,1},{1,2},{2,3},{4,5},{5,6},{6,7},{8,9},{9,10},{10,11},{12,13},{... | collective-permute-start | bytes 61448 | tf_op jit(solution)/shard_map/ppermute | solution.py:231
  39.8 4.7 %collective-permute-start.8 = (f32[10,4,128]{2,1,0:T(4,128)}, f32[10,4,128]{2,1,0:T(4,128)S(1)}, u32[]{:S(2)}, u32[]{:S(2)}) collective-permute-start(f32[10,4,128]{2,1,0:T(4,128)} %get-tuple-element.28), channel_id=1, source_target_pairs={{1,0},{2,1},{3,2},{5,4},{6,5},{7,6},{9,8},{10,9},{11,10},{13,12},{... | collective-permute-start | bytes 61448 | tf_op jit(solution)/shard_map/ppermute | solution.py:232
  42.0 2.5 %copy-start.11 = (f32[10,4,128]{2,1,0:T(4,128)}, f32[10,4,128]{2,1,0:T(4,128)S(1)}, u32[]{:S(2)}) copy-start(f32[10,4,128]{2,1,0:T(4,128)S(1)} %collective-permute-done.7.ralo_ref) | copy-start | bytes 61444
  44.6 0.6 copy-start.5
  49.2 12.4 %collective-permute-start.9 = (f32[10,16,128]{2,1,0:T(8,128)}, f32[10,16,128]{2,1,0:T(8,128)S(1)}, u32[]{:S(2)}, u32[]{:S(2)}) collective-permute-start(f32[10,16,128]{2,1,0:T(8,128)} %get-tuple-element.30), channel_id=1, source_target_pairs={{0,4},{4,0},{1,5},{5,1},{2,6},{6,2},{3,7},{7,3},{8,12},{12,8},{9,1... | collective-permute-start | bytes 245768 | tf_op jit(solution)/shard_map/ppermute | solution.py:230
  49.2 12.3 %collective-permute-start.10 = (f32[10,4,128]{2,1,0:T(4,128)}, f32[10,4,128]{2,1,0:T(4,128)S(1)}, u32[]{:S(2)}, u32[]{:S(2)}) collective-permute-start(f32[10,4,128]{2,1,0:T(4,128)} %get-tuple-element.31), channel_id=1, source_target_pairs={{0,1},{1,2},{2,3},{4,5},{5,6},{6,7},{8,9},{9,10},{10,11},{12,13},{... | collective-permute-start | bytes 61448 | tf_op jit(solution)/shard_map/ppermute | solution.py:231
  52.0 9.5 %collective-permute-start.11 = (f32[10,4,128]{2,1,0:T(4,128)}, f32[10,4,128]{2,1,0:T(4,128)S(1)}, u32[]{:S(2)}, u32[]{:S(2)}) collective-permute-start(f32[10,4,128]{2,1,0:T(4,128)} %get-tuple-element.32), channel_id=1, source_target_pairs={{1,0},{2,1},{3,2},{5,4},{6,5},{7,6},{9,8},{10,9},{11,10},{13,12},{... | collective-permute-start | bytes 61448 | tf_op jit(solution)/shard_map/ppermute | solution.py:232
  54.7 12.5 %copy-start.14 = (f32[3,10]{1,0:T(4,128)S(1)}, f32[3,10]{1,0:T(4,128)}, u32[]{:S(2)}) copy-start(f32[3,10]{1,0:T(4,128)} %param.17) | copy-start | bytes 364
  61.5 0.6 copy-start.8
  61.5 0.6 copy-start.3
  71.6 20.2 %all-to-all-start = ((f32[16,3,512]{2,1,0:T(4,128)}), f32[16,3,512]{2,1,0:T(4,128)S(1)}, u32[]{:S(2)}, u32[]{:S(2)}) async-start(f32[16,3,512]{2,1,0:T(4,128)} %bitcast.28), calls=%async_computation | async-start | bytes 262144 | tf_op jit(solution)/shard_map/all_to_all | solution.py:28
  (4 other events, 2.4 us)

commit v3 on v2

--- a/solution.py
+++ b/solution.py
@@ -117,7 +117,7 @@
         inc_ref[x] = lower_a + upper_a + lower_r + upper_r + lower_t + upper_t
         pack4 = pack4 + jnp.where(lane == x, pltpu.roll(q4, (x + 1) % lanes, 1), 0.0)
         pack5 = pack5 + jnp.where(lane == x, pltpu.roll(q5, x, 1), 0.0) if x else jnp.where(lane == 0, q5, 0.0)
-    pick = pick_ref[...]
+    pick = (pick_ref[...] == lax.broadcasted_iota(jnp.int32, (rows, rows), 1)).astype(jnp.bfloat16)
     got4 = exact_pick(pick, pack4)
     got5 = exact_pick(pick, pack5)
     up4 = pltpu.roll(got4, lanes - half, 1)
@@ -138,6 +138,18 @@
         out_ref[x] = psi + RELAX * residual / diag
     if edges:
         write_edges(mat_ref, wt_ref, out_ref, face_ref, axs_ref, q2_ref, q3_ref, comps, tile_r)
+
+
+def modes_kernel(where_ref, mode_ref, out_ref, *, blocks):
+    owned = where_ref.shape[1]
+    lanes = mode_ref.shape[1]
+    lane_of = where_ref[0:1, :]
+    row_of = where_ref[1:2, :]
+    pick = (lax.broadcasted_iota(jnp.int32, (lanes, owned), 0) == lane_of).astype(jnp.bfloat16)
+    hit = lax.broadcasted_iota(jnp.int32, (blocks, owned), 0) == row_of
+    for g in range(out_ref.shape[0]):
+        part = jnp.dot(mode_ref[pl.ds(g * blocks, blocks), :], pick, preferred_element_type=jnp.float32)
+        out_ref[pl.ds(g, 1), :] = jnp.sum(jnp.where(hit, part, 0.0), axis=0, keepdims=True)
 
 
 def vmem_spec():
@@ -221,7 +233,7 @@
     partner = pairing[0, 0]
     faces = face_coef.astype(jnp.float32).reshape(6, rows, pitch)
     diag = diag_coef.reshape(rows, pitch)
-    pick = (partner[:, None] == jnp.arange(rows, dtype=partner.dtype)[None, :]).astype(jnp.bfloat16)
+    pick = partner.astype(jnp.int32).reshape(rows, 1)
     up_r, down_r = neighbours("radial")
     psi = psi_start.reshape(comps, rows, pitch)
     src = source.reshape(comps, rows, pitch)
@@ -261,15 +273,13 @@
     gathered = sum_at_owner(in_order, "phase", 1)
     mine = lax.dynamic_slice_in_dim(order, lax.axis_index("phase") * owned, owned)
     count_k = mode_shape.shape[0]
-    mine_lane = (mine[None, :] % lanes == jnp.arange(lanes, dtype=mine.dtype)[:, None]).astype(jnp.bfloat16)
-    mode_lane = jnp.einsum(
-        "xl,lj->xj",
-        mode_shape.reshape(count_k * 3 * blocks, lanes),
-        mine_lane,
-        preferred_element_type=jnp.float32,
-    ).reshape(count_k, 3, blocks, owned)
-    mine_row = (mine // lanes)[None, None, None, :] == jnp.arange(blocks, dtype=mine.dtype)[None, None, :, None]
-    modes = jnp.sum(jnp.where(mine_row, mode_lane, 0.0), axis=2)
+    where = jnp.stack([mine % lanes, mine // lanes]).astype(jnp.int32)
+    modes = pl.pallas_call(
+        functools.partial(modes_kernel, blocks=blocks),
+        out_shape=jax.ShapeDtypeStruct((count_k * 3, owned), jnp.float32),
+        in_specs=[vmem_spec(), vmem_spec()],
+        out_specs=vmem_spec(),
+    )(where, mode_shape.reshape(count_k * 3 * blocks, lanes)).reshape(count_k, 3, owned)
     sens = modes[:, 0] * gathered[0] + modes[:, 1] * gathered[1] + modes[:, 2] * gathered[2]
     return (psi_out, sens.reshape(count_k, 1, 1, owned))
 

time: 93.3 us -> 89 us (0.954)
  the two profiles are of different devices: /device:TPU:3 before, /device:TPU:0 now
where the time goes in v3:
time: 89 us; the launch traced here: 87.5 us
  starting transfers between devices  29.2 us (33%)
  waiting for transfers between devices  20.2 us (23%)
  Pallas kernels  19.9 us (22%)
  local copies, waits for them, and re-layouts  8.07 us (9%)
  matrix products  4.42 us (5%)
  other arithmetic  3.45 us (4%)
  between operations  2.32 us (3%)
    ppermute x4, waiting for transfers between devices, body(): rahi = lax.ppermute(q3, 'radial', down_r)  15.5 us
    pallas_call x4, Pallas kernels, run_section(): pl.pallas_call(functools.partial(section_kernel, tile_r=tile_r, edges=edg...  15.4 us
    ppermute x4, starting transfers between devices, body(): ralo = lax.ppermute(q2, 'radial', up_r)  11.8 us
    all_to_all x1, starting transfers between devices, sum_at_owner(): blocks = lax.all_to_all(split_up(value, dim, count), axis, 0, 0, tiled=True)  7.88 us
    ppermute x4, starting transfers between devices, body(): rahi = lax.ppermute(q3, 'radial', down_r)  5.35 us
    ppermute x4, starting transfers between devices, body(): axr = lax.ppermute(axs, 'axial', [(0, 1), (1, 0)])  4.17 us
    unnamed x34, local copies, waits for them, and re-layouts  4.12 us
    dot_general x1, matrix products, body(): jnp.einsum('xl,lj->xj', weighted.reshape(dims * blocks, lanes), pick_lane...  3.98 us
  transfers between devices with their start and end apart: 13, of which 7 were waited for; matrix products, arithmetic and copies ran while one was open for 3% of the time, Pallas kernels for 3%

profile of v3, /device:TPU:0, one launch (start us, length us, event | category | flops | bytes accessed | tf_op | source)
XLA Modules:
  0.0 87.5 jit_solution(2592577214717354909)
XLA Ops:
  3.5 1.6 %bitcast_convert_fusion.face_ref = f32[6,64,128]{2,1,0:T(8,128)} fusion(bf16[6,4,16,128]{3,2,1,0:T(8,128)(2,1)} %param.13), kind=kLoop, calls=%fused_computation.11 | loop fusion | flops 49152 | bytes 294912 | tf_op jit(solution)/shard_map/reshape | solution.py:234
  5.7 1.9 %shard_map.122 = (f32[10,16,128]{2,1,0:T(8,128)}, f32[10,4,128]{2,1,0:T(4,128)}, f32[10,4,128]{2,1,0:T(4,128)}) custom-call(f32[600]{0:T(1024)} %reshape.300.mat_ref, f32[7]{0:T(128)} %stack.26.wt_ref, f32[10,64,128]{2,1,0:T(8,128)} %bitcast.88, f32[6,64,128]{2,1,0:T(8,128)} %bitcast_convert_fusion.face_ref), custom_call_target="tpu_custom_call" | custom-call | tf_op jit(solution)/shard_map/pallas_call | solution.py:174
  7.6 2.0 %collective-permute-start = (f32[10,16,128]{2,1,0:T(8,128)}, f32[10,16,128]{2,1,0:T(8,128)S(1)}, u32[]{:S(2)}, u32[]{:S(2)}) collective-permute-start(f32[10,16,128]{2,1,0:T(8,128)} %get-tuple-element.18), channel_id=1, source_target_pairs={{0,4},{4,0},{1,5},{5,1},{2,6},{6,2},{3,7},{7,3},{8,12},{12,8},{9,1... | collective-permute-start | bytes 245768 | tf_op jit(solution)/shard_map/ppermute | solution.py:242
  9.6 3.4 %collective-permute-start.1 = (f32[10,4,128]{2,1,0:T(4,128)}, f32[10,4,128]{2,1,0:T(4,128)S(1)}, u32[]{:S(2)}, u32[]{:S(2)}) collective-permute-start(f32[10,4,128]{2,1,0:T(4,128)} %get-tuple-element.19), channel_id=1, source_target_pairs={{0,1},{1,2},{2,3},{4,5},{5,6},{6,7},{8,9},{9,10},{10,11},{12,13},{... | collective-permute-start | bytes 61448 | tf_op jit(solution)/shard_map/ppermute | solution.py:243
  13.0 1.3 %collective-permute-start.2 = (f32[10,4,128]{2,1,0:T(4,128)}, f32[10,4,128]{2,1,0:T(4,128)S(1)}, u32[]{:S(2)}, u32[]{:S(2)}) collective-permute-start(f32[10,4,128]{2,1,0:T(4,128)} %get-tuple-element.20), channel_id=1, source_target_pairs={{1,0},{2,1},{3,2},{5,4},{6,5},{7,6},{9,8},{10,9},{11,10},{13,12},{... | collective-permute-start | bytes 61448 | tf_op jit(solution)/shard_map/ppermute | solution.py:244
  15.5 3.4 %collective-permute-done.2.rahi_ref = f32[10,4,128]{2,1,0:T(4,128)S(1)} collective-permute-done((f32[10,4,128]{2,1,0:T(4,128)}, f32[10,4,128]{2,1,0:T(4,128)S(1)}, u32[]{:S(2)}, u32[]{:S(2)}) %collective-permute-start.2) | collective-permute-done | bytes 20512 | tf_op jit(solution)/shard_map/ppermute | solution.py:244
  19.6 3.9 %shard_map.123 = (f32[10,64,128]{2,1,0:T(8,128)}, f32[10,16,128]{2,1,0:T(8,128)}, f32[10,4,128]{2,1,0:T(4,128)}, f32[10,4,128]{2,1,0:T(4,128)}) custom-call(f32[600]{0:T(1024)} %reshape.300.mat_ref, f32[7]{0:T(128)} %stack.26.wt_ref, f32[10,64,128]{2,1,0:T(8,128)} %bitcast.89, f32[10,64,128]{2,1,0:T(8,128)} %bitcast.82, ...), custom_call_target="tpu_custom_call" | custom-call | tf_op jit(solution)/shard_map/pallas_call | solution.py:184
  23.6 3.4 %collective-permute-start.4 = (f32[10,4,128]{2,1,0:T(4,128)}, f32[10,4,128]{2,1,0:T(4,128)S(1)}, u32[]{:S(2)}, u32[]{:S(2)}) collective-permute-start(f32[10,4,128]{2,1,0:T(4,128)} %get-tuple-element.23), channel_id=1, source_target_pairs={{0,1},{1,2},{2,3},{4,5},{5,6},{6,7},{8,9},{9,10},{10,11},{12,13},{... | collective-permute-start | bytes 61448 | tf_op jit(solution)/shard_map/ppermute | solution.py:243
  27.0 1.3 %collective-permute-start.5 = (f32[10,4,128]{2,1,0:T(4,128)}, f32[10,4,128]{2,1,0:T(4,128)S(1)}, u32[]{:S(2)}, u32[]{:S(2)}) collective-permute-start(f32[10,4,128]{2,1,0:T(4,128)} %get-tuple-element.24), channel_id=1, source_target_pairs={{1,0},{2,1},{3,2},{5,4},{6,5},{7,6},{9,8},{10,9},{11,10},{13,12},{... | collective-permute-start | bytes 61448 | tf_op jit(solution)/shard_map/ppermute | solution.py:244
  28.6 4.2 %collective-permute-done.5.rahi_ref = f32[10,4,128]{2,1,0:T(4,128)S(1)} collective-permute-done((f32[10,4,128]{2,1,0:T(4,128)}, f32[10,4,128]{2,1,0:T(4,128)S(1)}, u32[]{:S(2)}, u32[]{:S(2)}) %collective-permute-start.5) | collective-permute-done | bytes 20512 | tf_op jit(solution)/shard_map/ppermute | solution.py:244
  33.5 3.9 %shard_map.124 = (f32[10,64,128]{2,1,0:T(8,128)}, f32[10,16,128]{2,1,0:T(8,128)}, f32[10,4,128]{2,1,0:T(4,128)}, f32[10,4,128]{2,1,0:T(4,128)}) custom-call(f32[600]{0:T(1024)} %reshape.300.mat_ref, f32[7]{0:T(128)} %stack.26.wt_ref, f32[10,64,128]{2,1,0:T(8,128)} %get-tuple-element.21.psi_ref, f32[10,64,128]{2,1,0:T(8,128)} %bitcast.83, ...), custom_call_target="tpu_custom_call" | custom-call | tf_op jit(solution)/shard_map/pallas_call | solution.py:184
  37.4 1.9 %collective-permute-start.6 = (f32[10,16,128]{2,1,0:T(8,128)}, f32[10,16,128]{2,1,0:T(8,128)S(1)}, u32[]{:S(2)}, u32[]{:S(2)}) collective-permute-start(f32[10,16,128]{2,1,0:T(8,128)} %get-tuple-element.26), channel_id=1, source_target_pairs={{0,4},{4,0},{1,5},{5,1},{2,6},{6,2},{3,7},{7,3},{8,12},{12,8},{9,1... | collective-permute-start | bytes 245768 | tf_op jit(solution)/shard_map/ppermute | solution.py:242
  39.3 3.1 %collective-permute-start.7 = (f32[10,4,128]{2,1,0:T(4,128)}, f32[10,4,128]{2,1,0:T(4,128)S(1)}, u32[]{:S(2)}, u32[]{:S(2)}) collective-permute-start(f32[10,4,128]{2,1,0:T(4,128)} %get-tuple-element.27), channel_id=1, source_target_pairs={{0,1},{1,2},{2,3},{4,5},{5,6},{6,7},{8,9},{9,10},{10,11},{12,13},{... | collective-permute-start | bytes 61448 | tf_op jit(solution)/shard_map/ppermute | solution.py:243
  42.4 1.3 %collective-permute-start.8 = (f32[10,4,128]{2,1,0:T(4,128)}, f32[10,4,128]{2,1,0:T(4,128)S(1)}, u32[]{:S(2)}, u32[]{:S(2)}) collective-permute-start(f32[10,4,128]{2,1,0:T(4,128)} %get-tuple-element.28), channel_id=1, source_target_pairs={{1,0},{2,1},{3,2},{5,4},{6,5},{7,6},{9,8},{10,9},{11,10},{13,12},{... | collective-permute-start | bytes 61448 | tf_op jit(solution)/shard_map/ppermute | solution.py:244
  44.1 4.2 %collective-permute-done.8.rahi_ref = f32[10,4,128]{2,1,0:T(4,128)S(1)} collective-permute-done((f32[10,4,128]{2,1,0:T(4,128)}, f32[10,4,128]{2,1,0:T(4,128)S(1)}, u32[]{:S(2)}, u32[]{:S(2)}) %collective-permute-start.8) | collective-permute-done | bytes 20512 | tf_op jit(solution)/shard_map/ppermute | solution.py:244
  49.0 3.9 %shard_map.125 = (f32[10,64,128]{2,1,0:T(8,128)}, f32[10,16,128]{2,1,0:T(8,128)}, f32[10,4,128]{2,1,0:T(4,128)}, f32[10,4,128]{2,1,0:T(4,128)}) custom-call(f32[600]{0:T(1024)} %reshape.300.mat_ref, f32[7]{0:T(128)} %stack.26.wt_ref, f32[10,64,128]{2,1,0:T(8,128)} %get-tuple-element.25.psi_ref, f32[10,64,128]{2,1,0:T(8,128)} %bitcast.84, ...), custom_call_target="tpu_custom_call" | custom-call | tf_op jit(solution)/shard_map/pallas_call | solution.py:184
  53.0 1.9 %collective-permute-start.10 = (f32[10,4,128]{2,1,0:T(4,128)}, f32[10,4,128]{2,1,0:T(4,128)S(1)}, u32[]{:S(2)}, u32[]{:S(2)}) collective-permute-start(f32[10,4,128]{2,1,0:T(4,128)} %get-tuple-element.31), channel_id=1, source_target_pairs={{0,1},{1,2},{2,3},{4,5},{5,6},{6,7},{8,9},{9,10},{10,11},{12,13},{... | collective-permute-start | bytes 61448 | tf_op jit(solution)/shard_map/ppermute | solution.py:243
  54.9 1.5 %collective-permute-start.11 = (f32[10,4,128]{2,1,0:T(4,128)}, f32[10,4,128]{2,1,0:T(4,128)S(1)}, u32[]{:S(2)}, u32[]{:S(2)}) collective-permute-start(f32[10,4,128]{2,1,0:T(4,128)} %get-tuple-element.32), channel_id=1, source_target_pairs={{1,0},{2,1},{3,2},{5,4},{6,5},{7,6},{9,8},{10,9},{11,10},{13,12},{... | collective-permute-start | bytes 61448 | tf_op jit(solution)/shard_map/ppermute | solution.py:244
  57.1 3.7 %collective-permute-done.11.rahi_ref = f32[10,4,128]{2,1,0:T(4,128)S(1)} collective-permute-done((f32[10,4,128]{2,1,0:T(4,128)}, f32[10,4,128]{2,1,0:T(4,128)S(1)}, u32[]{:S(2)}, u32[]{:S(2)}) %collective-permute-start.11) | collective-permute-done | bytes 20512 | tf_op jit(solution)/shard_map/ppermute | solution.py:244
  61.5 3.7 %shard_map.126 = (f32[10,64,128]{2,1,0:T(8,128)}, f32[10,16,128]{2,1,0:T(8,128)}, f32[10,4,128]{2,1,0:T(4,128)}, f32[10,4,128]{2,1,0:T(4,128)}) custom-call(f32[600]{0:T(1024)} %reshape.300.mat_ref, f32[7]{0:T(128)} %stack.26.wt_ref, f32[10,64,128]{2,1,0:T(8,128)} %get-tuple-element.29.psi_ref, f32[10,64,128]{2,1,0:T(8,128)} %bitcast.85, ...), custom_call_target="tpu_custom_call" | custom-call | tf_op jit(solution)/shard_map/pallas_call | solution.py:184
  66.9 4.0 %fusion.3 = f32[3,8192]{1,0:T(4,128)} fusion(s32[8192]{0:T(1024)S(1)} %add_select_fusion, pred[64,8192]{1,0:T(8,128)(4,1)S(1)} %iota_compare_fusion.1, f32[1,3,64,128]{3,1,2,0:T(4,128)S(1)} %fusion.6), kind=kOutput, calls=%fused_computation.6 | convolution fusion | flops 2420088832 | bytes 753664 | tf_op jit(solution)/shard_map/xl,lj->xj/dot_general | solution.py:265
  70.9 7.9 %all-to-all-start = ((f32[16,3,512]{2,1,0:T(4,128)}), f32[16,3,512]{2,1,0:T(4,128)S(1)}, u32[]{:S(2)}, u32[]{:S(2)}) async-start(f32[16,3,512]{2,1,0:T(4,128)} %bitcast.26), calls=%async_computation | async-start | bytes 262144 | tf_op jit(solution)/shard_map/all_to_all | solution.py:28
  79.4 2.5 %shard_map.127 = f32[36,512]{1,0:T(8,128)} custom-call(s32[2,512]{1,0:T(2,128)} %pad_add_fusion.where_ref, bf16[2304,128]{1,0:T(8,128)(2,1)} %bitcast.90), custom_call_target="tpu_custom_call" | custom-call | tf_op jit(solution)/shard_map/pallas_call | solution.py:277
  82.9 3.9 %all-to-all-done = f32[16,3,512]{2,1,0:T(4,128)S(1)} async-done(((f32[16,3,512]{2,1,0:T(4,128)}), f32[16,3,512]{2,1,0:T(4,128)S(1)}, u32[]{:S(2)}, u32[]{:S(2)}) %all-to-all-start) | async-done | bytes 98336 | tf_op jit(solution)/shard_map/all_to_all | solution.py:28
  (62 shorter events, 11.3 us)
Async XLA Ops:
  0.6 65.8 %copy-start = (f32[3,10]{1,0:T(4,128)S(1)}, f32[3,10]{1,0:T(4,128)}, u32[]{:S(2)}) copy-start(f32[3,10]{1,0:T(4,128)} %param.17) | copy-start | bytes 364
  2.4 11.9 %copy-start.1 = (s32[1,1,8192]{2,1,0:T(1,128)S(1)}, s32[1,1,8192]{2,1,0:T(1,128)}, u32[]{:S(2)}) copy-start(s32[1,1,8192]{2,1,0:T(1,128)} %param.21) | copy-start | bytes 98308
  5.1 9.7 %copy-start.14 = (s32[1,1,64]{2,1,0:T(1,128)S(1)}, s32[1,1,64]{2,1,0:T(1,128)}, u32[]{:S(2)}) copy-start(s32[1,1,64]{2,1,0:T(1,128)} %param.20) | copy-start | bytes 772
  7.6 11.3 %collective-permute-start = (f32[10,16,128]{2,1,0:T(8,128)}, f32[10,16,128]{2,1,0:T(8,128)S(1)}, u32[]{:S(2)}, u32[]{:S(2)}) collective-permute-start(f32[10,16,128]{2,1,0:T(8,128)} %get-tuple-element.18), channel_id=1, source_target_pairs={{0,4},{4,0},{1,5},{5,1},{2,6},{6,2},{3,7},{7,3},{8,12},{12,8},{9,1... | collective-permute-start | bytes 245768 | tf_op jit(solution)/shard_map/ppermute | solution.py:242
  9.6 5.9 %collective-permute-start.1 = (f32[10,4,128]{2,1,0:T(4,128)}, f32[10,4,128]{2,1,0:T(4,128)S(1)}, u32[]{:S(2)}, u32[]{:S(2)}) collective-permute-start(f32[10,4,128]{2,1,0:T(4,128)} %get-tuple-element.19), channel_id=1, source_target_pairs={{0,1},{1,2},{2,3},{4,5},{5,6},{6,7},{8,9},{9,10},{10,11},{12,13},{... | collective-permute-start | bytes 61448 | tf_op jit(solution)/shard_map/ppermute | solution.py:243
  13.0 5.9 %collective-permute-start.2 = (f32[10,4,128]{2,1,0:T(4,128)}, f32[10,4,128]{2,1,0:T(4,128)S(1)}, u32[]{:S(2)}, u32[]{:S(2)}) collective-permute-start(f32[10,4,128]{2,1,0:T(4,128)} %get-tuple-element.20), channel_id=1, source_target_pairs={{1,0},{2,1},{3,2},{5,4},{6,5},{7,6},{9,8},{10,9},{11,10},{13,12},{... | collective-permute-start | bytes 61448 | tf_op jit(solution)/shard_map/ppermute | solution.py:244
  15.5 3.4 %copy-start.10 = (f32[10,4,128]{2,1,0:T(4,128)}, f32[10,4,128]{2,1,0:T(4,128)S(1)}, u32[]{:S(2)}) copy-start(f32[10,4,128]{2,1,0:T(4,128)S(1)} %collective-permute-done.1.ralo_ref) | copy-start | bytes 61444
  18.9 0.6 copy-start.4
  23.4 9.4 %collective-permute-start.3 = (f32[10,16,128]{2,1,0:T(8,128)}, f32[10,16,128]{2,1,0:T(8,128)S(1)}, u32[]{:S(2)}, u32[]{:S(2)}) collective-permute-start(f32[10,16,128]{2,1,0:T(8,128)} %get-tuple-element.22), channel_id=1, source_target_pairs={{0,4},{4,0},{1,5},{5,1},{2,6},{6,2},{3,7},{7,3},{8,12},{12,8},{9,1... | collective-permute-start | bytes 245768 | tf_op jit(solution)/shard_map/ppermute | solution.py:242
  23.6 5.1 %collective-permute-start.4 = (f32[10,4,128]{2,1,0:T(4,128)}, f32[10,4,128]{2,1,0:T(4,128)S(1)}, u32[]{:S(2)}, u32[]{:S(2)}) collective-permute-start(f32[10,4,128]{2,1,0:T(4,128)} %get-tuple-element.23), channel_id=1, source_target_pairs={{0,1},{1,2},{2,3},{4,5},{5,6},{6,7},{8,9},{9,10},{10,11},{12,13},{... | collective-permute-start | bytes 61448 | tf_op jit(solution)/shard_map/ppermute | solution.py:243
  27.0 5.9 %collective-permute-start.5 = (f32[10,4,128]{2,1,0:T(4,128)}, f32[10,4,128]{2,1,0:T(4,128)S(1)}, u32[]{:S(2)}, u32[]{:S(2)}) collective-permute-start(f32[10,4,128]{2,1,0:T(4,128)} %get-tuple-element.24), channel_id=1, source_target_pairs={{1,0},{2,1},{3,2},{5,4},{6,5},{7,6},{9,8},{10,9},{11,10},{13,12},{... | collective-permute-start | bytes 61448 | tf_op jit(solution)/shard_map/ppermute | solution.py:244
  28.6 4.2 %copy-start.6 = (f32[10,4,128]{2,1,0:T(4,128)}, f32[10,4,128]{2,1,0:T(4,128)S(1)}, u32[]{:S(2)}) copy-start(f32[10,4,128]{2,1,0:T(4,128)S(1)} %collective-permute-done.4.ralo_ref) | copy-start | bytes 61444
  32.8 0.6 copy-start.2
  37.4 10.9 %collective-permute-start.6 = (f32[10,16,128]{2,1,0:T(8,128)}, f32[10,16,128]{2,1,0:T(8,128)S(1)}, u32[]{:S(2)}, u32[]{:S(2)}) collective-permute-start(f32[10,16,128]{2,1,0:T(8,128)} %get-tuple-element.26), channel_id=1, source_target_pairs={{0,4},{4,0},{1,5},{5,1},{2,6},{6,2},{3,7},{7,3},{8,12},{12,8},{9,1... | collective-permute-start | bytes 245768 | tf_op jit(solution)/shard_map/ppermute | solution.py:242
  39.3 4.8 %collective-permute-start.7 = (f32[10,4,128]{2,1,0:T(4,128)}, f32[10,4,128]{2,1,0:T(4,128)S(1)}, u32[]{:S(2)}, u32[]{:S(2)}) collective-permute-start(f32[10,4,128]{2,1,0:T(4,128)} %get-tuple-element.27), channel_id=1, source_target_pairs={{0,1},{1,2},{2,3},{4,5},{5,6},{6,7},{8,9},{9,10},{10,11},{12,13},{... | collective-permute-start | bytes 61448 | tf_op jit(solution)/shard_map/ppermute | solution.py:243
  42.4 5.9 %collective-permute-start.8 = (f32[10,4,128]{2,1,0:T(4,128)}, f32[10,4,128]{2,1,0:T(4,128)S(1)}, u32[]{:S(2)}, u32[]{:S(2)}) collective-permute-start(f32[10,4,128]{2,1,0:T(4,128)} %get-tuple-element.28), channel_id=1, source_target_pairs={{1,0},{2,1},{3,2},{5,4},{6,5},{7,6},{9,8},{10,9},{11,10},{13,12},{... | collective-permute-start | bytes 61448 | tf_op jit(solution)/shard_map/ppermute | solution.py:244
  44.1 4.2 %copy-start.11 = (f32[10,4,128]{2,1,0:T(4,128)}, f32[10,4,128]{2,1,0:T(4,128)S(1)}, u32[]{:S(2)}) copy-start(f32[10,4,128]{2,1,0:T(4,128)S(1)} %collective-permute-done.7.ralo_ref) | copy-start | bytes 61444
  48.3 0.6 copy-start.5
  52.9 7.9 %collective-permute-start.9 = (f32[10,16,128]{2,1,0:T(8,128)}, f32[10,16,128]{2,1,0:T(8,128)S(1)}, u32[]{:S(2)}, u32[]{:S(2)}) collective-permute-start(f32[10,16,128]{2,1,0:T(8,128)} %get-tuple-element.30), channel_id=1, source_target_pairs={{0,4},{4,0},{1,5},{5,1},{2,6},{6,2},{3,7},{7,3},{8,12},{12,8},{9,1... | collective-permute-start | bytes 245768 | tf_op jit(solution)/shard_map/ppermute | solution.py:242
  53.0 4.1 %collective-permute-start.10 = (f32[10,4,128]{2,1,0:T(4,128)}, f32[10,4,128]{2,1,0:T(4,128)S(1)}, u32[]{:S(2)}, u32[]{:S(2)}) collective-permute-start(f32[10,4,128]{2,1,0:T(4,128)} %get-tuple-element.31), channel_id=1, source_target_pairs={{0,1},{1,2},{2,3},{4,5},{5,6},{6,7},{8,9},{9,10},{10,11},{12,13},{... | collective-permute-start | bytes 61448 | tf_op jit(solution)/shard_map/ppermute | solution.py:243
  54.9 5.9 %collective-permute-start.11 = (f32[10,4,128]{2,1,0:T(4,128)}, f32[10,4,128]{2,1,0:T(4,128)S(1)}, u32[]{:S(2)}, u32[]{:S(2)}) collective-permute-start(f32[10,4,128]{2,1,0:T(4,128)} %get-tuple-element.32), channel_id=1, source_target_pairs={{1,0},{2,1},{3,2},{5,4},{6,5},{7,6},{9,8},{10,9},{11,10},{13,12},{... | collective-permute-start | bytes 61448 | tf_op jit(solution)/shard_map/ppermute | solution.py:244
  57.1 3.7 %copy-start.8 = (f32[10,4,128]{2,1,0:T(4,128)}, f32[10,4,128]{2,1,0:T(4,128)S(1)}, u32[]{:S(2)}) copy-start(f32[10,4,128]{2,1,0:T(4,128)S(1)} %collective-permute-done.10.ralo_ref) | copy-start | bytes 61444
  60.8 0.6 copy-start.3
  70.9 15.9 %all-to-all-start = ((f32[16,3,512]{2,1,0:T(4,128)}), f32[16,3,512]{2,1,0:T(4,128)S(1)}, u32[]{:S(2)}, u32[]{:S(2)}) async-start(f32[16,3,512]{2,1,0:T(4,128)} %bitcast.26), calls=%async_computation | async-start | bytes 262144 | tf_op jit(solution)/shard_map/all_to_all | solution.py:28
  (4 other events, 2.4 us)

commit v4 on v3

--- a/solution.py
+++ b/solution.py
@@ -27,6 +27,19 @@
     count = lax.axis_size(axis)
     blocks = lax.all_to_all(split_up(value, dim, count), axis, 0, 0, tiled=True)
     return jnp.sum(blocks, axis=0)
+
+
+def sum_at_owner_paired(value, axis, dim):
+    count = lax.axis_size(axis)
+    blocks = split_up(value, dim, count)
+    core = lax.axis_index(axis) % 2
+    even, odd = blocks[0::2], blocks[1::2]
+    send = jnp.where(core == 0, odd, even)
+    keep = jnp.where(core == 0, even, odd)
+    got = lax.ppermute(send, axis, [(p, p ^ 1) for p in range(count)])
+    groups = [list(range(parity, count, 2)) for parity in range(2)]
+    mixed = lax.all_to_all(keep + got, axis, 0, 0, tiled=True, axis_index_groups=groups)
+    return jnp.sum(mixed, axis=0)
 
 
 def build_matrices(flux_jac):
@@ -270,7 +283,7 @@
     ).reshape(dims, blocks, cells)
     pick_row = row_of[None, None, :] == jnp.arange(blocks, dtype=order.dtype)[None, :, None]
     in_order = jnp.sum(jnp.where(pick_row, by_lane, 0.0), axis=1)
-    gathered = sum_at_owner(in_order, "phase", 1)
+    gathered = sum_at_owner_paired(in_order, "phase", 1) if owners % 2 == 0 else sum_at_owner(in_order, "phase", 1)
     mine = lax.dynamic_slice_in_dim(order, lax.axis_index("phase") * owned, owned)
     count_k = mode_shape.shape[0]
     where = jnp.stack([mine % lanes, mine // lanes]).astype(jnp.int32)

time: 89 us -> 89.4 us (level)
  waiting for transfers between devices: 20.2 us -> 21.2 us
    ppermute x0 -> x1, waiting for transfers between devices: none -> 1.21 us  [sum_at_owner_paired(): got = lax.ppermute(send, axis, [(p, p ^ 1) for p in range(count)])]
  transfers between devices with their start and end apart: 13 -> 14, of which waited for: 7 -> 8; matrix products, arithmetic and copies ran while one was open for 3% -> 3% of each run, Pallas kernels for 3% -> 3%
where the time goes in v4:
time: 89.4 us; the launch traced here: 88.7 us
  starting transfers between devices  29.1 us (33%)
  waiting for transfers between devices  21.2 us (24%)
  Pallas kernels  19.9 us (22%)
  local copies, waits for them, and re-layouts  8.11 us (9%)
  other arithmetic  4.12 us (5%)
  matrix products  3.77 us (4%)
  between operations  2.36 us (3%)
    ppermute x4, waiting for transfers between devices, body(): rahi = lax.ppermute(q3, 'radial', down_r)  15.8 us
    pallas_call x4, Pallas kernels, run_section(): pl.pallas_call(functools.partial(section_kernel, tile_r=tile_r, edges=edg...  15.4 us
    ppermute x4, starting transfers between devices, body(): ralo = lax.ppermute(q2, 'radial', up_r)  11.8 us
    all_to_all x1, starting transfers between devices, sum_at_owner_paired(): lax.all_to_all(keep + got, axis, 0, 0, tiled=True, axis_index_groups=groups)  7.78 us
    ppermute x4, starting transfers between devices, body(): rahi = lax.ppermute(q3, 'radial', down_r)  5.35 us
    ppermute x4, starting transfers between devices, body(): axr = lax.ppermute(axs, 'axial', [(0, 1), (1, 0)])  4.16 us
    unnamed x34, local copies, waits for them, and re-layouts  4.13 us
    all_to_all x1, waiting for transfers between devices, sum_at_owner_paired(): lax.all_to_all(keep + got, axis, 0, 0, tiled=True, axis_index_groups=groups)  3.76 us
  transfers between devices with their start and end apart: 14, of which 8 were waited for; matrix products, arithmetic and copies ran while one was open for 3% of the time, Pallas kernels for 3%

profile of v4, /device:TPU:0, one launch (start us, length us, event | category | flops | bytes accessed | tf_op | source)
XLA Modules:
  0.0 88.7 jit_solution(4681946508123241820)
XLA Ops:
  3.5 1.6 %bitcast_convert_fusion.face_ref = f32[6,64,128]{2,1,0:T(8,128)} fusion(bf16[6,4,16,128]{3,2,1,0:T(8,128)(2,1)} %param.13), kind=kLoop, calls=%fused_computation.11 | loop fusion | flops 49152 | bytes 294912 | tf_op jit(solution)/shard_map/reshape | solution.py:247
  5.7 1.9 %shard_map.122 = (f32[10,16,128]{2,1,0:T(8,128)}, f32[10,4,128]{2,1,0:T(4,128)}, f32[10,4,128]{2,1,0:T(4,128)}) custom-call(f32[600]{0:T(1024)} %reshape.300.mat_ref, f32[7]{0:T(128)} %stack.26.wt_ref, f32[10,64,128]{2,1,0:T(8,128)} %bitcast.88, f32[6,64,128]{2,1,0:T(8,128)} %bitcast_convert_fusion.face_ref), custom_call_target="tpu_custom_call" | custom-call | tf_op jit(solution)/shard_map/pallas_call | solution.py:187
  7.6 2.0 %collective-permute-start = (f32[10,16,128]{2,1,0:T(8,128)}, f32[10,16,128]{2,1,0:T(8,128)S(1)}, u32[]{:S(2)}, u32[]{:S(2)}) collective-permute-start(f32[10,16,128]{2,1,0:T(8,128)} %get-tuple-element.18), channel_id=1, source_target_pairs={{0,4},{4,0},{1,5},{5,1},{2,6},{6,2},{3,7},{7,3},{8,12},{12,8},{9,1... | collective-permute-start | bytes 245768 | tf_op jit(solution)/shard_map/ppermute | solution.py:255
  9.7 3.4 %collective-permute-start.1 = (f32[10,4,128]{2,1,0:T(4,128)}, f32[10,4,128]{2,1,0:T(4,128)S(1)}, u32[]{:S(2)}, u32[]{:S(2)}) collective-permute-start(f32[10,4,128]{2,1,0:T(4,128)} %get-tuple-element.19), channel_id=1, source_target_pairs={{0,1},{1,2},{2,3},{4,5},{5,6},{6,7},{8,9},{9,10},{10,11},{12,13},{... | collective-permute-start | bytes 61448 | tf_op jit(solution)/shard_map/ppermute | solution.py:256
  13.1 1.3 %collective-permute-start.2 = (f32[10,4,128]{2,1,0:T(4,128)}, f32[10,4,128]{2,1,0:T(4,128)S(1)}, u32[]{:S(2)}, u32[]{:S(2)}) collective-permute-start(f32[10,4,128]{2,1,0:T(4,128)} %get-tuple-element.20), channel_id=1, source_target_pairs={{1,0},{2,1},{3,2},{5,4},{6,5},{7,6},{9,8},{10,9},{11,10},{13,12},{... | collective-permute-start | bytes 61448 | tf_op jit(solution)/shard_map/ppermute | solution.py:257
  15.3 3.7 %collective-permute-done.2.rahi_ref = f32[10,4,128]{2,1,0:T(4,128)S(1)} collective-permute-done((f32[10,4,128]{2,1,0:T(4,128)}, f32[10,4,128]{2,1,0:T(4,128)S(1)}, u32[]{:S(2)}, u32[]{:S(2)}) %collective-permute-start.2) | collective-permute-done | bytes 20512 | tf_op jit(solution)/shard_map/ppermute | solution.py:257
  19.6 3.9 %shard_map.123 = (f32[10,64,128]{2,1,0:T(8,128)}, f32[10,16,128]{2,1,0:T(8,128)}, f32[10,4,128]{2,1,0:T(4,128)}, f32[10,4,128]{2,1,0:T(4,128)}) custom-call(f32[600]{0:T(1024)} %reshape.300.mat_ref, f32[7]{0:T(128)} %stack.26.wt_ref, f32[10,64,128]{2,1,0:T(8,128)} %bitcast.89, f32[10,64,128]{2,1,0:T(8,128)} %bitcast.82, ...), custom_call_target="tpu_custom_call" | custom-call | tf_op jit(solution)/shard_map/pallas_call | solution.py:197
  23.6 3.4 %collective-permute-start.4 = (f32[10,4,128]{2,1,0:T(4,128)}, f32[10,4,128]{2,1,0:T(4,128)S(1)}, u32[]{:S(2)}, u32[]{:S(2)}) collective-permute-start(f32[10,4,128]{2,1,0:T(4,128)} %get-tuple-element.23), channel_id=1, source_target_pairs={{0,1},{1,2},{2,3},{4,5},{5,6},{6,7},{8,9},{9,10},{10,11},{12,13},{... | collective-permute-start | bytes 61448 | tf_op jit(solution)/shard_map/ppermute | solution.py:256
  27.0 1.3 %collective-permute-start.5 = (f32[10,4,128]{2,1,0:T(4,128)}, f32[10,4,128]{2,1,0:T(4,128)S(1)}, u32[]{:S(2)}, u32[]{:S(2)}) collective-permute-start(f32[10,4,128]{2,1,0:T(4,128)} %get-tuple-element.24), channel_id=1, source_target_pairs={{1,0},{2,1},{3,2},{5,4},{6,5},{7,6},{9,8},{10,9},{11,10},{13,12},{... | collective-permute-start | bytes 61448 | tf_op jit(solution)/shard_map/ppermute | solution.py:257
  28.7 4.2 %collective-permute-done.5.rahi_ref = f32[10,4,128]{2,1,0:T(4,128)S(1)} collective-permute-done((f32[10,4,128]{2,1,0:T(4,128)}, f32[10,4,128]{2,1,0:T(4,128)S(1)}, u32[]{:S(2)}, u32[]{:S(2)}) %collective-permute-start.5) | collective-permute-done | bytes 20512 | tf_op jit(solution)/shard_map/ppermute | solution.py:257
  33.5 3.9 %shard_map.124 = (f32[10,64,128]{2,1,0:T(8,128)}, f32[10,16,128]{2,1,0:T(8,128)}, f32[10,4,128]{2,1,0:T(4,128)}, f32[10,4,128]{2,1,0:T(4,128)}) custom-call(f32[600]{0:T(1024)} %reshape.300.mat_ref, f32[7]{0:T(128)} %stack.26.wt_ref, f32[10,64,128]{2,1,0:T(8,128)} %get-tuple-element.21.psi_ref, f32[10,64,128]{2,1,0:T(8,128)} %bitcast.83, ...), custom_call_target="tpu_custom_call" | custom-call | tf_op jit(solution)/shard_map/pallas_call | solution.py:197
  37.5 1.9 %collective-permute-start.6 = (f32[10,16,128]{2,1,0:T(8,128)}, f32[10,16,128]{2,1,0:T(8,128)S(1)}, u32[]{:S(2)}, u32[]{:S(2)}) collective-permute-start(f32[10,16,128]{2,1,0:T(8,128)} %get-tuple-element.26), channel_id=1, source_target_pairs={{0,4},{4,0},{1,5},{5,1},{2,6},{6,2},{3,7},{7,3},{8,12},{12,8},{9,1... | collective-permute-start | bytes 245768 | tf_op jit(solution)/shard_map/ppermute | solution.py:255
  39.4 3.1 %collective-permute-start.7 = (f32[10,4,128]{2,1,0:T(4,128)}, f32[10,4,128]{2,1,0:T(4,128)S(1)}, u32[]{:S(2)}, u32[]{:S(2)}) collective-permute-start(f32[10,4,128]{2,1,0:T(4,128)} %get-tuple-element.27), channel_id=1, source_target_pairs={{0,1},{1,2},{2,3},{4,5},{5,6},{6,7},{8,9},{9,10},{10,11},{12,13},{... | collective-permute-start | bytes 61448 | tf_op jit(solution)/shard_map/ppermute | solution.py:256
  42.5 1.3 %collective-permute-start.8 = (f32[10,4,128]{2,1,0:T(4,128)}, f32[10,4,128]{2,1,0:T(4,128)S(1)}, u32[]{:S(2)}, u32[]{:S(2)}) collective-permute-start(f32[10,4,128]{2,1,0:T(4,128)} %get-tuple-element.28), channel_id=1, source_target_pairs={{1,0},{2,1},{3,2},{5,4},{6,5},{7,6},{9,8},{10,9},{11,10},{13,12},{... | collective-permute-start | bytes 61448 | tf_op jit(solution)/shard_map/ppermute | solution.py:257
  44.2 4.2 %collective-permute-done.8.rahi_ref = f32[10,4,128]{2,1,0:T(4,128)S(1)} collective-permute-done((f32[10,4,128]{2,1,0:T(4,128)}, f32[10,4,128]{2,1,0:T(4,128)S(1)}, u32[]{:S(2)}, u32[]{:S(2)}) %collective-permute-start.8) | collective-permute-done | bytes 20512 | tf_op jit(solution)/shard_map/ppermute | solution.py:257
  49.0 3.9 %shard_map.125 = (f32[10,64,128]{2,1,0:T(8,128)}, f32[10,16,128]{2,1,0:T(8,128)}, f32[10,4,128]{2,1,0:T(4,128)}, f32[10,4,128]{2,1,0:T(4,128)}) custom-call(f32[600]{0:T(1024)} %reshape.300.mat_ref, f32[7]{0:T(128)} %stack.26.wt_ref, f32[10,64,128]{2,1,0:T(8,128)} %get-tuple-element.25.psi_ref, f32[10,64,128]{2,1,0:T(8,128)} %bitcast.84, ...), custom_call_target="tpu_custom_call" | custom-call | tf_op jit(solution)/shard_map/pallas_call | solution.py:197
  53.1 1.9 %collective-permute-start.10 = (f32[10,4,128]{2,1,0:T(4,128)}, f32[10,4,128]{2,1,0:T(4,128)S(1)}, u32[]{:S(2)}, u32[]{:S(2)}) collective-permute-start(f32[10,4,128]{2,1,0:T(4,128)} %get-tuple-element.31), channel_id=1, source_target_pairs={{0,1},{1,2},{2,3},{4,5},{5,6},{6,7},{8,9},{9,10},{10,11},{12,13},{... | collective-permute-start | bytes 61448 | tf_op jit(solution)/shard_map/ppermute | solution.py:256
  55.0 1.5 %collective-permute-start.11 = (f32[10,4,128]{2,1,0:T(4,128)}, f32[10,4,128]{2,1,0:T(4,128)S(1)}, u32[]{:S(2)}, u32[]{:S(2)}) collective-permute-start(f32[10,4,128]{2,1,0:T(4,128)} %get-tuple-element.32), channel_id=1, source_target_pairs={{1,0},{2,1},{3,2},{5,4},{6,5},{7,6},{9,8},{10,9},{11,10},{13,12},{... | collective-permute-start | bytes 61448 | tf_op jit(solution)/shard_map/ppermute | solution.py:257
  57.2 3.7 %collective-permute-done.11.rahi_ref = f32[10,4,128]{2,1,0:T(4,128)S(1)} collective-permute-done((f32[10,4,128]{2,1,0:T(4,128)}, f32[10,4,128]{2,1,0:T(4,128)S(1)}, u32[]{:S(2)}, u32[]{:S(2)}) %collective-permute-start.11) | collective-permute-done | bytes 20512 | tf_op jit(solution)/shard_map/ppermute | solution.py:257
  61.5 3.7 %shard_map.126 = (f32[10,64,128]{2,1,0:T(8,128)}, f32[10,16,128]{2,1,0:T(8,128)}, f32[10,4,128]{2,1,0:T(4,128)}, f32[10,4,128]{2,1,0:T(4,128)}) custom-call(f32[600]{0:T(1024)} %reshape.300.mat_ref, f32[7]{0:T(128)} %stack.26.wt_ref, f32[10,64,128]{2,1,0:T(8,128)} %get-tuple-element.29.psi_ref, f32[10,64,128]{2,1,0:T(8,128)} %bitcast.85, ...), custom_call_target="tpu_custom_call" | custom-call | tf_op jit(solution)/shard_map/pallas_call | solution.py:197
  67.0 3.3 %fusion.3 = f32[3,8192]{1,0:T(4,128)S(1)} fusion(s32[8192]{0:T(1024)S(1)} %add_select_fusion, pred[64,8192]{1,0:T(8,128)(4,1)S(1)} %iota_compare_fusion.1, f32[1,3,64,128]{3,1,2,0:T(4,128)S(1)} %fusion.6), kind=kOutput, calls=%fused_computation.6 | convolution fusion | flops 2420088832 | bytes 753664 | tf_op jit(solution)/shard_map/xl,lj->xj/dot_general | solution.py:278
  72.3 7.8 %all-to-all-start = ((f32[8,3,512]{2,1,0:T(4,128)}), f32[8,3,512]{2,1,0:T(4,128)S(1)}, u32[]{:S(2)}, u32[]{:S(2)}) async-start(f32[8,3,512]{2,1,0:T(4,128)} %select_add_fusion), calls=%async_computation | async-start | bytes 131072 | tf_op jit(solution)/shard_map/all_to_all | solution.py:41
  80.7 2.6 %shard_map.127 = f32[36,512]{1,0:T(8,128)} custom-call(s32[2,512]{1,0:T(2,128)} %pad_add_fusion.where_ref, bf16[2304,128]{1,0:T(8,128)(2,1)} %bitcast.90), custom_call_target="tpu_custom_call" | custom-call | tf_op jit(solution)/shard_map/pallas_call | solution.py:290
  84.2 3.8 %all-to-all-done = f32[8,3,512]{2,1,0:T(4,128)S(1)} async-done(((f32[8,3,512]{2,1,0:T(4,128)}), f32[8,3,512]{2,1,0:T(4,128)S(1)}, u32[]{:S(2)}, u32[]{:S(2)}) %all-to-all-start) | async-done | bytes 49184 | tf_op jit(solution)/shard_map/all_to_all | solution.py:41
  (66 shorter events, 13.1 us)
Async XLA Ops:
  0.6 65.9 %copy-start = (f32[3,10]{1,0:T(4,128)S(1)}, f32[3,10]{1,0:T(4,128)}, u32[]{:S(2)}) copy-start(f32[3,10]{1,0:T(4,128)} %param.17) | copy-start | bytes 364
  2.4 12.0 %copy-start.1 = (s32[1,1,8192]{2,1,0:T(1,128)S(1)}, s32[1,1,8192]{2,1,0:T(1,128)}, u32[]{:S(2)}) copy-start(s32[1,1,8192]{2,1,0:T(1,128)} %param.21) | copy-start | bytes 98308
  2.4 12.1 %copy-start.14 = (s32[1,1,64]{2,1,0:T(1,128)S(1)}, s32[1,1,64]{2,1,0:T(1,128)}, u32[]{:S(2)}) copy-start(s32[1,1,64]{2,1,0:T(1,128)} %param.20) | copy-start | bytes 772
  7.6 11.3 %collective-permute-start = (f32[10,16,128]{2,1,0:T(8,128)}, f32[10,16,128]{2,1,0:T(8,128)S(1)}, u32[]{:S(2)}, u32[]{:S(2)}) collective-permute-start(f32[10,16,128]{2,1,0:T(8,128)} %get-tuple-element.18), channel_id=1, source_target_pairs={{0,4},{4,0},{1,5},{5,1},{2,6},{6,2},{3,7},{7,3},{8,12},{12,8},{9,1... | collective-permute-start | bytes 245768 | tf_op jit(solution)/shard_map/ppermute | solution.py:255
  9.7 5.6 %collective-permute-start.1 = (f32[10,4,128]{2,1,0:T(4,128)}, f32[10,4,128]{2,1,0:T(4,128)S(1)}, u32[]{:S(2)}, u32[]{:S(2)}) collective-permute-start(f32[10,4,128]{2,1,0:T(4,128)} %get-tuple-element.19), channel_id=1, source_target_pairs={{0,1},{1,2},{2,3},{4,5},{5,6},{6,7},{8,9},{9,10},{10,11},{12,13},{... | collective-permute-start | bytes 61448 | tf_op jit(solution)/shard_map/ppermute | solution.py:256
  13.1 5.9 %collective-permute-start.2 = (f32[10,4,128]{2,1,0:T(4,128)}, f32[10,4,128]{2,1,0:T(4,128)S(1)}, u32[]{:S(2)}, u32[]{:S(2)}) collective-permute-start(f32[10,4,128]{2,1,0:T(4,128)} %get-tuple-element.20), channel_id=1, source_target_pairs={{1,0},{2,1},{3,2},{5,4},{6,5},{7,6},{9,8},{10,9},{11,10},{13,12},{... | collective-permute-start | bytes 61448 | tf_op jit(solution)/shard_map/ppermute | solution.py:257
  15.3 3.7 %copy-start.11 = (f32[10,4,128]{2,1,0:T(4,128)}, f32[10,4,128]{2,1,0:T(4,128)S(1)}, u32[]{:S(2)}) copy-start(f32[10,4,128]{2,1,0:T(4,128)S(1)} %collective-permute-done.1.ralo_ref) | copy-start | bytes 61444
  19.0 0.6 copy-start.5
  23.5 9.4 %collective-permute-start.3 = (f32[10,16,128]{2,1,0:T(8,128)}, f32[10,16,128]{2,1,0:T(8,128)S(1)}, u32[]{:S(2)}, u32[]{:S(2)}) collective-permute-start(f32[10,16,128]{2,1,0:T(8,128)} %get-tuple-element.22), channel_id=1, source_target_pairs={{0,4},{4,0},{1,5},{5,1},{2,6},{6,2},{3,7},{7,3},{8,12},{12,8},{9,1... | collective-permute-start | bytes 245768 | tf_op jit(solution)/shard_map/ppermute | solution.py:255
  23.6 5.1 %collective-permute-start.4 = (f32[10,4,128]{2,1,0:T(4,128)}, f32[10,4,128]{2,1,0:T(4,128)S(1)}, u32[]{:S(2)}, u32[]{:S(2)}) collective-permute-start(f32[10,4,128]{2,1,0:T(4,128)} %get-tuple-element.23), channel_id=1, source_target_pairs={{0,1},{1,2},{2,3},{4,5},{5,6},{6,7},{8,9},{9,10},{10,11},{12,13},{... | collective-permute-start | bytes 61448 | tf_op jit(solution)/shard_map/ppermute | solution.py:256
  27.0 5.9 %collective-permute-start.5 = (f32[10,4,128]{2,1,0:T(4,128)}, f32[10,4,128]{2,1,0:T(4,128)S(1)}, u32[]{:S(2)}, u32[]{:S(2)}) collective-permute-start(f32[10,4,128]{2,1,0:T(4,128)} %get-tuple-element.24), channel_id=1, source_target_pairs={{1,0},{2,1},{3,2},{5,4},{6,5},{7,6},{9,8},{10,9},{11,10},{13,12},{... | collective-permute-start | bytes 61448 | tf_op jit(solution)/shard_map/ppermute | solution.py:257
  28.7 4.2 %copy-start.10 = (f32[10,4,128]{2,1,0:T(4,128)}, f32[10,4,128]{2,1,0:T(4,128)S(1)}, u32[]{:S(2)}) copy-start(f32[10,4,128]{2,1,0:T(4,128)S(1)} %collective-permute-done.4.ralo_ref) | copy-start | bytes 61444
  32.9 0.6 copy-start.4
  37.5 10.9 %collective-permute-start.6 = (f32[10,16,128]{2,1,0:T(8,128)}, f32[10,16,128]{2,1,0:T(8,128)S(1)}, u32[]{:S(2)}, u32[]{:S(2)}) collective-permute-start(f32[10,16,128]{2,1,0:T(8,128)} %get-tuple-element.26), channel_id=1, source_target_pairs={{0,4},{4,0},{1,5},{5,1},{2,6},{6,2},{3,7},{7,3},{8,12},{12,8},{9,1... | collective-permute-start | bytes 245768 | tf_op jit(solution)/shard_map/ppermute | solution.py:255
  39.4 4.8 %collective-permute-start.7 = (f32[10,4,128]{2,1,0:T(4,128)}, f32[10,4,128]{2,1,0:T(4,128)S(1)}, u32[]{:S(2)}, u32[]{:S(2)}) collective-permute-start(f32[10,4,128]{2,1,0:T(4,128)} %get-tuple-element.27), channel_id=1, source_target_pairs={{0,1},{1,2},{2,3},{4,5},{5,6},{6,7},{8,9},{9,10},{10,11},{12,13},{... | collective-permute-start | bytes 61448 | tf_op jit(solution)/shard_map/ppermute | solution.py:256
  42.5 5.9 %collective-permute-start.8 = (f32[10,4,128]{2,1,0:T(4,128)}, f32[10,4,128]{2,1,0:T(4,128)S(1)}, u32[]{:S(2)}, u32[]{:S(2)}) collective-permute-start(f32[10,4,128]{2,1,0:T(4,128)} %get-tuple-element.28), channel_id=1, source_target_pairs={{1,0},{2,1},{3,2},{5,4},{6,5},{7,6},{9,8},{10,9},{11,10},{13,12},{... | collective-permute-start | bytes 61448 | tf_op jit(solution)/shard_map/ppermute | solution.py:257
  44.2 4.2 %copy-start.8 = (f32[10,4,128]{2,1,0:T(4,128)}, f32[10,4,128]{2,1,0:T(4,128)S(1)}, u32[]{:S(2)}) copy-start(f32[10,4,128]{2,1,0:T(4,128)S(1)} %collective-permute-done.7.ralo_ref) | copy-start | bytes 61444
  53.0 7.9 %collective-permute-start.9 = (f32[10,16,128]{2,1,0:T(8,128)}, f32[10,16,128]{2,1,0:T(8,128)S(1)}, u32[]{:S(2)}, u32[]{:S(2)}) collective-permute-start(f32[10,16,128]{2,1,0:T(8,128)} %get-tuple-element.30), channel_id=1, source_target_pairs={{0,4},{4,0},{1,5},{5,1},{2,6},{6,2},{3,7},{7,3},{8,12},{12,8},{9,1... | collective-permute-start | bytes 245768 | tf_op jit(solution)/shard_map/ppermute | solution.py:255
  53.1 4.1 %collective-permute-start.10 = (f32[10,4,128]{2,1,0:T(4,128)}, f32[10,4,128]{2,1,0:T(4,128)S(1)}, u32[]{:S(2)}, u32[]{:S(2)}) collective-permute-start(f32[10,4,128]{2,1,0:T(4,128)} %get-tuple-element.31), channel_id=1, source_target_pairs={{0,1},{1,2},{2,3},{4,5},{5,6},{6,7},{8,9},{9,10},{10,11},{12,13},{... | collective-permute-start | bytes 61448 | tf_op jit(solution)/shard_map/ppermute | solution.py:256
  55.0 5.9 %collective-permute-start.11 = (f32[10,4,128]{2,1,0:T(4,128)}, f32[10,4,128]{2,1,0:T(4,128)S(1)}, u32[]{:S(2)}, u32[]{:S(2)}) collective-permute-start(f32[10,4,128]{2,1,0:T(4,128)} %get-tuple-element.32), channel_id=1, source_target_pairs={{1,0},{2,1},{3,2},{5,4},{6,5},{7,6},{9,8},{10,9},{11,10},{13,12},{... | collective-permute-start | bytes 61448 | tf_op jit(solution)/shard_map/ppermute | solution.py:257
  57.2 3.7 %copy-start.6 = (f32[10,4,128]{2,1,0:T(4,128)}, f32[10,4,128]{2,1,0:T(4,128)S(1)}, u32[]{:S(2)}) copy-start(f32[10,4,128]{2,1,0:T(4,128)S(1)} %collective-permute-done.10.ralo_ref) | copy-start | bytes 61444
  60.9 0.6 copy-start.2
  70.3 1.3 %collective-permute-start.12 = (f32[8,3,512]{2,1,0:T(4,128)S(1)}, f32[8,3,512]{2,1,0:T(4,128)S(1)}, u32[]{:S(2)}, u32[]{:S(2)}) collective-permute-start(f32[8,3,512]{2,1,0:T(4,128)S(1)} %slice_select_fusion), channel_id=1, source_target_pairs={{0,8},{8,0},{16,24},{24,16},{32,40},{40,32},{48,56},{56,48},{64,72... | collective-permute-start | bytes 147464 | tf_op jit(solution)/shard_map/ppermute | solution.py:39
  72.3 15.6 %all-to-all-start = ((f32[8,3,512]{2,1,0:T(4,128)}), f32[8,3,512]{2,1,0:T(4,128)S(1)}, u32[]{:S(2)}, u32[]{:S(2)}) async-start(f32[8,3,512]{2,1,0:T(4,128)} %select_add_fusion), calls=%async_computation | async-start | bytes 131072 | tf_op jit(solution)/shard_map/all_to_all | solution.py:41
  (5 other events, 3.1 us)

commit v5 on v4

--- a/solution.py
+++ b/solution.py
@@ -88,22 +88,19 @@
     write_edges(mat_ref, wt_ref, psi_ref, face_ref, axs_ref, q2_ref, q3_ref, psi_ref.shape[0], tile_r)
 
 
-def section_kernel(
-    mat_ref, wt_ref, psi_ref, src_ref, face_ref, diag_ref, pick_ref, axr_ref, ralo_ref, rahi_ref,
-    out_ref, axs_ref, q2_ref, q3_ref, inc_ref, *, tile_r, edges,
+def interior_kernel(
+    mat_ref, wt_ref, psi_ref, src_ref, face_ref, diag_ref, pick_ref, res_ref, inc_ref, *, tile_r,
 ):
     comps, rows, lanes = psi_ref.shape
     half = comps // 2
-    layers = rows // tile_r
     lane = lax.broadcasted_iota(jnp.int32, (rows, lanes), 1)
     row = lax.broadcasted_iota(jnp.int32, (rows, lanes), 0) % tile_r
     omega = wt_ref[2]
     cosine = wt_ref[3]
     sine = wt_ref[4]
-    from_below = wt_ref[5]
-    from_above = wt_ref[6]
     pack4 = jnp.zeros((rows, lanes), jnp.float32)
     pack5 = jnp.zeros((rows, lanes), jnp.float32)
+    edge = jnp.zeros((tile_r, lanes), jnp.float32)
     load = lambda c: psi_ref[c]
     for x in range(comps):
         q0 = face_ref[0] * applied(mat_ref, 0, x, comps, load)
@@ -112,19 +109,10 @@
         q3 = face_ref[3] * applied(mat_ref, 3, x, comps, load)
         q4 = face_ref[4] * applied(mat_ref, 4, x, comps, load)
         q5 = face_ref[5] * applied(mat_ref, 5, x, comps, load)
-        got = axr_ref[x]
-        lower_a = jnp.concatenate([got * from_below, q0[: rows - tile_r]], axis=0)
-        upper_a = jnp.concatenate([q1[tile_r:], got * from_above], axis=0)
-        low_r = ralo_ref[x]
-        high_r = rahi_ref[x]
-        low_rows = jnp.concatenate(
-            [jnp.broadcast_to(low_r[j : j + 1, :], (tile_r, lanes)) for j in range(layers)], axis=0
-        )
-        high_rows = jnp.concatenate(
-            [jnp.broadcast_to(high_r[j : j + 1, :], (tile_r, lanes)) for j in range(layers)], axis=0
-        )
-        lower_r = jnp.where(row == 0, low_rows, pltpu.roll(q2, 1, 0))
-        upper_r = jnp.where(row == tile_r - 1, high_rows, pltpu.roll(q3, rows - 1, 0))
+        lower_a = jnp.concatenate([edge, q0[: rows - tile_r]], axis=0)
+        upper_a = jnp.concatenate([q1[tile_r:], edge], axis=0)
+        lower_r = jnp.where(row == 0, 0.0, pltpu.roll(q2, 1, 0))
+        upper_r = jnp.where(row == tile_r - 1, 0.0, pltpu.roll(q3, rows - 1, 0))
         lower_t = jnp.where(lane == 0, 0.0, pltpu.roll(q4, 1, 1))
         upper_t = jnp.where(lane == lanes - 1, 0.0, pltpu.roll(q5, lanes - 1, 1))
         inc_ref[x] = lower_a + upper_a + lower_r + upper_r + lower_t + upper_t
@@ -147,8 +135,33 @@
         incoming = inc_ref[x] + jnp.where(lane == 0, at_start, 0.0) + jnp.where(lane == lanes - 1, at_end, 0.0)
         psi = psi_ref[x]
         swapped = psi_ref[x + half] if x < half else -psi_ref[x - half]
-        residual = src_ref[x] - (diag * psi + omega * swapped) + incoming
-        out_ref[x] = psi + RELAX * residual / diag
+        res_ref[x] = src_ref[x] - (diag * psi + omega * swapped) + incoming
+
+
+def fixup_kernel(
+    mat_ref, wt_ref, psi_ref, res_ref, face_ref, diag_ref, axr_ref, ralo_ref, rahi_ref,
+    out_ref, axs_ref, q2_ref, q3_ref, *, tile_r, edges,
+):
+    comps, rows, lanes = psi_ref.shape
+    layers = rows // tile_r
+    row = lax.broadcasted_iota(jnp.int32, (rows, lanes), 0) % tile_r
+    from_below = wt_ref[5]
+    from_above = wt_ref[6]
+    middle = jnp.zeros((rows - 2 * tile_r, lanes), jnp.float32)
+    diag = diag_ref[...]
+    for x in range(comps):
+        got = axr_ref[x]
+        low_r = ralo_ref[x]
+        high_r = rahi_ref[x]
+        low_rows = jnp.concatenate(
+            [jnp.broadcast_to(low_r[j : j + 1, :], (tile_r, lanes)) for j in range(layers)], axis=0
+        )
+        high_rows = jnp.concatenate(
+            [jnp.broadcast_to(high_r[j : j + 1, :], (tile_r, lanes)) for j in range(layers)], axis=0
+        )
+        halo = jnp.concatenate([got * from_below, middle, got * from_above], axis=0)
+        halo = halo + jnp.where(row == 0, low_rows, 0.0) + jnp.where(row == tile_r - 1, high_rows, 0.0)
+        out_ref[x] = psi_ref[x] + RELAX * (res_ref[x] + halo) / diag
     if edges:
         write_edges(mat_ref, wt_ref, out_ref, face_ref, axs_ref, q2_ref, q3_ref, comps, tile_r)
 
@@ -192,15 +205,25 @@
     )(mat, weights, psi, face)
 
 
-def run_section(mat, weights, psi, src, face, diag, pick, axr, ralo, rahi, tile_r, edges):
+def run_interior(mat, weights, psi, src, face, diag, pick, tile_r):
     comps, rows, lanes = psi.shape
     return pl.pallas_call(
-        functools.partial(section_kernel, tile_r=tile_r, edges=edges),
+        functools.partial(interior_kernel, tile_r=tile_r),
+        out_shape=jax.ShapeDtypeStruct(psi.shape, jnp.float32),
+        in_specs=[smem_spec(), smem_spec()] + [vmem_spec() for _ in range(5)],
+        out_specs=vmem_spec(),
+        scratch_shapes=[pltpu.VMEM((comps, rows, lanes), jnp.float32)],
+    )(mat, weights, psi, src, face, diag, pick)
+
+
+def run_fixup(mat, weights, psi, res, face, diag, axr, ralo, rahi, tile_r, edges):
+    comps, rows, lanes = psi.shape
+    return pl.pallas_call(
+        functools.partial(fixup_kernel, tile_r=tile_r, edges=edges),
         out_shape=(jax.ShapeDtypeStruct(psi.shape, jnp.float32),) + edge_shapes(comps, rows, tile_r),
-        in_specs=[smem_spec(), smem_spec()] + [vmem_spec() for _ in range(8)],
+        in_specs=[smem_spec(), smem_spec()] + [vmem_spec() for _ in range(7)],
         out_specs=tuple(vmem_spec() for _ in range(4)),
-        scratch_shapes=[pltpu.VMEM((comps, rows, lanes), jnp.float32)],
-    )(mat, weights, psi, src, face, diag, pick, axr, ralo, rahi)
+    )(mat, weights, psi, res, face, diag, axr, ralo, rahi)
 
 
 def neighbours(axis):
@@ -255,8 +278,9 @@
         axr = lax.ppermute(axs, "axial", [(0, 1), (1, 0)])
         ralo = lax.ppermute(q2, "radial", up_r)
         rahi = lax.ppermute(q3, "radial", down_r)
-        psi, axs, q2, q3 = run_section(
-            mat, weights, psi, src, faces, diag, pick, axr, ralo, rahi, tile_r, section < ITERS - 1
+        res = run_interior(mat, weights, psi, src, faces, diag, pick, tile_r)
+        psi, axs, q2, q3 = run_fixup(
+            mat, weights, psi, res, faces, diag, axr, ralo, rahi, tile_r, section < ITERS - 1
         )
     psi_out = psi.reshape(psi_start.shape)
     heights = jnp.einsum(

time: 89.4 us -> 89.2 us (level); the launches traced: 88.7 us -> 87.5 us
  waiting for transfers between devices: 21.2 us -> 7.01 us
  Pallas kernels: 19.9 us -> 27.3 us
  starting transfers between devices: 29.1 us -> 32.5 us
  local copies, waits for them, and re-layouts: 8.11 us -> 10.4 us
    ppermute x4, waiting for transfers between devices: 15.8 us -> 2.01 us  [body(): rahi = lax.ppermute(q3, 'radial', down_r)]
    pallas_call x4 -> x8, Pallas kernels: 15.4 us -> 22.8 us  [the longest x4 14.3 us: run_interior(): pl.pallas_call(functools.partial(interior_kernel, tile_r=tile_r), out_sha...]
    ppermute x4, starting transfers between devices: 11.8 us -> 15.1 us  [body(): ralo = lax.ppermute(q2, 'radial', up_r)]
    unnamed x34, local copies, waits for them, and re-layouts: 4.13 us -> 6.49 us
  transfers between devices with their start and end apart: 14 -> 14, of which waited for: 8 -> 6; matrix products, arithmetic and copies ran while one was open for 3% -> 3% of each run, Pallas kernels for 3% -> 19%
where the time goes in v5:
time: 89.2 us; the launch traced here: 87.5 us
  starting transfers between devices  32.5 us (36%)
  Pallas kernels  27.3 us (31%)
  local copies, waits for them, and re-layouts  10.4 us (12%)
  waiting for transfers between devices  7.01 us (8%)
  other arithmetic  4.12 us (5%)
  matrix products  3.77 us (4%)
  between operations  2.34 us (3%)
    ppermute x4, starting transfers between devices, body(): ralo = lax.ppermute(q2, 'radial', up_r)  15.1 us
    pallas_call x4, Pallas kernels, run_interior(): pl.pallas_call(functools.partial(interior_kernel, tile_r=tile_r), out_sha...  14.3 us
    pallas_call x4, Pallas kernels, run_fixup(): pl.pallas_call(functools.partial(fixup_kernel, tile_r=tile_r, edges=edges...  8.59 us
    all_to_all x1, starting transfers between devices, sum_at_owner_paired(): lax.all_to_all(keep + got, axis, 0, 0, tiled=True, axis_index_groups=groups)  7.78 us
    unnamed x34, local copies, waits for them, and re-layouts  6.49 us
    ppermute x4, starting transfers between devices, body(): rahi = lax.ppermute(q3, 'radial', down_r)  5.35 us
    ppermute x4, starting transfers between devices, body(): axr = lax.ppermute(axs, 'axial', [(0, 1), (1, 0)])  4.16 us
    all_to_all x1, waiting for transfers between devices, sum_at_owner_paired(): lax.all_to_all(keep + got, axis, 0, 0, tiled=True, axis_index_groups=groups)  3.76 us
  transfers between devices with their start and end apart: 14, of which 6 were waited for; matrix products, arithmetic and copies ran while one was open for 3% of the time, Pallas kernels for 19%

profile of v5, /device:TPU:0, one launch (start us, length us, event | category | flops | bytes accessed | tf_op | source)
XLA Modules:
  0.0 87.5 jit_solution(6831104271954643140)
XLA Ops:
  3.5 1.6 %bitcast_convert_fusion.face_ref = f32[6,64,128]{2,1,0:T(8,128)} fusion(bf16[6,4,16,128]{3,2,1,0:T(8,128)(2,1)} %param.13), kind=kLoop, calls=%fused_computation.11 | loop fusion | flops 49152 | bytes 294912 | tf_op jit(solution)/shard_map/reshape | solution.py:270
  5.7 1.9 %shard_map.123 = (f32[10,16,128]{2,1,0:T(8,128)}, f32[10,4,128]{2,1,0:T(4,128)}, f32[10,4,128]{2,1,0:T(4,128)}) custom-call(f32[600]{0:T(1024)} %reshape.300.mat_ref, f32[7]{0:T(128)} %stack.26.wt_ref, f32[10,64,128]{2,1,0:T(8,128)} %bitcast.86, f32[6,64,128]{2,1,0:T(8,128)} %bitcast_convert_fusion.face_ref), custom_call_target="tpu_custom_call" | custom-call | tf_op jit(solution)/shard_map/pallas_call | solution.py:200
  7.6 2.0 %collective-permute-start = (f32[10,16,128]{2,1,0:T(8,128)}, f32[10,16,128]{2,1,0:T(8,128)S(1)}, u32[]{:S(2)}, u32[]{:S(2)}) collective-permute-start(f32[10,16,128]{2,1,0:T(8,128)} %get-tuple-element.18), channel_id=1, source_target_pairs={{0,4},{4,0},{1,5},{5,1},{2,6},{6,2},{3,7},{7,3},{8,12},{12,8},{9,1... | collective-permute-start | bytes 245768 | tf_op jit(solution)/shard_map/ppermute | solution.py:278
  9.6 3.4 %collective-permute-start.1 = (f32[10,4,128]{2,1,0:T(4,128)}, f32[10,4,128]{2,1,0:T(4,128)S(1)}, u32[]{:S(2)}, u32[]{:S(2)}) collective-permute-start(f32[10,4,128]{2,1,0:T(4,128)} %get-tuple-element.19), channel_id=1, source_target_pairs={{0,1},{1,2},{2,3},{4,5},{5,6},{6,7},{8,9},{9,10},{10,11},{12,13},{... | collective-permute-start | bytes 61448 | tf_op jit(solution)/shard_map/ppermute | solution.py:279
  13.0 1.3 %collective-permute-start.2 = (f32[10,4,128]{2,1,0:T(4,128)}, f32[10,4,128]{2,1,0:T(4,128)S(1)}, u32[]{:S(2)}, u32[]{:S(2)}) collective-permute-start(f32[10,4,128]{2,1,0:T(4,128)} %get-tuple-element.20), channel_id=1, source_target_pairs={{1,0},{2,1},{3,2},{5,4},{6,5},{7,6},{9,8},{10,9},{11,10},{13,12},{... | collective-permute-start | bytes 61448 | tf_op jit(solution)/shard_map/ppermute | solution.py:280
  15.2 3.6 %shard_map.122.res_ref = f32[10,64,128]{2,1,0:T(8,128)} custom-call(f32[600]{0:T(1024)} %reshape.300.mat_ref, f32[7]{0:T(128)} %stack.26.wt_ref, f32[10,64,128]{2,1,0:T(8,128)} %bitcast.87, f32[10,64,128]{2,1,0:T(8,128)} %bitcast.82, f32[6,64,128]{2,1,0:T(8,128)} %bitcast_convert_fusion.face_ref, f32[64,128]{1,0:T(8,128)} %bitcast.89, s32[64,1]{1,0:T(8,128)} %copy.38.pick_ref), custom_call_target="tpu_custom_call" | custom-call | tf_op jit(solution)/shard_map/pallas_call | solution.py:210
  20.2 2.2 %shard_map.124 = (f32[10,64,128]{2,1,0:T(8,128)}, f32[10,16,128]{2,1,0:T(8,128)}, f32[10,4,128]{2,1,0:T(4,128)}, f32[10,4,128]{2,1,0:T(4,128)}) custom-call(f32[600]{0:T(1024)} %reshape.300.mat_ref, f32[7]{0:T(128)} %stack.26.wt_ref, f32[10,64,128]{2,1,0:T(8,128)} %bitcast.88, f32[10,64,128]{2,1,0:T(8,128)} %shard_map.122.res_ref, ...), custom_call_target="tpu_custom_call" | custom-call | tf_op jit(solution)/shard_map/pallas_call | solution.py:221
  22.4 4.4 %collective-permute-start.4 = (f32[10,4,128]{2,1,0:T(4,128)}, f32[10,4,128]{2,1,0:T(4,128)S(1)}, u32[]{:S(2)}, u32[]{:S(2)}) collective-permute-start(f32[10,4,128]{2,1,0:T(4,128)} %get-tuple-element.23), channel_id=1, source_target_pairs={{0,1},{1,2},{2,3},{4,5},{5,6},{6,7},{8,9},{9,10},{10,11},{12,13},{... | collective-permute-start | bytes 61448 | tf_op jit(solution)/shard_map/ppermute | solution.py:279
  26.9 1.3 %collective-permute-start.5 = (f32[10,4,128]{2,1,0:T(4,128)}, f32[10,4,128]{2,1,0:T(4,128)S(1)}, u32[]{:S(2)}, u32[]{:S(2)}) collective-permute-start(f32[10,4,128]{2,1,0:T(4,128)} %get-tuple-element.24), channel_id=1, source_target_pairs={{1,0},{2,1},{3,2},{5,4},{6,5},{7,6},{9,8},{10,9},{11,10},{13,12},{... | collective-permute-start | bytes 61448 | tf_op jit(solution)/shard_map/ppermute | solution.py:280
  28.4 3.6 %shard_map.125.res_ref = f32[10,64,128]{2,1,0:T(8,128)} custom-call(f32[600]{0:T(1024)} %reshape.300.mat_ref, f32[7]{0:T(128)} %stack.26.wt_ref, f32[10,64,128]{2,1,0:T(8,128)} %get-tuple-element.21.psi_ref, f32[10,64,128]{2,1,0:T(8,128)} %bitcast.83, f32[6,64,128]{2,1,0:T(8,128)} %bitcast_convert_fusion.face_ref, f32[64,128]{1,0:T(8,128)} %bitcast.91, ...), custom_call_target="tpu_custom_call" | custom-call | tf_op jit(solution)/shard_map/pallas_call | solution.py:210
  34.0 2.2 %shard_map.126 = (f32[10,64,128]{2,1,0:T(8,128)}, f32[10,16,128]{2,1,0:T(8,128)}, f32[10,4,128]{2,1,0:T(4,128)}, f32[10,4,128]{2,1,0:T(4,128)}) custom-call(f32[600]{0:T(1024)} %reshape.300.mat_ref, f32[7]{0:T(128)} %stack.26.wt_ref, f32[10,64,128]{2,1,0:T(8,128)} %get-tuple-element.21.psi_ref, f32[10,64,128]{2,1,0:T(8,128)} %shard_map.125.res_ref, ...), custom_call_target="tpu_custom_call" | custom-call | tf_op jit(solution)/shard_map/pallas_call | solution.py:221
  36.2 1.9 %collective-permute-start.6 = (f32[10,16,128]{2,1,0:T(8,128)}, f32[10,16,128]{2,1,0:T(8,128)S(1)}, u32[]{:S(2)}, u32[]{:S(2)}) collective-permute-start(f32[10,16,128]{2,1,0:T(8,128)} %get-tuple-element.26), channel_id=1, source_target_pairs={{0,4},{4,0},{1,5},{5,1},{2,6},{6,2},{3,7},{7,3},{8,12},{12,8},{9,1... | collective-permute-start | bytes 245768 | tf_op jit(solution)/shard_map/ppermute | solution.py:278
  38.1 3.8 %collective-permute-start.7 = (f32[10,4,128]{2,1,0:T(4,128)}, f32[10,4,128]{2,1,0:T(4,128)S(1)}, u32[]{:S(2)}, u32[]{:S(2)}) collective-permute-start(f32[10,4,128]{2,1,0:T(4,128)} %get-tuple-element.27), channel_id=1, source_target_pairs={{0,1},{1,2},{2,3},{4,5},{5,6},{6,7},{8,9},{9,10},{10,11},{12,13},{... | collective-permute-start | bytes 61448 | tf_op jit(solution)/shard_map/ppermute | solution.py:279
  41.9 1.3 %collective-permute-start.8 = (f32[10,4,128]{2,1,0:T(4,128)}, f32[10,4,128]{2,1,0:T(4,128)S(1)}, u32[]{:S(2)}, u32[]{:S(2)}) collective-permute-start(f32[10,4,128]{2,1,0:T(4,128)} %get-tuple-element.28), channel_id=1, source_target_pairs={{1,0},{2,1},{3,2},{5,4},{6,5},{7,6},{9,8},{10,9},{11,10},{13,12},{... | collective-permute-start | bytes 61448 | tf_op jit(solution)/shard_map/ppermute | solution.py:280
  43.2 3.6 %shard_map.127.res_ref = f32[10,64,128]{2,1,0:T(8,128)} custom-call(f32[600]{0:T(1024)} %reshape.300.mat_ref, f32[7]{0:T(128)} %stack.26.wt_ref, f32[10,64,128]{2,1,0:T(8,128)} %get-tuple-element.25.psi_ref, f32[10,64,128]{2,1,0:T(8,128)} %bitcast.84, f32[6,64,128]{2,1,0:T(8,128)} %bitcast_convert_fusion.face_ref, f32[64,128]{1,0:T(8,128)} %bitcast.93, ...), custom_call_target="tpu_custom_call" | custom-call | tf_op jit(solution)/shard_map/pallas_call | solution.py:210
  49.0 2.2 %shard_map.128 = (f32[10,64,128]{2,1,0:T(8,128)}, f32[10,16,128]{2,1,0:T(8,128)}, f32[10,4,128]{2,1,0:T(4,128)}, f32[10,4,128]{2,1,0:T(4,128)}) custom-call(f32[600]{0:T(1024)} %reshape.300.mat_ref, f32[7]{0:T(128)} %stack.26.wt_ref, f32[10,64,128]{2,1,0:T(8,128)} %get-tuple-element.25.psi_ref, f32[10,64,128]{2,1,0:T(8,128)} %shard_map.127.res_ref, ...), custom_call_target="tpu_custom_call" | custom-call | tf_op jit(solution)/shard_map/pallas_call | solution.py:221
  51.4 3.5 %collective-permute-start.10 = (f32[10,4,128]{2,1,0:T(4,128)}, f32[10,4,128]{2,1,0:T(4,128)S(1)}, u32[]{:S(2)}, u32[]{:S(2)}) collective-permute-start(f32[10,4,128]{2,1,0:T(4,128)} %get-tuple-element.31), channel_id=1, source_target_pairs={{0,1},{1,2},{2,3},{4,5},{5,6},{6,7},{8,9},{9,10},{10,11},{12,13},{... | collective-permute-start | bytes 61448 | tf_op jit(solution)/shard_map/ppermute | solution.py:279
  54.9 1.5 %collective-permute-start.11 = (f32[10,4,128]{2,1,0:T(4,128)}, f32[10,4,128]{2,1,0:T(4,128)S(1)}, u32[]{:S(2)}, u32[]{:S(2)}) collective-permute-start(f32[10,4,128]{2,1,0:T(4,128)} %get-tuple-element.32), channel_id=1, source_target_pairs={{1,0},{2,1},{3,2},{5,4},{6,5},{7,6},{9,8},{10,9},{11,10},{13,12},{... | collective-permute-start | bytes 61448 | tf_op jit(solution)/shard_map/ppermute | solution.py:280
  57.1 3.6 %shard_map.129.res_ref = f32[10,64,128]{2,1,0:T(8,128)} custom-call(f32[600]{0:T(1024)} %reshape.300.mat_ref, f32[7]{0:T(128)} %stack.26.wt_ref, f32[10,64,128]{2,1,0:T(8,128)} %get-tuple-element.29.psi_ref, f32[10,64,128]{2,1,0:T(8,128)} %bitcast.85, f32[6,64,128]{2,1,0:T(8,128)} %bitcast_convert_fusion.face_ref, f32[64,128]{1,0:T(8,128)} %bitcast.95, ...), custom_call_target="tpu_custom_call" | custom-call | tf_op jit(solution)/shard_map/pallas_call | solution.py:210
  62.0 2.0 %shard_map.130 = (f32[10,64,128]{2,1,0:T(8,128)}, f32[10,16,128]{2,1,0:T(8,128)}, f32[10,4,128]{2,1,0:T(4,128)}, f32[10,4,128]{2,1,0:T(4,128)}) custom-call(f32[600]{0:T(1024)} %reshape.300.mat_ref, f32[7]{0:T(128)} %stack.26.wt_ref, f32[10,64,128]{2,1,0:T(8,128)} %get-tuple-element.29.psi_ref, f32[10,64,128]{2,1,0:T(8,128)} %shard_map.129.res_ref, ...), custom_call_target="tpu_custom_call" | custom-call | tf_op jit(solution)/shard_map/pallas_call | solution.py:221
  65.8 3.3 %fusion.3 = f32[3,8192]{1,0:T(4,128)S(1)} fusion(s32[8192]{0:T(1024)S(1)} %add_select_fusion, pred[64,8192]{1,0:T(8,128)(4,1)S(1)} %iota_compare_fusion.1, f32[1,3,64,128]{3,1,2,0:T(4,128)S(1)} %fusion.6), kind=kOutput, calls=%fused_computation.6 | convolution fusion | flops 2420088832 | bytes 753664 | tf_op jit(solution)/shard_map/xl,lj->xj/dot_general | solution.py:302
  71.2 7.8 %all-to-all-start = ((f32[8,3,512]{2,1,0:T(4,128)}), f32[8,3,512]{2,1,0:T(4,128)S(1)}, u32[]{:S(2)}, u32[]{:S(2)}) async-start(f32[8,3,512]{2,1,0:T(4,128)} %select_add_fusion), calls=%async_computation | async-start | bytes 131072 | tf_op jit(solution)/shard_map/all_to_all | solution.py:41
  79.6 2.6 %shard_map.131 = f32[36,512]{1,0:T(8,128)} custom-call(s32[2,512]{1,0:T(2,128)} %pad_add_fusion.where_ref, bf16[2304,128]{1,0:T(8,128)(2,1)} %bitcast.99), custom_call_target="tpu_custom_call" | custom-call | tf_op jit(solution)/shard_map/pallas_call | solution.py:314
  83.1 3.8 %all-to-all-done = f32[8,3,512]{2,1,0:T(4,128)S(1)} async-done(((f32[8,3,512]{2,1,0:T(4,128)}), f32[8,3,512]{2,1,0:T(4,128)S(1)}, u32[]{:S(2)}, u32[]{:S(2)}) %all-to-all-start) | async-done | bytes 49184 | tf_op jit(solution)/shard_map/all_to_all | solution.py:41
  (70 shorter events, 17.0 us)
Async XLA Ops:
  0.6 64.7 %copy-start = (f32[3,10]{1,0:T(4,128)S(1)}, f32[3,10]{1,0:T(4,128)}, u32[]{:S(2)}) copy-start(f32[3,10]{1,0:T(4,128)} %param.17) | copy-start | bytes 364
  2.4 11.9 %copy-start.1 = (s32[1,1,8192]{2,1,0:T(1,128)S(1)}, s32[1,1,8192]{2,1,0:T(1,128)}, u32[]{:S(2)}) copy-start(s32[1,1,8192]{2,1,0:T(1,128)} %param.21) | copy-start | bytes 98308
  2.4 12.1 %copy-start.14 = (s32[1,1,64]{2,1,0:T(1,128)S(1)}, s32[1,1,64]{2,1,0:T(1,128)}, u32[]{:S(2)}) copy-start(s32[1,1,64]{2,1,0:T(1,128)} %param.20) | copy-start | bytes 772
  7.6 11.3 %collective-permute-start = (f32[10,16,128]{2,1,0:T(8,128)}, f32[10,16,128]{2,1,0:T(8,128)S(1)}, u32[]{:S(2)}, u32[]{:S(2)}) collective-permute-start(f32[10,16,128]{2,1,0:T(8,128)} %get-tuple-element.18), channel_id=1, source_target_pairs={{0,4},{4,0},{1,5},{5,1},{2,6},{6,2},{3,7},{7,3},{8,12},{12,8},{9,1... | collective-permute-start | bytes 245768 | tf_op jit(solution)/shard_map/ppermute | solution.py:278
  9.6 9.1 %collective-permute-start.1 = (f32[10,4,128]{2,1,0:T(4,128)}, f32[10,4,128]{2,1,0:T(4,128)S(1)}, u32[]{:S(2)}, u32[]{:S(2)}) collective-permute-start(f32[10,4,128]{2,1,0:T(4,128)} %get-tuple-element.19), channel_id=1, source_target_pairs={{0,1},{1,2},{2,3},{4,5},{5,6},{6,7},{8,9},{9,10},{10,11},{12,13},{... | collective-permute-start | bytes 61448 | tf_op jit(solution)/shard_map/ppermute | solution.py:279
  13.0 5.9 %collective-permute-start.2 = (f32[10,4,128]{2,1,0:T(4,128)}, f32[10,4,128]{2,1,0:T(4,128)S(1)}, u32[]{:S(2)}, u32[]{:S(2)}) collective-permute-start(f32[10,4,128]{2,1,0:T(4,128)} %get-tuple-element.20), channel_id=1, source_target_pairs={{1,0},{2,1},{3,2},{5,4},{6,5},{7,6},{9,8},{10,9},{11,10},{13,12},{... | collective-permute-start | bytes 61448 | tf_op jit(solution)/shard_map/ppermute | solution.py:280
  19.5 0.6 copy-start.5
  22.3 10.4 %collective-permute-start.3 = (f32[10,16,128]{2,1,0:T(8,128)}, f32[10,16,128]{2,1,0:T(8,128)S(1)}, u32[]{:S(2)}, u32[]{:S(2)}) collective-permute-start(f32[10,16,128]{2,1,0:T(8,128)} %get-tuple-element.22), channel_id=1, source_target_pairs={{0,4},{4,0},{1,5},{5,1},{2,6},{6,2},{3,7},{7,3},{8,12},{12,8},{9,1... | collective-permute-start | bytes 245768 | tf_op jit(solution)/shard_map/ppermute | solution.py:278
  22.4 9.6 %collective-permute-start.4 = (f32[10,4,128]{2,1,0:T(4,128)}, f32[10,4,128]{2,1,0:T(4,128)S(1)}, u32[]{:S(2)}, u32[]{:S(2)}) collective-permute-start(f32[10,4,128]{2,1,0:T(4,128)} %get-tuple-element.23), channel_id=1, source_target_pairs={{0,1},{1,2},{2,3},{4,5},{5,6},{6,7},{8,9},{9,10},{10,11},{12,13},{... | collective-permute-start | bytes 61448 | tf_op jit(solution)/shard_map/ppermute | solution.py:279
  26.9 5.9 %collective-permute-start.5 = (f32[10,4,128]{2,1,0:T(4,128)}, f32[10,4,128]{2,1,0:T(4,128)S(1)}, u32[]{:S(2)}, u32[]{:S(2)}) collective-permute-start(f32[10,4,128]{2,1,0:T(4,128)} %get-tuple-element.24), channel_id=1, source_target_pairs={{1,0},{2,1},{3,2},{5,4},{6,5},{7,6},{9,8},{10,9},{11,10},{13,12},{... | collective-permute-start | bytes 61448 | tf_op jit(solution)/shard_map/ppermute | solution.py:280
  32.0 0.7 copy-start.10
  32.7 0.6 copy-start.12
  33.4 0.6 copy-start.4
  36.2 11.6 %collective-permute-start.6 = (f32[10,16,128]{2,1,0:T(8,128)}, f32[10,16,128]{2,1,0:T(8,128)S(1)}, u32[]{:S(2)}, u32[]{:S(2)}) collective-permute-start(f32[10,16,128]{2,1,0:T(8,128)} %get-tuple-element.26), channel_id=1, source_target_pairs={{0,4},{4,0},{1,5},{5,1},{2,6},{6,2},{3,7},{7,3},{8,12},{12,8},{9,1... | collective-permute-start | bytes 245768 | tf_op jit(solution)/shard_map/ppermute | solution.py:278
  38.1 8.7 %collective-permute-start.7 = (f32[10,4,128]{2,1,0:T(4,128)}, f32[10,4,128]{2,1,0:T(4,128)S(1)}, u32[]{:S(2)}, u32[]{:S(2)}) collective-permute-start(f32[10,4,128]{2,1,0:T(4,128)} %get-tuple-element.27), channel_id=1, source_target_pairs={{0,1},{1,2},{2,3},{4,5},{5,6},{6,7},{8,9},{9,10},{10,11},{12,13},{... | collective-permute-start | bytes 61448 | tf_op jit(solution)/shard_map/ppermute | solution.py:279
  41.9 5.9 %collective-permute-start.8 = (f32[10,4,128]{2,1,0:T(4,128)}, f32[10,4,128]{2,1,0:T(4,128)S(1)}, u32[]{:S(2)}, u32[]{:S(2)}) collective-permute-start(f32[10,4,128]{2,1,0:T(4,128)} %get-tuple-element.28), channel_id=1, source_target_pairs={{1,0},{2,1},{3,2},{5,4},{6,5},{7,6},{9,8},{10,9},{11,10},{13,12},{... | collective-permute-start | bytes 61448 | tf_op jit(solution)/shard_map/ppermute | solution.py:280
  46.8 1.0 %copy-start.8 = (f32[10,4,128]{2,1,0:T(4,128)}, f32[10,4,128]{2,1,0:T(4,128)S(1)}, u32[]{:S(2)}) copy-start(f32[10,4,128]{2,1,0:T(4,128)S(1)} %collective-permute-done.7.ralo_ref) | copy-start | bytes 61444
  48.4 0.6 copy-start.3
  51.2 9.6 %collective-permute-start.9 = (f32[10,16,128]{2,1,0:T(8,128)}, f32[10,16,128]{2,1,0:T(8,128)S(1)}, u32[]{:S(2)}, u32[]{:S(2)}) collective-permute-start(f32[10,16,128]{2,1,0:T(8,128)} %get-tuple-element.30), channel_id=1, source_target_pairs={{0,4},{4,0},{1,5},{5,1},{2,6},{6,2},{3,7},{7,3},{8,12},{12,8},{9,1... | collective-permute-start | bytes 245768 | tf_op jit(solution)/shard_map/ppermute | solution.py:278
  51.4 9.3 %collective-permute-start.10 = (f32[10,4,128]{2,1,0:T(4,128)}, f32[10,4,128]{2,1,0:T(4,128)S(1)}, u32[]{:S(2)}, u32[]{:S(2)}) collective-permute-start(f32[10,4,128]{2,1,0:T(4,128)} %get-tuple-element.31), channel_id=1, source_target_pairs={{0,1},{1,2},{2,3},{4,5},{5,6},{6,7},{8,9},{9,10},{10,11},{12,13},{... | collective-permute-start | bytes 61448 | tf_op jit(solution)/shard_map/ppermute | solution.py:279
  54.9 5.9 %collective-permute-start.11 = (f32[10,4,128]{2,1,0:T(4,128)}, f32[10,4,128]{2,1,0:T(4,128)S(1)}, u32[]{:S(2)}, u32[]{:S(2)}) collective-permute-start(f32[10,4,128]{2,1,0:T(4,128)} %get-tuple-element.32), channel_id=1, source_target_pairs={{1,0},{2,1},{3,2},{5,4},{6,5},{7,6},{9,8},{10,9},{11,10},{13,12},{... | collective-permute-start | bytes 61448 | tf_op jit(solution)/shard_map/ppermute | solution.py:280
  61.4 0.6 copy-start.2
  69.2 1.3 %collective-permute-start.12 = (f32[8,3,512]{2,1,0:T(4,128)S(1)}, f32[8,3,512]{2,1,0:T(4,128)S(1)}, u32[]{:S(2)}, u32[]{:S(2)}) collective-permute-start(f32[8,3,512]{2,1,0:T(4,128)S(1)} %slice_select_fusion), channel_id=1, source_target_pairs={{0,8},{8,0},{16,24},{24,16},{32,40},{40,32},{48,56},{56,48},{64,72... | collective-permute-start | bytes 147464 | tf_op jit(solution)/shard_map/ppermute | solution.py:39
  71.2 15.6 %all-to-all-start = ((f32[8,3,512]{2,1,0:T(4,128)}), f32[8,3,512]{2,1,0:T(4,128)S(1)}, u32[]{:S(2)}, u32[]{:S(2)}) async-start(f32[8,3,512]{2,1,0:T(4,128)} %select_add_fusion), calls=%async_computation | async-start | bytes 131072 | tf_op jit(solution)/shard_map/all_to_all | solution.py:41
  (5 other events, 3.0 us)

commit v6 on v5

--- a/solution.py
+++ b/solution.py
@@ -15,6 +15,7 @@
 RELAX = 0.8
 LANES = 128
 SMEM = pltpu.MemorySpace.SMEM
+METRIC = 8
 
 
 def split_up(value, dim, count):
@@ -74,8 +75,8 @@
     bottom = pl.ds(0, tile_r)
     r_top = pl.ds(tile_r - 1, layers, stride=tile_r)
     r_bottom = pl.ds(0, layers, stride=tile_r)
-    keep_top = wt_ref[1]
-    keep_bottom = wt_ref[0]
+    keep_top = wt_ref[6 * comps * comps + 1]
+    keep_bottom = wt_ref[6 * comps * comps + 0]
     for x in range(comps):
         up = face_ref[0, top, :] * applied(mat_ref, 0, x, comps, lambda c: psi_ref[c, top, :])
         down = face_ref[1, bottom, :] * applied(mat_ref, 1, x, comps, lambda c: psi_ref[c, bottom, :])
@@ -95,9 +96,9 @@
     half = comps // 2
     lane = lax.broadcasted_iota(jnp.int32, (rows, lanes), 1)
     row = lax.broadcasted_iota(jnp.int32, (rows, lanes), 0) % tile_r
-    omega = wt_ref[2]
-    cosine = wt_ref[3]
-    sine = wt_ref[4]
+    omega = wt_ref[6 * comps * comps + 2]
+    cosine = wt_ref[6 * comps * comps + 3]
+    sine = wt_ref[6 * comps * comps + 4]
     pack4 = jnp.zeros((rows, lanes), jnp.float32)
     pack5 = jnp.zeros((rows, lanes), jnp.float32)
     edge = jnp.zeros((tile_r, lanes), jnp.float32)
@@ -140,13 +141,13 @@
 
 def fixup_kernel(
     mat_ref, wt_ref, psi_ref, res_ref, face_ref, diag_ref, axr_ref, ralo_ref, rahi_ref,
-    out_ref, axs_ref, q2_ref, q3_ref, *, tile_r, edges,
+    out_ref, axs_ref, *radial_refs, tile_r, edges, dims,
 ):
     comps, rows, lanes = psi_ref.shape
     layers = rows // tile_r
     row = lax.broadcasted_iota(jnp.int32, (rows, lanes), 0) % tile_r
-    from_below = wt_ref[5]
-    from_above = wt_ref[6]
+    from_below = wt_ref[6 * comps * comps + 5]
+    from_above = wt_ref[6 * comps * comps + 6]
     middle = jnp.zeros((rows - 2 * tile_r, lanes), jnp.float32)
     diag = diag_ref[...]
     for x in range(comps):
@@ -163,7 +164,13 @@
         halo = halo + jnp.where(row == 0, low_rows, 0.0) + jnp.where(row == tile_r - 1, high_rows, 0.0)
         out_ref[x] = psi_ref[x] + RELAX * (res_ref[x] + halo) / diag
     if edges:
-        write_edges(mat_ref, wt_ref, out_ref, face_ref, axs_ref, q2_ref, q3_ref, comps, tile_r)
+        write_edges(mat_ref, wt_ref, out_ref, face_ref, axs_ref, *radial_refs, comps, tile_r)
+    else:
+        for d in range(dims):
+            height = wt_ref[6 * comps * comps + METRIC + d * comps] * out_ref[0]
+            for c in range(1, comps):
+                height = height + wt_ref[6 * comps * comps + METRIC + d * comps + c] * out_ref[c]
+            axs_ref[d] = wt_ref[6 * comps * comps + METRIC - 1] * height
 
 
 def modes_kernel(where_ref, mode_ref, out_ref, *, blocks):
@@ -216,13 +223,14 @@
     )(mat, weights, psi, src, face, diag, pick)
 
 
-def run_fixup(mat, weights, psi, res, face, diag, axr, ralo, rahi, tile_r, edges):
+def run_fixup(mat, weights, psi, res, face, diag, axr, ralo, rahi, tile_r, edges, dims):
     comps, rows, lanes = psi.shape
+    tail = edge_shapes(comps, rows, tile_r) if edges else (jax.ShapeDtypeStruct((dims, rows, lanes), jnp.float32),)
     return pl.pallas_call(
-        functools.partial(fixup_kernel, tile_r=tile_r, edges=edges),
-        out_shape=(jax.ShapeDtypeStruct(psi.shape, jnp.float32),) + edge_shapes(comps, rows, tile_r),
+        functools.partial(fixup_kernel, tile_r=tile_r, edges=edges, dims=dims),
+        out_shape=(jax.ShapeDtypeStruct(psi.shape, jnp.float32),) + tail,
         in_specs=[smem_spec(), smem_spec()] + [vmem_spec() for _ in range(7)],
-        out_specs=tuple(vmem_spec() for _ in range(4)),
+        out_specs=tuple(vmem_spec() for _ in range(1 + len(tail))),
     )(mat, weights, psi, res, face, diag, axr, ralo, rahi)
 
 
@@ -255,7 +263,8 @@
     me_axial = lax.axis_index("axial")
     lower_side = (me_axial == 0).astype(jnp.float32)
     upper_side = 1.0 - lower_side
-    weights = jnp.stack(
+    dims = metric.shape[0]
+    scalars = jnp.stack(
         [
             upper_side,
             lower_side,
@@ -264,8 +273,13 @@
             jnp.sin(angle),
             upper_side,
             lower_side,
+            phase_weight[0],
         ]
     ).astype(jnp.float32)
+    weights = jnp.concatenate([scalars, metric.reshape(-1)])
+    mat_weights = jnp.concatenate([mat, weights])
+    mat = mat_weights
+    weights = mat_weights
     partner = pairing[0, 0]
     faces = face_coef.astype(jnp.float32).reshape(6, rows, pitch)
     diag = diag_coef.reshape(rows, pitch)
@@ -279,17 +293,15 @@
         ralo = lax.ppermute(q2, "radial", up_r)
         rahi = lax.ppermute(q3, "radial", down_r)
         res = run_interior(mat, weights, psi, src, faces, diag, pick, tile_r)
-        psi, axs, q2, q3 = run_fixup(
-            mat, weights, psi, res, faces, diag, axr, ralo, rahi, tile_r, section < ITERS - 1
-        )
+        if section < ITERS - 1:
+            psi, axs, q2, q3 = run_fixup(
+                mat, weights, psi, res, faces, diag, axr, ralo, rahi, tile_r, True, dims
+            )
+        else:
+            psi, weighted = run_fixup(
+                mat, weights, psi, res, faces, diag, axr, ralo, rahi, tile_r, False, dims
+            )
     psi_out = psi.reshape(psi_start.shape)
-    heights = jnp.einsum(
-        "dc,cn->dn",
-        metric,
-        psi.reshape(comps, cells),
-        precision=lax.Precision.HIGHEST,
-    )
-    weighted = phase_weight[0] * heights
     order = owner_order[0, 0]
     owners = lax.axis_size("phase")
     owned = cells // owners

time: 89.2 us -> 88.6 us (level)
  local copies, waits for them, and re-layouts: 10.4 us -> 9.32 us
    unnamed x34 -> x30, local copies, waits for them, and re-layouts: 6.49 us -> 5.15 us
where the time goes in v6:
time: 88.6 us; the launch traced here: 87.5 us
  starting transfers between devices  32.5 us (37%)
  Pallas kernels  27.3 us (31%)
  local copies, waits for them, and re-layouts  9.32 us (11%)
  waiting for transfers between devices  7.67 us (9%)
  matrix products  4.2 us (5%)
  other arithmetic  4.13 us (5%)
  between operations  2.31 us (3%)
    ppermute x4, starting transfers between devices, body(): ralo = lax.ppermute(q2, 'radial', up_r)  15.1 us
    pallas_call x4, Pallas kernels, run_interior(): pl.pallas_call(functools.partial(interior_kernel, tile_r=tile_r), out_sha...  14.3 us
    pallas_call x4, Pallas kernels, run_fixup(): pl.pallas_call(functools.partial(fixup_kernel, tile_r=tile_r, edges=edges...  8.6 us
    all_to_all x1, starting transfers between devices, sum_at_owner_paired(): lax.all_to_all(keep + got, axis, 0, 0, tiled=True, axis_index_groups=groups)  7.79 us
    ppermute x4, starting transfers between devices, body(): rahi = lax.ppermute(q3, 'radial', down_r)  5.35 us
    unnamed x30, local copies, waits for them, and re-layouts  5.15 us
    dot_general x1, matrix products, body(): jnp.einsum('xl,lj->xj', weighted.reshape(dims * blocks, lanes), pick_lane...  4.2 us
    ppermute x4, starting transfers between devices, body(): axr = lax.ppermute(axs, 'axial', [(0, 1), (1, 0)])  4.16 us
  transfers between devices with their start and end apart: 14, of which 6 were waited for; matrix products, arithmetic and copies ran while one was open for 3% of the time, Pallas kernels for 19%

profile of v6, /device:TPU:0, one launch (start us, length us, event | category | flops | bytes accessed | tf_op | source)
XLA Modules:
  0.0 87.5 jit_solution(16108809269304996951)
XLA Ops:
  4.3 1.6 %bitcast_convert_fusion.face_ref = f32[6,64,128]{2,1,0:T(8,128)} fusion(bf16[6,4,16,128]{3,2,1,0:T(8,128)(2,1)} %param.13), kind=kLoop, calls=%fused_computation.7 | loop fusion | flops 49152 | bytes 294912 | tf_op jit(solution)/shard_map/reshape | solution.py:284
  6.5 1.9 %shard_map.123 = (f32[10,16,128]{2,1,0:T(8,128)}, f32[10,4,128]{2,1,0:T(4,128)}, f32[10,4,128]{2,1,0:T(4,128)}) custom-call(f32[638]{0:T(1024)} %concatenate.15.mat_ref.wt_ref, f32[638]{0:T(1024)} %concatenate.15.mat_ref.wt_ref, f32[10,64,128]{2,1,0:T(8,128)} %bitcast.74, f32[6,64,128]{2,1,0:T(8,128)} %bitcast_convert_fusion.face_ref), custom_call_target="tpu_custom_call" | custom-call | tf_op jit(solution)/shard_map/pallas_call | solution.py:207
  8.5 2.0 %collective-permute-start = (f32[10,16,128]{2,1,0:T(8,128)}, f32[10,16,128]{2,1,0:T(8,128)S(1)}, u32[]{:S(2)}, u32[]{:S(2)}) collective-permute-start(f32[10,16,128]{2,1,0:T(8,128)} %get-tuple-element.19), channel_id=1, source_target_pairs={{0,4},{4,0},{1,5},{5,1},{2,6},{6,2},{3,7},{7,3},{8,12},{12,8},{9,1... | collective-permute-start | bytes 245768 | tf_op jit(solution)/shard_map/ppermute | solution.py:292
  10.5 3.4 %collective-permute-start.1 = (f32[10,4,128]{2,1,0:T(4,128)}, f32[10,4,128]{2,1,0:T(4,128)S(1)}, u32[]{:S(2)}, u32[]{:S(2)}) collective-permute-start(f32[10,4,128]{2,1,0:T(4,128)} %get-tuple-element.20), channel_id=1, source_target_pairs={{0,1},{1,2},{2,3},{4,5},{5,6},{6,7},{8,9},{9,10},{10,11},{12,13},{... | collective-permute-start | bytes 61448 | tf_op jit(solution)/shard_map/ppermute | solution.py:293
  13.9 1.3 %collective-permute-start.2 = (f32[10,4,128]{2,1,0:T(4,128)}, f32[10,4,128]{2,1,0:T(4,128)S(1)}, u32[]{:S(2)}, u32[]{:S(2)}) collective-permute-start(f32[10,4,128]{2,1,0:T(4,128)} %get-tuple-element.21), channel_id=1, source_target_pairs={{1,0},{2,1},{3,2},{5,4},{6,5},{7,6},{9,8},{10,9},{11,10},{13,12},{... | collective-permute-start | bytes 61448 | tf_op jit(solution)/shard_map/ppermute | solution.py:294
  16.1 3.6 %shard_map.122.res_ref = f32[10,64,128]{2,1,0:T(8,128)} custom-call(f32[638]{0:T(1024)} %concatenate.15.mat_ref.wt_ref, f32[638]{0:T(1024)} %concatenate.15.mat_ref.wt_ref, f32[10,64,128]{2,1,0:T(8,128)} %bitcast.75, f32[10,64,128]{2,1,0:T(8,128)} %bitcast.70, f32[6,64,128]{2,1,0:T(8,128)} %bitcast_convert_fusion.face_ref, f32[64,128]{1,0:T(8,128)} %bitcast.77, ...), custom_call_target="tpu_custom_call" | custom-call | tf_op jit(solution)/shard_map/pallas_call | solution.py:217
  21.0 2.2 %shard_map.124 = (f32[10,64,128]{2,1,0:T(8,128)}, f32[10,16,128]{2,1,0:T(8,128)}, f32[10,4,128]{2,1,0:T(4,128)}, f32[10,4,128]{2,1,0:T(4,128)}) custom-call(f32[638]{0:T(1024)} %concatenate.15.mat_ref.wt_ref, f32[638]{0:T(1024)} %concatenate.15.mat_ref.wt_ref, f32[10,64,128]{2,1,0:T(8,128)} %bitcast.76, f32[10,64,128]{2,1,0:T(8,128)} %shard_map.122.res_ref, ...), custom_call_target="tpu_custom_call" | custom-call | tf_op jit(solution)/shard_map/pallas_call | solution.py:229
  23.3 4.4 %collective-permute-start.4 = (f32[10,4,128]{2,1,0:T(4,128)}, f32[10,4,128]{2,1,0:T(4,128)S(1)}, u32[]{:S(2)}, u32[]{:S(2)}) collective-permute-start(f32[10,4,128]{2,1,0:T(4,128)} %get-tuple-element.24), channel_id=1, source_target_pairs={{0,1},{1,2},{2,3},{4,5},{5,6},{6,7},{8,9},{9,10},{10,11},{12,13},{... | collective-permute-start | bytes 61448 | tf_op jit(solution)/shard_map/ppermute | solution.py:293
  27.7 1.3 %collective-permute-start.5 = (f32[10,4,128]{2,1,0:T(4,128)}, f32[10,4,128]{2,1,0:T(4,128)S(1)}, u32[]{:S(2)}, u32[]{:S(2)}) collective-permute-start(f32[10,4,128]{2,1,0:T(4,128)} %get-tuple-element.25), channel_id=1, source_target_pairs={{1,0},{2,1},{3,2},{5,4},{6,5},{7,6},{9,8},{10,9},{11,10},{13,12},{... | collective-permute-start | bytes 61448 | tf_op jit(solution)/shard_map/ppermute | solution.py:294
  29.3 3.6 %shard_map.125.res_ref = f32[10,64,128]{2,1,0:T(8,128)} custom-call(f32[638]{0:T(1024)} %concatenate.15.mat_ref.wt_ref, f32[638]{0:T(1024)} %concatenate.15.mat_ref.wt_ref, f32[10,64,128]{2,1,0:T(8,128)} %get-tuple-element.22.psi_ref, f32[10,64,128]{2,1,0:T(8,128)} %bitcast.71, f32[6,64,128]{2,1,0:T(8,128)} %bitcast_convert_fusion.face_ref, ...), custom_call_target="tpu_custom_call" | custom-call | tf_op jit(solution)/shard_map/pallas_call | solution.py:217
  34.8 2.2 %shard_map.126 = (f32[10,64,128]{2,1,0:T(8,128)}, f32[10,16,128]{2,1,0:T(8,128)}, f32[10,4,128]{2,1,0:T(4,128)}, f32[10,4,128]{2,1,0:T(4,128)}) custom-call(f32[638]{0:T(1024)} %concatenate.15.mat_ref.wt_ref, f32[638]{0:T(1024)} %concatenate.15.mat_ref.wt_ref, f32[10,64,128]{2,1,0:T(8,128)} %get-tuple-element.22.psi_ref, f32[10,64,128]{2,1,0:T(8,128)} %shard_map.125.res_ref, ...), custom_call_target="tpu_custom_call" | custom-call | tf_op jit(solution)/shard_map/pallas_call | solution.py:229
  37.0 1.9 %collective-permute-start.6 = (f32[10,16,128]{2,1,0:T(8,128)}, f32[10,16,128]{2,1,0:T(8,128)S(1)}, u32[]{:S(2)}, u32[]{:S(2)}) collective-permute-start(f32[10,16,128]{2,1,0:T(8,128)} %get-tuple-element.27), channel_id=1, source_target_pairs={{0,4},{4,0},{1,5},{5,1},{2,6},{6,2},{3,7},{7,3},{8,12},{12,8},{9,1... | collective-permute-start | bytes 245768 | tf_op jit(solution)/shard_map/ppermute | solution.py:292
  38.9 3.8 %collective-permute-start.7 = (f32[10,4,128]{2,1,0:T(4,128)}, f32[10,4,128]{2,1,0:T(4,128)S(1)}, u32[]{:S(2)}, u32[]{:S(2)}) collective-permute-start(f32[10,4,128]{2,1,0:T(4,128)} %get-tuple-element.28), channel_id=1, source_target_pairs={{0,1},{1,2},{2,3},{4,5},{5,6},{6,7},{8,9},{9,10},{10,11},{12,13},{... | collective-permute-start | bytes 61448 | tf_op jit(solution)/shard_map/ppermute | solution.py:293
  42.8 1.3 %collective-permute-start.8 = (f32[10,4,128]{2,1,0:T(4,128)}, f32[10,4,128]{2,1,0:T(4,128)S(1)}, u32[]{:S(2)}, u32[]{:S(2)}) collective-permute-start(f32[10,4,128]{2,1,0:T(4,128)} %get-tuple-element.29), channel_id=1, source_target_pairs={{1,0},{2,1},{3,2},{5,4},{6,5},{7,6},{9,8},{10,9},{11,10},{13,12},{... | collective-permute-start | bytes 61448 | tf_op jit(solution)/shard_map/ppermute | solution.py:294
  44.1 3.6 %shard_map.127.res_ref = f32[10,64,128]{2,1,0:T(8,128)} custom-call(f32[638]{0:T(1024)} %concatenate.15.mat_ref.wt_ref, f32[638]{0:T(1024)} %concatenate.15.mat_ref.wt_ref, f32[10,64,128]{2,1,0:T(8,128)} %get-tuple-element.26.psi_ref, f32[10,64,128]{2,1,0:T(8,128)} %bitcast.72, f32[6,64,128]{2,1,0:T(8,128)} %bitcast_convert_fusion.face_ref, ...), custom_call_target="tpu_custom_call" | custom-call | tf_op jit(solution)/shard_map/pallas_call | solution.py:217
  49.9 2.2 %shard_map.128 = (f32[10,64,128]{2,1,0:T(8,128)}, f32[10,16,128]{2,1,0:T(8,128)}, f32[10,4,128]{2,1,0:T(4,128)}, f32[10,4,128]{2,1,0:T(4,128)}) custom-call(f32[638]{0:T(1024)} %concatenate.15.mat_ref.wt_ref, f32[638]{0:T(1024)} %concatenate.15.mat_ref.wt_ref, f32[10,64,128]{2,1,0:T(8,128)} %get-tuple-element.26.psi_ref, f32[10,64,128]{2,1,0:T(8,128)} %shard_map.127.res_ref, ...), custom_call_target="tpu_custom_call" | custom-call | tf_op jit(solution)/shard_map/pallas_call | solution.py:229
  52.2 3.5 %collective-permute-start.10 = (f32[10,4,128]{2,1,0:T(4,128)}, f32[10,4,128]{2,1,0:T(4,128)S(1)}, u32[]{:S(2)}, u32[]{:S(2)}) collective-permute-start(f32[10,4,128]{2,1,0:T(4,128)} %get-tuple-element.32), channel_id=1, source_target_pairs={{0,1},{1,2},{2,3},{4,5},{5,6},{6,7},{8,9},{9,10},{10,11},{12,13},{... | collective-permute-start | bytes 61448 | tf_op jit(solution)/shard_map/ppermute | solution.py:293
  55.8 1.5 %collective-permute-start.11 = (f32[10,4,128]{2,1,0:T(4,128)}, f32[10,4,128]{2,1,0:T(4,128)S(1)}, u32[]{:S(2)}, u32[]{:S(2)}) collective-permute-start(f32[10,4,128]{2,1,0:T(4,128)} %get-tuple-element.33), channel_id=1, source_target_pairs={{1,0},{2,1},{3,2},{5,4},{6,5},{7,6},{9,8},{10,9},{11,10},{13,12},{... | collective-permute-start | bytes 61448 | tf_op jit(solution)/shard_map/ppermute | solution.py:294
  57.3 3.6 %shard_map.129.res_ref = f32[10,64,128]{2,1,0:T(8,128)} custom-call(f32[638]{0:T(1024)} %concatenate.15.mat_ref.wt_ref, f32[638]{0:T(1024)} %concatenate.15.mat_ref.wt_ref, f32[10,64,128]{2,1,0:T(8,128)} %get-tuple-element.30.psi_ref, f32[10,64,128]{2,1,0:T(8,128)} %bitcast.73, f32[6,64,128]{2,1,0:T(8,128)} %bitcast_convert_fusion.face_ref, ...), custom_call_target="tpu_custom_call" | custom-call | tf_op jit(solution)/shard_map/pallas_call | solution.py:217
  62.9 2.0 %shard_map.130 = (f32[10,64,128]{2,1,0:T(8,128)}, f32[3,64,128]{2,1,0:T(8,128)}) custom-call(f32[638]{0:T(1024)} %concatenate.15.mat_ref.wt_ref, f32[638]{0:T(1024)} %concatenate.15.mat_ref.wt_ref, f32[10,64,128]{2,1,0:T(8,128)} %get-tuple-element.30.psi_ref, f32[10,64,128]{2,1,0:T(8,128)} %shard_map.129.res_ref, ...), custom_call_target="tpu_custom_call" | custom-call | tf_op jit(solution)/shard_map/pallas_call | solution.py:229
  64.9 4.2 %fusion.3 = f32[3,8192]{1,0:T(4,128)S(1)} fusion(f32[3,64,128]{2,1,0:T(8,128)} %get-tuple-element.35, s32[8192]{0:T(1024)S(1)} %add_select_fusion, pred[64,8192]{1,0:T(8,128)(4,1)S(1)} %iota_compare_fusion.1), kind=kOutput, calls=%fused_computation.5 | convolution fusion | flops 2420088832 | bytes 753664 | tf_op jit(solution)/shard_map/xl,lj->xj/dot_general | solution.py:314
  71.1 7.8 %all-to-all-start = ((f32[8,3,512]{2,1,0:T(4,128)}), f32[8,3,512]{2,1,0:T(4,128)S(1)}, u32[]{:S(2)}, u32[]{:S(2)}) async-start(f32[8,3,512]{2,1,0:T(4,128)} %select_add_fusion), calls=%async_computation | async-start | bytes 131072 | tf_op jit(solution)/shard_map/all_to_all | solution.py:42
  79.5 2.6 %shard_map.131 = f32[36,512]{1,0:T(8,128)} custom-call(s32[2,512]{1,0:T(2,128)} %pad_add_fusion.where_ref, bf16[2304,128]{1,0:T(8,128)(2,1)} %bitcast.85), custom_call_target="tpu_custom_call" | custom-call | tf_op jit(solution)/shard_map/pallas_call | solution.py:326
  83.0 3.8 %all-to-all-done = f32[8,3,512]{2,1,0:T(4,128)S(1)} async-done(((f32[8,3,512]{2,1,0:T(4,128)}), f32[8,3,512]{2,1,0:T(4,128)S(1)}, u32[]{:S(2)}, u32[]{:S(2)}) %all-to-all-start) | async-done | bytes 49184 | tf_op jit(solution)/shard_map/all_to_all | solution.py:42
  (66 shorter events, 16.1 us)
Async XLA Ops:
  1.8 13.4 %copy-start = (s32[1,1,8192]{2,1,0:T(1,128)S(1)}, s32[1,1,8192]{2,1,0:T(1,128)}, u32[]{:S(2)}) copy-start(s32[1,1,8192]{2,1,0:T(1,128)} %param.21) | copy-start | bytes 98308
  1.9 13.5 %copy-start.13 = (s32[1,1,64]{2,1,0:T(1,128)S(1)}, s32[1,1,64]{2,1,0:T(1,128)}, u32[]{:S(2)}) copy-start(s32[1,1,64]{2,1,0:T(1,128)} %param.20) | copy-start | bytes 772
  8.5 11.3 %collective-permute-start = (f32[10,16,128]{2,1,0:T(8,128)}, f32[10,16,128]{2,1,0:T(8,128)S(1)}, u32[]{:S(2)}, u32[]{:S(2)}) collective-permute-start(f32[10,16,128]{2,1,0:T(8,128)} %get-tuple-element.19), channel_id=1, source_target_pairs={{0,4},{4,0},{1,5},{5,1},{2,6},{6,2},{3,7},{7,3},{8,12},{12,8},{9,1... | collective-permute-start | bytes 245768 | tf_op jit(solution)/shard_map/ppermute | solution.py:292
  10.5 9.1 %collective-permute-start.1 = (f32[10,4,128]{2,1,0:T(4,128)}, f32[10,4,128]{2,1,0:T(4,128)S(1)}, u32[]{:S(2)}, u32[]{:S(2)}) collective-permute-start(f32[10,4,128]{2,1,0:T(4,128)} %get-tuple-element.20), channel_id=1, source_target_pairs={{0,1},{1,2},{2,3},{4,5},{5,6},{6,7},{8,9},{9,10},{10,11},{12,13},{... | collective-permute-start | bytes 61448 | tf_op jit(solution)/shard_map/ppermute | solution.py:293
  13.9 5.9 %collective-permute-start.2 = (f32[10,4,128]{2,1,0:T(4,128)}, f32[10,4,128]{2,1,0:T(4,128)S(1)}, u32[]{:S(2)}, u32[]{:S(2)}) collective-permute-start(f32[10,4,128]{2,1,0:T(4,128)} %get-tuple-element.21), channel_id=1, source_target_pairs={{1,0},{2,1},{3,2},{5,4},{6,5},{7,6},{9,8},{10,9},{11,10},{13,12},{... | collective-permute-start | bytes 61448 | tf_op jit(solution)/shard_map/ppermute | solution.py:294
  19.6 0.6 copy-start.10
  20.4 0.6 copy-start.4
  23.2 10.4 %collective-permute-start.3 = (f32[10,16,128]{2,1,0:T(8,128)}, f32[10,16,128]{2,1,0:T(8,128)S(1)}, u32[]{:S(2)}, u32[]{:S(2)}) collective-permute-start(f32[10,16,128]{2,1,0:T(8,128)} %get-tuple-element.23), channel_id=1, source_target_pairs={{0,4},{4,0},{1,5},{5,1},{2,6},{6,2},{3,7},{7,3},{8,12},{12,8},{9,1... | collective-permute-start | bytes 245768 | tf_op jit(solution)/shard_map/ppermute | solution.py:292
  23.3 9.6 %collective-permute-start.4 = (f32[10,4,128]{2,1,0:T(4,128)}, f32[10,4,128]{2,1,0:T(4,128)S(1)}, u32[]{:S(2)}, u32[]{:S(2)}) collective-permute-start(f32[10,4,128]{2,1,0:T(4,128)} %get-tuple-element.24), channel_id=1, source_target_pairs={{0,1},{1,2},{2,3},{4,5},{5,6},{6,7},{8,9},{9,10},{10,11},{12,13},{... | collective-permute-start | bytes 61448 | tf_op jit(solution)/shard_map/ppermute | solution.py:293
  27.7 5.9 %collective-permute-start.5 = (f32[10,4,128]{2,1,0:T(4,128)}, f32[10,4,128]{2,1,0:T(4,128)S(1)}, u32[]{:S(2)}, u32[]{:S(2)}) collective-permute-start(f32[10,4,128]{2,1,0:T(4,128)} %get-tuple-element.25), channel_id=1, source_target_pairs={{1,0},{2,1},{3,2},{5,4},{6,5},{7,6},{9,8},{10,9},{11,10},{13,12},{... | collective-permute-start | bytes 61448 | tf_op jit(solution)/shard_map/ppermute | solution.py:294
  32.9 0.7 copy-start.9
  34.2 0.6 copy-start.3
  37.0 11.6 %collective-permute-start.6 = (f32[10,16,128]{2,1,0:T(8,128)}, f32[10,16,128]{2,1,0:T(8,128)S(1)}, u32[]{:S(2)}, u32[]{:S(2)}) collective-permute-start(f32[10,16,128]{2,1,0:T(8,128)} %get-tuple-element.27), channel_id=1, source_target_pairs={{0,4},{4,0},{1,5},{5,1},{2,6},{6,2},{3,7},{7,3},{8,12},{12,8},{9,1... | collective-permute-start | bytes 245768 | tf_op jit(solution)/shard_map/ppermute | solution.py:292
  38.9 8.7 %collective-permute-start.7 = (f32[10,4,128]{2,1,0:T(4,128)}, f32[10,4,128]{2,1,0:T(4,128)S(1)}, u32[]{:S(2)}, u32[]{:S(2)}) collective-permute-start(f32[10,4,128]{2,1,0:T(4,128)} %get-tuple-element.28), channel_id=1, source_target_pairs={{0,1},{1,2},{2,3},{4,5},{5,6},{6,7},{8,9},{9,10},{10,11},{12,13},{... | collective-permute-start | bytes 61448 | tf_op jit(solution)/shard_map/ppermute | solution.py:293
  42.8 5.9 %collective-permute-start.8 = (f32[10,4,128]{2,1,0:T(4,128)}, f32[10,4,128]{2,1,0:T(4,128)S(1)}, u32[]{:S(2)}, u32[]{:S(2)}) collective-permute-start(f32[10,4,128]{2,1,0:T(4,128)} %get-tuple-element.29), channel_id=1, source_target_pairs={{1,0},{2,1},{3,2},{5,4},{6,5},{7,6},{9,8},{10,9},{11,10},{13,12},{... | collective-permute-start | bytes 61448 | tf_op jit(solution)/shard_map/ppermute | solution.py:294
  47.7 1.0 %copy-start.7 = (f32[10,4,128]{2,1,0:T(4,128)}, f32[10,4,128]{2,1,0:T(4,128)S(1)}, u32[]{:S(2)}) copy-start(f32[10,4,128]{2,1,0:T(4,128)S(1)} %collective-permute-done.7.ralo_ref) | copy-start | bytes 61444
  49.2 0.6 copy-start.2
  52.1 9.6 %collective-permute-start.9 = (f32[10,16,128]{2,1,0:T(8,128)}, f32[10,16,128]{2,1,0:T(8,128)S(1)}, u32[]{:S(2)}, u32[]{:S(2)}) collective-permute-start(f32[10,16,128]{2,1,0:T(8,128)} %get-tuple-element.31), channel_id=1, source_target_pairs={{0,4},{4,0},{1,5},{5,1},{2,6},{6,2},{3,7},{7,3},{8,12},{12,8},{9,1... | collective-permute-start | bytes 245768 | tf_op jit(solution)/shard_map/ppermute | solution.py:292
  52.2 8.6 %collective-permute-start.10 = (f32[10,4,128]{2,1,0:T(4,128)}, f32[10,4,128]{2,1,0:T(4,128)S(1)}, u32[]{:S(2)}, u32[]{:S(2)}) collective-permute-start(f32[10,4,128]{2,1,0:T(4,128)} %get-tuple-element.32), channel_id=1, source_target_pairs={{0,1},{1,2},{2,3},{4,5},{5,6},{6,7},{8,9},{9,10},{10,11},{12,13},{... | collective-permute-start | bytes 61448 | tf_op jit(solution)/shard_map/ppermute | solution.py:293
  55.8 5.9 %collective-permute-start.11 = (f32[10,4,128]{2,1,0:T(4,128)}, f32[10,4,128]{2,1,0:T(4,128)S(1)}, u32[]{:S(2)}, u32[]{:S(2)}) collective-permute-start(f32[10,4,128]{2,1,0:T(4,128)} %get-tuple-element.33), channel_id=1, source_target_pairs={{1,0},{2,1},{3,2},{5,4},{6,5},{7,6},{9,8},{10,9},{11,10},{13,12},{... | collective-permute-start | bytes 61448 | tf_op jit(solution)/shard_map/ppermute | solution.py:294
  60.8 0.8 copy-start.5
  62.2 0.6 copy-start.1
  69.1 1.3 %collective-permute-start.12 = (f32[8,3,512]{2,1,0:T(4,128)S(1)}, f32[8,3,512]{2,1,0:T(4,128)S(1)}, u32[]{:S(2)}, u32[]{:S(2)}) collective-permute-start(f32[8,3,512]{2,1,0:T(4,128)S(1)} %slice_select_fusion), channel_id=1, source_target_pairs={{0,8},{8,0},{16,24},{24,16},{32,40},{40,32},{48,56},{56,48},{64,72... | collective-permute-start | bytes 147464 | tf_op jit(solution)/shard_map/ppermute | solution.py:40
  71.1 15.6 %all-to-all-start = ((f32[8,3,512]{2,1,0:T(4,128)}), f32[8,3,512]{2,1,0:T(4,128)S(1)}, u32[]{:S(2)}, u32[]{:S(2)}) async-start(f32[8,3,512]{2,1,0:T(4,128)} %select_add_fusion), calls=%async_computation | async-start | bytes 131072 | tf_op jit(solution)/shard_map/all_to_all | solution.py:42
  (4 other events, 2.4 us)

commit v7 on v6

--- a/solution.py
+++ b/solution.py
@@ -89,36 +89,56 @@
     write_edges(mat_ref, wt_ref, psi_ref, face_ref, axs_ref, q2_ref, q3_ref, psi_ref.shape[0], tile_r)
 
 
+def gauss_pair(gauss_ref, d, x, half, sum_ref, psi_ref):
+    base = (d * 3) * half * half + x * half
+    def dot(which, load):
+        start = base + which * half * half
+        total = gauss_ref[start] * load(0)
+        for c in range(1, half):
+            total = total + gauss_ref[start + c] * load(c)
+        return total
+    shared = dot(0, lambda c: sum_ref[c])
+    real = shared + dot(1, lambda c: psi_ref[c + half])
+    imag = shared - dot(2, lambda c: psi_ref[c])
+    return real, imag
+
+
 def interior_kernel(
-    mat_ref, wt_ref, psi_ref, src_ref, face_ref, diag_ref, pick_ref, res_ref, inc_ref, *, tile_r,
+    mat_ref, wt_ref, psi_ref, src_ref, face_ref, diag_ref, pick_ref, res_ref, inc_ref, sum_ref, *, tile_r,
 ):
     comps, rows, lanes = psi_ref.shape
     half = comps // 2
+    gauss_ref = mat_ref
+    gauss_at = 6 * comps * comps + METRIC + 64
     lane = lax.broadcasted_iota(jnp.int32, (rows, lanes), 1)
     row = lax.broadcasted_iota(jnp.int32, (rows, lanes), 0) % tile_r
     omega = wt_ref[6 * comps * comps + 2]
     cosine = wt_ref[6 * comps * comps + 3]
     sine = wt_ref[6 * comps * comps + 4]
+    for c in range(half):
+        sum_ref[c] = psi_ref[c] + psi_ref[c + half]
     pack4 = jnp.zeros((rows, lanes), jnp.float32)
     pack5 = jnp.zeros((rows, lanes), jnp.float32)
     edge = jnp.zeros((tile_r, lanes), jnp.float32)
-    load = lambda c: psi_ref[c]
-    for x in range(comps):
-        q0 = face_ref[0] * applied(mat_ref, 0, x, comps, load)
-        q1 = face_ref[1] * applied(mat_ref, 1, x, comps, load)
-        q2 = face_ref[2] * applied(mat_ref, 2, x, comps, load)
-        q3 = face_ref[3] * applied(mat_ref, 3, x, comps, load)
-        q4 = face_ref[4] * applied(mat_ref, 4, x, comps, load)
-        q5 = face_ref[5] * applied(mat_ref, 5, x, comps, load)
-        lower_a = jnp.concatenate([edge, q0[: rows - tile_r]], axis=0)
-        upper_a = jnp.concatenate([q1[tile_r:], edge], axis=0)
-        lower_r = jnp.where(row == 0, 0.0, pltpu.roll(q2, 1, 0))
-        upper_r = jnp.where(row == tile_r - 1, 0.0, pltpu.roll(q3, rows - 1, 0))
-        lower_t = jnp.where(lane == 0, 0.0, pltpu.roll(q4, 1, 1))
-        upper_t = jnp.where(lane == lanes - 1, 0.0, pltpu.roll(q5, lanes - 1, 1))
-        inc_ref[x] = lower_a + upper_a + lower_r + upper_r + lower_t + upper_t
-        pack4 = pack4 + jnp.where(lane == x, pltpu.roll(q4, (x + 1) % lanes, 1), 0.0)
-        pack5 = pack5 + jnp.where(lane == x, pltpu.roll(q5, x, 1), 0.0) if x else jnp.where(lane == 0, q5, 0.0)
+    shifted = gauss_ref.at[pl.ds(gauss_at, 6 * 3 * half * half)]
+    for x in range(half):
+        pair = [(x, 0), (x + half, 1)]
+        q = [[None, None] for _ in range(6)]
+        for d in range(6):
+            real, imag = gauss_pair(shifted, d, x, half, sum_ref, psi_ref)
+            q[d][0] = face_ref[d] * real
+            q[d][1] = face_ref[d] * imag
+        for comp, k in pair:
+            q0, q1, q2, q3, q4, q5 = (q[d][k] for d in range(6))
+            lower_a = jnp.concatenate([edge, q0[: rows - tile_r]], axis=0)
+            upper_a = jnp.concatenate([q1[tile_r:], edge], axis=0)
+            lower_r = jnp.where(row == 0, 0.0, pltpu.roll(q2, 1, 0))
+            upper_r = jnp.where(row == tile_r - 1, 0.0, pltpu.roll(q3, rows - 1, 0))
+            lower_t = jnp.where(lane == 0, 0.0, pltpu.roll(q4, 1, 1))
+            upper_t = jnp.where(lane == lanes - 1, 0.0, pltpu.roll(q5, lanes - 1, 1))
+            inc_ref[comp] = lower_a + upper_a + lower_r + upper_r + lower_t + upper_t
+            pack4 = pack4 + jnp.where(lane == comp, pltpu.roll(q4, (comp + 1) % lanes, 1), 0.0)
+            pack5 = pack5 + jnp.where(lane == comp, pltpu.roll(q5, comp, 1), 0.0) if comp else jnp.where(lane == 0, q5, 0.0)
     pick = (pick_ref[...] == lax.broadcasted_iota(jnp.int32, (rows, rows), 1)).astype(jnp.bfloat16)
     got4 = exact_pick(pick, pack4)
     got5 = exact_pick(pick, pack5)
@@ -219,7 +239,7 @@
         out_shape=jax.ShapeDtypeStruct(psi.shape, jnp.float32),
         in_specs=[smem_spec(), smem_spec()] + [vmem_spec() for _ in range(5)],
         out_specs=vmem_spec(),
-        scratch_shapes=[pltpu.VMEM((comps, rows, lanes), jnp.float32)],
+        scratch_shapes=[pltpu.VMEM((comps, rows, lanes), jnp.float32), pltpu.VMEM((comps // 2, rows, lanes), jnp.float32)],
     )(mat, weights, psi, src, face, diag, pick)
 
 
@@ -277,7 +297,11 @@
         ]
     ).astype(jnp.float32)
     weights = jnp.concatenate([scalars, metric.reshape(-1)])
-    mat_weights = jnp.concatenate([mat, weights])
+    real_t = jnp.swapaxes(flux_jac[:, 0], 1, 2)
+    imag_t = jnp.swapaxes(flux_jac[:, 1], 1, 2)
+    gauss = jnp.stack([real_t, imag_t - real_t, real_t + imag_t], axis=1).reshape(-1)
+    pad = jnp.zeros((METRIC + 64 - weights.shape[0],), jnp.float32)
+    mat_weights = jnp.concatenate([mat, weights, pad, gauss])
     mat = mat_weights
     weights = mat_weights
     partner = pairing[0, 0]

time: 88.6 us -> 86.4 us (0.975)
  Pallas kernels: 27.3 us -> 26.2 us
  waiting for transfers between devices: 7.67 us -> 8.77 us
    pallas_call x4, Pallas kernels: 14.3 us -> 13.2 us  [run_interior(): pl.pallas_call(functools.partial(interior_kernel, tile_r=tile_r), out_sha...]
    ppermute x4, waiting for transfers between devices: 2.67 us -> 3.76 us  [body(): rahi = lax.ppermute(q3, 'radial', down_r)]
    unnamed x30 -> x34, local copies, waits for them, and re-layouts: 5.15 us -> 5.16 us
  transfers between devices with their start and end apart: 14 -> 14, of which waited for: 6 -> 6; matrix products, arithmetic and copies ran while one was open for 3% -> 3% of each run, Pallas kernels for 19% -> 18%
where the time goes in v7:
time: 86.4 us; the launch traced here: 85.7 us
  starting transfers between devices  31.8 us (37%)
  Pallas kernels  26.2 us (30%)
  local copies, waits for them, and re-layouts  9.04 us (10%)
  waiting for transfers between devices  8.77 us (10%)
  matrix products  4.2 us (5%)
  other arithmetic  3.26 us (4%)
  between operations  2.36 us (3%)
    ppermute x4, starting transfers between devices, body(): ralo = lax.ppermute(q2, 'radial', up_r)  14.4 us
    pallas_call x4, Pallas kernels, run_interior(): pl.pallas_call(functools.partial(interior_kernel, tile_r=tile_r), out_sha...  13.2 us
    pallas_call x4, Pallas kernels, run_fixup(): pl.pallas_call(functools.partial(fixup_kernel, tile_r=tile_r, edges=edges...  8.61 us
    all_to_all x1, starting transfers between devices, sum_at_owner_paired(): lax.all_to_all(keep + got, axis, 0, 0, tiled=True, axis_index_groups=groups)  7.78 us
    ppermute x4, starting transfers between devices, body(): rahi = lax.ppermute(q3, 'radial', down_r)  5.35 us
    unnamed x34, local copies, waits for them, and re-layouts  5.16 us
    dot_general x1, matrix products, body(): jnp.einsum('xl,lj->xj', weighted.reshape(dims * blocks, lanes), pick_lane...  4.2 us
    ppermute x4, starting transfers between devices, body(): axr = lax.ppermute(axs, 'axial', [(0, 1), (1, 0)])  4.16 us
  transfers between devices with their start and end apart: 14, of which 6 were waited for; matrix products, arithmetic and copies ran while one was open for 3% of the time, Pallas kernels for 18%

profile of v7, /device:TPU:0, one launch (start us, length us, event | category | flops | bytes accessed | tf_op | source)
XLA Modules:
  0.0 85.7 jit_solution(2569663623698249384)
XLA Ops:
  5.5 1.9 %shard_map.123 = (f32[10,16,128]{2,1,0:T(8,128)}, f32[10,4,128]{2,1,0:T(4,128)}, f32[10,4,128]{2,1,0:T(4,128)}) custom-call(f32[1122]{0:T(1024)} %concatenate.15.mat_ref.wt_ref, f32[1122]{0:T(1024)} %concatenate.15.mat_ref.wt_ref, f32[10,64,128]{2,1,0:T(8,128)} %bitcast.84, f32[6,64,128]{2,1,0:T(8,128)} %bitcast_convert_fusion.face_ref), custom_call_target="tpu_custom_call" | custom-call | tf_op jit(solution)/shard_map/pallas_call | solution.py:227
  7.4 2.0 %collective-permute-start = (f32[10,16,128]{2,1,0:T(8,128)}, f32[10,16,128]{2,1,0:T(8,128)S(1)}, u32[]{:S(2)}, u32[]{:S(2)}) collective-permute-start(f32[10,16,128]{2,1,0:T(8,128)} %get-tuple-element.19), channel_id=1, source_target_pairs={{0,4},{4,0},{1,5},{5,1},{2,6},{6,2},{3,7},{7,3},{8,12},{12,8},{9,1... | collective-permute-start | bytes 245768 | tf_op jit(solution)/shard_map/ppermute | solution.py:316
  9.4 3.4 %collective-permute-start.1 = (f32[10,4,128]{2,1,0:T(4,128)}, f32[10,4,128]{2,1,0:T(4,128)S(1)}, u32[]{:S(2)}, u32[]{:S(2)}) collective-permute-start(f32[10,4,128]{2,1,0:T(4,128)} %get-tuple-element.20), channel_id=1, source_target_pairs={{0,1},{1,2},{2,3},{4,5},{5,6},{6,7},{8,9},{9,10},{10,11},{12,13},{... | collective-permute-start | bytes 61448 | tf_op jit(solution)/shard_map/ppermute | solution.py:317
  12.8 1.3 %collective-permute-start.2 = (f32[10,4,128]{2,1,0:T(4,128)}, f32[10,4,128]{2,1,0:T(4,128)S(1)}, u32[]{:S(2)}, u32[]{:S(2)}) collective-permute-start(f32[10,4,128]{2,1,0:T(4,128)} %get-tuple-element.21), channel_id=1, source_target_pairs={{1,0},{2,1},{3,2},{5,4},{6,5},{7,6},{9,8},{10,9},{11,10},{13,12},{... | collective-permute-start | bytes 61448 | tf_op jit(solution)/shard_map/ppermute | solution.py:318
  15.0 3.3 %shard_map.122.res_ref = f32[10,64,128]{2,1,0:T(8,128)} custom-call(f32[1122]{0:T(1024)} %concatenate.15.mat_ref.wt_ref, f32[1122]{0:T(1024)} %concatenate.15.mat_ref.wt_ref, f32[10,64,128]{2,1,0:T(8,128)} %bitcast.85, f32[10,64,128]{2,1,0:T(8,128)} %bitcast.80, f32[6,64,128]{2,1,0:T(8,128)} %bitcast_convert_fusion.face_ref, f32[64,128]{1,0:T(8,128)} %bitcast.87, ...), custom_call_target="tpu_custom_call" | custom-call | tf_op jit(solution)/shard_map/pallas_call | solution.py:237
  19.9 2.2 %shard_map.124 = (f32[10,64,128]{2,1,0:T(8,128)}, f32[10,16,128]{2,1,0:T(8,128)}, f32[10,4,128]{2,1,0:T(4,128)}, f32[10,4,128]{2,1,0:T(4,128)}) custom-call(f32[1122]{0:T(1024)} %concatenate.15.mat_ref.wt_ref, f32[1122]{0:T(1024)} %concatenate.15.mat_ref.wt_ref, f32[10,64,128]{2,1,0:T(8,128)} %bitcast.86, f32[10,64,128]{2,1,0:T(8,128)} %shard_map.122.res_ref, ...), custom_call_target="tpu_custom_call" | custom-call | tf_op jit(solution)/shard_map/pallas_call | solution.py:249
  22.2 4.1 %collective-permute-start.4 = (f32[10,4,128]{2,1,0:T(4,128)}, f32[10,4,128]{2,1,0:T(4,128)S(1)}, u32[]{:S(2)}, u32[]{:S(2)}) collective-permute-start(f32[10,4,128]{2,1,0:T(4,128)} %get-tuple-element.24), channel_id=1, source_target_pairs={{0,1},{1,2},{2,3},{4,5},{5,6},{6,7},{8,9},{9,10},{10,11},{12,13},{... | collective-permute-start | bytes 61448 | tf_op jit(solution)/shard_map/ppermute | solution.py:317
  26.4 1.3 %collective-permute-start.5 = (f32[10,4,128]{2,1,0:T(4,128)}, f32[10,4,128]{2,1,0:T(4,128)S(1)}, u32[]{:S(2)}, u32[]{:S(2)}) collective-permute-start(f32[10,4,128]{2,1,0:T(4,128)} %get-tuple-element.25), channel_id=1, source_target_pairs={{1,0},{2,1},{3,2},{5,4},{6,5},{7,6},{9,8},{10,9},{11,10},{13,12},{... | collective-permute-start | bytes 61448 | tf_op jit(solution)/shard_map/ppermute | solution.py:318
  28.0 3.3 %shard_map.125.res_ref = f32[10,64,128]{2,1,0:T(8,128)} custom-call(f32[1122]{0:T(1024)} %concatenate.15.mat_ref.wt_ref, f32[1122]{0:T(1024)} %concatenate.15.mat_ref.wt_ref, f32[10,64,128]{2,1,0:T(8,128)} %get-tuple-element.22.psi_ref, f32[10,64,128]{2,1,0:T(8,128)} %bitcast.81, f32[6,64,128]{2,1,0:T(8,128)} %bitcast_convert_fusion.face_ref, ...), custom_call_target="tpu_custom_call" | custom-call | tf_op jit(solution)/shard_map/pallas_call | solution.py:237
  33.5 2.2 %shard_map.126 = (f32[10,64,128]{2,1,0:T(8,128)}, f32[10,16,128]{2,1,0:T(8,128)}, f32[10,4,128]{2,1,0:T(4,128)}, f32[10,4,128]{2,1,0:T(4,128)}) custom-call(f32[1122]{0:T(1024)} %concatenate.15.mat_ref.wt_ref, f32[1122]{0:T(1024)} %concatenate.15.mat_ref.wt_ref, f32[10,64,128]{2,1,0:T(8,128)} %get-tuple-element.22.psi_ref, ...), custom_call_target="tpu_custom_call" | custom-call | tf_op jit(solution)/shard_map/pallas_call | solution.py:249
  35.7 1.9 %collective-permute-start.6 = (f32[10,16,128]{2,1,0:T(8,128)}, f32[10,16,128]{2,1,0:T(8,128)S(1)}, u32[]{:S(2)}, u32[]{:S(2)}) collective-permute-start(f32[10,16,128]{2,1,0:T(8,128)} %get-tuple-element.27), channel_id=1, source_target_pairs={{0,4},{4,0},{1,5},{5,1},{2,6},{6,2},{3,7},{7,3},{8,12},{12,8},{9,1... | collective-permute-start | bytes 245768 | tf_op jit(solution)/shard_map/ppermute | solution.py:316
  37.6 3.5 %collective-permute-start.7 = (f32[10,4,128]{2,1,0:T(4,128)}, f32[10,4,128]{2,1,0:T(4,128)S(1)}, u32[]{:S(2)}, u32[]{:S(2)}) collective-permute-start(f32[10,4,128]{2,1,0:T(4,128)} %get-tuple-element.28), channel_id=1, source_target_pairs={{0,1},{1,2},{2,3},{4,5},{5,6},{6,7},{8,9},{9,10},{10,11},{12,13},{... | collective-permute-start | bytes 61448 | tf_op jit(solution)/shard_map/ppermute | solution.py:317
  41.1 1.3 %collective-permute-start.8 = (f32[10,4,128]{2,1,0:T(4,128)}, f32[10,4,128]{2,1,0:T(4,128)S(1)}, u32[]{:S(2)}, u32[]{:S(2)}) collective-permute-start(f32[10,4,128]{2,1,0:T(4,128)} %get-tuple-element.29), channel_id=1, source_target_pairs={{1,0},{2,1},{3,2},{5,4},{6,5},{7,6},{9,8},{10,9},{11,10},{13,12},{... | collective-permute-start | bytes 61448 | tf_op jit(solution)/shard_map/ppermute | solution.py:318
  42.5 3.3 %shard_map.127.res_ref = f32[10,64,128]{2,1,0:T(8,128)} custom-call(f32[1122]{0:T(1024)} %concatenate.15.mat_ref.wt_ref, f32[1122]{0:T(1024)} %concatenate.15.mat_ref.wt_ref, f32[10,64,128]{2,1,0:T(8,128)} %get-tuple-element.26.psi_ref, f32[10,64,128]{2,1,0:T(8,128)} %bitcast.82, f32[6,64,128]{2,1,0:T(8,128)} %bitcast_convert_fusion.face_ref, ...), custom_call_target="tpu_custom_call" | custom-call | tf_op jit(solution)/shard_map/pallas_call | solution.py:237
  45.8 1.3 %collective-permute-done.8.rahi_ref = f32[10,4,128]{2,1,0:T(4,128)S(1)} collective-permute-done((f32[10,4,128]{2,1,0:T(4,128)}, f32[10,4,128]{2,1,0:T(4,128)S(1)}, u32[]{:S(2)}, u32[]{:S(2)}) %collective-permute-start.8) | collective-permute-done | bytes 20512 | tf_op jit(solution)/shard_map/ppermute | solution.py:318
  48.3 2.2 %shard_map.128 = (f32[10,64,128]{2,1,0:T(8,128)}, f32[10,16,128]{2,1,0:T(8,128)}, f32[10,4,128]{2,1,0:T(4,128)}, f32[10,4,128]{2,1,0:T(4,128)}) custom-call(f32[1122]{0:T(1024)} %concatenate.15.mat_ref.wt_ref, f32[1122]{0:T(1024)} %concatenate.15.mat_ref.wt_ref, f32[10,64,128]{2,1,0:T(8,128)} %get-tuple-element.26.psi_ref, ...), custom_call_target="tpu_custom_call" | custom-call | tf_op jit(solution)/shard_map/pallas_call | solution.py:249
  50.6 3.4 %collective-permute-start.10 = (f32[10,4,128]{2,1,0:T(4,128)}, f32[10,4,128]{2,1,0:T(4,128)S(1)}, u32[]{:S(2)}, u32[]{:S(2)}) collective-permute-start(f32[10,4,128]{2,1,0:T(4,128)} %get-tuple-element.32), channel_id=1, source_target_pairs={{0,1},{1,2},{2,3},{4,5},{5,6},{6,7},{8,9},{9,10},{10,11},{12,13},{... | collective-permute-start | bytes 61448 | tf_op jit(solution)/shard_map/ppermute | solution.py:317
  54.0 1.5 %collective-permute-start.11 = (f32[10,4,128]{2,1,0:T(4,128)}, f32[10,4,128]{2,1,0:T(4,128)S(1)}, u32[]{:S(2)}, u32[]{:S(2)}) collective-permute-start(f32[10,4,128]{2,1,0:T(4,128)} %get-tuple-element.33), channel_id=1, source_target_pairs={{1,0},{2,1},{3,2},{5,4},{6,5},{7,6},{9,8},{10,9},{11,10},{13,12},{... | collective-permute-start | bytes 61448 | tf_op jit(solution)/shard_map/ppermute | solution.py:318
  55.5 3.3 %shard_map.129.res_ref = f32[10,64,128]{2,1,0:T(8,128)} custom-call(f32[1122]{0:T(1024)} %concatenate.15.mat_ref.wt_ref, f32[1122]{0:T(1024)} %concatenate.15.mat_ref.wt_ref, f32[10,64,128]{2,1,0:T(8,128)} %get-tuple-element.30.psi_ref, f32[10,64,128]{2,1,0:T(8,128)} %bitcast.83, f32[6,64,128]{2,1,0:T(8,128)} %bitcast_convert_fusion.face_ref, ...), custom_call_target="tpu_custom_call" | custom-call | tf_op jit(solution)/shard_map/pallas_call | solution.py:237
  61.1 2.0 %shard_map.130 = (f32[10,64,128]{2,1,0:T(8,128)}, f32[3,64,128]{2,1,0:T(8,128)}) custom-call(f32[1122]{0:T(1024)} %concatenate.15.mat_ref.wt_ref, f32[1122]{0:T(1024)} %concatenate.15.mat_ref.wt_ref, f32[10,64,128]{2,1,0:T(8,128)} %get-tuple-element.30.psi_ref, f32[10,64,128]{2,1,0:T(8,128)} %shard_map.129.res_ref, ...), custom_call_target="tpu_custom_call" | custom-call | tf_op jit(solution)/shard_map/pallas_call | solution.py:249
  63.1 4.2 %fusion.3 = f32[3,8192]{1,0:T(4,128)S(1)} fusion(f32[3,64,128]{2,1,0:T(8,128)} %get-tuple-element.35, s32[8192]{0:T(1024)S(1)} %add_select_fusion, pred[64,8192]{1,0:T(8,128)(4,1)S(1)} %iota_compare_fusion.1), kind=kOutput, calls=%fused_computation.5 | convolution fusion | flops 2420088832 | bytes 753664 | tf_op jit(solution)/shard_map/xl,lj->xj/dot_general | solution.py:338
  69.3 7.8 %all-to-all-start = ((f32[8,3,512]{2,1,0:T(4,128)}), f32[8,3,512]{2,1,0:T(4,128)S(1)}, u32[]{:S(2)}, u32[]{:S(2)}) async-start(f32[8,3,512]{2,1,0:T(4,128)} %select_add_fusion), calls=%async_computation | async-start | bytes 131072 | tf_op jit(solution)/shard_map/all_to_all | solution.py:42
  77.7 2.6 %shard_map.131 = f32[36,512]{1,0:T(8,128)} custom-call(s32[2,512]{1,0:T(2,128)} %pad_add_fusion.where_ref, bf16[2304,128]{1,0:T(8,128)(2,1)} %bitcast.95), custom_call_target="tpu_custom_call" | custom-call | tf_op jit(solution)/shard_map/pallas_call | solution.py:350
  81.2 3.8 %all-to-all-done = f32[8,3,512]{2,1,0:T(4,128)S(1)} async-done(((f32[8,3,512]{2,1,0:T(4,128)}), f32[8,3,512]{2,1,0:T(4,128)S(1)}, u32[]{:S(2)}, u32[]{:S(2)}) %all-to-all-start) | async-done | bytes 49184 | tf_op jit(solution)/shard_map/all_to_all | solution.py:42
  (74 shorter events, 16.3 us)
Async XLA Ops:
  0.6 3.3 %copy-start.14 = (f32[3,10]{1,0:T(4,128)S(1)}, f32[3,10]{1,0:T(4,128)}, u32[]{:S(2)}) copy-start(f32[3,10]{1,0:T(4,128)} %param.17) | copy-start | bytes 364
  0.6 3.4 %copy-start.1 = (bf16[6,4,16,128]{3,2,1,0:T(8,128)(2,1)S(1)}, bf16[6,4,16,128]{3,2,1,0:T(8,128)(2,1)}, u32[]{:S(2)}) copy-start(bf16[6,4,16,128]{3,2,1,0:T(8,128)(2,1)} %param.13) | copy-start | bytes 294916
  2.3 11.8 %copy-start = (s32[1,1,8192]{2,1,0:T(1,128)S(1)}, s32[1,1,8192]{2,1,0:T(1,128)}, u32[]{:S(2)}) copy-start(s32[1,1,8192]{2,1,0:T(1,128)} %param.21) | copy-start | bytes 98308
  2.3 11.9 %copy-start.15 = (s32[1,1,64]{2,1,0:T(1,128)S(1)}, s32[1,1,64]{2,1,0:T(1,128)}, u32[]{:S(2)}) copy-start(s32[1,1,64]{2,1,0:T(1,128)} %param.20) | copy-start | bytes 772
  7.4 11.3 %collective-permute-start = (f32[10,16,128]{2,1,0:T(8,128)}, f32[10,16,128]{2,1,0:T(8,128)S(1)}, u32[]{:S(2)}, u32[]{:S(2)}) collective-permute-start(f32[10,16,128]{2,1,0:T(8,128)} %get-tuple-element.19), channel_id=1, source_target_pairs={{0,4},{4,0},{1,5},{5,1},{2,6},{6,2},{3,7},{7,3},{8,12},{12,8},{9,1... | collective-permute-start | bytes 245768 | tf_op jit(solution)/shard_map/ppermute | solution.py:316
  9.4 8.9 %collective-permute-start.1 = (f32[10,4,128]{2,1,0:T(4,128)}, f32[10,4,128]{2,1,0:T(4,128)S(1)}, u32[]{:S(2)}, u32[]{:S(2)}) collective-permute-start(f32[10,4,128]{2,1,0:T(4,128)} %get-tuple-element.20), channel_id=1, source_target_pairs={{0,1},{1,2},{2,3},{4,5},{5,6},{6,7},{8,9},{9,10},{10,11},{12,13},{... | collective-permute-start | bytes 61448 | tf_op jit(solution)/shard_map/ppermute | solution.py:317
  12.8 5.9 %collective-permute-start.2 = (f32[10,4,128]{2,1,0:T(4,128)}, f32[10,4,128]{2,1,0:T(4,128)S(1)}, u32[]{:S(2)}, u32[]{:S(2)}) collective-permute-start(f32[10,4,128]{2,1,0:T(4,128)} %get-tuple-element.21), channel_id=1, source_target_pairs={{1,0},{2,1},{3,2},{5,4},{6,5},{7,6},{9,8},{10,9},{11,10},{13,12},{... | collective-permute-start | bytes 61448 | tf_op jit(solution)/shard_map/ppermute | solution.py:318
  19.3 0.6 copy-start.5
  22.1 10.1 %collective-permute-start.3 = (f32[10,16,128]{2,1,0:T(8,128)}, f32[10,16,128]{2,1,0:T(8,128)S(1)}, u32[]{:S(2)}, u32[]{:S(2)}) collective-permute-start(f32[10,16,128]{2,1,0:T(8,128)} %get-tuple-element.23), channel_id=1, source_target_pairs={{0,4},{4,0},{1,5},{5,1},{2,6},{6,2},{3,7},{7,3},{8,12},{12,8},{9,1... | collective-permute-start | bytes 245768 | tf_op jit(solution)/shard_map/ppermute | solution.py:316
  22.2 9.0 %collective-permute-start.4 = (f32[10,4,128]{2,1,0:T(4,128)}, f32[10,4,128]{2,1,0:T(4,128)S(1)}, u32[]{:S(2)}, u32[]{:S(2)}) collective-permute-start(f32[10,4,128]{2,1,0:T(4,128)} %get-tuple-element.24), channel_id=1, source_target_pairs={{0,1},{1,2},{2,3},{4,5},{5,6},{6,7},{8,9},{9,10},{10,11},{12,13},{... | collective-permute-start | bytes 61448 | tf_op jit(solution)/shard_map/ppermute | solution.py:317
  26.4 5.9 %collective-permute-start.5 = (f32[10,4,128]{2,1,0:T(4,128)}, f32[10,4,128]{2,1,0:T(4,128)S(1)}, u32[]{:S(2)}, u32[]{:S(2)}) collective-permute-start(f32[10,4,128]{2,1,0:T(4,128)} %get-tuple-element.25), channel_id=1, source_target_pairs={{1,0},{2,1},{3,2},{5,4},{6,5},{7,6},{9,8},{10,9},{11,10},{13,12},{... | collective-permute-start | bytes 61448 | tf_op jit(solution)/shard_map/ppermute | solution.py:318
  31.3 1.0 %copy-start.10 = (f32[10,4,128]{2,1,0:T(4,128)}, f32[10,4,128]{2,1,0:T(4,128)S(1)}, u32[]{:S(2)}) copy-start(f32[10,4,128]{2,1,0:T(4,128)S(1)} %collective-permute-done.4.ralo_ref) | copy-start | bytes 61444
  32.9 0.6 copy-start.4
  35.7 11.4 %collective-permute-start.6 = (f32[10,16,128]{2,1,0:T(8,128)}, f32[10,16,128]{2,1,0:T(8,128)S(1)}, u32[]{:S(2)}, u32[]{:S(2)}) collective-permute-start(f32[10,16,128]{2,1,0:T(8,128)} %get-tuple-element.27), channel_id=1, source_target_pairs={{0,4},{4,0},{1,5},{5,1},{2,6},{6,2},{3,7},{7,3},{8,12},{12,8},{9,1... | collective-permute-start | bytes 245768 | tf_op jit(solution)/shard_map/ppermute | solution.py:316
  37.6 8.2 %collective-permute-start.7 = (f32[10,4,128]{2,1,0:T(4,128)}, f32[10,4,128]{2,1,0:T(4,128)S(1)}, u32[]{:S(2)}, u32[]{:S(2)}) collective-permute-start(f32[10,4,128]{2,1,0:T(4,128)} %get-tuple-element.28), channel_id=1, source_target_pairs={{0,1},{1,2},{2,3},{4,5},{5,6},{6,7},{8,9},{9,10},{10,11},{12,13},{... | collective-permute-start | bytes 61448 | tf_op jit(solution)/shard_map/ppermute | solution.py:317
  41.1 5.9 %collective-permute-start.8 = (f32[10,4,128]{2,1,0:T(4,128)}, f32[10,4,128]{2,1,0:T(4,128)S(1)}, u32[]{:S(2)}, u32[]{:S(2)}) collective-permute-start(f32[10,4,128]{2,1,0:T(4,128)} %get-tuple-element.29), channel_id=1, source_target_pairs={{1,0},{2,1},{3,2},{5,4},{6,5},{7,6},{9,8},{10,9},{11,10},{13,12},{... | collective-permute-start | bytes 61448 | tf_op jit(solution)/shard_map/ppermute | solution.py:318
  45.8 1.3 %copy-start.8 = (f32[10,4,128]{2,1,0:T(4,128)}, f32[10,4,128]{2,1,0:T(4,128)S(1)}, u32[]{:S(2)}) copy-start(f32[10,4,128]{2,1,0:T(4,128)S(1)} %collective-permute-done.7.ralo_ref) | copy-start | bytes 61444
  47.6 0.6 copy-start.3
  50.5 9.4 %collective-permute-start.9 = (f32[10,16,128]{2,1,0:T(8,128)}, f32[10,16,128]{2,1,0:T(8,128)S(1)}, u32[]{:S(2)}, u32[]{:S(2)}) collective-permute-start(f32[10,16,128]{2,1,0:T(8,128)} %get-tuple-element.31), channel_id=1, source_target_pairs={{0,4},{4,0},{1,5},{5,1},{2,6},{6,2},{3,7},{7,3},{8,12},{12,8},{9,1... | collective-permute-start | bytes 245768 | tf_op jit(solution)/shard_map/ppermute | solution.py:316
  50.6 8.2 %collective-permute-start.10 = (f32[10,4,128]{2,1,0:T(4,128)}, f32[10,4,128]{2,1,0:T(4,128)S(1)}, u32[]{:S(2)}, u32[]{:S(2)}) collective-permute-start(f32[10,4,128]{2,1,0:T(4,128)} %get-tuple-element.32), channel_id=1, source_target_pairs={{0,1},{1,2},{2,3},{4,5},{5,6},{6,7},{8,9},{9,10},{10,11},{12,13},{... | collective-permute-start | bytes 61448 | tf_op jit(solution)/shard_map/ppermute | solution.py:317
  54.0 5.9 %collective-permute-start.11 = (f32[10,4,128]{2,1,0:T(4,128)}, f32[10,4,128]{2,1,0:T(4,128)S(1)}, u32[]{:S(2)}, u32[]{:S(2)}) collective-permute-start(f32[10,4,128]{2,1,0:T(4,128)} %get-tuple-element.33), channel_id=1, source_target_pairs={{1,0},{2,1},{3,2},{5,4},{6,5},{7,6},{9,8},{10,9},{11,10},{13,12},{... | collective-permute-start | bytes 61448 | tf_op jit(solution)/shard_map/ppermute | solution.py:318
  58.8 1.1 %copy-start.6 = (f32[10,4,128]{2,1,0:T(4,128)}, f32[10,4,128]{2,1,0:T(4,128)S(1)}, u32[]{:S(2)}) copy-start(f32[10,4,128]{2,1,0:T(4,128)S(1)} %collective-permute-done.10.ralo_ref) | copy-start | bytes 61444
  67.3 1.3 %collective-permute-start.12 = (f32[8,3,512]{2,1,0:T(4,128)S(1)}, f32[8,3,512]{2,1,0:T(4,128)S(1)}, u32[]{:S(2)}, u32[]{:S(2)}) collective-permute-start(f32[8,3,512]{2,1,0:T(4,128)S(1)} %slice_select_fusion), channel_id=1, source_target_pairs={{0,8},{8,0},{16,24},{24,16},{32,40},{40,32},{48,56},{56,48},{64,72... | collective-permute-start | bytes 147464 | tf_op jit(solution)/shard_map/ppermute | solution.py:40
  69.3 15.6 %all-to-all-start = ((f32[8,3,512]{2,1,0:T(4,128)}), f32[8,3,512]{2,1,0:T(4,128)S(1)}, u32[]{:S(2)}, u32[]{:S(2)}) async-start(f32[8,3,512]{2,1,0:T(4,128)} %select_add_fusion), calls=%async_computation | async-start | bytes 131072 | tf_op jit(solution)/shard_map/all_to_all | solution.py:42
  (6 other events, 3.6 us)

commit v8 on v7

--- a/solution.py
+++ b/solution.py
@@ -85,7 +85,9 @@
         q3_ref[x] = face_ref[3, r_bottom, :] * applied(mat_ref, 3, x, comps, lambda c: psi_ref[c, r_bottom, :])
 
 
-def edges_kernel(mat_ref, wt_ref, psi_ref, face_ref, axs_ref, q2_ref, q3_ref, *, tile_r):
+def edges_kernel(mat_ref, wt_ref, psi_ref, coef_ref, axs_ref, q2_ref, q3_ref, face_ref, *, tile_r):
+    for d in range(face_ref.shape[0]):
+        face_ref[d] = coef_ref[d].astype(jnp.float32)
     write_edges(mat_ref, wt_ref, psi_ref, face_ref, axs_ref, q2_ref, q3_ref, psi_ref.shape[0], tile_r)
 
 
@@ -226,9 +228,9 @@
     comps, rows, _ = psi.shape
     return pl.pallas_call(
         functools.partial(edges_kernel, tile_r=tile_r),
-        out_shape=edge_shapes(comps, rows, tile_r),
+        out_shape=edge_shapes(comps, rows, tile_r) + (jax.ShapeDtypeStruct(face.shape, jnp.float32),),
         in_specs=[smem_spec(), smem_spec(), vmem_spec(), vmem_spec()],
-        out_specs=tuple(vmem_spec() for _ in range(3)),
+        out_specs=tuple(vmem_spec() for _ in range(4)),
     )(mat, weights, psi, face)
 
 
@@ -305,13 +307,13 @@
     mat = mat_weights
     weights = mat_weights
     partner = pairing[0, 0]
-    faces = face_coef.astype(jnp.float32).reshape(6, rows, pitch)
+    coefs = face_coef.reshape(face_coef.shape[0], rows, pitch)
     diag = diag_coef.reshape(rows, pitch)
     pick = partner.astype(jnp.int32).reshape(rows, 1)
     up_r, down_r = neighbours("radial")
     psi = psi_start.reshape(comps, rows, pitch)
     src = source.reshape(comps, rows, pitch)
-    axs, q2, q3 = run_edges(mat, weights, psi, faces, tile_r)
+    axs, q2, q3, faces = run_edges(mat, weights, psi, coefs, tile_r)
     for section in range(ITERS):
         axr = lax.ppermute(axs, "axial", [(0, 1), (1, 0)])
         ralo = lax.ppermute(q2, "radial", up_r)

time: 86.4 us -> 85.7 us (level)
    unnamed x34 -> x32, local copies, waits for them, and re-layouts: 5.16 us -> 5.18 us
  transfers between devices with their start and end apart: 14 -> 14, of which waited for: 6 -> 6; matrix products, arithmetic and copies ran while one was open for 3% -> 3% of each run, Pallas kernels for 18% -> 19%
where the time goes in v8:
time: 85.7 us; the launch traced here: 84.9 us
  starting transfers between devices  31.8 us (37%)
  Pallas kernels  26.2 us (31%)
  local copies, waits for them, and re-layouts  9.05 us (11%)
  waiting for transfers between devices  8.77 us (10%)
  matrix products  4.2 us (5%)
  other arithmetic  2.56 us (3%)
  between operations  2.34 us (3%)
    ppermute x4, starting transfers between devices, body(): ralo = lax.ppermute(q2, 'radial', up_r)  14.4 us
    pallas_call x4, Pallas kernels, run_interior(): pl.pallas_call(functools.partial(interior_kernel, tile_r=tile_r), out_sha...  13.2 us
    pallas_call x4, Pallas kernels, run_fixup(): pl.pallas_call(functools.partial(fixup_kernel, tile_r=tile_r, edges=edges...  8.6 us
    all_to_all x1, starting transfers between devices, sum_at_owner_paired(): lax.all_to_all(keep + got, axis, 0, 0, tiled=True, axis_index_groups=groups)  7.79 us
    ppermute x4, starting transfers between devices, body(): rahi = lax.ppermute(q3, 'radial', down_r)  5.35 us
    unnamed x32, local copies, waits for them, and re-layouts  5.18 us
    dot_general x1, matrix products, body(): jnp.einsum('xl,lj->xj', weighted.reshape(dims * blocks, lanes), pick_lane...  4.2 us
    ppermute x4, starting transfers between devices, body(): axr = lax.ppermute(axs, 'axial', [(0, 1), (1, 0)])  4.16 us
  transfers between devices with their start and end apart: 14, of which 6 were waited for; matrix products, arithmetic and copies ran while one was open for 3% of the time, Pallas kernels for 19%

profile of v8, /device:TPU:0, one launch (start us, length us, event | category | flops | bytes accessed | tf_op | source)
XLA Modules:
  0.0 84.9 jit_solution(17872157154281249037)
XLA Ops:
  4.7 1.9 %shard_map.122 = (f32[10,16,128]{2,1,0:T(8,128)}, f32[10,4,128]{2,1,0:T(4,128)}, f32[10,4,128]{2,1,0:T(4,128)}, f32[6,64,128]{2,1,0:T(8,128)}) custom-call(f32[1122]{0:T(1024)} %concatenate.15.mat_ref.wt_ref, f32[1122]{0:T(1024)} %concatenate.15.mat_ref.wt_ref, f32[10,64,128]{2,1,0:T(8,128)} %bitcast.82, bf16[6,64,128]{2,1,0:T(8,128)(2,1)} %bitcast.101), custom_call_target="tpu_custom_call" | custom-call | tf_op jit(solution)/shard_map/pallas_call | solution.py:229
  6.6 2.0 %collective-permute-start = (f32[10,16,128]{2,1,0:T(8,128)}, f32[10,16,128]{2,1,0:T(8,128)S(1)}, u32[]{:S(2)}, u32[]{:S(2)}) collective-permute-start(f32[10,16,128]{2,1,0:T(8,128)} %get-tuple-element.21), channel_id=1, source_target_pairs={{0,4},{4,0},{1,5},{5,1},{2,6},{6,2},{3,7},{7,3},{8,12},{12,8},{9,1... | collective-permute-start | bytes 245768 | tf_op jit(solution)/shard_map/ppermute | solution.py:318
  8.6 3.4 %collective-permute-start.1 = (f32[10,4,128]{2,1,0:T(4,128)}, f32[10,4,128]{2,1,0:T(4,128)S(1)}, u32[]{:S(2)}, u32[]{:S(2)}) collective-permute-start(f32[10,4,128]{2,1,0:T(4,128)} %get-tuple-element.22), channel_id=1, source_target_pairs={{0,1},{1,2},{2,3},{4,5},{5,6},{6,7},{8,9},{9,10},{10,11},{12,13},{... | collective-permute-start | bytes 61448 | tf_op jit(solution)/shard_map/ppermute | solution.py:319
  12.0 1.3 %collective-permute-start.2 = (f32[10,4,128]{2,1,0:T(4,128)}, f32[10,4,128]{2,1,0:T(4,128)S(1)}, u32[]{:S(2)}, u32[]{:S(2)}) collective-permute-start(f32[10,4,128]{2,1,0:T(4,128)} %get-tuple-element.23), channel_id=1, source_target_pairs={{1,0},{2,1},{3,2},{5,4},{6,5},{7,6},{9,8},{10,9},{11,10},{13,12},{... | collective-permute-start | bytes 61448 | tf_op jit(solution)/shard_map/ppermute | solution.py:320
  14.2 3.3 %shard_map.123.res_ref = f32[10,64,128]{2,1,0:T(8,128)} custom-call(f32[1122]{0:T(1024)} %concatenate.15.mat_ref.wt_ref, f32[1122]{0:T(1024)} %concatenate.15.mat_ref.wt_ref, f32[10,64,128]{2,1,0:T(8,128)} %bitcast.83, f32[10,64,128]{2,1,0:T(8,128)} %bitcast.78, f32[6,64,128]{2,1,0:T(8,128)} %get-tuple-element.20.face_ref, f32[64,128]{1,0:T(8,128)} %bitcast.85, ...), custom_call_target="tpu_custom_call" | custom-call | tf_op jit(solution)/shard_map/pallas_call | solution.py:239
  19.2 2.2 %shard_map.124 = (f32[10,64,128]{2,1,0:T(8,128)}, f32[10,16,128]{2,1,0:T(8,128)}, f32[10,4,128]{2,1,0:T(4,128)}, f32[10,4,128]{2,1,0:T(4,128)}) custom-call(f32[1122]{0:T(1024)} %concatenate.15.mat_ref.wt_ref, f32[1122]{0:T(1024)} %concatenate.15.mat_ref.wt_ref, f32[10,64,128]{2,1,0:T(8,128)} %bitcast.84, f32[10,64,128]{2,1,0:T(8,128)} %shard_map.123.res_ref, ...), custom_call_target="tpu_custom_call" | custom-call | tf_op jit(solution)/shard_map/pallas_call | solution.py:251
  21.5 4.1 %collective-permute-start.4 = (f32[10,4,128]{2,1,0:T(4,128)}, f32[10,4,128]{2,1,0:T(4,128)S(1)}, u32[]{:S(2)}, u32[]{:S(2)}) collective-permute-start(f32[10,4,128]{2,1,0:T(4,128)} %get-tuple-element.26), channel_id=1, source_target_pairs={{0,1},{1,2},{2,3},{4,5},{5,6},{6,7},{8,9},{9,10},{10,11},{12,13},{... | collective-permute-start | bytes 61448 | tf_op jit(solution)/shard_map/ppermute | solution.py:319
  25.6 1.3 %collective-permute-start.5 = (f32[10,4,128]{2,1,0:T(4,128)}, f32[10,4,128]{2,1,0:T(4,128)S(1)}, u32[]{:S(2)}, u32[]{:S(2)}) collective-permute-start(f32[10,4,128]{2,1,0:T(4,128)} %get-tuple-element.27), channel_id=1, source_target_pairs={{1,0},{2,1},{3,2},{5,4},{6,5},{7,6},{9,8},{10,9},{11,10},{13,12},{... | collective-permute-start | bytes 61448 | tf_op jit(solution)/shard_map/ppermute | solution.py:320
  27.2 3.3 %shard_map.125.res_ref = f32[10,64,128]{2,1,0:T(8,128)} custom-call(f32[1122]{0:T(1024)} %concatenate.15.mat_ref.wt_ref, f32[1122]{0:T(1024)} %concatenate.15.mat_ref.wt_ref, f32[10,64,128]{2,1,0:T(8,128)} %get-tuple-element.24.psi_ref, f32[10,64,128]{2,1,0:T(8,128)} %bitcast.79, f32[6,64,128]{2,1,0:T(8,128)} %get-tuple-element.20.face_ref, ...), custom_call_target="tpu_custom_call" | custom-call | tf_op jit(solution)/shard_map/pallas_call | solution.py:239
  32.7 2.2 %shard_map.126 = (f32[10,64,128]{2,1,0:T(8,128)}, f32[10,16,128]{2,1,0:T(8,128)}, f32[10,4,128]{2,1,0:T(4,128)}, f32[10,4,128]{2,1,0:T(4,128)}) custom-call(f32[1122]{0:T(1024)} %concatenate.15.mat_ref.wt_ref, f32[1122]{0:T(1024)} %concatenate.15.mat_ref.wt_ref, f32[10,64,128]{2,1,0:T(8,128)} %get-tuple-element.24.psi_ref, ...), custom_call_target="tpu_custom_call" | custom-call | tf_op jit(solution)/shard_map/pallas_call | solution.py:251
  34.9 1.9 %collective-permute-start.6 = (f32[10,16,128]{2,1,0:T(8,128)}, f32[10,16,128]{2,1,0:T(8,128)S(1)}, u32[]{:S(2)}, u32[]{:S(2)}) collective-permute-start(f32[10,16,128]{2,1,0:T(8,128)} %get-tuple-element.29), channel_id=1, source_target_pairs={{0,4},{4,0},{1,5},{5,1},{2,6},{6,2},{3,7},{7,3},{8,12},{12,8},{9,1... | collective-permute-start | bytes 245768 | tf_op jit(solution)/shard_map/ppermute | solution.py:318
  36.8 3.5 %collective-permute-start.7 = (f32[10,4,128]{2,1,0:T(4,128)}, f32[10,4,128]{2,1,0:T(4,128)S(1)}, u32[]{:S(2)}, u32[]{:S(2)}) collective-permute-start(f32[10,4,128]{2,1,0:T(4,128)} %get-tuple-element.30), channel_id=1, source_target_pairs={{0,1},{1,2},{2,3},{4,5},{5,6},{6,7},{8,9},{9,10},{10,11},{12,13},{... | collective-permute-start | bytes 61448 | tf_op jit(solution)/shard_map/ppermute | solution.py:319
  40.4 1.3 %collective-permute-start.8 = (f32[10,4,128]{2,1,0:T(4,128)}, f32[10,4,128]{2,1,0:T(4,128)S(1)}, u32[]{:S(2)}, u32[]{:S(2)}) collective-permute-start(f32[10,4,128]{2,1,0:T(4,128)} %get-tuple-element.31), channel_id=1, source_target_pairs={{1,0},{2,1},{3,2},{5,4},{6,5},{7,6},{9,8},{10,9},{11,10},{13,12},{... | collective-permute-start | bytes 61448 | tf_op jit(solution)/shard_map/ppermute | solution.py:320
  41.7 3.3 %shard_map.127.res_ref = f32[10,64,128]{2,1,0:T(8,128)} custom-call(f32[1122]{0:T(1024)} %concatenate.15.mat_ref.wt_ref, f32[1122]{0:T(1024)} %concatenate.15.mat_ref.wt_ref, f32[10,64,128]{2,1,0:T(8,128)} %get-tuple-element.28.psi_ref, f32[10,64,128]{2,1,0:T(8,128)} %bitcast.80, f32[6,64,128]{2,1,0:T(8,128)} %get-tuple-element.20.face_ref, ...), custom_call_target="tpu_custom_call" | custom-call | tf_op jit(solution)/shard_map/pallas_call | solution.py:239
  45.0 1.3 %collective-permute-done.8.rahi_ref = f32[10,4,128]{2,1,0:T(4,128)S(1)} collective-permute-done((f32[10,4,128]{2,1,0:T(4,128)}, f32[10,4,128]{2,1,0:T(4,128)S(1)}, u32[]{:S(2)}, u32[]{:S(2)}) %collective-permute-start.8) | collective-permute-done | bytes 20512 | tf_op jit(solution)/shard_map/ppermute | solution.py:320
  47.5 2.2 %shard_map.128 = (f32[10,64,128]{2,1,0:T(8,128)}, f32[10,16,128]{2,1,0:T(8,128)}, f32[10,4,128]{2,1,0:T(4,128)}, f32[10,4,128]{2,1,0:T(4,128)}) custom-call(f32[1122]{0:T(1024)} %concatenate.15.mat_ref.wt_ref, f32[1122]{0:T(1024)} %concatenate.15.mat_ref.wt_ref, f32[10,64,128]{2,1,0:T(8,128)} %get-tuple-element.28.psi_ref, ...), custom_call_target="tpu_custom_call" | custom-call | tf_op jit(solution)/shard_map/pallas_call | solution.py:251
  49.8 3.4 %collective-permute-start.10 = (f32[10,4,128]{2,1,0:T(4,128)}, f32[10,4,128]{2,1,0:T(4,128)S(1)}, u32[]{:S(2)}, u32[]{:S(2)}) collective-permute-start(f32[10,4,128]{2,1,0:T(4,128)} %get-tuple-element.34), channel_id=1, source_target_pairs={{0,1},{1,2},{2,3},{4,5},{5,6},{6,7},{8,9},{9,10},{10,11},{12,13},{... | collective-permute-start | bytes 61448 | tf_op jit(solution)/shard_map/ppermute | solution.py:319
  53.2 1.5 %collective-permute-start.11 = (f32[10,4,128]{2,1,0:T(4,128)}, f32[10,4,128]{2,1,0:T(4,128)S(1)}, u32[]{:S(2)}, u32[]{:S(2)}) collective-permute-start(f32[10,4,128]{2,1,0:T(4,128)} %get-tuple-element.35), channel_id=1, source_target_pairs={{1,0},{2,1},{3,2},{5,4},{6,5},{7,6},{9,8},{10,9},{11,10},{13,12},{... | collective-permute-start | bytes 61448 | tf_op jit(solution)/shard_map/ppermute | solution.py:320
  54.7 3.3 %shard_map.129.res_ref = f32[10,64,128]{2,1,0:T(8,128)} custom-call(f32[1122]{0:T(1024)} %concatenate.15.mat_ref.wt_ref, f32[1122]{0:T(1024)} %concatenate.15.mat_ref.wt_ref, f32[10,64,128]{2,1,0:T(8,128)} %get-tuple-element.32.psi_ref, f32[10,64,128]{2,1,0:T(8,128)} %bitcast.81, f32[6,64,128]{2,1,0:T(8,128)} %get-tuple-element.20.face_ref, ...), custom_call_target="tpu_custom_call" | custom-call | tf_op jit(solution)/shard_map/pallas_call | solution.py:239
  60.3 2.0 %shard_map.130 = (f32[10,64,128]{2,1,0:T(8,128)}, f32[3,64,128]{2,1,0:T(8,128)}) custom-call(f32[1122]{0:T(1024)} %concatenate.15.mat_ref.wt_ref, f32[1122]{0:T(1024)} %concatenate.15.mat_ref.wt_ref, f32[10,64,128]{2,1,0:T(8,128)} %get-tuple-element.32.psi_ref, f32[10,64,128]{2,1,0:T(8,128)} %shard_map.129.res_ref, ...), custom_call_target="tpu_custom_call" | custom-call | tf_op jit(solution)/shard_map/pallas_call | solution.py:251
  62.4 4.2 %fusion.3 = f32[3,8192]{1,0:T(4,128)S(1)} fusion(f32[3,64,128]{2,1,0:T(8,128)} %get-tuple-element.37, s32[8192]{0:T(1024)S(1)} %add_select_fusion, pred[64,8192]{1,0:T(8,128)(4,1)S(1)} %iota_compare_fusion.1), kind=kOutput, calls=%fused_computation.5 | convolution fusion | flops 2420088832 | bytes 753664 | tf_op jit(solution)/shard_map/xl,lj->xj/dot_general | solution.py:340
  68.6 7.8 %all-to-all-start = ((f32[8,3,512]{2,1,0:T(4,128)}), f32[8,3,512]{2,1,0:T(4,128)S(1)}, u32[]{:S(2)}, u32[]{:S(2)}) async-start(f32[8,3,512]{2,1,0:T(4,128)} %select_add_fusion), calls=%async_computation | async-start | bytes 131072 | tf_op jit(solution)/shard_map/all_to_all | solution.py:42
  77.0 2.6 %shard_map.131 = f32[36,512]{1,0:T(8,128)} custom-call(s32[2,512]{1,0:T(2,128)} %pad_add_fusion.where_ref, bf16[2304,128]{1,0:T(8,128)(2,1)} %bitcast.93), custom_call_target="tpu_custom_call" | custom-call | tf_op jit(solution)/shard_map/pallas_call | solution.py:352
  80.5 3.8 %all-to-all-done = f32[8,3,512]{2,1,0:T(4,128)S(1)} async-done(((f32[8,3,512]{2,1,0:T(4,128)}), f32[8,3,512]{2,1,0:T(4,128)S(1)}, u32[]{:S(2)}, u32[]{:S(2)}) %all-to-all-start) | async-done | bytes 49184 | tf_op jit(solution)/shard_map/all_to_all | solution.py:42
  (71 shorter events, 15.6 us)
Async XLA Ops:
  0.6 3.3 %copy-start.13 = (f32[3,10]{1,0:T(4,128)S(1)}, f32[3,10]{1,0:T(4,128)}, u32[]{:S(2)}) copy-start(f32[3,10]{1,0:T(4,128)} %param.17) | copy-start | bytes 364
  1.9 11.5 %copy-start = (s32[1,1,8192]{2,1,0:T(1,128)S(1)}, s32[1,1,8192]{2,1,0:T(1,128)}, u32[]{:S(2)}) copy-start(s32[1,1,8192]{2,1,0:T(1,128)} %param.21) | copy-start | bytes 98308
  1.9 11.6 %copy-start.14 = (s32[1,1,64]{2,1,0:T(1,128)S(1)}, s32[1,1,64]{2,1,0:T(1,128)}, u32[]{:S(2)}) copy-start(s32[1,1,64]{2,1,0:T(1,128)} %param.20) | copy-start | bytes 772
  6.6 11.3 %collective-permute-start = (f32[10,16,128]{2,1,0:T(8,128)}, f32[10,16,128]{2,1,0:T(8,128)S(1)}, u32[]{:S(2)}, u32[]{:S(2)}) collective-permute-start(f32[10,16,128]{2,1,0:T(8,128)} %get-tuple-element.21), channel_id=1, source_target_pairs={{0,4},{4,0},{1,5},{5,1},{2,6},{6,2},{3,7},{7,3},{8,12},{12,8},{9,1... | collective-permute-start | bytes 245768 | tf_op jit(solution)/shard_map/ppermute | solution.py:318
  8.6 8.9 %collective-permute-start.1 = (f32[10,4,128]{2,1,0:T(4,128)}, f32[10,4,128]{2,1,0:T(4,128)S(1)}, u32[]{:S(2)}, u32[]{:S(2)}) collective-permute-start(f32[10,4,128]{2,1,0:T(4,128)} %get-tuple-element.22), channel_id=1, source_target_pairs={{0,1},{1,2},{2,3},{4,5},{5,6},{6,7},{8,9},{9,10},{10,11},{12,13},{... | collective-permute-start | bytes 61448 | tf_op jit(solution)/shard_map/ppermute | solution.py:319
  12.0 5.9 %collective-permute-start.2 = (f32[10,4,128]{2,1,0:T(4,128)}, f32[10,4,128]{2,1,0:T(4,128)S(1)}, u32[]{:S(2)}, u32[]{:S(2)}) collective-permute-start(f32[10,4,128]{2,1,0:T(4,128)} %get-tuple-element.23), channel_id=1, source_target_pairs={{1,0},{2,1},{3,2},{5,4},{6,5},{7,6},{9,8},{10,9},{11,10},{13,12},{... | collective-permute-start | bytes 61448 | tf_op jit(solution)/shard_map/ppermute | solution.py:320
  18.5 0.7 copy-start.4
  21.4 10.1 %collective-permute-start.3 = (f32[10,16,128]{2,1,0:T(8,128)}, f32[10,16,128]{2,1,0:T(8,128)S(1)}, u32[]{:S(2)}, u32[]{:S(2)}) collective-permute-start(f32[10,16,128]{2,1,0:T(8,128)} %get-tuple-element.25), channel_id=1, source_target_pairs={{0,4},{4,0},{1,5},{5,1},{2,6},{6,2},{3,7},{7,3},{8,12},{12,8},{9,1... | collective-permute-start | bytes 245768 | tf_op jit(solution)/shard_map/ppermute | solution.py:318
  21.5 9.0 %collective-permute-start.4 = (f32[10,4,128]{2,1,0:T(4,128)}, f32[10,4,128]{2,1,0:T(4,128)S(1)}, u32[]{:S(2)}, u32[]{:S(2)}) collective-permute-start(f32[10,4,128]{2,1,0:T(4,128)} %get-tuple-element.26), channel_id=1, source_target_pairs={{0,1},{1,2},{2,3},{4,5},{5,6},{6,7},{8,9},{9,10},{10,11},{12,13},{... | collective-permute-start | bytes 61448 | tf_op jit(solution)/shard_map/ppermute | solution.py:319
  25.6 5.9 %collective-permute-start.5 = (f32[10,4,128]{2,1,0:T(4,128)}, f32[10,4,128]{2,1,0:T(4,128)S(1)}, u32[]{:S(2)}, u32[]{:S(2)}) collective-permute-start(f32[10,4,128]{2,1,0:T(4,128)} %get-tuple-element.27), channel_id=1, source_target_pairs={{1,0},{2,1},{3,2},{5,4},{6,5},{7,6},{9,8},{10,9},{11,10},{13,12},{... | collective-permute-start | bytes 61448 | tf_op jit(solution)/shard_map/ppermute | solution.py:320
  30.5 1.0 %copy-start.9 = (f32[10,4,128]{2,1,0:T(4,128)}, f32[10,4,128]{2,1,0:T(4,128)S(1)}, u32[]{:S(2)}) copy-start(f32[10,4,128]{2,1,0:T(4,128)S(1)} %collective-permute-done.4.ralo_ref) | copy-start | bytes 61444
  32.1 0.6 copy-start.3
  34.9 11.4 %collective-permute-start.6 = (f32[10,16,128]{2,1,0:T(8,128)}, f32[10,16,128]{2,1,0:T(8,128)S(1)}, u32[]{:S(2)}, u32[]{:S(2)}) collective-permute-start(f32[10,16,128]{2,1,0:T(8,128)} %get-tuple-element.29), channel_id=1, source_target_pairs={{0,4},{4,0},{1,5},{5,1},{2,6},{6,2},{3,7},{7,3},{8,12},{12,8},{9,1... | collective-permute-start | bytes 245768 | tf_op jit(solution)/shard_map/ppermute | solution.py:318
  36.8 8.2 %collective-permute-start.7 = (f32[10,4,128]{2,1,0:T(4,128)}, f32[10,4,128]{2,1,0:T(4,128)S(1)}, u32[]{:S(2)}, u32[]{:S(2)}) collective-permute-start(f32[10,4,128]{2,1,0:T(4,128)} %get-tuple-element.30), channel_id=1, source_target_pairs={{0,1},{1,2},{2,3},{4,5},{5,6},{6,7},{8,9},{9,10},{10,11},{12,13},{... | collective-permute-start | bytes 61448 | tf_op jit(solution)/shard_map/ppermute | solution.py:319
  40.4 5.9 %collective-permute-start.8 = (f32[10,4,128]{2,1,0:T(4,128)}, f32[10,4,128]{2,1,0:T(4,128)S(1)}, u32[]{:S(2)}, u32[]{:S(2)}) collective-permute-start(f32[10,4,128]{2,1,0:T(4,128)} %get-tuple-element.31), channel_id=1, source_target_pairs={{1,0},{2,1},{3,2},{5,4},{6,5},{7,6},{9,8},{10,9},{11,10},{13,12},{... | collective-permute-start | bytes 61448 | tf_op jit(solution)/shard_map/ppermute | solution.py:320
  45.0 1.3 %copy-start.7 = (f32[10,4,128]{2,1,0:T(4,128)}, f32[10,4,128]{2,1,0:T(4,128)S(1)}, u32[]{:S(2)}) copy-start(f32[10,4,128]{2,1,0:T(4,128)S(1)} %collective-permute-done.7.ralo_ref) | copy-start | bytes 61444
  46.9 0.6 copy-start.2
  49.7 9.4 %collective-permute-start.9 = (f32[10,16,128]{2,1,0:T(8,128)}, f32[10,16,128]{2,1,0:T(8,128)S(1)}, u32[]{:S(2)}, u32[]{:S(2)}) collective-permute-start(f32[10,16,128]{2,1,0:T(8,128)} %get-tuple-element.33), channel_id=1, source_target_pairs={{0,4},{4,0},{1,5},{5,1},{2,6},{6,2},{3,7},{7,3},{8,12},{12,8},{9,1... | collective-permute-start | bytes 245768 | tf_op jit(solution)/shard_map/ppermute | solution.py:318
  49.8 8.2 %collective-permute-start.10 = (f32[10,4,128]{2,1,0:T(4,128)}, f32[10,4,128]{2,1,0:T(4,128)S(1)}, u32[]{:S(2)}, u32[]{:S(2)}) collective-permute-start(f32[10,4,128]{2,1,0:T(4,128)} %get-tuple-element.34), channel_id=1, source_target_pairs={{0,1},{1,2},{2,3},{4,5},{5,6},{6,7},{8,9},{9,10},{10,11},{12,13},{... | collective-permute-start | bytes 61448 | tf_op jit(solution)/shard_map/ppermute | solution.py:319
  53.2 5.9 %collective-permute-start.11 = (f32[10,4,128]{2,1,0:T(4,128)}, f32[10,4,128]{2,1,0:T(4,128)S(1)}, u32[]{:S(2)}, u32[]{:S(2)}) collective-permute-start(f32[10,4,128]{2,1,0:T(4,128)} %get-tuple-element.35), channel_id=1, source_target_pairs={{1,0},{2,1},{3,2},{5,4},{6,5},{7,6},{9,8},{10,9},{11,10},{13,12},{... | collective-permute-start | bytes 61448 | tf_op jit(solution)/shard_map/ppermute | solution.py:320
  58.0 1.1 %copy-start.5 = (f32[10,4,128]{2,1,0:T(4,128)}, f32[10,4,128]{2,1,0:T(4,128)S(1)}, u32[]{:S(2)}) copy-start(f32[10,4,128]{2,1,0:T(4,128)S(1)} %collective-permute-done.10.ralo_ref) | copy-start | bytes 61444
  59.7 0.6 copy-start.1
  66.6 1.3 %collective-permute-start.12 = (f32[8,3,512]{2,1,0:T(4,128)S(1)}, f32[8,3,512]{2,1,0:T(4,128)S(1)}, u32[]{:S(2)}, u32[]{:S(2)}) collective-permute-start(f32[8,3,512]{2,1,0:T(4,128)S(1)} %slice_select_fusion), channel_id=1, source_target_pairs={{0,8},{8,0},{16,24},{24,16},{32,40},{40,32},{48,56},{56,48},{64,72... | collective-permute-start | bytes 147464 | tf_op jit(solution)/shard_map/ppermute | solution.py:40
  68.6 15.6 %all-to-all-start = ((f32[8,3,512]{2,1,0:T(4,128)}), f32[8,3,512]{2,1,0:T(4,128)S(1)}, u32[]{:S(2)}, u32[]{:S(2)}) async-start(f32[8,3,512]{2,1,0:T(4,128)} %select_add_fusion), calls=%async_computation | async-start | bytes 131072 | tf_op jit(solution)/shard_map/all_to_all | solution.py:42
  (5 other events, 3.0 us)

commit v9 on v8

--- a/solution.py
+++ b/solution.py
@@ -51,14 +51,15 @@
     return jnp.concatenate([top_rows, low_rows], axis=1)
 
 
-def exact_pick(pick, values):
+def exact_pick(pick_t, values):
     first = values.astype(jnp.bfloat16)
     rest = values - first.astype(jnp.float32)
     second = rest.astype(jnp.bfloat16)
     third = (rest - second.astype(jnp.float32)).astype(jnp.bfloat16)
-    out = jnp.dot(pick, first, preferred_element_type=jnp.float32)
-    out = out + jnp.dot(pick, second, preferred_element_type=jnp.float32)
-    return out + jnp.dot(pick, third, preferred_element_type=jnp.float32)
+    dims = (((0,), (0,)), ((), ()))
+    out = lax.dot_general(pick_t, first, dims, preferred_element_type=jnp.float32)
+    out = out + lax.dot_general(pick_t, second, dims, preferred_element_type=jnp.float32)
+    return out + lax.dot_general(pick_t, third, dims, preferred_element_type=jnp.float32)
 
 
 def applied(mat_ref, d, x, comps, load):
@@ -141,7 +142,7 @@
             inc_ref[comp] = lower_a + upper_a + lower_r + upper_r + lower_t + upper_t
             pack4 = pack4 + jnp.where(lane == comp, pltpu.roll(q4, (comp + 1) % lanes, 1), 0.0)
             pack5 = pack5 + jnp.where(lane == comp, pltpu.roll(q5, comp, 1), 0.0) if comp else jnp.where(lane == 0, q5, 0.0)
-    pick = (pick_ref[...] == lax.broadcasted_iota(jnp.int32, (rows, rows), 1)).astype(jnp.bfloat16)
+    pick = (pick_ref[...] == lax.broadcasted_iota(jnp.int32, (rows, rows), 0)).astype(jnp.bfloat16)
     got4 = exact_pick(pick, pack4)
     got5 = exact_pick(pick, pack5)
     up4 = pltpu.roll(got4, lanes - half, 1)
@@ -309,7 +310,7 @@
     partner = pairing[0, 0]
     coefs = face_coef.reshape(face_coef.shape[0], rows, pitch)
     diag = diag_coef.reshape(rows, pitch)
-    pick = partner.astype(jnp.int32).reshape(rows, 1)
+    pick = partner.astype(jnp.int32).reshape(1, rows)
     up_r, down_r = neighbours("radial")
     psi = psi_start.reshape(comps, rows, pitch)
     src = source.reshape(comps, rows, pitch)

time: 85.7 us -> 85 us (level)
    unnamed x32 -> x30, local copies, waits for them, and re-layouts: 5.18 us -> 5.15 us
  transfers between devices with their start and end apart: 14 -> 14, of which waited for: 6 -> 6; matrix products, arithmetic and copies ran while one was open for 3% -> 2% of each run, Pallas kernels for 19% -> 19%
where the time goes in v9:
time: 85 us; the launch traced here: 84.2 us
  starting transfers between devices  31.1 us (37%)
  Pallas kernels  26.3 us (31%)
  waiting for transfers between devices  9.42 us (11%)
  local copies, waits for them, and re-layouts  8.33 us (10%)
  matrix products  4.2 us (5%)
  other arithmetic  2.55 us (3%)
  between operations  2.33 us (3%)
    ppermute x4, starting transfers between devices, body(): ralo = lax.ppermute(q2, 'radial', up_r)  13.8 us
    pallas_call x4, Pallas kernels, run_interior(): pl.pallas_call(functools.partial(interior_kernel, tile_r=tile_r), out_sha...  13.2 us
    pallas_call x4, Pallas kernels, run_fixup(): pl.pallas_call(functools.partial(fixup_kernel, tile_r=tile_r, edges=edges...  8.63 us
    all_to_all x1, starting transfers between devices, sum_at_owner_paired(): lax.all_to_all(keep + got, axis, 0, 0, tiled=True, axis_index_groups=groups)  7.79 us
    ppermute x4, starting transfers between devices, body(): rahi = lax.ppermute(q3, 'radial', down_r)  5.35 us
    unnamed x30, local copies, waits for them, and re-layouts  5.15 us
    ppermute x4, waiting for transfers between devices, body(): rahi = lax.ppermute(q3, 'radial', down_r)  4.42 us
    dot_general x1, matrix products, body(): jnp.einsum('xl,lj->xj', weighted.reshape(dims * blocks, lanes), pick_lane...  4.2 us
  transfers between devices with their start and end apart: 14, of which 6 were waited for; matrix products, arithmetic and copies ran while one was open for 2% of the time, Pallas kernels for 19%

profile of v9, /device:TPU:0, one launch (start us, length us, event | category | flops | bytes accessed | tf_op | source)
XLA Modules:
  0.0 84.2 jit_solution(15438192400926751147)
XLA Ops:
  4.7 1.9 %shard_map.122 = (f32[10,16,128]{2,1,0:T(8,128)}, f32[10,4,128]{2,1,0:T(4,128)}, f32[10,4,128]{2,1,0:T(4,128)}, f32[6,64,128]{2,1,0:T(8,128)}) custom-call(f32[1122]{0:T(1024)} %concatenate.15.mat_ref.wt_ref, f32[1122]{0:T(1024)} %concatenate.15.mat_ref.wt_ref, f32[10,64,128]{2,1,0:T(8,128)} %bitcast.82, bf16[6,64,128]{2,1,0:T(8,128)(2,1)} %bitcast.101), custom_call_target="tpu_custom_call" | custom-call | tf_op jit(solution)/shard_map/pallas_call | solution.py:230
  6.6 2.0 %collective-permute-start = (f32[10,16,128]{2,1,0:T(8,128)}, f32[10,16,128]{2,1,0:T(8,128)S(1)}, u32[]{:S(2)}, u32[]{:S(2)}) collective-permute-start(f32[10,16,128]{2,1,0:T(8,128)} %get-tuple-element.21), channel_id=1, source_target_pairs={{0,4},{4,0},{1,5},{5,1},{2,6},{6,2},{3,7},{7,3},{8,12},{12,8},{9,1... | collective-permute-start | bytes 245768 | tf_op jit(solution)/shard_map/ppermute | solution.py:319
  8.6 3.4 %collective-permute-start.1 = (f32[10,4,128]{2,1,0:T(4,128)}, f32[10,4,128]{2,1,0:T(4,128)S(1)}, u32[]{:S(2)}, u32[]{:S(2)}) collective-permute-start(f32[10,4,128]{2,1,0:T(4,128)} %get-tuple-element.22), channel_id=1, source_target_pairs={{0,1},{1,2},{2,3},{4,5},{5,6},{6,7},{8,9},{9,10},{10,11},{12,13},{... | collective-permute-start | bytes 61448 | tf_op jit(solution)/shard_map/ppermute | solution.py:320
  12.0 1.3 %collective-permute-start.2 = (f32[10,4,128]{2,1,0:T(4,128)}, f32[10,4,128]{2,1,0:T(4,128)S(1)}, u32[]{:S(2)}, u32[]{:S(2)}) collective-permute-start(f32[10,4,128]{2,1,0:T(4,128)} %get-tuple-element.23), channel_id=1, source_target_pairs={{1,0},{2,1},{3,2},{5,4},{6,5},{7,6},{9,8},{10,9},{11,10},{13,12},{... | collective-permute-start | bytes 61448 | tf_op jit(solution)/shard_map/ppermute | solution.py:321
  13.5 3.3 %shard_map.123.res_ref = f32[10,64,128]{2,1,0:T(8,128)} custom-call(f32[1122]{0:T(1024)} %concatenate.15.mat_ref.wt_ref, f32[1122]{0:T(1024)} %concatenate.15.mat_ref.wt_ref, f32[10,64,128]{2,1,0:T(8,128)} %bitcast.83, f32[10,64,128]{2,1,0:T(8,128)} %bitcast.78, f32[6,64,128]{2,1,0:T(8,128)} %get-tuple-element.20.face_ref, f32[64,128]{1,0:T(8,128)} %bitcast.85, ...), custom_call_target="tpu_custom_call" | custom-call | tf_op jit(solution)/shard_map/pallas_call | solution.py:240
  19.2 2.2 %shard_map.124 = (f32[10,64,128]{2,1,0:T(8,128)}, f32[10,16,128]{2,1,0:T(8,128)}, f32[10,4,128]{2,1,0:T(4,128)}, f32[10,4,128]{2,1,0:T(4,128)}) custom-call(f32[1122]{0:T(1024)} %concatenate.15.mat_ref.wt_ref, f32[1122]{0:T(1024)} %concatenate.15.mat_ref.wt_ref, f32[10,64,128]{2,1,0:T(8,128)} %bitcast.84, f32[10,64,128]{2,1,0:T(8,128)} %shard_map.123.res_ref, ...), custom_call_target="tpu_custom_call" | custom-call | tf_op jit(solution)/shard_map/pallas_call | solution.py:252
  21.5 3.4 %collective-permute-start.4 = (f32[10,4,128]{2,1,0:T(4,128)}, f32[10,4,128]{2,1,0:T(4,128)S(1)}, u32[]{:S(2)}, u32[]{:S(2)}) collective-permute-start(f32[10,4,128]{2,1,0:T(4,128)} %get-tuple-element.26), channel_id=1, source_target_pairs={{0,1},{1,2},{2,3},{4,5},{5,6},{6,7},{8,9},{9,10},{10,11},{12,13},{... | collective-permute-start | bytes 61448 | tf_op jit(solution)/shard_map/ppermute | solution.py:320
  24.9 1.3 %collective-permute-start.5 = (f32[10,4,128]{2,1,0:T(4,128)}, f32[10,4,128]{2,1,0:T(4,128)S(1)}, u32[]{:S(2)}, u32[]{:S(2)}) collective-permute-start(f32[10,4,128]{2,1,0:T(4,128)} %get-tuple-element.27), channel_id=1, source_target_pairs={{1,0},{2,1},{3,2},{5,4},{6,5},{7,6},{9,8},{10,9},{11,10},{13,12},{... | collective-permute-start | bytes 61448 | tf_op jit(solution)/shard_map/ppermute | solution.py:321
  26.5 3.3 %shard_map.125.res_ref = f32[10,64,128]{2,1,0:T(8,128)} custom-call(f32[1122]{0:T(1024)} %concatenate.15.mat_ref.wt_ref, f32[1122]{0:T(1024)} %concatenate.15.mat_ref.wt_ref, f32[10,64,128]{2,1,0:T(8,128)} %get-tuple-element.24.psi_ref, f32[10,64,128]{2,1,0:T(8,128)} %bitcast.79, f32[6,64,128]{2,1,0:T(8,128)} %get-tuple-element.20.face_ref, ...), custom_call_target="tpu_custom_call" | custom-call | tf_op jit(solution)/shard_map/pallas_call | solution.py:240
  32.0 2.2 %shard_map.126 = (f32[10,64,128]{2,1,0:T(8,128)}, f32[10,16,128]{2,1,0:T(8,128)}, f32[10,4,128]{2,1,0:T(4,128)}, f32[10,4,128]{2,1,0:T(4,128)}) custom-call(f32[1122]{0:T(1024)} %concatenate.15.mat_ref.wt_ref, f32[1122]{0:T(1024)} %concatenate.15.mat_ref.wt_ref, f32[10,64,128]{2,1,0:T(8,128)} %get-tuple-element.24.psi_ref, ...), custom_call_target="tpu_custom_call" | custom-call | tf_op jit(solution)/shard_map/pallas_call | solution.py:252
  34.2 1.9 %collective-permute-start.6 = (f32[10,16,128]{2,1,0:T(8,128)}, f32[10,16,128]{2,1,0:T(8,128)S(1)}, u32[]{:S(2)}, u32[]{:S(2)}) collective-permute-start(f32[10,16,128]{2,1,0:T(8,128)} %get-tuple-element.29), channel_id=1, source_target_pairs={{0,4},{4,0},{1,5},{5,1},{2,6},{6,2},{3,7},{7,3},{8,12},{12,8},{9,1... | collective-permute-start | bytes 245768 | tf_op jit(solution)/shard_map/ppermute | solution.py:319
  36.1 3.5 %collective-permute-start.7 = (f32[10,4,128]{2,1,0:T(4,128)}, f32[10,4,128]{2,1,0:T(4,128)S(1)}, u32[]{:S(2)}, u32[]{:S(2)}) collective-permute-start(f32[10,4,128]{2,1,0:T(4,128)} %get-tuple-element.30), channel_id=1, source_target_pairs={{0,1},{1,2},{2,3},{4,5},{5,6},{6,7},{8,9},{9,10},{10,11},{12,13},{... | collective-permute-start | bytes 61448 | tf_op jit(solution)/shard_map/ppermute | solution.py:320
  39.7 1.3 %collective-permute-start.8 = (f32[10,4,128]{2,1,0:T(4,128)}, f32[10,4,128]{2,1,0:T(4,128)S(1)}, u32[]{:S(2)}, u32[]{:S(2)}) collective-permute-start(f32[10,4,128]{2,1,0:T(4,128)} %get-tuple-element.31), channel_id=1, source_target_pairs={{1,0},{2,1},{3,2},{5,4},{6,5},{7,6},{9,8},{10,9},{11,10},{13,12},{... | collective-permute-start | bytes 61448 | tf_op jit(solution)/shard_map/ppermute | solution.py:321
  41.0 3.3 %shard_map.127.res_ref = f32[10,64,128]{2,1,0:T(8,128)} custom-call(f32[1122]{0:T(1024)} %concatenate.15.mat_ref.wt_ref, f32[1122]{0:T(1024)} %concatenate.15.mat_ref.wt_ref, f32[10,64,128]{2,1,0:T(8,128)} %get-tuple-element.28.psi_ref, f32[10,64,128]{2,1,0:T(8,128)} %bitcast.80, f32[6,64,128]{2,1,0:T(8,128)} %get-tuple-element.20.face_ref, ...), custom_call_target="tpu_custom_call" | custom-call | tf_op jit(solution)/shard_map/pallas_call | solution.py:240
  44.3 1.3 %collective-permute-done.8.rahi_ref = f32[10,4,128]{2,1,0:T(4,128)S(1)} collective-permute-done((f32[10,4,128]{2,1,0:T(4,128)}, f32[10,4,128]{2,1,0:T(4,128)S(1)}, u32[]{:S(2)}, u32[]{:S(2)}) %collective-permute-start.8) | collective-permute-done | bytes 20512 | tf_op jit(solution)/shard_map/ppermute | solution.py:321
  46.8 2.2 %shard_map.128 = (f32[10,64,128]{2,1,0:T(8,128)}, f32[10,16,128]{2,1,0:T(8,128)}, f32[10,4,128]{2,1,0:T(4,128)}, f32[10,4,128]{2,1,0:T(4,128)}) custom-call(f32[1122]{0:T(1024)} %concatenate.15.mat_ref.wt_ref, f32[1122]{0:T(1024)} %concatenate.15.mat_ref.wt_ref, f32[10,64,128]{2,1,0:T(8,128)} %get-tuple-element.28.psi_ref, ...), custom_call_target="tpu_custom_call" | custom-call | tf_op jit(solution)/shard_map/pallas_call | solution.py:252
  49.1 3.4 %collective-permute-start.10 = (f32[10,4,128]{2,1,0:T(4,128)}, f32[10,4,128]{2,1,0:T(4,128)S(1)}, u32[]{:S(2)}, u32[]{:S(2)}) collective-permute-start(f32[10,4,128]{2,1,0:T(4,128)} %get-tuple-element.34), channel_id=1, source_target_pairs={{0,1},{1,2},{2,3},{4,5},{5,6},{6,7},{8,9},{9,10},{10,11},{12,13},{... | collective-permute-start | bytes 61448 | tf_op jit(solution)/shard_map/ppermute | solution.py:320
  52.5 1.5 %collective-permute-start.11 = (f32[10,4,128]{2,1,0:T(4,128)}, f32[10,4,128]{2,1,0:T(4,128)S(1)}, u32[]{:S(2)}, u32[]{:S(2)}) collective-permute-start(f32[10,4,128]{2,1,0:T(4,128)} %get-tuple-element.35), channel_id=1, source_target_pairs={{1,0},{2,1},{3,2},{5,4},{6,5},{7,6},{9,8},{10,9},{11,10},{13,12},{... | collective-permute-start | bytes 61448 | tf_op jit(solution)/shard_map/ppermute | solution.py:321
  54.0 3.3 %shard_map.129.res_ref = f32[10,64,128]{2,1,0:T(8,128)} custom-call(f32[1122]{0:T(1024)} %concatenate.15.mat_ref.wt_ref, f32[1122]{0:T(1024)} %concatenate.15.mat_ref.wt_ref, f32[10,64,128]{2,1,0:T(8,128)} %get-tuple-element.32.psi_ref, f32[10,64,128]{2,1,0:T(8,128)} %bitcast.81, f32[6,64,128]{2,1,0:T(8,128)} %get-tuple-element.20.face_ref, ...), custom_call_target="tpu_custom_call" | custom-call | tf_op jit(solution)/shard_map/pallas_call | solution.py:240
  59.6 2.0 %shard_map.130 = (f32[10,64,128]{2,1,0:T(8,128)}, f32[3,64,128]{2,1,0:T(8,128)}) custom-call(f32[1122]{0:T(1024)} %concatenate.15.mat_ref.wt_ref, f32[1122]{0:T(1024)} %concatenate.15.mat_ref.wt_ref, f32[10,64,128]{2,1,0:T(8,128)} %get-tuple-element.32.psi_ref, f32[10,64,128]{2,1,0:T(8,128)} %shard_map.129.res_ref, ...), custom_call_target="tpu_custom_call" | custom-call | tf_op jit(solution)/shard_map/pallas_call | solution.py:252
  61.7 4.2 %fusion.3 = f32[3,8192]{1,0:T(4,128)S(1)} fusion(f32[3,64,128]{2,1,0:T(8,128)} %get-tuple-element.37, s32[8192]{0:T(1024)S(1)} %add_select_fusion, pred[64,8192]{1,0:T(8,128)(4,1)S(1)} %iota_compare_fusion.1), kind=kOutput, calls=%fused_computation.5 | convolution fusion | flops 2420088832 | bytes 753664 | tf_op jit(solution)/shard_map/xl,lj->xj/dot_general | solution.py:341
  67.9 7.8 %all-to-all-start = ((f32[8,3,512]{2,1,0:T(4,128)}), f32[8,3,512]{2,1,0:T(4,128)S(1)}, u32[]{:S(2)}, u32[]{:S(2)}) async-start(f32[8,3,512]{2,1,0:T(4,128)} %select_add_fusion), calls=%async_computation | async-start | bytes 131072 | tf_op jit(solution)/shard_map/all_to_all | solution.py:42
  76.3 2.6 %shard_map.131 = f32[36,512]{1,0:T(8,128)} custom-call(s32[2,512]{1,0:T(2,128)} %pad_add_fusion.where_ref, bf16[2304,128]{1,0:T(8,128)(2,1)} %bitcast.93), custom_call_target="tpu_custom_call" | custom-call | tf_op jit(solution)/shard_map/pallas_call | solution.py:353
  79.8 3.8 %all-to-all-done = f32[8,3,512]{2,1,0:T(4,128)S(1)} async-done(((f32[8,3,512]{2,1,0:T(4,128)}), f32[8,3,512]{2,1,0:T(4,128)S(1)}, u32[]{:S(2)}, u32[]{:S(2)}) %all-to-all-start) | async-done | bytes 49184 | tf_op jit(solution)/shard_map/all_to_all | solution.py:42
  (68 shorter events, 15.6 us)
Async XLA Ops:
  0.6 3.3 %copy-start.13 = (f32[3,10]{1,0:T(4,128)S(1)}, f32[3,10]{1,0:T(4,128)}, u32[]{:S(2)}) copy-start(f32[3,10]{1,0:T(4,128)} %param.17) | copy-start | bytes 364
  1.9 11.5 %copy-start = (s32[1,1,8192]{2,1,0:T(1,128)S(1)}, s32[1,1,8192]{2,1,0:T(1,128)}, u32[]{:S(2)}) copy-start(s32[1,1,8192]{2,1,0:T(1,128)} %param.21) | copy-start | bytes 98308
  6.6 11.3 %collective-permute-start = (f32[10,16,128]{2,1,0:T(8,128)}, f32[10,16,128]{2,1,0:T(8,128)S(1)}, u32[]{:S(2)}, u32[]{:S(2)}) collective-permute-start(f32[10,16,128]{2,1,0:T(8,128)} %get-tuple-element.21), channel_id=1, source_target_pairs={{0,4},{4,0},{1,5},{5,1},{2,6},{6,2},{3,7},{7,3},{8,12},{12,8},{9,1... | collective-permute-start | bytes 245768 | tf_op jit(solution)/shard_map/ppermute | solution.py:319
  8.6 8.2 %collective-permute-start.1 = (f32[10,4,128]{2,1,0:T(4,128)}, f32[10,4,128]{2,1,0:T(4,128)S(1)}, u32[]{:S(2)}, u32[]{:S(2)}) collective-permute-start(f32[10,4,128]{2,1,0:T(4,128)} %get-tuple-element.22), channel_id=1, source_target_pairs={{0,1},{1,2},{2,3},{4,5},{5,6},{6,7},{8,9},{9,10},{10,11},{12,13},{... | collective-permute-start | bytes 61448 | tf_op jit(solution)/shard_map/ppermute | solution.py:320
  12.0 5.9 %collective-permute-start.2 = (f32[10,4,128]{2,1,0:T(4,128)}, f32[10,4,128]{2,1,0:T(4,128)S(1)}, u32[]{:S(2)}, u32[]{:S(2)}) collective-permute-start(f32[10,4,128]{2,1,0:T(4,128)} %get-tuple-element.23), channel_id=1, source_target_pairs={{1,0},{2,1},{3,2},{5,4},{6,5},{7,6},{9,8},{10,9},{11,10},{13,12},{... | collective-permute-start | bytes 61448 | tf_op jit(solution)/shard_map/ppermute | solution.py:321
  16.8 1.1 %copy-start.10 = (f32[10,4,128]{2,1,0:T(4,128)}, f32[10,4,128]{2,1,0:T(4,128)S(1)}, u32[]{:S(2)}) copy-start(f32[10,4,128]{2,1,0:T(4,128)S(1)} %collective-permute-done.1.ralo_ref) | copy-start | bytes 61444
  18.5 0.6 copy-start.4
  21.4 9.4 %collective-permute-start.3 = (f32[10,16,128]{2,1,0:T(8,128)}, f32[10,16,128]{2,1,0:T(8,128)S(1)}, u32[]{:S(2)}, u32[]{:S(2)}) collective-permute-start(f32[10,16,128]{2,1,0:T(8,128)} %get-tuple-element.25), channel_id=1, source_target_pairs={{0,4},{4,0},{1,5},{5,1},{2,6},{6,2},{3,7},{7,3},{8,12},{12,8},{9,1... | collective-permute-start | bytes 245768 | tf_op jit(solution)/shard_map/ppermute | solution.py:319
  21.5 8.3 %collective-permute-start.4 = (f32[10,4,128]{2,1,0:T(4,128)}, f32[10,4,128]{2,1,0:T(4,128)S(1)}, u32[]{:S(2)}, u32[]{:S(2)}) collective-permute-start(f32[10,4,128]{2,1,0:T(4,128)} %get-tuple-element.26), channel_id=1, source_target_pairs={{0,1},{1,2},{2,3},{4,5},{5,6},{6,7},{8,9},{9,10},{10,11},{12,13},{... | collective-permute-start | bytes 61448 | tf_op jit(solution)/shard_map/ppermute | solution.py:320
  24.9 5.9 %collective-permute-start.5 = (f32[10,4,128]{2,1,0:T(4,128)}, f32[10,4,128]{2,1,0:T(4,128)S(1)}, u32[]{:S(2)}, u32[]{:S(2)}) collective-permute-start(f32[10,4,128]{2,1,0:T(4,128)} %get-tuple-element.27), channel_id=1, source_target_pairs={{1,0},{2,1},{3,2},{5,4},{6,5},{7,6},{9,8},{10,9},{11,10},{13,12},{... | collective-permute-start | bytes 61448 | tf_op jit(solution)/shard_map/ppermute | solution.py:321
  29.8 1.0 %copy-start.9 = (f32[10,4,128]{2,1,0:T(4,128)}, f32[10,4,128]{2,1,0:T(4,128)S(1)}, u32[]{:S(2)}) copy-start(f32[10,4,128]{2,1,0:T(4,128)S(1)} %collective-permute-done.4.ralo_ref) | copy-start | bytes 61444
  31.4 0.6 copy-start.3
  34.2 11.4 %collective-permute-start.6 = (f32[10,16,128]{2,1,0:T(8,128)}, f32[10,16,128]{2,1,0:T(8,128)S(1)}, u32[]{:S(2)}, u32[]{:S(2)}) collective-permute-start(f32[10,16,128]{2,1,0:T(8,128)} %get-tuple-element.29), channel_id=1, source_target_pairs={{0,4},{4,0},{1,5},{5,1},{2,6},{6,2},{3,7},{7,3},{8,12},{12,8},{9,1... | collective-permute-start | bytes 245768 | tf_op jit(solution)/shard_map/ppermute | solution.py:319
  36.1 8.2 %collective-permute-start.7 = (f32[10,4,128]{2,1,0:T(4,128)}, f32[10,4,128]{2,1,0:T(4,128)S(1)}, u32[]{:S(2)}, u32[]{:S(2)}) collective-permute-start(f32[10,4,128]{2,1,0:T(4,128)} %get-tuple-element.30), channel_id=1, source_target_pairs={{0,1},{1,2},{2,3},{4,5},{5,6},{6,7},{8,9},{9,10},{10,11},{12,13},{... | collective-permute-start | bytes 61448 | tf_op jit(solution)/shard_map/ppermute | solution.py:320
  39.7 5.9 %collective-permute-start.8 = (f32[10,4,128]{2,1,0:T(4,128)}, f32[10,4,128]{2,1,0:T(4,128)S(1)}, u32[]{:S(2)}, u32[]{:S(2)}) collective-permute-start(f32[10,4,128]{2,1,0:T(4,128)} %get-tuple-element.31), channel_id=1, source_target_pairs={{1,0},{2,1},{3,2},{5,4},{6,5},{7,6},{9,8},{10,9},{11,10},{13,12},{... | collective-permute-start | bytes 61448 | tf_op jit(solution)/shard_map/ppermute | solution.py:321
  44.3 1.3 %copy-start.7 = (f32[10,4,128]{2,1,0:T(4,128)}, f32[10,4,128]{2,1,0:T(4,128)S(1)}, u32[]{:S(2)}) copy-start(f32[10,4,128]{2,1,0:T(4,128)S(1)} %collective-permute-done.7.ralo_ref) | copy-start | bytes 61444
  46.2 0.6 copy-start.2
  49.0 9.4 %collective-permute-start.9 = (f32[10,16,128]{2,1,0:T(8,128)}, f32[10,16,128]{2,1,0:T(8,128)S(1)}, u32[]{:S(2)}, u32[]{:S(2)}) collective-permute-start(f32[10,16,128]{2,1,0:T(8,128)} %get-tuple-element.33), channel_id=1, source_target_pairs={{0,4},{4,0},{1,5},{5,1},{2,6},{6,2},{3,7},{7,3},{8,12},{12,8},{9,1... | collective-permute-start | bytes 245768 | tf_op jit(solution)/shard_map/ppermute | solution.py:319
  49.1 8.2 %collective-permute-start.10 = (f32[10,4,128]{2,1,0:T(4,128)}, f32[10,4,128]{2,1,0:T(4,128)S(1)}, u32[]{:S(2)}, u32[]{:S(2)}) collective-permute-start(f32[10,4,128]{2,1,0:T(4,128)} %get-tuple-element.34), channel_id=1, source_target_pairs={{0,1},{1,2},{2,3},{4,5},{5,6},{6,7},{8,9},{9,10},{10,11},{12,13},{... | collective-permute-start | bytes 61448 | tf_op jit(solution)/shard_map/ppermute | solution.py:320
  52.5 5.9 %collective-permute-start.11 = (f32[10,4,128]{2,1,0:T(4,128)}, f32[10,4,128]{2,1,0:T(4,128)S(1)}, u32[]{:S(2)}, u32[]{:S(2)}) collective-permute-start(f32[10,4,128]{2,1,0:T(4,128)} %get-tuple-element.35), channel_id=1, source_target_pairs={{1,0},{2,1},{3,2},{5,4},{6,5},{7,6},{9,8},{10,9},{11,10},{13,12},{... | collective-permute-start | bytes 61448 | tf_op jit(solution)/shard_map/ppermute | solution.py:321
  57.4 1.1 %copy-start.5 = (f32[10,4,128]{2,1,0:T(4,128)}, f32[10,4,128]{2,1,0:T(4,128)S(1)}, u32[]{:S(2)}) copy-start(f32[10,4,128]{2,1,0:T(4,128)S(1)} %collective-permute-done.10.ralo_ref) | copy-start | bytes 61444
  59.0 0.6 copy-start.1
  65.9 1.3 %collective-permute-start.12 = (f32[8,3,512]{2,1,0:T(4,128)S(1)}, f32[8,3,512]{2,1,0:T(4,128)S(1)}, u32[]{:S(2)}, u32[]{:S(2)}) collective-permute-start(f32[8,3,512]{2,1,0:T(4,128)S(1)} %slice_select_fusion), channel_id=1, source_target_pairs={{0,8},{8,0},{16,24},{24,16},{32,40},{40,32},{48,56},{56,48},{64,72... | collective-permute-start | bytes 147464 | tf_op jit(solution)/shard_map/ppermute | solution.py:40
  67.9 15.6 %all-to-all-start = ((f32[8,3,512]{2,1,0:T(4,128)}), f32[8,3,512]{2,1,0:T(4,128)S(1)}, u32[]{:S(2)}, u32[]{:S(2)}) async-start(f32[8,3,512]{2,1,0:T(4,128)} %select_add_fusion), calls=%async_computation | async-start | bytes 131072 | tf_op jit(solution)/shard_map/all_to_all | solution.py:42
  (4 other events, 2.4 us)

commit v10 on v9

--- a/solution.py
+++ b/solution.py
@@ -163,7 +163,7 @@
 
 
 def fixup_kernel(
-    mat_ref, wt_ref, psi_ref, res_ref, face_ref, diag_ref, axr_ref, ralo_ref, rahi_ref,
+    mat_ref, wt_ref, metric_ref, psi_ref, res_ref, face_ref, diag_ref, axr_ref, ralo_ref, rahi_ref,
     out_ref, axs_ref, *radial_refs, tile_r, edges, dims,
 ):
     comps, rows, lanes = psi_ref.shape
@@ -190,9 +190,9 @@
         write_edges(mat_ref, wt_ref, out_ref, face_ref, axs_ref, *radial_refs, comps, tile_r)
     else:
         for d in range(dims):
-            height = wt_ref[6 * comps * comps + METRIC + d * comps] * out_ref[0]
+            height = metric_ref[d * comps] * out_ref[0]
             for c in range(1, comps):
-                height = height + wt_ref[6 * comps * comps + METRIC + d * comps + c] * out_ref[c]
+                height = height + metric_ref[d * comps + c] * out_ref[c]
             axs_ref[d] = wt_ref[6 * comps * comps + METRIC - 1] * height
 
 
@@ -246,15 +246,15 @@
     )(mat, weights, psi, src, face, diag, pick)
 
 
-def run_fixup(mat, weights, psi, res, face, diag, axr, ralo, rahi, tile_r, edges, dims):
+def run_fixup(mat, weights, metric_flat, psi, res, face, diag, axr, ralo, rahi, tile_r, edges, dims):
     comps, rows, lanes = psi.shape
     tail = edge_shapes(comps, rows, tile_r) if edges else (jax.ShapeDtypeStruct((dims, rows, lanes), jnp.float32),)
     return pl.pallas_call(
         functools.partial(fixup_kernel, tile_r=tile_r, edges=edges, dims=dims),
         out_shape=(jax.ShapeDtypeStruct(psi.shape, jnp.float32),) + tail,
-        in_specs=[smem_spec(), smem_spec()] + [vmem_spec() for _ in range(7)],
+        in_specs=[smem_spec(), smem_spec(), smem_spec()] + [vmem_spec() for _ in range(7)],
         out_specs=tuple(vmem_spec() for _ in range(1 + len(tail))),
-    )(mat, weights, psi, res, face, diag, axr, ralo, rahi)
+    )(mat, weights, metric_flat, psi, res, face, diag, axr, ralo, rahi)
 
 
 def neighbours(axis):
@@ -299,7 +299,8 @@
             phase_weight[0],
         ]
     ).astype(jnp.float32)
-    weights = jnp.concatenate([scalars, metric.reshape(-1)])
+    weights = scalars
+    metric_flat = metric.reshape(-1)
     real_t = jnp.swapaxes(flux_jac[:, 0], 1, 2)
     imag_t = jnp.swapaxes(flux_jac[:, 1], 1, 2)
     gauss = jnp.stack([real_t, imag_t - real_t, real_t + imag_t], axis=1).reshape(-1)
@@ -322,11 +323,11 @@
         res = run_interior(mat, weights, psi, src, faces, diag, pick, tile_r)
         if section < ITERS - 1:
             psi, axs, q2, q3 = run_fixup(
-                mat, weights, psi, res, faces, diag, axr, ralo, rahi, tile_r, True, dims
+                mat, weights, metric_flat, psi, res, faces, diag, axr, ralo, rahi, tile_r, True, dims
             )
         else:
             psi, weighted = run_fixup(
-                mat, weights, psi, res, faces, diag, axr, ralo, rahi, tile_r, False, dims
+                mat, weights, metric_flat, psi, res, faces, diag, axr, ralo, rahi, tile_r, False, dims
             )
     psi_out = psi.reshape(psi_start.shape)
     order = owner_order[0, 0]

time: 85 us -> 85.5 us (level)
  transfers between devices with their start and end apart: 14 -> 14, of which waited for: 6 -> 6; matrix products, arithmetic and copies ran while one was open for 2% -> 3% of each run, Pallas kernels for 19% -> 19%
where the time goes in v10:
time: 85.5 us; the launch traced here: 84.8 us
  starting transfers between devices  31.8 us (37%)
  Pallas kernels  26.3 us (31%)
  local copies, waits for them, and re-layouts  8.86 us (10%)
  waiting for transfers between devices  8.81 us (10%)
  matrix products  4.2 us (5%)
  other arithmetic  2.55 us (3%)
  between operations  2.33 us (3%)
    ppermute x4, starting transfers between devices, body(): ralo = lax.ppermute(q2, 'radial', up_r)  14.4 us
    pallas_call x4, Pallas kernels, run_interior(): pl.pallas_call(functools.partial(interior_kernel, tile_r=tile_r), out_sha...  13.2 us
    pallas_call x4, Pallas kernels, run_fixup(): pl.pallas_call(functools.partial(fixup_kernel, tile_r=tile_r, edges=edges...  8.62 us
    all_to_all x1, starting transfers between devices, sum_at_owner_paired(): lax.all_to_all(keep + got, axis, 0, 0, tiled=True, axis_index_groups=groups)  7.78 us
    ppermute x4, starting transfers between devices, body(): rahi = lax.ppermute(q3, 'radial', down_r)  5.35 us
    unnamed x30, local copies, waits for them, and re-layouts  5.15 us
    dot_general x1, matrix products, body(): jnp.einsum('xl,lj->xj', weighted.reshape(dims * blocks, lanes), pick_lane...  4.2 us
    ppermute x4, starting transfers between devices, body(): axr = lax.ppermute(axs, 'axial', [(0, 1), (1, 0)])  4.16 us
  transfers between devices with their start and end apart: 14, of which 6 were waited for; matrix products, arithmetic and copies ran while one was open for 3% of the time, Pallas kernels for 19%

profile of v10, /device:TPU:0, one launch (start us, length us, event | category | flops | bytes accessed | tf_op | source)
XLA Modules:
  0.0 84.8 jit_solution(15595088671026827446)
XLA Ops:
  4.6 1.9 %shard_map.122 = (f32[10,16,128]{2,1,0:T(8,128)}, f32[10,4,128]{2,1,0:T(4,128)}, f32[10,4,128]{2,1,0:T(4,128)}, f32[6,64,128]{2,1,0:T(8,128)}) custom-call(f32[1122]{0:T(1024)} %concatenate.15.mat_ref.wt_ref, f32[1122]{0:T(1024)} %concatenate.15.mat_ref.wt_ref, f32[10,64,128]{2,1,0:T(8,128)} %bitcast.82, bf16[6,64,128]{2,1,0:T(8,128)(2,1)} %bitcast.101), custom_call_target="tpu_custom_call" | custom-call | tf_op jit(solution)/shard_map/pallas_call | solution.py:230
  6.5 2.0 %collective-permute-start = (f32[10,16,128]{2,1,0:T(8,128)}, f32[10,16,128]{2,1,0:T(8,128)S(1)}, u32[]{:S(2)}, u32[]{:S(2)}) collective-permute-start(f32[10,16,128]{2,1,0:T(8,128)} %get-tuple-element.21), channel_id=1, source_target_pairs={{0,4},{4,0},{1,5},{5,1},{2,6},{6,2},{3,7},{7,3},{8,12},{12,8},{9,1... | collective-permute-start | bytes 245768 | tf_op jit(solution)/shard_map/ppermute | solution.py:320
  8.6 3.4 %collective-permute-start.1 = (f32[10,4,128]{2,1,0:T(4,128)}, f32[10,4,128]{2,1,0:T(4,128)S(1)}, u32[]{:S(2)}, u32[]{:S(2)}) collective-permute-start(f32[10,4,128]{2,1,0:T(4,128)} %get-tuple-element.22), channel_id=1, source_target_pairs={{0,1},{1,2},{2,3},{4,5},{5,6},{6,7},{8,9},{9,10},{10,11},{12,13},{... | collective-permute-start | bytes 61448 | tf_op jit(solution)/shard_map/ppermute | solution.py:321
  12.0 1.3 %collective-permute-start.2 = (f32[10,4,128]{2,1,0:T(4,128)}, f32[10,4,128]{2,1,0:T(4,128)S(1)}, u32[]{:S(2)}, u32[]{:S(2)}) collective-permute-start(f32[10,4,128]{2,1,0:T(4,128)} %get-tuple-element.23), channel_id=1, source_target_pairs={{1,0},{2,1},{3,2},{5,4},{6,5},{7,6},{9,8},{10,9},{11,10},{13,12},{... | collective-permute-start | bytes 61448 | tf_op jit(solution)/shard_map/ppermute | solution.py:322
  14.0 3.3 %shard_map.123.res_ref = f32[10,64,128]{2,1,0:T(8,128)} custom-call(f32[1122]{0:T(1024)} %concatenate.15.mat_ref.wt_ref, f32[1122]{0:T(1024)} %concatenate.15.mat_ref.wt_ref, f32[10,64,128]{2,1,0:T(8,128)} %bitcast.83, f32[10,64,128]{2,1,0:T(8,128)} %bitcast.78, f32[6,64,128]{2,1,0:T(8,128)} %get-tuple-element.20.face_ref, f32[64,128]{1,0:T(8,128)} %bitcast.85, ...), custom_call_target="tpu_custom_call" | custom-call | tf_op jit(solution)/shard_map/pallas_call | solution.py:240
  19.1 2.2 %shard_map.124 = (f32[10,64,128]{2,1,0:T(8,128)}, f32[10,16,128]{2,1,0:T(8,128)}, f32[10,4,128]{2,1,0:T(4,128)}, f32[10,4,128]{2,1,0:T(4,128)}) custom-call(f32[1122]{0:T(1024)} %concatenate.15.mat_ref.wt_ref, f32[1122]{0:T(1024)} %concatenate.15.mat_ref.wt_ref, f32[30]{0:T(128)} %reshape.303.metric_ref, f32[10,64,128]{2,1,0:T(8,128)} %bitcast.84, ...), custom_call_target="tpu_custom_call" | custom-call | tf_op jit(solution)/shard_map/pallas_call | solution.py:252
  21.4 4.0 %collective-permute-start.4 = (f32[10,4,128]{2,1,0:T(4,128)}, f32[10,4,128]{2,1,0:T(4,128)S(1)}, u32[]{:S(2)}, u32[]{:S(2)}) collective-permute-start(f32[10,4,128]{2,1,0:T(4,128)} %get-tuple-element.26), channel_id=1, source_target_pairs={{0,1},{1,2},{2,3},{4,5},{5,6},{6,7},{8,9},{9,10},{10,11},{12,13},{... | collective-permute-start | bytes 61448 | tf_op jit(solution)/shard_map/ppermute | solution.py:321
  25.4 1.3 %collective-permute-start.5 = (f32[10,4,128]{2,1,0:T(4,128)}, f32[10,4,128]{2,1,0:T(4,128)S(1)}, u32[]{:S(2)}, u32[]{:S(2)}) collective-permute-start(f32[10,4,128]{2,1,0:T(4,128)} %get-tuple-element.27), channel_id=1, source_target_pairs={{1,0},{2,1},{3,2},{5,4},{6,5},{7,6},{9,8},{10,9},{11,10},{13,12},{... | collective-permute-start | bytes 61448 | tf_op jit(solution)/shard_map/ppermute | solution.py:322
  27.0 3.3 %shard_map.125.res_ref = f32[10,64,128]{2,1,0:T(8,128)} custom-call(f32[1122]{0:T(1024)} %concatenate.15.mat_ref.wt_ref, f32[1122]{0:T(1024)} %concatenate.15.mat_ref.wt_ref, f32[10,64,128]{2,1,0:T(8,128)} %get-tuple-element.24.psi_ref, f32[10,64,128]{2,1,0:T(8,128)} %bitcast.79, f32[6,64,128]{2,1,0:T(8,128)} %get-tuple-element.20.face_ref, ...), custom_call_target="tpu_custom_call" | custom-call | tf_op jit(solution)/shard_map/pallas_call | solution.py:240
  32.5 2.2 %shard_map.126 = (f32[10,64,128]{2,1,0:T(8,128)}, f32[10,16,128]{2,1,0:T(8,128)}, f32[10,4,128]{2,1,0:T(4,128)}, f32[10,4,128]{2,1,0:T(4,128)}) custom-call(f32[1122]{0:T(1024)} %concatenate.15.mat_ref.wt_ref, f32[1122]{0:T(1024)} %concatenate.15.mat_ref.wt_ref, f32[30]{0:T(128)} %reshape.303.metric_ref, f32[10,64,128]{2,1,0:T(8,128)} %get-tuple-element.24.psi_ref, ...), custom_call_target="tpu_custom_call" | custom-call | tf_op jit(solution)/shard_map/pallas_call | solution.py:252
  34.7 1.9 %collective-permute-start.6 = (f32[10,16,128]{2,1,0:T(8,128)}, f32[10,16,128]{2,1,0:T(8,128)S(1)}, u32[]{:S(2)}, u32[]{:S(2)}) collective-permute-start(f32[10,16,128]{2,1,0:T(8,128)} %get-tuple-element.29), channel_id=1, source_target_pairs={{0,4},{4,0},{1,5},{5,1},{2,6},{6,2},{3,7},{7,3},{8,12},{12,8},{9,1... | collective-permute-start | bytes 245768 | tf_op jit(solution)/shard_map/ppermute | solution.py:320
  36.7 3.5 %collective-permute-start.7 = (f32[10,4,128]{2,1,0:T(4,128)}, f32[10,4,128]{2,1,0:T(4,128)S(1)}, u32[]{:S(2)}, u32[]{:S(2)}) collective-permute-start(f32[10,4,128]{2,1,0:T(4,128)} %get-tuple-element.30), channel_id=1, source_target_pairs={{0,1},{1,2},{2,3},{4,5},{5,6},{6,7},{8,9},{9,10},{10,11},{12,13},{... | collective-permute-start | bytes 61448 | tf_op jit(solution)/shard_map/ppermute | solution.py:321
  40.2 1.3 %collective-permute-start.8 = (f32[10,4,128]{2,1,0:T(4,128)}, f32[10,4,128]{2,1,0:T(4,128)S(1)}, u32[]{:S(2)}, u32[]{:S(2)}) collective-permute-start(f32[10,4,128]{2,1,0:T(4,128)} %get-tuple-element.31), channel_id=1, source_target_pairs={{1,0},{2,1},{3,2},{5,4},{6,5},{7,6},{9,8},{10,9},{11,10},{13,12},{... | collective-permute-start | bytes 61448 | tf_op jit(solution)/shard_map/ppermute | solution.py:322
  41.5 3.3 %shard_map.127.res_ref = f32[10,64,128]{2,1,0:T(8,128)} custom-call(f32[1122]{0:T(1024)} %concatenate.15.mat_ref.wt_ref, f32[1122]{0:T(1024)} %concatenate.15.mat_ref.wt_ref, f32[10,64,128]{2,1,0:T(8,128)} %get-tuple-element.28.psi_ref, f32[10,64,128]{2,1,0:T(8,128)} %bitcast.80, f32[6,64,128]{2,1,0:T(8,128)} %get-tuple-element.20.face_ref, ...), custom_call_target="tpu_custom_call" | custom-call | tf_op jit(solution)/shard_map/pallas_call | solution.py:240
  44.8 1.3 %collective-permute-done.8.rahi_ref = f32[10,4,128]{2,1,0:T(4,128)S(1)} collective-permute-done((f32[10,4,128]{2,1,0:T(4,128)}, f32[10,4,128]{2,1,0:T(4,128)S(1)}, u32[]{:S(2)}, u32[]{:S(2)}) %collective-permute-start.8) | collective-permute-done | bytes 20512 | tf_op jit(solution)/shard_map/ppermute | solution.py:322
  47.3 2.2 %shard_map.128 = (f32[10,64,128]{2,1,0:T(8,128)}, f32[10,16,128]{2,1,0:T(8,128)}, f32[10,4,128]{2,1,0:T(4,128)}, f32[10,4,128]{2,1,0:T(4,128)}) custom-call(f32[1122]{0:T(1024)} %concatenate.15.mat_ref.wt_ref, f32[1122]{0:T(1024)} %concatenate.15.mat_ref.wt_ref, f32[30]{0:T(128)} %reshape.303.metric_ref, f32[10,64,128]{2,1,0:T(8,128)} %get-tuple-element.28.psi_ref, ...), custom_call_target="tpu_custom_call" | custom-call | tf_op jit(solution)/shard_map/pallas_call | solution.py:252
  49.7 3.4 %collective-permute-start.10 = (f32[10,4,128]{2,1,0:T(4,128)}, f32[10,4,128]{2,1,0:T(4,128)S(1)}, u32[]{:S(2)}, u32[]{:S(2)}) collective-permute-start(f32[10,4,128]{2,1,0:T(4,128)} %get-tuple-element.34), channel_id=1, source_target_pairs={{0,1},{1,2},{2,3},{4,5},{5,6},{6,7},{8,9},{9,10},{10,11},{12,13},{... | collective-permute-start | bytes 61448 | tf_op jit(solution)/shard_map/ppermute | solution.py:321
  53.1 1.5 %collective-permute-start.11 = (f32[10,4,128]{2,1,0:T(4,128)}, f32[10,4,128]{2,1,0:T(4,128)S(1)}, u32[]{:S(2)}, u32[]{:S(2)}) collective-permute-start(f32[10,4,128]{2,1,0:T(4,128)} %get-tuple-element.35), channel_id=1, source_target_pairs={{1,0},{2,1},{3,2},{5,4},{6,5},{7,6},{9,8},{10,9},{11,10},{13,12},{... | collective-permute-start | bytes 61448 | tf_op jit(solution)/shard_map/ppermute | solution.py:322
  54.6 3.3 %shard_map.129.res_ref = f32[10,64,128]{2,1,0:T(8,128)} custom-call(f32[1122]{0:T(1024)} %concatenate.15.mat_ref.wt_ref, f32[1122]{0:T(1024)} %concatenate.15.mat_ref.wt_ref, f32[10,64,128]{2,1,0:T(8,128)} %get-tuple-element.32.psi_ref, f32[10,64,128]{2,1,0:T(8,128)} %bitcast.81, f32[6,64,128]{2,1,0:T(8,128)} %get-tuple-element.20.face_ref, ...), custom_call_target="tpu_custom_call" | custom-call | tf_op jit(solution)/shard_map/pallas_call | solution.py:240
  60.2 2.0 %shard_map.130 = (f32[10,64,128]{2,1,0:T(8,128)}, f32[3,64,128]{2,1,0:T(8,128)}) custom-call(f32[1122]{0:T(1024)} %concatenate.15.mat_ref.wt_ref, f32[1122]{0:T(1024)} %concatenate.15.mat_ref.wt_ref, f32[30]{0:T(128)} %reshape.303.metric_ref, f32[10,64,128]{2,1,0:T(8,128)} %get-tuple-element.32.psi_ref, f32[10,64,128]{2,1,0:T(8,128)} %shard_map.129.res_ref, ...), custom_call_target="tpu_custom_call" | custom-call | tf_op jit(solution)/shard_map/pallas_call | solution.py:252
  62.2 4.2 %fusion.3 = f32[3,8192]{1,0:T(4,128)S(1)} fusion(f32[3,64,128]{2,1,0:T(8,128)} %get-tuple-element.37, s32[8192]{0:T(1024)S(1)} %add_select_fusion, pred[64,8192]{1,0:T(8,128)(4,1)S(1)} %iota_compare_fusion.1), kind=kOutput, calls=%fused_computation.5 | convolution fusion | flops 2420088832 | bytes 753664 | tf_op jit(solution)/shard_map/xl,lj->xj/dot_general | solution.py:342
  68.4 7.8 %all-to-all-start = ((f32[8,3,512]{2,1,0:T(4,128)}), f32[8,3,512]{2,1,0:T(4,128)S(1)}, u32[]{:S(2)}, u32[]{:S(2)}) async-start(f32[8,3,512]{2,1,0:T(4,128)} %select_add_fusion), calls=%async_computation | async-start | bytes 131072 | tf_op jit(solution)/shard_map/all_to_all | solution.py:42
  76.8 2.6 %shard_map.131 = f32[36,512]{1,0:T(8,128)} custom-call(s32[2,512]{1,0:T(2,128)} %pad_add_fusion.where_ref, bf16[2304,128]{1,0:T(8,128)(2,1)} %bitcast.93), custom_call_target="tpu_custom_call" | custom-call | tf_op jit(solution)/shard_map/pallas_call | solution.py:354
  80.3 3.8 %all-to-all-done = f32[8,3,512]{2,1,0:T(4,128)S(1)} async-done(((f32[8,3,512]{2,1,0:T(4,128)}), f32[8,3,512]{2,1,0:T(4,128)S(1)}, u32[]{:S(2)}, u32[]{:S(2)}) %all-to-all-start) | async-done | bytes 49184 | tf_op jit(solution)/shard_map/all_to_all | solution.py:42
  (68 shorter events, 15.5 us)
Async XLA Ops:
  1.9 11.4 %copy-start = (s32[1,1,8192]{2,1,0:T(1,128)S(1)}, s32[1,1,8192]{2,1,0:T(1,128)}, u32[]{:S(2)}) copy-start(s32[1,1,8192]{2,1,0:T(1,128)} %param.21) | copy-start | bytes 98308
  1.9 11.5 %copy-start.13 = (f32[3,10]{1,0:T(4,128)S(1)}, f32[3,10]{1,0:T(4,128)}, u32[]{:S(2)}) copy-start(f32[3,10]{1,0:T(4,128)} %param.17) | copy-start | bytes 364
  6.5 11.3 %collective-permute-start = (f32[10,16,128]{2,1,0:T(8,128)}, f32[10,16,128]{2,1,0:T(8,128)S(1)}, u32[]{:S(2)}, u32[]{:S(2)}) collective-permute-start(f32[10,16,128]{2,1,0:T(8,128)} %get-tuple-element.21), channel_id=1, source_target_pairs={{0,4},{4,0},{1,5},{5,1},{2,6},{6,2},{3,7},{7,3},{8,12},{12,8},{9,1... | collective-permute-start | bytes 245768 | tf_op jit(solution)/shard_map/ppermute | solution.py:320
  8.6 8.8 %collective-permute-start.1 = (f32[10,4,128]{2,1,0:T(4,128)}, f32[10,4,128]{2,1,0:T(4,128)S(1)}, u32[]{:S(2)}, u32[]{:S(2)}) collective-permute-start(f32[10,4,128]{2,1,0:T(4,128)} %get-tuple-element.22), channel_id=1, source_target_pairs={{0,1},{1,2},{2,3},{4,5},{5,6},{6,7},{8,9},{9,10},{10,11},{12,13},{... | collective-permute-start | bytes 61448 | tf_op jit(solution)/shard_map/ppermute | solution.py:321
  12.0 5.9 %collective-permute-start.2 = (f32[10,4,128]{2,1,0:T(4,128)}, f32[10,4,128]{2,1,0:T(4,128)S(1)}, u32[]{:S(2)}, u32[]{:S(2)}) collective-permute-start(f32[10,4,128]{2,1,0:T(4,128)} %get-tuple-element.23), channel_id=1, source_target_pairs={{1,0},{2,1},{3,2},{5,4},{6,5},{7,6},{9,8},{10,9},{11,10},{13,12},{... | collective-permute-start | bytes 61448 | tf_op jit(solution)/shard_map/ppermute | solution.py:322
  17.3 0.6 copy-start.10
  18.4 0.6 copy-start.4
  21.3 10.1 %collective-permute-start.3 = (f32[10,16,128]{2,1,0:T(8,128)}, f32[10,16,128]{2,1,0:T(8,128)S(1)}, u32[]{:S(2)}, u32[]{:S(2)}) collective-permute-start(f32[10,16,128]{2,1,0:T(8,128)} %get-tuple-element.25), channel_id=1, source_target_pairs={{0,4},{4,0},{1,5},{5,1},{2,6},{6,2},{3,7},{7,3},{8,12},{12,8},{9,1... | collective-permute-start | bytes 245768 | tf_op jit(solution)/shard_map/ppermute | solution.py:320
  21.4 8.9 %collective-permute-start.4 = (f32[10,4,128]{2,1,0:T(4,128)}, f32[10,4,128]{2,1,0:T(4,128)S(1)}, u32[]{:S(2)}, u32[]{:S(2)}) collective-permute-start(f32[10,4,128]{2,1,0:T(4,128)} %get-tuple-element.26), channel_id=1, source_target_pairs={{0,1},{1,2},{2,3},{4,5},{5,6},{6,7},{8,9},{9,10},{10,11},{12,13},{... | collective-permute-start | bytes 61448 | tf_op jit(solution)/shard_map/ppermute | solution.py:321
  25.4 5.9 %collective-permute-start.5 = (f32[10,4,128]{2,1,0:T(4,128)}, f32[10,4,128]{2,1,0:T(4,128)S(1)}, u32[]{:S(2)}, u32[]{:S(2)}) collective-permute-start(f32[10,4,128]{2,1,0:T(4,128)} %get-tuple-element.27), channel_id=1, source_target_pairs={{1,0},{2,1},{3,2},{5,4},{6,5},{7,6},{9,8},{10,9},{11,10},{13,12},{... | collective-permute-start | bytes 61448 | tf_op jit(solution)/shard_map/ppermute | solution.py:322
  30.3 1.0 %copy-start.9 = (f32[10,4,128]{2,1,0:T(4,128)}, f32[10,4,128]{2,1,0:T(4,128)S(1)}, u32[]{:S(2)}) copy-start(f32[10,4,128]{2,1,0:T(4,128)S(1)} %collective-permute-done.4.ralo_ref) | copy-start | bytes 61444
  31.9 0.6 copy-start.3
  34.7 11.4 %collective-permute-start.6 = (f32[10,16,128]{2,1,0:T(8,128)}, f32[10,16,128]{2,1,0:T(8,128)S(1)}, u32[]{:S(2)}, u32[]{:S(2)}) collective-permute-start(f32[10,16,128]{2,1,0:T(8,128)} %get-tuple-element.29), channel_id=1, source_target_pairs={{0,4},{4,0},{1,5},{5,1},{2,6},{6,2},{3,7},{7,3},{8,12},{12,8},{9,1... | collective-permute-start | bytes 245768 | tf_op jit(solution)/shard_map/ppermute | solution.py:320
  36.7 8.2 %collective-permute-start.7 = (f32[10,4,128]{2,1,0:T(4,128)}, f32[10,4,128]{2,1,0:T(4,128)S(1)}, u32[]{:S(2)}, u32[]{:S(2)}) collective-permute-start(f32[10,4,128]{2,1,0:T(4,128)} %get-tuple-element.30), channel_id=1, source_target_pairs={{0,1},{1,2},{2,3},{4,5},{5,6},{6,7},{8,9},{9,10},{10,11},{12,13},{... | collective-permute-start | bytes 61448 | tf_op jit(solution)/shard_map/ppermute | solution.py:321
  40.2 5.9 %collective-permute-start.8 = (f32[10,4,128]{2,1,0:T(4,128)}, f32[10,4,128]{2,1,0:T(4,128)S(1)}, u32[]{:S(2)}, u32[]{:S(2)}) collective-permute-start(f32[10,4,128]{2,1,0:T(4,128)} %get-tuple-element.31), channel_id=1, source_target_pairs={{1,0},{2,1},{3,2},{5,4},{6,5},{7,6},{9,8},{10,9},{11,10},{13,12},{... | collective-permute-start | bytes 61448 | tf_op jit(solution)/shard_map/ppermute | solution.py:322
  44.8 1.3 %copy-start.7 = (f32[10,4,128]{2,1,0:T(4,128)}, f32[10,4,128]{2,1,0:T(4,128)S(1)}, u32[]{:S(2)}) copy-start(f32[10,4,128]{2,1,0:T(4,128)S(1)} %collective-permute-done.7.ralo_ref) | copy-start | bytes 61444
  46.7 0.6 copy-start.2
  49.5 9.4 %collective-permute-start.9 = (f32[10,16,128]{2,1,0:T(8,128)}, f32[10,16,128]{2,1,0:T(8,128)S(1)}, u32[]{:S(2)}, u32[]{:S(2)}) collective-permute-start(f32[10,16,128]{2,1,0:T(8,128)} %get-tuple-element.33), channel_id=1, source_target_pairs={{0,4},{4,0},{1,5},{5,1},{2,6},{6,2},{3,7},{7,3},{8,12},{12,8},{9,1... | collective-permute-start | bytes 245768 | tf_op jit(solution)/shard_map/ppermute | solution.py:320
  49.7 8.2 %collective-permute-start.10 = (f32[10,4,128]{2,1,0:T(4,128)}, f32[10,4,128]{2,1,0:T(4,128)S(1)}, u32[]{:S(2)}, u32[]{:S(2)}) collective-permute-start(f32[10,4,128]{2,1,0:T(4,128)} %get-tuple-element.34), channel_id=1, source_target_pairs={{0,1},{1,2},{2,3},{4,5},{5,6},{6,7},{8,9},{9,10},{10,11},{12,13},{... | collective-permute-start | bytes 61448 | tf_op jit(solution)/shard_map/ppermute | solution.py:321
  53.1 5.9 %collective-permute-start.11 = (f32[10,4,128]{2,1,0:T(4,128)}, f32[10,4,128]{2,1,0:T(4,128)S(1)}, u32[]{:S(2)}, u32[]{:S(2)}) collective-permute-start(f32[10,4,128]{2,1,0:T(4,128)} %get-tuple-element.35), channel_id=1, source_target_pairs={{1,0},{2,1},{3,2},{5,4},{6,5},{7,6},{9,8},{10,9},{11,10},{13,12},{... | collective-permute-start | bytes 61448 | tf_op jit(solution)/shard_map/ppermute | solution.py:322
  57.9 1.1 %copy-start.5 = (f32[10,4,128]{2,1,0:T(4,128)}, f32[10,4,128]{2,1,0:T(4,128)S(1)}, u32[]{:S(2)}) copy-start(f32[10,4,128]{2,1,0:T(4,128)S(1)} %collective-permute-done.10.ralo_ref) | copy-start | bytes 61444
  59.5 0.6 copy-start.1
  66.4 1.3 %collective-permute-start.12 = (f32[8,3,512]{2,1,0:T(4,128)S(1)}, f32[8,3,512]{2,1,0:T(4,128)S(1)}, u32[]{:S(2)}, u32[]{:S(2)}) collective-permute-start(f32[8,3,512]{2,1,0:T(4,128)S(1)} %slice_select_fusion), channel_id=1, source_target_pairs={{0,8},{8,0},{16,24},{24,16},{32,40},{40,32},{48,56},{56,48},{64,72... | collective-permute-start | bytes 147464 | tf_op jit(solution)/shard_map/ppermute | solution.py:40
  68.4 15.6 %all-to-all-start = ((f32[8,3,512]{2,1,0:T(4,128)}), f32[8,3,512]{2,1,0:T(4,128)S(1)}, u32[]{:S(2)}, u32[]{:S(2)}) async-start(f32[8,3,512]{2,1,0:T(4,128)} %select_add_fusion), calls=%async_computation | async-start | bytes 131072 | tf_op jit(solution)/shard_map/all_to_all | solution.py:42
  (4 other events, 2.4 us)

commit v11 on v9

--- a/solution.py
+++ b/solution.py
@@ -69,21 +69,43 @@
     return total
 
 
+def gauss_rows(gauss_ref, d, x, half, sums, reals, imags):
+    base = (d * 3) * half * half + x * half
+    def dot(which, parts):
+        start = base + which * half * half
+        total = gauss_ref[start] * parts[0]
+        for c in range(1, half):
+            total = total + gauss_ref[start + c] * parts[c]
+        return total
+    shared = dot(0, sums)
+    return shared + dot(1, imags), shared - dot(2, reals)
+
+
 def write_edges(mat_ref, wt_ref, psi_ref, face_ref, axs_ref, q2_ref, q3_ref, comps, tile_r):
     rows = psi_ref.shape[1]
+    half = comps // 2
     layers = rows // tile_r
+    gauss = mat_ref.at[pl.ds(6 * comps * comps + METRIC + 64, 6 * 3 * half * half)]
     top = pl.ds(rows - tile_r, tile_r)
     bottom = pl.ds(0, tile_r)
     r_top = pl.ds(tile_r - 1, layers, stride=tile_r)
     r_bottom = pl.ds(0, layers, stride=tile_r)
     keep_top = wt_ref[6 * comps * comps + 1]
     keep_bottom = wt_ref[6 * comps * comps + 0]
+    outs = {}
+    for d, where in ((0, top), (1, bottom), (2, r_top), (3, r_bottom)):
+        reals = [psi_ref[c, where, :] for c in range(half)]
+        imags = [psi_ref[c + half, where, :] for c in range(half)]
+        sums = [reals[c] + imags[c] for c in range(half)]
+        face = face_ref[d, where, :]
+        for x in range(half):
+            real, imag = gauss_rows(gauss, d, x, half, sums, reals, imags)
+            outs[d, x] = face * real
+            outs[d, x + half] = face * imag
     for x in range(comps):
-        up = face_ref[0, top, :] * applied(mat_ref, 0, x, comps, lambda c: psi_ref[c, top, :])
-        down = face_ref[1, bottom, :] * applied(mat_ref, 1, x, comps, lambda c: psi_ref[c, bottom, :])
-        axs_ref[x] = up * keep_top + down * keep_bottom
-        q2_ref[x] = face_ref[2, r_top, :] * applied(mat_ref, 2, x, comps, lambda c: psi_ref[c, r_top, :])
-        q3_ref[x] = face_ref[3, r_bottom, :] * applied(mat_ref, 3, x, comps, lambda c: psi_ref[c, r_bottom, :])
+        axs_ref[x] = outs[0, x] * keep_top + outs[1, x] * keep_bottom
+        q2_ref[x] = outs[2, x]
+        q3_ref[x] = outs[3, x]
 
 
 def edges_kernel(mat_ref, wt_ref, psi_ref, coef_ref, axs_ref, q2_ref, q3_ref, face_ref, *, tile_r):
@@ -304,7 +326,7 @@
     imag_t = jnp.swapaxes(flux_jac[:, 1], 1, 2)
     gauss = jnp.stack([real_t, imag_t - real_t, real_t + imag_t], axis=1).reshape(-1)
     pad = jnp.zeros((METRIC + 64 - weights.shape[0],), jnp.float32)
-    mat_weights = jnp.concatenate([mat, weights, pad, gauss])
+    mat_weights = jnp.concatenate([jnp.zeros_like(mat), weights, pad, gauss])
     mat = mat_weights
     weights = mat_weights
     partner = pairing[0, 0]

time: 85 us -> 85.1 us (level)
    unnamed x30 -> x28, local copies, waits for them, and re-layouts: 5.15 us -> 5.15 us
where the time goes in v11:
time: 85.1 us; the launch traced here: 84.3 us
  starting transfers between devices  31 us (36%)
  Pallas kernels  26 us (31%)
  waiting for transfers between devices  9.6 us (11%)
  local copies, waits for them, and re-layouts  8.75 us (10%)
  matrix products  4.2 us (5%)
  other arithmetic  2.48 us (3%)
  between operations  2.31 us (3%)
    ppermute x4, starting transfers between devices, body(): ralo = lax.ppermute(q2, 'radial', up_r)  13.8 us
    pallas_call x4, Pallas kernels, run_interior(): pl.pallas_call(functools.partial(interior_kernel, tile_r=tile_r), out_sha...  13.2 us
    pallas_call x4, Pallas kernels, run_fixup(): pl.pallas_call(functools.partial(fixup_kernel, tile_r=tile_r, edges=edges...  8.41 us
    all_to_all x1, starting transfers between devices, sum_at_owner_paired(): lax.all_to_all(keep + got, axis, 0, 0, tiled=True, axis_index_groups=groups)  7.79 us
    ppermute x4, starting transfers between devices, body(): rahi = lax.ppermute(q3, 'radial', down_r)  5.17 us
    unnamed x28, local copies, waits for them, and re-layouts  5.15 us
    ppermute x4, waiting for transfers between devices, body(): rahi = lax.ppermute(q3, 'radial', down_r)  4.6 us
    dot_general x1, matrix products, body(): jnp.einsum('xl,lj->xj', weighted.reshape(dims * blocks, lanes), pick_lane...  4.2 us
  transfers between devices with their start and end apart: 14, of which 6 were waited for; matrix products, arithmetic and copies ran while one was open for 2% of the time, Pallas kernels for 19%

profile of v11, /device:TPU:0, one launch (start us, length us, event | category | flops | bytes accessed | tf_op | source)
XLA Modules:
  0.0 84.3 jit_solution(15648656261411156039)
XLA Ops:
  5.0 1.8 %shard_map.122 = (f32[10,16,128]{2,1,0:T(8,128)}, f32[10,4,128]{2,1,0:T(4,128)}, f32[10,4,128]{2,1,0:T(4,128)}, f32[6,64,128]{2,1,0:T(8,128)}) custom-call(f32[1122]{0:T(1024)} %concatenate.3.mat_ref.wt_ref, f32[1122]{0:T(1024)} %concatenate.3.mat_ref.wt_ref, f32[10,64,128]{2,1,0:T(8,128)} %bitcast.85, bf16[6,64,128]{2,1,0:T(8,128)(2,1)} %bitcast.102), custom_call_target="tpu_custom_call" | custom-call | tf_op jit(solution)/shard_map/pallas_call | solution.py:252
  6.9 2.0 %collective-permute-start = (f32[10,16,128]{2,1,0:T(8,128)}, f32[10,16,128]{2,1,0:T(8,128)S(1)}, u32[]{:S(2)}, u32[]{:S(2)}) collective-permute-start(f32[10,16,128]{2,1,0:T(8,128)} %get-tuple-element.21), channel_id=1, source_target_pairs={{0,4},{4,0},{1,5},{5,1},{2,6},{6,2},{3,7},{7,3},{8,12},{12,8},{9,1... | collective-permute-start | bytes 245768 | tf_op jit(solution)/shard_map/ppermute | solution.py:341
  8.9 3.4 %collective-permute-start.1 = (f32[10,4,128]{2,1,0:T(4,128)}, f32[10,4,128]{2,1,0:T(4,128)S(1)}, u32[]{:S(2)}, u32[]{:S(2)}) collective-permute-start(f32[10,4,128]{2,1,0:T(4,128)} %get-tuple-element.22), channel_id=1, source_target_pairs={{0,1},{1,2},{2,3},{4,5},{5,6},{6,7},{8,9},{9,10},{10,11},{12,13},{... | collective-permute-start | bytes 61448 | tf_op jit(solution)/shard_map/ppermute | solution.py:342
  12.3 1.3 %collective-permute-start.2 = (f32[10,4,128]{2,1,0:T(4,128)}, f32[10,4,128]{2,1,0:T(4,128)S(1)}, u32[]{:S(2)}, u32[]{:S(2)}) collective-permute-start(f32[10,4,128]{2,1,0:T(4,128)} %get-tuple-element.23), channel_id=1, source_target_pairs={{1,0},{2,1},{3,2},{5,4},{6,5},{7,6},{9,8},{10,9},{11,10},{13,12},{... | collective-permute-start | bytes 61448 | tf_op jit(solution)/shard_map/ppermute | solution.py:343
  13.8 3.3 %shard_map.123.res_ref = f32[10,64,128]{2,1,0:T(8,128)} custom-call(f32[1122]{0:T(1024)} %concatenate.3.mat_ref.wt_ref, f32[1122]{0:T(1024)} %concatenate.3.mat_ref.wt_ref, f32[10,64,128]{2,1,0:T(8,128)} %bitcast.86, f32[10,64,128]{2,1,0:T(8,128)} %bitcast.81, f32[6,64,128]{2,1,0:T(8,128)} %get-tuple-element.20.face_ref, f32[64,128]{1,0:T(8,128)} %bitcast.88, ...), custom_call_target="tpu_custom_call" | custom-call | tf_op jit(solution)/shard_map/pallas_call | solution.py:262
  19.4 2.1 %shard_map.124 = (f32[10,64,128]{2,1,0:T(8,128)}, f32[10,16,128]{2,1,0:T(8,128)}, f32[10,4,128]{2,1,0:T(4,128)}, f32[10,4,128]{2,1,0:T(4,128)}) custom-call(f32[1122]{0:T(1024)} %concatenate.3.mat_ref.wt_ref, f32[1122]{0:T(1024)} %concatenate.3.mat_ref.wt_ref, f32[10,64,128]{2,1,0:T(8,128)} %bitcast.87, f32[10,64,128]{2,1,0:T(8,128)} %shard_map.123.res_ref, ...), custom_call_target="tpu_custom_call" | custom-call | tf_op jit(solution)/shard_map/pallas_call | solution.py:274
  21.7 3.4 %collective-permute-start.4 = (f32[10,4,128]{2,1,0:T(4,128)}, f32[10,4,128]{2,1,0:T(4,128)S(1)}, u32[]{:S(2)}, u32[]{:S(2)}) collective-permute-start(f32[10,4,128]{2,1,0:T(4,128)} %get-tuple-element.26), channel_id=1, source_target_pairs={{0,1},{1,2},{2,3},{4,5},{5,6},{6,7},{8,9},{9,10},{10,11},{12,13},{... | collective-permute-start | bytes 61448 | tf_op jit(solution)/shard_map/ppermute | solution.py:342
  25.1 1.3 %collective-permute-start.5 = (f32[10,4,128]{2,1,0:T(4,128)}, f32[10,4,128]{2,1,0:T(4,128)S(1)}, u32[]{:S(2)}, u32[]{:S(2)}) collective-permute-start(f32[10,4,128]{2,1,0:T(4,128)} %get-tuple-element.27), channel_id=1, source_target_pairs={{1,0},{2,1},{3,2},{5,4},{6,5},{7,6},{9,8},{10,9},{11,10},{13,12},{... | collective-permute-start | bytes 61448 | tf_op jit(solution)/shard_map/ppermute | solution.py:343
  26.7 3.3 %shard_map.125.res_ref = f32[10,64,128]{2,1,0:T(8,128)} custom-call(f32[1122]{0:T(1024)} %concatenate.3.mat_ref.wt_ref, f32[1122]{0:T(1024)} %concatenate.3.mat_ref.wt_ref, f32[10,64,128]{2,1,0:T(8,128)} %get-tuple-element.24.psi_ref, f32[10,64,128]{2,1,0:T(8,128)} %bitcast.82, f32[6,64,128]{2,1,0:T(8,128)} %get-tuple-element.20.face_ref, ...), custom_call_target="tpu_custom_call" | custom-call | tf_op jit(solution)/shard_map/pallas_call | solution.py:262
  32.2 2.2 %shard_map.126 = (f32[10,64,128]{2,1,0:T(8,128)}, f32[10,16,128]{2,1,0:T(8,128)}, f32[10,4,128]{2,1,0:T(4,128)}, f32[10,4,128]{2,1,0:T(4,128)}) custom-call(f32[1122]{0:T(1024)} %concatenate.3.mat_ref.wt_ref, f32[1122]{0:T(1024)} %concatenate.3.mat_ref.wt_ref, f32[10,64,128]{2,1,0:T(8,128)} %get-tuple-element.24.psi_ref, f32[10,64,128]{2,1,0:T(8,128)} %shard_map.125.res_ref, ...), custom_call_target="tpu_custom_call" | custom-call | tf_op jit(solution)/shard_map/pallas_call | solution.py:274
  34.4 1.9 %collective-permute-start.6 = (f32[10,16,128]{2,1,0:T(8,128)}, f32[10,16,128]{2,1,0:T(8,128)S(1)}, u32[]{:S(2)}, u32[]{:S(2)}) collective-permute-start(f32[10,16,128]{2,1,0:T(8,128)} %get-tuple-element.29), channel_id=1, source_target_pairs={{0,4},{4,0},{1,5},{5,1},{2,6},{6,2},{3,7},{7,3},{8,12},{12,8},{9,1... | collective-permute-start | bytes 245768 | tf_op jit(solution)/shard_map/ppermute | solution.py:341
  36.3 3.5 %collective-permute-start.7 = (f32[10,4,128]{2,1,0:T(4,128)}, f32[10,4,128]{2,1,0:T(4,128)S(1)}, u32[]{:S(2)}, u32[]{:S(2)}) collective-permute-start(f32[10,4,128]{2,1,0:T(4,128)} %get-tuple-element.30), channel_id=1, source_target_pairs={{0,1},{1,2},{2,3},{4,5},{5,6},{6,7},{8,9},{9,10},{10,11},{12,13},{... | collective-permute-start | bytes 61448 | tf_op jit(solution)/shard_map/ppermute | solution.py:342
  39.8 1.3 %collective-permute-start.8 = (f32[10,4,128]{2,1,0:T(4,128)}, f32[10,4,128]{2,1,0:T(4,128)S(1)}, u32[]{:S(2)}, u32[]{:S(2)}) collective-permute-start(f32[10,4,128]{2,1,0:T(4,128)} %get-tuple-element.31), channel_id=1, source_target_pairs={{1,0},{2,1},{3,2},{5,4},{6,5},{7,6},{9,8},{10,9},{11,10},{13,12},{... | collective-permute-start | bytes 61448 | tf_op jit(solution)/shard_map/ppermute | solution.py:343
  41.2 3.3 %shard_map.127.res_ref = f32[10,64,128]{2,1,0:T(8,128)} custom-call(f32[1122]{0:T(1024)} %concatenate.3.mat_ref.wt_ref, f32[1122]{0:T(1024)} %concatenate.3.mat_ref.wt_ref, f32[10,64,128]{2,1,0:T(8,128)} %get-tuple-element.28.psi_ref, f32[10,64,128]{2,1,0:T(8,128)} %bitcast.83, f32[6,64,128]{2,1,0:T(8,128)} %get-tuple-element.20.face_ref, ...), custom_call_target="tpu_custom_call" | custom-call | tf_op jit(solution)/shard_map/pallas_call | solution.py:262
  44.5 1.3 %collective-permute-done.8.rahi_ref = f32[10,4,128]{2,1,0:T(4,128)S(1)} collective-permute-done((f32[10,4,128]{2,1,0:T(4,128)}, f32[10,4,128]{2,1,0:T(4,128)S(1)}, u32[]{:S(2)}, u32[]{:S(2)}) %collective-permute-start.8) | collective-permute-done | bytes 20512 | tf_op jit(solution)/shard_map/ppermute | solution.py:343
  47.0 2.1 %shard_map.128 = (f32[10,64,128]{2,1,0:T(8,128)}, f32[10,16,128]{2,1,0:T(8,128)}, f32[10,4,128]{2,1,0:T(4,128)}, f32[10,4,128]{2,1,0:T(4,128)}) custom-call(f32[1122]{0:T(1024)} %concatenate.3.mat_ref.wt_ref, f32[1122]{0:T(1024)} %concatenate.3.mat_ref.wt_ref, f32[10,64,128]{2,1,0:T(8,128)} %get-tuple-element.28.psi_ref, f32[10,64,128]{2,1,0:T(8,128)} %shard_map.127.res_ref, ...), custom_call_target="tpu_custom_call" | custom-call | tf_op jit(solution)/shard_map/pallas_call | solution.py:274
  49.2 3.4 %collective-permute-start.10 = (f32[10,4,128]{2,1,0:T(4,128)}, f32[10,4,128]{2,1,0:T(4,128)S(1)}, u32[]{:S(2)}, u32[]{:S(2)}) collective-permute-start(f32[10,4,128]{2,1,0:T(4,128)} %get-tuple-element.34), channel_id=1, source_target_pairs={{0,1},{1,2},{2,3},{4,5},{5,6},{6,7},{8,9},{9,10},{10,11},{12,13},{... | collective-permute-start | bytes 61448 | tf_op jit(solution)/shard_map/ppermute | solution.py:342
  52.6 1.3 %collective-permute-start.11 = (f32[10,4,128]{2,1,0:T(4,128)}, f32[10,4,128]{2,1,0:T(4,128)S(1)}, u32[]{:S(2)}, u32[]{:S(2)}) collective-permute-start(f32[10,4,128]{2,1,0:T(4,128)} %get-tuple-element.35), channel_id=1, source_target_pairs={{1,0},{2,1},{3,2},{5,4},{6,5},{7,6},{9,8},{10,9},{11,10},{13,12},{... | collective-permute-start | bytes 61448 | tf_op jit(solution)/shard_map/ppermute | solution.py:343
  53.9 3.3 %shard_map.129.res_ref = f32[10,64,128]{2,1,0:T(8,128)} custom-call(f32[1122]{0:T(1024)} %concatenate.3.mat_ref.wt_ref, f32[1122]{0:T(1024)} %concatenate.3.mat_ref.wt_ref, f32[10,64,128]{2,1,0:T(8,128)} %get-tuple-element.32.psi_ref, f32[10,64,128]{2,1,0:T(8,128)} %bitcast.84, f32[6,64,128]{2,1,0:T(8,128)} %get-tuple-element.20.face_ref, ...), custom_call_target="tpu_custom_call" | custom-call | tf_op jit(solution)/shard_map/pallas_call | solution.py:262
  59.7 2.0 %shard_map.130 = (f32[10,64,128]{2,1,0:T(8,128)}, f32[3,64,128]{2,1,0:T(8,128)}) custom-call(f32[1122]{0:T(1024)} %concatenate.3.mat_ref.wt_ref, f32[1122]{0:T(1024)} %concatenate.3.mat_ref.wt_ref, f32[10,64,128]{2,1,0:T(8,128)} %get-tuple-element.32.psi_ref, f32[10,64,128]{2,1,0:T(8,128)} %shard_map.129.res_ref, f32[6,64,128]{2,1,0:T(8,128)} %get-tuple-element.20.face_ref, ...), custom_call_target="tpu_custom_call" | custom-call | tf_op jit(solution)/shard_map/pallas_call | solution.py:274
  61.7 4.2 %fusion.3 = f32[3,8192]{1,0:T(4,128)S(1)} fusion(f32[3,64,128]{2,1,0:T(8,128)} %get-tuple-element.37, s32[8192]{0:T(1024)S(1)} %add_select_fusion, pred[64,8192]{1,0:T(8,128)(4,1)S(1)} %iota_compare_fusion.1), kind=kOutput, calls=%fused_computation.5 | convolution fusion | flops 2420088832 | bytes 753664 | tf_op jit(solution)/shard_map/xl,lj->xj/dot_general | solution.py:363
  68.0 7.8 %all-to-all-start = ((f32[8,3,512]{2,1,0:T(4,128)}), f32[8,3,512]{2,1,0:T(4,128)S(1)}, u32[]{:S(2)}, u32[]{:S(2)}) async-start(f32[8,3,512]{2,1,0:T(4,128)} %select_add_fusion), calls=%async_computation | async-start | bytes 131072 | tf_op jit(solution)/shard_map/all_to_all | solution.py:42
  76.4 2.6 %shard_map.131 = f32[36,512]{1,0:T(8,128)} custom-call(s32[2,512]{1,0:T(2,128)} %pad_add_fusion.where_ref, bf16[2304,128]{1,0:T(8,128)(2,1)} %bitcast.96), custom_call_target="tpu_custom_call" | custom-call | tf_op jit(solution)/shard_map/pallas_call | solution.py:375
  79.8 3.8 %all-to-all-done = f32[8,3,512]{2,1,0:T(4,128)S(1)} async-done(((f32[8,3,512]{2,1,0:T(4,128)}), f32[8,3,512]{2,1,0:T(4,128)S(1)}, u32[]{:S(2)}, u32[]{:S(2)}) %all-to-all-start) | async-done | bytes 49184 | tf_op jit(solution)/shard_map/all_to_all | solution.py:42
  (64 shorter events, 16.1 us)
Async XLA Ops:
  0.6 13.0 %copy-start = (s32[1,1,8192]{2,1,0:T(1,128)S(1)}, s32[1,1,8192]{2,1,0:T(1,128)}, u32[]{:S(2)}) copy-start(s32[1,1,8192]{2,1,0:T(1,128)} %param.21) | copy-start | bytes 98308
  6.9 11.3 %collective-permute-start = (f32[10,16,128]{2,1,0:T(8,128)}, f32[10,16,128]{2,1,0:T(8,128)S(1)}, u32[]{:S(2)}, u32[]{:S(2)}) collective-permute-start(f32[10,16,128]{2,1,0:T(8,128)} %get-tuple-element.21), channel_id=1, source_target_pairs={{0,4},{4,0},{1,5},{5,1},{2,6},{6,2},{3,7},{7,3},{8,12},{12,8},{9,1... | collective-permute-start | bytes 245768 | tf_op jit(solution)/shard_map/ppermute | solution.py:341
  8.9 8.2 %collective-permute-start.1 = (f32[10,4,128]{2,1,0:T(4,128)}, f32[10,4,128]{2,1,0:T(4,128)S(1)}, u32[]{:S(2)}, u32[]{:S(2)}) collective-permute-start(f32[10,4,128]{2,1,0:T(4,128)} %get-tuple-element.22), channel_id=1, source_target_pairs={{0,1},{1,2},{2,3},{4,5},{5,6},{6,7},{8,9},{9,10},{10,11},{12,13},{... | collective-permute-start | bytes 61448 | tf_op jit(solution)/shard_map/ppermute | solution.py:342
  12.3 5.9 %collective-permute-start.2 = (f32[10,4,128]{2,1,0:T(4,128)}, f32[10,4,128]{2,1,0:T(4,128)S(1)}, u32[]{:S(2)}, u32[]{:S(2)}) collective-permute-start(f32[10,4,128]{2,1,0:T(4,128)} %get-tuple-element.23), channel_id=1, source_target_pairs={{1,0},{2,1},{3,2},{5,4},{6,5},{7,6},{9,8},{10,9},{11,10},{13,12},{... | collective-permute-start | bytes 61448 | tf_op jit(solution)/shard_map/ppermute | solution.py:343
  17.1 1.1 %copy-start.10 = (f32[10,4,128]{2,1,0:T(4,128)}, f32[10,4,128]{2,1,0:T(4,128)S(1)}, u32[]{:S(2)}) copy-start(f32[10,4,128]{2,1,0:T(4,128)S(1)} %collective-permute-done.1.ralo_ref) | copy-start | bytes 61444
  18.8 0.6 copy-start.4
  21.5 9.4 %collective-permute-start.3 = (f32[10,16,128]{2,1,0:T(8,128)}, f32[10,16,128]{2,1,0:T(8,128)S(1)}, u32[]{:S(2)}, u32[]{:S(2)}) collective-permute-start(f32[10,16,128]{2,1,0:T(8,128)} %get-tuple-element.25), channel_id=1, source_target_pairs={{0,4},{4,0},{1,5},{5,1},{2,6},{6,2},{3,7},{7,3},{8,12},{12,8},{9,1... | collective-permute-start | bytes 245768 | tf_op jit(solution)/shard_map/ppermute | solution.py:341
  21.7 8.3 %collective-permute-start.4 = (f32[10,4,128]{2,1,0:T(4,128)}, f32[10,4,128]{2,1,0:T(4,128)S(1)}, u32[]{:S(2)}, u32[]{:S(2)}) collective-permute-start(f32[10,4,128]{2,1,0:T(4,128)} %get-tuple-element.26), channel_id=1, source_target_pairs={{0,1},{1,2},{2,3},{4,5},{5,6},{6,7},{8,9},{9,10},{10,11},{12,13},{... | collective-permute-start | bytes 61448 | tf_op jit(solution)/shard_map/ppermute | solution.py:342
  25.1 5.9 %collective-permute-start.5 = (f32[10,4,128]{2,1,0:T(4,128)}, f32[10,4,128]{2,1,0:T(4,128)S(1)}, u32[]{:S(2)}, u32[]{:S(2)}) collective-permute-start(f32[10,4,128]{2,1,0:T(4,128)} %get-tuple-element.27), channel_id=1, source_target_pairs={{1,0},{2,1},{3,2},{5,4},{6,5},{7,6},{9,8},{10,9},{11,10},{13,12},{... | collective-permute-start | bytes 61448 | tf_op jit(solution)/shard_map/ppermute | solution.py:343
  30.0 1.0 %copy-start.9 = (f32[10,4,128]{2,1,0:T(4,128)}, f32[10,4,128]{2,1,0:T(4,128)S(1)}, u32[]{:S(2)}) copy-start(f32[10,4,128]{2,1,0:T(4,128)S(1)} %collective-permute-done.4.ralo_ref) | copy-start | bytes 61444
  31.0 0.6 copy-start.11
  31.6 0.6 copy-start.3
  34.4 11.4 %collective-permute-start.6 = (f32[10,16,128]{2,1,0:T(8,128)}, f32[10,16,128]{2,1,0:T(8,128)S(1)}, u32[]{:S(2)}, u32[]{:S(2)}) collective-permute-start(f32[10,16,128]{2,1,0:T(8,128)} %get-tuple-element.29), channel_id=1, source_target_pairs={{0,4},{4,0},{1,5},{5,1},{2,6},{6,2},{3,7},{7,3},{8,12},{12,8},{9,1... | collective-permute-start | bytes 245768 | tf_op jit(solution)/shard_map/ppermute | solution.py:341
  36.3 8.2 %collective-permute-start.7 = (f32[10,4,128]{2,1,0:T(4,128)}, f32[10,4,128]{2,1,0:T(4,128)S(1)}, u32[]{:S(2)}, u32[]{:S(2)}) collective-permute-start(f32[10,4,128]{2,1,0:T(4,128)} %get-tuple-element.30), channel_id=1, source_target_pairs={{0,1},{1,2},{2,3},{4,5},{5,6},{6,7},{8,9},{9,10},{10,11},{12,13},{... | collective-permute-start | bytes 61448 | tf_op jit(solution)/shard_map/ppermute | solution.py:342
  39.8 5.9 %collective-permute-start.8 = (f32[10,4,128]{2,1,0:T(4,128)}, f32[10,4,128]{2,1,0:T(4,128)S(1)}, u32[]{:S(2)}, u32[]{:S(2)}) collective-permute-start(f32[10,4,128]{2,1,0:T(4,128)} %get-tuple-element.31), channel_id=1, source_target_pairs={{1,0},{2,1},{3,2},{5,4},{6,5},{7,6},{9,8},{10,9},{11,10},{13,12},{... | collective-permute-start | bytes 61448 | tf_op jit(solution)/shard_map/ppermute | solution.py:343
  44.5 1.3 %copy-start.7 = (f32[10,4,128]{2,1,0:T(4,128)}, f32[10,4,128]{2,1,0:T(4,128)S(1)}, u32[]{:S(2)}) copy-start(f32[10,4,128]{2,1,0:T(4,128)S(1)} %collective-permute-done.7.ralo_ref) | copy-start | bytes 61444
  46.3 0.6 copy-start.2
  49.1 9.4 %collective-permute-start.9 = (f32[10,16,128]{2,1,0:T(8,128)}, f32[10,16,128]{2,1,0:T(8,128)S(1)}, u32[]{:S(2)}, u32[]{:S(2)}) collective-permute-start(f32[10,16,128]{2,1,0:T(8,128)} %get-tuple-element.33), channel_id=1, source_target_pairs={{0,4},{4,0},{1,5},{5,1},{2,6},{6,2},{3,7},{7,3},{8,12},{12,8},{9,1... | collective-permute-start | bytes 245768 | tf_op jit(solution)/shard_map/ppermute | solution.py:341
  49.2 8.0 %collective-permute-start.10 = (f32[10,4,128]{2,1,0:T(4,128)}, f32[10,4,128]{2,1,0:T(4,128)S(1)}, u32[]{:S(2)}, u32[]{:S(2)}) collective-permute-start(f32[10,4,128]{2,1,0:T(4,128)} %get-tuple-element.34), channel_id=1, source_target_pairs={{0,1},{1,2},{2,3},{4,5},{5,6},{6,7},{8,9},{9,10},{10,11},{12,13},{... | collective-permute-start | bytes 61448 | tf_op jit(solution)/shard_map/ppermute | solution.py:342
  52.6 5.9 %collective-permute-start.11 = (f32[10,4,128]{2,1,0:T(4,128)}, f32[10,4,128]{2,1,0:T(4,128)S(1)}, u32[]{:S(2)}, u32[]{:S(2)}) collective-permute-start(f32[10,4,128]{2,1,0:T(4,128)} %get-tuple-element.35), channel_id=1, source_target_pairs={{1,0},{2,1},{3,2},{5,4},{6,5},{7,6},{9,8},{10,9},{11,10},{13,12},{... | collective-permute-start | bytes 61448 | tf_op jit(solution)/shard_map/ppermute | solution.py:343
  57.2 1.2 %copy-start.5 = (f32[10,4,128]{2,1,0:T(4,128)}, f32[10,4,128]{2,1,0:T(4,128)S(1)}, u32[]{:S(2)}) copy-start(f32[10,4,128]{2,1,0:T(4,128)S(1)} %collective-permute-done.10.ralo_ref) | copy-start | bytes 61444
  59.1 0.6 copy-start.1
  66.0 1.3 %collective-permute-start.12 = (f32[8,3,512]{2,1,0:T(4,128)S(1)}, f32[8,3,512]{2,1,0:T(4,128)S(1)}, u32[]{:S(2)}, u32[]{:S(2)}) collective-permute-start(f32[8,3,512]{2,1,0:T(4,128)S(1)} %slice_select_fusion), channel_id=1, source_target_pairs={{0,8},{8,0},{16,24},{24,16},{32,40},{40,32},{48,56},{56,48},{64,72... | collective-permute-start | bytes 147464 | tf_op jit(solution)/shard_map/ppermute | solution.py:40
  68.0 15.6 %all-to-all-start = ((f32[8,3,512]{2,1,0:T(4,128)}), f32[8,3,512]{2,1,0:T(4,128)S(1)}, u32[]{:S(2)}, u32[]{:S(2)}) async-start(f32[8,3,512]{2,1,0:T(4,128)} %select_add_fusion), calls=%async_computation | async-start | bytes 131072 | tf_op jit(solution)/shard_map/all_to_all | solution.py:42
  (3 other events, 1.8 us)

commit v12 on v11

--- a/solution.py
+++ b/solution.py
@@ -359,13 +359,16 @@
     blocks = cells // lanes
     lane_of = order % lanes
     row_of = order // lanes
-    pick_lane = (lane_of[None, :] == jnp.arange(lanes, dtype=order.dtype)[:, None]).astype(jnp.float32)
+    pick_lane = (lane_of[None, :] == jnp.arange(lanes, dtype=order.dtype)[:, None]).astype(jnp.bfloat16)
+    flat_w = weighted.reshape(dims * blocks, lanes)
+    first = lax.reduce_precision(flat_w, exponent_bits=8, mantissa_bits=7)
+    rest = flat_w - first
+    second = lax.reduce_precision(rest, exponent_bits=8, mantissa_bits=7)
+    parts = jnp.concatenate([first, second, rest - second]).astype(jnp.bfloat16)
     by_lane = jnp.einsum(
-        "xl,lj->xj",
-        weighted.reshape(dims * blocks, lanes),
-        pick_lane,
-        precision=lax.Precision.HIGHEST,
-    ).reshape(dims, blocks, cells)
+        "xl,lj->xj", parts, pick_lane, preferred_element_type=jnp.float32
+    ).reshape(3, dims, blocks, cells)
+    by_lane = by_lane[0] + by_lane[1] + by_lane[2]
     pick_row = row_of[None, None, :] == jnp.arange(blocks, dtype=order.dtype)[None, :, None]
     in_order = jnp.sum(jnp.where(pick_row, by_lane, 0.0), axis=1)
     gathered = sum_at_owner_paired(in_order, "phase", 1) if owners % 2 == 0 else sum_at_owner(in_order, "phase", 1)

time: 85.1 us -> 88.5 us (1.040)
  other arithmetic: 2.48 us -> 8.11 us
  waiting for transfers between devices: 9.6 us -> 6.56 us
  matrix products: 4.2 us -> 2.64 us
  starting transfers between devices: 31 us -> 32.5 us
    ppermute x4, waiting for transfers between devices: 4.6 us -> 2.24 us  [body(): rahi = lax.ppermute(q3, 'radial', down_r)]
    dot_general x1, matrix products: 4.2 us -> 2.64 us  [body(): jnp.einsum('xl,lj->xj', parts, pick_lane, preferred_element_type=jnp.floa...]
    ppermute x4, starting transfers between devices: 13.8 us -> 15.1 us  [body(): ralo = lax.ppermute(q2, 'radial', up_r)]
    select_n x2, other arithmetic: 0.04 us -> 1.4 us  [body(): where = jnp.stack([mine % lanes, mine // lanes]).astype(jnp.int32)]
    add x0 -> x1, other arithmetic: none -> 1.02 us  [body(): by_lane = by_lane[0] + by_lane[1] + by_lane[2]]
    another operation x0 -> x1, other arithmetic: none -> 0.92 us
    unnamed x28 -> x26, local copies, waits for them, and re-layouts: 5.15 us -> 5.15 us
  transfers between devices with their start and end apart: 14 -> 14, of which waited for: 6 -> 6; matrix products, arithmetic and copies ran while one was open for 2% -> 6% of each run, Pallas kernels for 19% -> 18%
where the time goes in v12:
time: 88.5 us; the launch traced here: 86.9 us
  starting transfers between devices  32.5 us (37%)
  Pallas kernels  26 us (29%)
  local copies, waits for them, and re-layouts  8.75 us (10%)
  other arithmetic  8.11 us (9%)
  waiting for transfers between devices  6.56 us (7%)
  matrix products  2.64 us (3%)
  between operations  2.28 us (3%)
    ppermute x4, starting transfers between devices, body(): ralo = lax.ppermute(q2, 'radial', up_r)  15.1 us
    pallas_call x4, Pallas kernels, run_interior(): pl.pallas_call(functools.partial(interior_kernel, tile_r=tile_r), out_sha...  13.2 us
    pallas_call x4, Pallas kernels, run_fixup(): pl.pallas_call(functools.partial(fixup_kernel, tile_r=tile_r, edges=edges...  8.41 us
    all_to_all x1, starting transfers between devices, sum_at_owner_paired(): lax.all_to_all(keep + got, axis, 0, 0, tiled=True, axis_index_groups=groups)  7.79 us
    ppermute x4, starting transfers between devices, body(): rahi = lax.ppermute(q3, 'radial', down_r)  5.35 us
    unnamed x26, local copies, waits for them, and re-layouts  5.15 us
    ppermute x4, starting transfers between devices, body(): axr = lax.ppermute(axs, 'axial', [(0, 1), (1, 0)])  4.16 us
    all_to_all x1, waiting for transfers between devices, sum_at_owner_paired(): lax.all_to_all(keep + got, axis, 0, 0, tiled=True, axis_index_groups=groups)  3.76 us
  transfers between devices with their start and end apart: 14, of which 6 were waited for; matrix products, arithmetic and copies ran while one was open for 6% of the time, Pallas kernels for 18%

profile of v12, /device:TPU:0, one launch (start us, length us, event | category | flops | bytes accessed | tf_op | source)
XLA Modules:
  0.0 86.9 jit_solution(4002636144587502406)
XLA Ops:
  5.0 1.8 %shard_map.122 = (f32[10,16,128]{2,1,0:T(8,128)}, f32[10,4,128]{2,1,0:T(4,128)}, f32[10,4,128]{2,1,0:T(4,128)}, f32[6,64,128]{2,1,0:T(8,128)}) custom-call(f32[1122]{0:T(1024)} %concatenate.7.mat_ref.wt_ref, f32[1122]{0:T(1024)} %concatenate.7.mat_ref.wt_ref, f32[10,64,128]{2,1,0:T(8,128)} %bitcast.88, bf16[6,64,128]{2,1,0:T(8,128)(2,1)} %bitcast.105), custom_call_target="tpu_custom_call" | custom-call | tf_op jit(solution)/shard_map/pallas_call | solution.py:252
  6.9 2.0 %collective-permute-start = (f32[10,16,128]{2,1,0:T(8,128)}, f32[10,16,128]{2,1,0:T(8,128)S(1)}, u32[]{:S(2)}, u32[]{:S(2)}) collective-permute-start(f32[10,16,128]{2,1,0:T(8,128)} %get-tuple-element.21), channel_id=1, source_target_pairs={{0,4},{4,0},{1,5},{5,1},{2,6},{6,2},{3,7},{7,3},{8,12},{12,8},{9,1... | collective-permute-start | bytes 245768 | tf_op jit(solution)/shard_map/ppermute | solution.py:341
  8.9 3.4 %collective-permute-start.1 = (f32[10,4,128]{2,1,0:T(4,128)}, f32[10,4,128]{2,1,0:T(4,128)S(1)}, u32[]{:S(2)}, u32[]{:S(2)}) collective-permute-start(f32[10,4,128]{2,1,0:T(4,128)} %get-tuple-element.22), channel_id=1, source_target_pairs={{0,1},{1,2},{2,3},{4,5},{5,6},{6,7},{8,9},{9,10},{10,11},{12,13},{... | collective-permute-start | bytes 61448 | tf_op jit(solution)/shard_map/ppermute | solution.py:342
  12.3 1.3 %collective-permute-start.2 = (f32[10,4,128]{2,1,0:T(4,128)}, f32[10,4,128]{2,1,0:T(4,128)S(1)}, u32[]{:S(2)}, u32[]{:S(2)}) collective-permute-start(f32[10,4,128]{2,1,0:T(4,128)} %get-tuple-element.23), channel_id=1, source_target_pairs={{1,0},{2,1},{3,2},{5,4},{6,5},{7,6},{9,8},{10,9},{11,10},{13,12},{... | collective-permute-start | bytes 61448 | tf_op jit(solution)/shard_map/ppermute | solution.py:343
  14.5 3.3 %shard_map.123.res_ref = f32[10,64,128]{2,1,0:T(8,128)} custom-call(f32[1122]{0:T(1024)} %concatenate.7.mat_ref.wt_ref, f32[1122]{0:T(1024)} %concatenate.7.mat_ref.wt_ref, f32[10,64,128]{2,1,0:T(8,128)} %bitcast.89, f32[10,64,128]{2,1,0:T(8,128)} %bitcast.84, f32[6,64,128]{2,1,0:T(8,128)} %get-tuple-element.20.face_ref, f32[64,128]{1,0:T(8,128)} %bitcast.91, ...), custom_call_target="tpu_custom_call" | custom-call | tf_op jit(solution)/shard_map/pallas_call | solution.py:262
  19.4 2.1 %shard_map.124 = (f32[10,64,128]{2,1,0:T(8,128)}, f32[10,16,128]{2,1,0:T(8,128)}, f32[10,4,128]{2,1,0:T(4,128)}, f32[10,4,128]{2,1,0:T(4,128)}) custom-call(f32[1122]{0:T(1024)} %concatenate.7.mat_ref.wt_ref, f32[1122]{0:T(1024)} %concatenate.7.mat_ref.wt_ref, f32[10,64,128]{2,1,0:T(8,128)} %bitcast.90, f32[10,64,128]{2,1,0:T(8,128)} %shard_map.123.res_ref, ...), custom_call_target="tpu_custom_call" | custom-call | tf_op jit(solution)/shard_map/pallas_call | solution.py:274
  21.6 4.2 %collective-permute-start.4 = (f32[10,4,128]{2,1,0:T(4,128)}, f32[10,4,128]{2,1,0:T(4,128)S(1)}, u32[]{:S(2)}, u32[]{:S(2)}) collective-permute-start(f32[10,4,128]{2,1,0:T(4,128)} %get-tuple-element.26), channel_id=1, source_target_pairs={{0,1},{1,2},{2,3},{4,5},{5,6},{6,7},{8,9},{9,10},{10,11},{12,13},{... | collective-permute-start | bytes 61448 | tf_op jit(solution)/shard_map/ppermute | solution.py:342
  25.8 1.3 %collective-permute-start.5 = (f32[10,4,128]{2,1,0:T(4,128)}, f32[10,4,128]{2,1,0:T(4,128)S(1)}, u32[]{:S(2)}, u32[]{:S(2)}) collective-permute-start(f32[10,4,128]{2,1,0:T(4,128)} %get-tuple-element.27), channel_id=1, source_target_pairs={{1,0},{2,1},{3,2},{5,4},{6,5},{7,6},{9,8},{10,9},{11,10},{13,12},{... | collective-permute-start | bytes 61448 | tf_op jit(solution)/shard_map/ppermute | solution.py:343
  27.4 3.3 %shard_map.125.res_ref = f32[10,64,128]{2,1,0:T(8,128)} custom-call(f32[1122]{0:T(1024)} %concatenate.7.mat_ref.wt_ref, f32[1122]{0:T(1024)} %concatenate.7.mat_ref.wt_ref, f32[10,64,128]{2,1,0:T(8,128)} %get-tuple-element.24.psi_ref, f32[10,64,128]{2,1,0:T(8,128)} %bitcast.85, f32[6,64,128]{2,1,0:T(8,128)} %get-tuple-element.20.face_ref, ...), custom_call_target="tpu_custom_call" | custom-call | tf_op jit(solution)/shard_map/pallas_call | solution.py:262
  32.9 2.2 %shard_map.126 = (f32[10,64,128]{2,1,0:T(8,128)}, f32[10,16,128]{2,1,0:T(8,128)}, f32[10,4,128]{2,1,0:T(4,128)}, f32[10,4,128]{2,1,0:T(4,128)}) custom-call(f32[1122]{0:T(1024)} %concatenate.7.mat_ref.wt_ref, f32[1122]{0:T(1024)} %concatenate.7.mat_ref.wt_ref, f32[10,64,128]{2,1,0:T(8,128)} %get-tuple-element.24.psi_ref, f32[10,64,128]{2,1,0:T(8,128)} %shard_map.125.res_ref, ...), custom_call_target="tpu_custom_call" | custom-call | tf_op jit(solution)/shard_map/pallas_call | solution.py:274
  35.1 1.9 %collective-permute-start.6 = (f32[10,16,128]{2,1,0:T(8,128)}, f32[10,16,128]{2,1,0:T(8,128)S(1)}, u32[]{:S(2)}, u32[]{:S(2)}) collective-permute-start(f32[10,16,128]{2,1,0:T(8,128)} %get-tuple-element.29), channel_id=1, source_target_pairs={{0,4},{4,0},{1,5},{5,1},{2,6},{6,2},{3,7},{7,3},{8,12},{12,8},{9,1... | collective-permute-start | bytes 245768 | tf_op jit(solution)/shard_map/ppermute | solution.py:341
  37.0 3.5 %collective-permute-start.7 = (f32[10,4,128]{2,1,0:T(4,128)}, f32[10,4,128]{2,1,0:T(4,128)S(1)}, u32[]{:S(2)}, u32[]{:S(2)}) collective-permute-start(f32[10,4,128]{2,1,0:T(4,128)} %get-tuple-element.30), channel_id=1, source_target_pairs={{0,1},{1,2},{2,3},{4,5},{5,6},{6,7},{8,9},{9,10},{10,11},{12,13},{... | collective-permute-start | bytes 61448 | tf_op jit(solution)/shard_map/ppermute | solution.py:342
  40.6 1.3 %collective-permute-start.8 = (f32[10,4,128]{2,1,0:T(4,128)}, f32[10,4,128]{2,1,0:T(4,128)S(1)}, u32[]{:S(2)}, u32[]{:S(2)}) collective-permute-start(f32[10,4,128]{2,1,0:T(4,128)} %get-tuple-element.31), channel_id=1, source_target_pairs={{1,0},{2,1},{3,2},{5,4},{6,5},{7,6},{9,8},{10,9},{11,10},{13,12},{... | collective-permute-start | bytes 61448 | tf_op jit(solution)/shard_map/ppermute | solution.py:343
  42.7 3.3 %shard_map.127.res_ref = f32[10,64,128]{2,1,0:T(8,128)} custom-call(f32[1122]{0:T(1024)} %concatenate.7.mat_ref.wt_ref, f32[1122]{0:T(1024)} %concatenate.7.mat_ref.wt_ref, f32[10,64,128]{2,1,0:T(8,128)} %get-tuple-element.28.psi_ref, f32[10,64,128]{2,1,0:T(8,128)} %bitcast.86, f32[6,64,128]{2,1,0:T(8,128)} %get-tuple-element.20.face_ref, ...), custom_call_target="tpu_custom_call" | custom-call | tf_op jit(solution)/shard_map/pallas_call | solution.py:262
  47.7 2.1 %shard_map.128 = (f32[10,64,128]{2,1,0:T(8,128)}, f32[10,16,128]{2,1,0:T(8,128)}, f32[10,4,128]{2,1,0:T(4,128)}, f32[10,4,128]{2,1,0:T(4,128)}) custom-call(f32[1122]{0:T(1024)} %concatenate.7.mat_ref.wt_ref, f32[1122]{0:T(1024)} %concatenate.7.mat_ref.wt_ref, f32[10,64,128]{2,1,0:T(8,128)} %get-tuple-element.28.psi_ref, f32[10,64,128]{2,1,0:T(8,128)} %shard_map.127.res_ref, ...), custom_call_target="tpu_custom_call" | custom-call | tf_op jit(solution)/shard_map/pallas_call | solution.py:274
  49.9 4.0 %collective-permute-start.10 = (f32[10,4,128]{2,1,0:T(4,128)}, f32[10,4,128]{2,1,0:T(4,128)S(1)}, u32[]{:S(2)}, u32[]{:S(2)}) collective-permute-start(f32[10,4,128]{2,1,0:T(4,128)} %get-tuple-element.34), channel_id=1, source_target_pairs={{0,1},{1,2},{2,3},{4,5},{5,6},{6,7},{8,9},{9,10},{10,11},{12,13},{... | collective-permute-start | bytes 61448 | tf_op jit(solution)/shard_map/ppermute | solution.py:342
  54.0 1.5 %collective-permute-start.11 = (f32[10,4,128]{2,1,0:T(4,128)}, f32[10,4,128]{2,1,0:T(4,128)S(1)}, u32[]{:S(2)}, u32[]{:S(2)}) collective-permute-start(f32[10,4,128]{2,1,0:T(4,128)} %get-tuple-element.35), channel_id=1, source_target_pairs={{1,0},{2,1},{3,2},{5,4},{6,5},{7,6},{9,8},{10,9},{11,10},{13,12},{... | collective-permute-start | bytes 61448 | tf_op jit(solution)/shard_map/ppermute | solution.py:343
  56.2 3.3 %shard_map.129.res_ref = f32[10,64,128]{2,1,0:T(8,128)} custom-call(f32[1122]{0:T(1024)} %concatenate.7.mat_ref.wt_ref, f32[1122]{0:T(1024)} %concatenate.7.mat_ref.wt_ref, f32[10,64,128]{2,1,0:T(8,128)} %get-tuple-element.32.psi_ref, f32[10,64,128]{2,1,0:T(8,128)} %bitcast.87, f32[6,64,128]{2,1,0:T(8,128)} %get-tuple-element.20.face_ref, ...), custom_call_target="tpu_custom_call" | custom-call | tf_op jit(solution)/shard_map/pallas_call | solution.py:262
  61.1 2.0 %shard_map.130 = (f32[10,64,128]{2,1,0:T(8,128)}, f32[3,64,128]{2,1,0:T(8,128)}) custom-call(f32[1122]{0:T(1024)} %concatenate.7.mat_ref.wt_ref, f32[1122]{0:T(1024)} %concatenate.7.mat_ref.wt_ref, f32[10,64,128]{2,1,0:T(8,128)} %get-tuple-element.32.psi_ref, f32[10,64,128]{2,1,0:T(8,128)} %shard_map.129.res_ref, f32[6,64,128]{2,1,0:T(8,128)} %get-tuple-element.20.face_ref, ...), custom_call_target="tpu_custom_call" | custom-call | tf_op jit(solution)/shard_map/pallas_call | solution.py:274
  64.0 2.6 %fusion = f32[576,8192]{1,0:T(8,128)S(1)} fusion(s32[8192]{0:T(1024)S(1)} %add_select_fusion, bf16[192,128]{1,0:T(8,128)(2,1)S(1)} %get-tuple-element.41, bf16[192,128]{1,0:T(8,128)(2,1)S(1)} %get-tuple-element.42, bf16[192,128]{1,0:T(8,128)(2,1)S(1)} %get-tuple-element.40), kind=kOutput, calls=%fused_computation.4 | convolution fusion | flops 1209450496 | bytes 19054592 | tf_op jit(solution)/shard_map/xl,lj->xj/dot_general | solution.py:368
  66.7 1.0 %slice_add_fusion = f32[192,8192]{1,0:T(8,128)S(1)} fusion(f32[576,8192]{1,0:T(8,128)S(1)} %fusion), kind=kLoop, calls=%fused_computation | loop fusion | flops 3145728 | bytes 25165824 | tf_op jit(solution)/shard_map/add | solution.py:371
  70.6 7.8 %all-to-all-start = ((f32[8,3,512]{2,1,0:T(4,128)}), f32[8,3,512]{2,1,0:T(4,128)S(1)}, u32[]{:S(2)}, u32[]{:S(2)}) async-start(f32[8,3,512]{2,1,0:T(4,128)} %select_add_fusion), calls=%async_computation | async-start | bytes 131072 | tf_op jit(solution)/shard_map/all_to_all | solution.py:42
  78.9 2.6 %shard_map.131 = f32[36,512]{1,0:T(8,128)} custom-call(s32[2,512]{1,0:T(2,128)} %pad_add_fusion.where_ref, bf16[2304,128]{1,0:T(8,128)(2,1)} %bitcast.101), custom_call_target="tpu_custom_call" | custom-call | tf_op jit(solution)/shard_map/pallas_call | solution.py:378
  82.4 3.8 %all-to-all-done = f32[8,3,512]{2,1,0:T(4,128)S(1)} async-done(((f32[8,3,512]{2,1,0:T(4,128)}), f32[8,3,512]{2,1,0:T(4,128)S(1)}, u32[]{:S(2)}, u32[]{:S(2)}) %all-to-all-start) | async-done | bytes 49184 | tf_op jit(solution)/shard_map/all_to_all | solution.py:42
  (65 shorter events, 18.9 us)
Async XLA Ops:
  6.9 11.3 %collective-permute-start = (f32[10,16,128]{2,1,0:T(8,128)}, f32[10,16,128]{2,1,0:T(8,128)S(1)}, u32[]{:S(2)}, u32[]{:S(2)}) collective-permute-start(f32[10,16,128]{2,1,0:T(8,128)} %get-tuple-element.21), channel_id=1, source_target_pairs={{0,4},{4,0},{1,5},{5,1},{2,6},{6,2},{3,7},{7,3},{8,12},{12,8},{9,1... | collective-permute-start | bytes 245768 | tf_op jit(solution)/shard_map/ppermute | solution.py:341
  8.9 8.9 %collective-permute-start.1 = (f32[10,4,128]{2,1,0:T(4,128)}, f32[10,4,128]{2,1,0:T(4,128)S(1)}, u32[]{:S(2)}, u32[]{:S(2)}) collective-permute-start(f32[10,4,128]{2,1,0:T(4,128)} %get-tuple-element.22), channel_id=1, source_target_pairs={{0,1},{1,2},{2,3},{4,5},{5,6},{6,7},{8,9},{9,10},{10,11},{12,13},{... | collective-permute-start | bytes 61448 | tf_op jit(solution)/shard_map/ppermute | solution.py:342
  12.3 5.9 %collective-permute-start.2 = (f32[10,4,128]{2,1,0:T(4,128)}, f32[10,4,128]{2,1,0:T(4,128)S(1)}, u32[]{:S(2)}, u32[]{:S(2)}) collective-permute-start(f32[10,4,128]{2,1,0:T(4,128)} %get-tuple-element.23), channel_id=1, source_target_pairs={{1,0},{2,1},{3,2},{5,4},{6,5},{7,6},{9,8},{10,9},{11,10},{13,12},{... | collective-permute-start | bytes 61448 | tf_op jit(solution)/shard_map/ppermute | solution.py:343
  17.8 0.6 copy-start.9
  18.8 0.6 copy-start.3
  21.5 10.2 %collective-permute-start.3 = (f32[10,16,128]{2,1,0:T(8,128)}, f32[10,16,128]{2,1,0:T(8,128)S(1)}, u32[]{:S(2)}, u32[]{:S(2)}) collective-permute-start(f32[10,16,128]{2,1,0:T(8,128)} %get-tuple-element.25), channel_id=1, source_target_pairs={{0,4},{4,0},{1,5},{5,1},{2,6},{6,2},{3,7},{7,3},{8,12},{12,8},{9,1... | collective-permute-start | bytes 245768 | tf_op jit(solution)/shard_map/ppermute | solution.py:341
  21.6 9.1 %collective-permute-start.4 = (f32[10,4,128]{2,1,0:T(4,128)}, f32[10,4,128]{2,1,0:T(4,128)S(1)}, u32[]{:S(2)}, u32[]{:S(2)}) collective-permute-start(f32[10,4,128]{2,1,0:T(4,128)} %get-tuple-element.26), channel_id=1, source_target_pairs={{0,1},{1,2},{2,3},{4,5},{5,6},{6,7},{8,9},{9,10},{10,11},{12,13},{... | collective-permute-start | bytes 61448 | tf_op jit(solution)/shard_map/ppermute | solution.py:342
  25.8 5.9 %collective-permute-start.5 = (f32[10,4,128]{2,1,0:T(4,128)}, f32[10,4,128]{2,1,0:T(4,128)S(1)}, u32[]{:S(2)}, u32[]{:S(2)}) collective-permute-start(f32[10,4,128]{2,1,0:T(4,128)} %get-tuple-element.27), channel_id=1, source_target_pairs={{1,0},{2,1},{3,2},{5,4},{6,5},{7,6},{9,8},{10,9},{11,10},{13,12},{... | collective-permute-start | bytes 61448 | tf_op jit(solution)/shard_map/ppermute | solution.py:343
  30.7 1.0 %copy-start.8 = (f32[10,4,128]{2,1,0:T(4,128)}, f32[10,4,128]{2,1,0:T(4,128)S(1)}, u32[]{:S(2)}) copy-start(f32[10,4,128]{2,1,0:T(4,128)S(1)} %collective-permute-done.4.ralo_ref) | copy-start | bytes 61444
  31.7 0.6 copy-start.10
  32.3 0.6 copy-start.2
  35.1 11.4 %collective-permute-start.6 = (f32[10,16,128]{2,1,0:T(8,128)}, f32[10,16,128]{2,1,0:T(8,128)S(1)}, u32[]{:S(2)}, u32[]{:S(2)}) collective-permute-start(f32[10,16,128]{2,1,0:T(8,128)} %get-tuple-element.29), channel_id=1, source_target_pairs={{0,4},{4,0},{1,5},{5,1},{2,6},{6,2},{3,7},{7,3},{8,12},{12,8},{9,1... | collective-permute-start | bytes 245768 | tf_op jit(solution)/shard_map/ppermute | solution.py:341
  37.0 8.9 %collective-permute-start.7 = (f32[10,4,128]{2,1,0:T(4,128)}, f32[10,4,128]{2,1,0:T(4,128)S(1)}, u32[]{:S(2)}, u32[]{:S(2)}) collective-permute-start(f32[10,4,128]{2,1,0:T(4,128)} %get-tuple-element.30), channel_id=1, source_target_pairs={{0,1},{1,2},{2,3},{4,5},{5,6},{6,7},{8,9},{9,10},{10,11},{12,13},{... | collective-permute-start | bytes 61448 | tf_op jit(solution)/shard_map/ppermute | solution.py:342
  40.6 5.9 %collective-permute-start.8 = (f32[10,4,128]{2,1,0:T(4,128)}, f32[10,4,128]{2,1,0:T(4,128)S(1)}, u32[]{:S(2)}, u32[]{:S(2)}) collective-permute-start(f32[10,4,128]{2,1,0:T(4,128)} %get-tuple-element.31), channel_id=1, source_target_pairs={{1,0},{2,1},{3,2},{5,4},{6,5},{7,6},{9,8},{10,9},{11,10},{13,12},{... | collective-permute-start | bytes 61448 | tf_op jit(solution)/shard_map/ppermute | solution.py:343
  46.0 0.6 copy-start.6
  46.5 0.6 copy-start.7
  47.1 0.6 copy-start.1
  49.8 10.0 %collective-permute-start.9 = (f32[10,16,128]{2,1,0:T(8,128)}, f32[10,16,128]{2,1,0:T(8,128)S(1)}, u32[]{:S(2)}, u32[]{:S(2)}) collective-permute-start(f32[10,16,128]{2,1,0:T(8,128)} %get-tuple-element.33), channel_id=1, source_target_pairs={{0,4},{4,0},{1,5},{5,1},{2,6},{6,2},{3,7},{7,3},{8,12},{12,8},{9,1... | collective-permute-start | bytes 245768 | tf_op jit(solution)/shard_map/ppermute | solution.py:341
  49.9 9.5 %collective-permute-start.10 = (f32[10,4,128]{2,1,0:T(4,128)}, f32[10,4,128]{2,1,0:T(4,128)S(1)}, u32[]{:S(2)}, u32[]{:S(2)}) collective-permute-start(f32[10,4,128]{2,1,0:T(4,128)} %get-tuple-element.34), channel_id=1, source_target_pairs={{0,1},{1,2},{2,3},{4,5},{5,6},{6,7},{8,9},{9,10},{10,11},{12,13},{... | collective-permute-start | bytes 61448 | tf_op jit(solution)/shard_map/ppermute | solution.py:342
  54.0 5.9 %collective-permute-start.11 = (f32[10,4,128]{2,1,0:T(4,128)}, f32[10,4,128]{2,1,0:T(4,128)S(1)}, u32[]{:S(2)}, u32[]{:S(2)}) collective-permute-start(f32[10,4,128]{2,1,0:T(4,128)} %get-tuple-element.35), channel_id=1, source_target_pairs={{1,0},{2,1},{3,2},{5,4},{6,5},{7,6},{9,8},{10,9},{11,10},{13,12},{... | collective-permute-start | bytes 61448 | tf_op jit(solution)/shard_map/ppermute | solution.py:343
  59.5 0.6 copy-start.4
  60.5 0.6 copy-start
  68.6 1.3 %collective-permute-start.12 = (f32[8,3,512]{2,1,0:T(4,128)S(1)}, f32[8,3,512]{2,1,0:T(4,128)S(1)}, u32[]{:S(2)}, u32[]{:S(2)}) collective-permute-start(f32[8,3,512]{2,1,0:T(4,128)S(1)} %slice_select_fusion), channel_id=1, source_target_pairs={{0,8},{8,0},{16,24},{24,16},{32,40},{40,32},{48,56},{56,48},{64,72... | collective-permute-start | bytes 147464 | tf_op jit(solution)/shard_map/ppermute | solution.py:40
  70.6 15.6 %all-to-all-start = ((f32[8,3,512]{2,1,0:T(4,128)}), f32[8,3,512]{2,1,0:T(4,128)S(1)}, u32[]{:S(2)}, u32[]{:S(2)}) async-start(f32[8,3,512]{2,1,0:T(4,128)} %select_add_fusion), calls=%async_computation | async-start | bytes 131072 | tf_op jit(solution)/shard_map/all_to_all | solution.py:42
  (2 other events, 1.2 us)
